TPU v7x, 128 devices: a whole 4x4x4 slice. The times are simulated.
128 devices in a mesh: gy: 64 (over z, y, x), pa: 2 (over core).
Axes of the slice: x: 4, y: 4, z: 4, core: 2. Of those that a mesh axis runs over, the one named last changes fastest.
Arguments:
- mass_per_volume: float32 [512, 128, 128], P('gy', 'pa'), may hold values from 0.5 to 1.5
- mass_flux_vector: float32 [3, 512, 128, 128], P(None, 'gy', 'pa'), may hold values from -1.5 to 1.5
- total_heat_content: float32 [512, 128, 128], P('gy', 'pa'), may hold values from 1.6 to 4.4
Outputs:
- time_rate: float32 [5, 512, 128, 128], P(None, 'gy', 'pa')
- smoothed: float32 [5, 512, 128, 128], P(None, 'gy', 'pa')
All inputs are finite; a program needn't handle non-finite values.
Results may differ from a plain program's by a relative error of at most 0.0003.
Values sent between devices are 32-bit elements; how exact they have to be, the bound alone decides.
No kernel may reach another device: no remote copies, remote signals or barrier semaphores. Data moves between devices by JAX's collectives and lax.ppermute only.
A program may use at most 256 MiB of HBM per device.

v0:
```python
import jax
import jax.numpy as jnp
import numpy as np
from jax import lax
from jax.sharding import PartitionSpec as P

GAMMA_GAS = 1.4
PRANDTL = 0.72
VISCOSITY = 0.25
ALPHA_FILTER = 0.499
ALPHA_SLOPE = 0.498
STRETCH = 1.2
STREAM_STEP = 1.0
SPAN_STEP = 0.5
HIGHEST = lax.Precision.HIGHEST


def entering(value, axis, join, neutral, backward):
    count, mine = (lax.axis_size(axis), lax.axis_index(axis))
    pieces = jax.tree.map(lambda part: lax.all_gather(part, axis), value)
    if backward:
        pieces = jax.tree.map(lambda part: part[::-1], pieces)
        mine = count - 1 - mine
    running = jax.tree.map(
        lambda part, zero: jnp.full_like(part, 0) + jnp.asarray(zero, part.dtype), value, neutral
    )

    def lap(position, running):
        longer = join(running, jax.tree.map(lambda part: part[position], pieces))
        return jax.tree.map(lambda new, old: jnp.where(position < mine, new, old), longer, running)

    return lax.fori_loop(0, count - 1, lap, running)


def extended(block, sides, width):
    for axis, dim in sides:
        count = lax.axis_size(axis)
        forward = [(i, i + 1) for i in range(count - 1)]
        backward = [(target, source) for source, target in forward]
        low = lax.ppermute(
            lax.slice_in_dim(block, block.shape[dim] - width, None, axis=dim), axis, forward
        )
        high = lax.ppermute(lax.slice_in_dim(block, 0, width, axis=dim), axis, backward)
        block = jnp.concatenate([low, block, high], axis=dim)
    return block


def slope_weights():
    near_weight = (2.0 + ALPHA_SLOPE) / 3.0
    far_weight = (4.0 * ALPHA_SLOPE - 1.0) / 12.0
    return (near_weight, far_weight)


def system_rows(system_kind, points):
    lower = np.zeros(points)
    middle = np.ones(points)
    upper = np.zeros(points)
    weights = np.zeros((7, points))
    if system_kind == "slope":
        near_weight, far_weight = slope_weights()
        lower[:] = ALPHA_SLOPE
        upper[:] = ALPHA_SLOPE
        weights[1] = -far_weight
        weights[2] = -near_weight
        weights[4] = near_weight
        weights[5] = far_weight
        for edge_row in (1, points - 2):
            lower[edge_row] = 0.25
            upper[edge_row] = 0.25
            weights[:, edge_row] = 0.0
            weights[2, edge_row] = -0.75
            weights[4, edge_row] = 0.75
        lower[0] = 0.0
        upper[0] = 2.0
        weights[:, 0] = 0.0
        weights[3, 0] = -2.5
        weights[4, 0] = 2.0
        weights[5, 0] = 0.5
        lower[points - 1] = 2.0
        upper[points - 1] = 0.0
        weights[:, points - 1] = 0.0
        weights[3, points - 1] = 2.5
        weights[2, points - 1] = -2.0
        weights[1, points - 1] = -0.5
    else:
        strength = ALPHA_FILTER
        lower[:] = strength
        upper[:] = strength
        weights[3] = 11.0 / 16.0 + 5.0 * strength / 8.0
        weights[2] = 15.0 / 64.0 + 17.0 * strength / 32.0
        weights[4] = weights[2]
        weights[1] = -3.0 / 32.0 + 3.0 * strength / 16.0
        weights[5] = weights[1]
        weights[0] = 1.0 / 64.0 - strength / 32.0
        weights[6] = weights[0]
        for edge_row in (2, points - 3):
            weights[:, edge_row] = 0.0
            weights[3, edge_row] = 5.0 / 8.0 + 3.0 * strength / 4.0
            weights[2, edge_row] = 0.25 + strength / 2.0
            weights[4, edge_row] = 0.25 + strength / 2.0
            weights[1, edge_row] = -1.0 / 16.0 + strength / 8.0
            weights[5, edge_row] = -1.0 / 16.0 + strength / 8.0
        for edge_row in (1, points - 2):
            weights[:, edge_row] = 0.0
            weights[3, edge_row] = 0.5 + strength
            weights[2, edge_row] = 0.25 + strength / 2.0
            weights[4, edge_row] = 0.25 + strength / 2.0
        for edge_row in (0, points - 1):
            lower[edge_row] = 0.0
            upper[edge_row] = 0.0
            weights[:, edge_row] = 0.0
            weights[3, edge_row] = 1.0
    return (lower, middle, upper, weights)


def inverse_metric(points):
    places = 2.0 * np.arange(points) / (points - 1) - 1.0
    growth = np.exp(STRETCH * places)
    cosh_values = 0.5 * (growth + 1.0 / growth)
    edge_growth = np.exp(STRETCH)
    tanh_value = (edge_growth - 1.0 / edge_growth) / (edge_growth + 1.0 / edge_growth)
    return tanh_value * cosh_values**2 / (0.64 * STRETCH)


def periodic_matrix(points, spacing):
    near_weight, far_weight = slope_weights()
    wave_numbers = np.arange(1, points // 2)
    angles = 2.0 * np.pi * wave_numbers / points
    modified = (2.0 * near_weight * np.sin(angles) + 2.0 * far_weight * np.sin(2.0 * angles)) / (
        1.0 + 2.0 * ALPHA_SLOPE * np.cos(angles)
    )
    phases = np.arange(points)[:, None] * wave_numbers[None, :] % points
    circulant = -2.0 / (points * spacing) * (np.sin(2.0 * np.pi * phases / points) @ modified)
    shifts = (np.arange(points)[:, None] - np.arange(points)[None, :]) % points
    return circulant[shifts].T


def lower_inverse(diagonal, below):
    size_rows = diagonal.shape[0]
    result = np.zeros((size_rows, size_rows))
    for row_at in range(size_rows):
        result[row_at, row_at] = 1.0 / diagonal[row_at]
        if row_at > 0:
            result[row_at, :row_at] = (
                -below[row_at] * result[row_at - 1, :row_at] / diagonal[row_at]
            )
    return result


def upper_inverse(diagonal, above):
    size_rows = diagonal.shape[0]
    result = np.zeros((size_rows, size_rows))
    for row_at in range(size_rows - 1, -1, -1):
        result[row_at, row_at] = 1.0 / diagonal[row_at]
        if row_at < size_rows - 1:
            result[row_at, row_at + 1 :] = (
                -above[row_at] * result[row_at + 1, row_at + 1 :] / diagonal[row_at]
            )
    return result


def chain_tables(system_kind, points, block_rows):
    lower, middle, upper, weights = system_rows(system_kind, points)
    forward_den = np.zeros(points)
    forward_ratio = np.zeros(points)
    carried = 0.0
    for row_at in range(points):
        forward_den[row_at] = middle[row_at] - lower[row_at] * carried
        forward_ratio[row_at] = upper[row_at] / forward_den[row_at]
        carried = forward_ratio[row_at]
    backward_den = np.zeros(points)
    backward_ratio = np.zeros(points)
    carried = 0.0
    for row_at in range(points - 1, -1, -1):
        backward_den[row_at] = middle[row_at] - upper[row_at] * carried
        backward_ratio[row_at] = lower[row_at] / backward_den[row_at]
        carried = backward_ratio[row_at]
    before_ratio = np.concatenate([np.zeros(1), forward_ratio[:-1]])
    after_ratio = np.concatenate([backward_ratio[1:], np.zeros(1)])
    twist_den = middle - lower * before_ratio - upper * after_ratio
    blocks = points // block_rows
    lift_inverse = np.zeros((blocks, block_rows, block_rows))
    settle_inverse = np.zeros((blocks, block_rows, block_rows))
    descend_inverse = np.zeros((blocks, block_rows, block_rows))
    lift_gain = np.zeros((blocks, block_rows))
    settle_gain = np.zeros((blocks, block_rows))
    descend_gain = np.zeros((blocks, block_rows))
    for block_at in range(blocks):
        first_row = block_at * block_rows
        last_row = first_row + block_rows - 1
        window = slice(first_row, last_row + 1)
        lift_inverse[block_at] = lower_inverse(forward_den[window], lower[window])
        lift_gain[block_at] = -lower[first_row] * lift_inverse[block_at][:, 0]
        settle_inverse[block_at] = upper_inverse(np.ones(block_rows), forward_ratio[window])
        settle_gain[block_at] = -forward_ratio[last_row] * settle_inverse[block_at][:, -1]
        descend_inverse[block_at] = upper_inverse(backward_den[window], upper[window])
        descend_gain[block_at] = -upper[last_row] * descend_inverse[block_at][:, -1]
    shaped = (blocks, block_rows)
    return (
        lift_inverse,
        lift_gain,
        settle_inverse,
        settle_gain,
        descend_inverse,
        descend_gain,
        lower.reshape(shaped),
        upper.reshape(shaped),
        twist_den.reshape(shaped),
        weights.reshape(7, blocks, block_rows).transpose(1, 0, 2),
    )


def section_tables(kind_list, points, block_rows, position):
    per_kind = {
        "slope": chain_tables("slope", points, block_rows),
        "smooth": chain_tables("smooth", points, block_rows),
    }
    picked = []
    for member in range(10):
        stacked = np.stack([per_kind[kind_name][member] for kind_name in kind_list])
        picked.append(
            lax.dynamic_index_in_dim(jnp.asarray(stacked, jnp.float32), position, 1, keepdims=False)
        )
    return picked


def stencil_sum(padded, weights, rim_rows):
    rows_here = padded.shape[1] - 2 * rim_rows
    summed = jnp.zeros((padded.shape[0], rows_here, padded.shape[2]), jnp.float32)
    for offset in range(-rim_rows, rim_rows + 1):
        summed = (
            summed
            + weights[:, 3 + offset, :, None]
            * padded[:, rim_rows + offset : rim_rows + offset + rows_here]
        )
    return summed


def affine_combine(earlier, nearer):
    return (nearer[0] * earlier[0], nearer[0][:, None] * earlier[1] + nearer[1])


def lift_scan(gain_last, value_last):
    neutral = (jnp.ones_like(gain_last), jnp.zeros_like(value_last))
    return entering((gain_last, value_last), "gy", affine_combine, neutral, False)[1]


def settle_scan(gain_first, value_first):
    neutral = (jnp.ones_like(gain_first), jnp.zeros_like(value_first))
    return entering((gain_first, value_first), "gy", affine_combine, neutral, True)[1]


def chain_solve(right_side, tables):
    (
        lift_inverse,
        lift_gain,
        settle_inverse,
        settle_gain,
        descend_inverse,
        descend_gain,
        lower_rows,
        upper_rows,
        twist_rows,
    ) = tables[:9]
    forward = jnp.einsum("fij,fjl->fil", lift_inverse, right_side, precision=HIGHEST)
    arriving = lift_scan(lift_gain[:, -1], forward[:, -1])
    forward = forward + lift_gain[:, :, None] * arriving[:, None, :]
    settled = jnp.einsum("fij,fjl->fil", settle_inverse, forward, precision=HIGHEST)
    coming = settle_scan(settle_gain[:, 0], settled[:, 0])
    return settled + settle_gain[:, :, None] * coming[:, None, :]


def stream_slope(fields, stream_matrix):
    flat_rows = fields.reshape(-1, stream_matrix.shape[0])
    return jnp.dot(
        flat_rows, stream_matrix, precision=HIGHEST, preferred_element_type=jnp.float32
    ).reshape(fields.shape)


def span_slope(fields, span_matrix):
    turned = jnp.einsum(
        "fyzx,zw->fywx",
        lax.all_to_all(fields, "pa", split_axis=3, concat_axis=2, tiled=True),
        span_matrix,
        precision=HIGHEST,
    )
    return lax.all_to_all(turned, "pa", split_axis=2, concat_axis=3, tiled=True)


def recover_basic_quantities(mass_per_volume, mass_flux_vector, total_heat_content):
    fluid_speed_vector = mass_flux_vector / mass_per_volume[None]
    kinetic = 0.5 * jnp.sum(fluid_speed_vector * mass_flux_vector, axis=0)
    thermo_push = (GAMMA_GAS - 1.0) * (total_heat_content - kinetic)
    thermo_warmth = thermo_push / mass_per_volume
    return (fluid_speed_vector, thermo_push, thermo_warmth)


def flux_along(
    direction, mass_flux_vector, total_heat_content, fluid_speed_vector, thermo_push, gradients
):
    divergence = gradients[0][0] + gradients[1][1] + gradients[2][2]
    conduct = VISCOSITY * GAMMA_GAS / ((GAMMA_GAS - 1.0) * PRANDTL)
    rows_out = [mass_flux_vector[direction]]
    energy_flux = (total_heat_content + thermo_push) * fluid_speed_vector[direction]
    for component in range(3):
        stress = VISCOSITY * (gradients[direction][component] + gradients[component][direction])
        if component == direction:
            stress = stress - 2.0 / 3.0 * VISCOSITY * divergence
            rows_out.append(
                mass_flux_vector[component] * fluid_speed_vector[direction] + thermo_push - stress
            )
        else:
            rows_out.append(mass_flux_vector[component] * fluid_speed_vector[direction] - stress)
        energy_flux = energy_flux - fluid_speed_vector[component] * stress
    energy_flux = energy_flux - conduct * gradients[direction][3]
    rows_out.append(energy_flux)
    return jnp.stack(rows_out)


def per_device(mass_per_volume, mass_flux_vector, total_heat_content):
    block_rows, span_own, stream_cells = mass_per_volume.shape
    line_count = span_own * stream_cells
    points = block_rows * lax.axis_size("gy")
    position = lax.axis_index("gy")
    stream_matrix = jnp.asarray(periodic_matrix(stream_cells, STREAM_STEP), jnp.float32)
    span_matrix = jnp.asarray(
        periodic_matrix(span_own * lax.axis_size("pa"), SPAN_STEP), jnp.float32
    )
    metric_full = jnp.asarray(inverse_metric(points), jnp.float32)
    metric_here = lax.dynamic_slice_in_dim(metric_full, position * block_rows, block_rows)
    state_all = jnp.concatenate(
        [mass_per_volume[None], mass_flux_vector, total_heat_content[None]], axis=0
    ).reshape(5, block_rows, line_count)
    section_kinds = ["smooth"] * 5 + ["slope"] * 4
    padded = extended(state_all, (("gy", 1),), 3)
    global_rows = position * block_rows - 3 + jnp.arange(block_rows + 6)
    inside = (global_rows >= 0) & (global_rows < points)
    safe_density = jnp.where(inside[:, None], padded[0], 1.0)
    padded_fluid_speed, padded_thermo_push, padded_thermo_warmth = recover_basic_quantities(
        safe_density, padded[1:4], padded[4]
    )
    padded_basic_quantities = jnp.concatenate(
        [padded_fluid_speed, padded_thermo_warmth[None]], axis=0
    )
    tables = section_tables(section_kinds, points, block_rows, position)
    right_side = stencil_sum(
        jnp.concatenate([padded, padded_basic_quantities], axis=0), tables[9], 3
    )
    solved = chain_solve(right_side, tables)
    smoothed_flat = solved[:5]
    slopes = solved[5:]
    wall_grad = slopes * metric_here[None, :, None]
    basic_quantities = padded_basic_quantities[:, 3 : 3 + block_rows]
    thermo_push = padded_thermo_push[3 : 3 + block_rows]
    fluid_speed_vector = basic_quantities[:3]
    grid_shape = (block_rows, span_own, stream_cells)
    grad_stream = stream_slope(basic_quantities, stream_matrix)
    grad_span = span_slope(basic_quantities.reshape((4,) + grid_shape), span_matrix).reshape(
        4, block_rows, line_count
    )
    gradients = [grad_stream, wall_grad, grad_span]
    momentum_flat = state_all[1:4]
    energy_flat = state_all[4]
    time_rate = -stream_slope(
        flux_along(0, momentum_flat, energy_flat, fluid_speed_vector, thermo_push, gradients),
        stream_matrix,
    )
    flux_wall = flux_along(
        1, momentum_flat, energy_flat, fluid_speed_vector, thermo_push, gradients
    )
    flux_padded = extended(flux_wall, (("gy", 1),), 2)
    tables = section_tables(["slope"] * 5, points, block_rows, position)
    flux_side = stencil_sum(flux_padded, tables[9], 2)
    wall_solved = chain_solve(flux_side, tables)
    wall_term = wall_solved * metric_here[None, :, None]
    time_rate = time_rate - wall_term
    flux_span = flux_along(
        2, momentum_flat, energy_flat, fluid_speed_vector, thermo_push, gradients
    )
    time_rate = time_rate - span_slope(flux_span.reshape((5,) + grid_shape), span_matrix).reshape(
        5, block_rows, line_count
    )
    own_rows = position * block_rows + jnp.arange(block_rows)
    at_wall = (own_rows == 0) | (own_rows == points - 1)
    held_rows = jnp.where(at_wall[None, :, None], 0.0, time_rate[1:4])
    time_rate = jnp.concatenate([time_rate[:1], held_rows, time_rate[4:]], axis=0)
    return (time_rate.reshape((5,) + grid_shape), smoothed_flat.reshape((5,) + grid_shape))


def solution(mesh):
    placed = (P("gy", "pa", None), P(None, "gy", "pa", None), P("gy", "pa", None))
    return jax.shard_map(
        per_device,
        mesh=mesh,
        in_specs=placed,
        out_specs=(P(None, "gy", "pa", None), P(None, "gy", "pa", None)),
        check_vma=False,
    )
```

profile of v0, /device:TPU:30, one launch (start us, length us, event | category | flops | bytes accessed | tf_op | source)
XLA Modules:
  0.0 1422.6 jit_solution(6548106128009721531)
XLA Ops:
  20.9 8.4 collective-permute-done
  29.3 7.1 collective-permute-done.1
  52.9 304.0 %all-reduce.4 = (f32[576]{0:T(1024)S(1)}, f32[576]{0:T(1024)S(1)}, f32[320]{0:T(512)}, f32[320]{0:T(512)}) all-reduce(f32[576]{0:T(1024)S(1)} %bitcast_dynamic-update-slice_fusion.2, f32[576]{0:T(1024)S(1)} %bitcast_dynamic-update-slice_fusion.1, f32[320]{0:T(512)S(1)} %dynamic-update-slice.2, ...), channel_id=2, replica_groups=mesh['gy'=64,'pa'=2] {'gy'}, use_global_device_ids=true, to_apply=%add | all-reduce | flops 1792 | bytes 14336
  357.0 53.6 %reduce = f32[576,8192]{1,0:T(8,128)} reduce(f32[576,1,8192]{2,1,0:T(1,128)} %all-gather.13.cloned.1.call-done, f32[]{:T(128)} %constant.229), dimensions={1}, to_apply=%all-gather.1.reduce_sub_computation | reduce | bytes 37748740 | tf_op jit(solution)/shard_map/all_gather | solution.py:20
  410.5 18.7 %reshape.188 = f32[64,9,8192]{2,1,0:T(8,128)} reshape(f32[576,8192]{1,0:T(8,128)} %reduce) | data formatting | bytes 37748736 | tf_op jit(solution)/shard_map/all_gather | solution.py:20
  429.2 76.3 %while.56 = (s32[]{:T(128)}, f32[9,8192]{1,0:T(8,128)S(1)}, s32[]{:T(128)}, f32[64,9]{1,0:T(8,128)S(1)}, f32[64,9,8192]{2,1,0:T(8,128)}, /*index=5*/s32[]{:T(128)}, s32[]{:T(128)}) while((s32[]{:T(128)}, f32[9,8192]{1,0:T(8,128)S(1)}, s32[]{:T(128)}, f32[64,9]{1,0:T(8,128)S(1)}, f32[64,9,8192]{2,1,0:T(8,128)}, ...), condition=%wide.region_2.3_spmd.clone, body=%wide.region_1.2_spmd.clone.sunk | while | flops 294916 | bytes 884949 | solution.py:32
  511.8 9.8 all-gather.17.cloned.1.call-start
  536.5 6.6 all_to_all.66
  573.1 6.8 all_to_all.67
  611.3 45.7 %all-gather.15.cloned.1.call-done = f32[576,1,8192]{2,1,0:T(1,128)} async-done(((f32[9,1,8192]{2,1,0:T(1,128)}), f32[576,1,8192]{2,1,0:T(1,128)}) %all-gather.15.cloned.1.call-update) | async-done | bytes 18874384 | tf_op jit(solution)/shard_map/all_gather | solution.py:20
  656.9 54.0 %reduce.1 = f32[576,8192]{1,0:T(8,128)} reduce(f32[576,1,8192]{2,1,0:T(1,128)} %all-gather.15.cloned.1.call-done, f32[]{:T(128)} %constant.229), dimensions={1}, to_apply=%all-gather.3.reduce_sub_computation | reduce | bytes 37748740 | tf_op jit(solution)/shard_map/all_gather | solution.py:20
  710.9 18.7 %reshape.190 = f32[64,9,8192]{2,1,0:T(8,128)} reshape(f32[576,8192]{1,0:T(8,128)} %reduce.1) | data formatting | bytes 37748736 | tf_op jit(solution)/shard_map/all_gather | solution.py:20
  729.6 22.7 %rev.13 = f32[64,9,8192]{2,1,0:T(8,128)} reverse(f32[64,9,8192]{2,1,0:T(8,128)} %reshape.190), dimensions={0} | reverse | bytes 37748736 | tf_op jit(solution)/shard_map/rev | solution.py:22
  752.3 118.0 %while.57 = (s32[]{:T(128)}, f32[9,8192]{1,0:T(8,128)S(1)}, s32[]{:T(128)}, f32[64,9]{1,0:T(8,128)}, f32[64,9,8192]{2,1,0:T(8,128)}, /*index=5*/s32[]{:T(128)}, s32[]{:T(128)}) while((s32[]{:T(128)}, f32[9,8192]{1,0:T(8,128)S(1)}, s32[]{:T(128)}, f32[64,9]{1,0:T(8,128)}, f32[64,9,8192]{2,1,0:T(8,128)}, /*index=5*/s32[]{:T(128)}, ...), condition=%wide.region_4.5_spmd.clone, body=%wide.region_3.4_spmd.clone.sunk | while | flops 294916 | bytes 884949 | solution.py:32
  889.5 7.1 collective-permute-done.3
  902.4 85.1 %all-gather.17.cloned.1.call-done = f32[320,1,8192]{2,1,0:T(1,128)} async-done(((f32[5,1,8192]{2,1,0:T(1,128)}), f32[320,1,8192]{2,1,0:T(1,128)}) %all-gather.17.cloned.1.call-update) | async-done | bytes 10485776 | tf_op jit(solution)/shard_map/all_gather | solution.py:20
  987.5 30.8 %reduce.3 = f32[320,8192]{1,0:T(8,128)} reduce(f32[320,1,8192]{2,1,0:T(1,128)} %all-gather.17.cloned.1.call-done, f32[]{:T(128)} %constant.229), dimensions={1}, to_apply=%all-gather.5.reduce_sub_computation | reduce | bytes 20971524 | tf_op jit(solution)/shard_map/all_gather | solution.py:20
  1018.3 11.4 reshape.192
  1029.7 110.6 %while.58 = (s32[]{:T(128)}, f32[5,8192]{1,0:T(8,128)S(1)}, s32[]{:T(128)}, f32[64,5]{1,0:T(8,128)}, f32[64,5,8192]{2,1,0:T(8,128)}, /*index=5*/s32[]{:T(128)}, s32[]{:T(128)}) while((s32[]{:T(128)}, f32[5,8192]{1,0:T(8,128)S(1)}, s32[]{:T(128)}, f32[64,5]{1,0:T(8,128)}, f32[64,5,8192]{2,1,0:T(8,128)}, /*index=5*/s32[]{:T(128)}, ...), condition=%wide.region_6.7_spmd.clone, body=%wide.region_5.6_spmd.clone.sunk | while | flops 163844 | bytes 491685 | solution.py:32
  1219.3 6.2 all_to_all.69
  1248.0 30.6 %reduce.5 = f32[320,8192]{1,0:T(8,128)} reduce(f32[320,1,8192]{2,1,0:T(1,128)} %all-gather.19.cloned.1.call-done, f32[]{:T(128)} %constant.229), dimensions={1}, to_apply=%all-gather.7.reduce_sub_computation | reduce | bytes 20971524 | tf_op jit(solution)/shard_map/all_gather | solution.py:20
  1278.6 11.4 reshape.194
  1290.0 11.6 rev.15
  1301.6 110.4 %while.59 = (s32[]{:T(128)}, f32[5,8192]{1,0:T(8,128)S(1)}, s32[]{:T(128)}, f32[64,5]{1,0:T(8,128)}, f32[64,5,8192]{2,1,0:T(8,128)}, /*index=5*/s32[]{:T(128)}, s32[]{:T(128)}) while((s32[]{:T(128)}, f32[5,8192]{1,0:T(8,128)S(1)}, s32[]{:T(128)}, f32[64,5]{1,0:T(8,128)}, f32[64,5,8192]{2,1,0:T(8,128)}, /*index=5*/s32[]{:T(128)}, ...), condition=%wide.region_8.9_spmd.clone, body=%wide.region_7.8_spmd.clone.sunk | while | flops 163844 | bytes 491685 | solution.py:32
  (761 shorter events, 650.8 us)
Async XLA Ops:
  7.2 2.4 copy-start.14
  7.2 349.8 %all-gather.13.cloned.1.call-start = ((), (), s32[]{:S(2)}) async-start(), calls=%async_computation.4 | async-start | bytes 19169280 | tf_op jit(solution)/shard_map/all_gather | solution.py:20
  10.8 18.6 %collective-permute-start = (f32[5,3,8192]{2,1,0:T(4,128)}, f32[5,3,8192]{2,1,0:T(4,128)S(1)}, u32[]{:S(2)}, u32[]{:S(2)}) collective-permute-start(f32[5,3,8192]{2,1,0:T(4,128)} %get-tuple-element.526), channel_id=1, source_target_pairs={{0,2},{2,4},{4,6},{6,8},{8,10},{10,12},{12,14},{14,16},{16,18},{18... | collective-permute-start | bytes 1474568 | tf_op jit(solution)/shard_map/ppermute | solution.py:40
  14.2 22.3 %collective-permute-start.1 = (f32[5,3,8192]{2,1,0:T(4,128)S(1)}, f32[5,3,8192]{2,1,0:T(4,128)S(1)}, u32[]{:S(2)}, u32[]{:S(2)}) collective-permute-start(f32[5,3,8192]{2,1,0:T(4,128)S(1)} %get-tuple-element.527), channel_id=1, source_target_pairs={{2,0},{4,2},{6,4},{8,6},{10,8},{12,10},{14,12},{16,14},{18,16},{20... | collective-permute-start | bytes 1474568 | tf_op jit(solution)/shard_map/ppermute | solution.py:43
  41.1 7.4 copy-start.51
  48.4 608.5 %all-gather.15.cloned.1.call-start = ((), (), s32[]{:S(2)}) async-start(), calls=%async_computation.5 | async-start | bytes 19169280 | tf_op jit(solution)/shard_map/all_gather | solution.py:20
  51.9 358.6 %copy-start.42 = (f32[5,8]{1,0:T(8,128)}, f32[5,8]{1,0:T(8,128)S(1)}, u32[]{:S(2)}) copy-start(f32[5,8]{1,0:T(8,128)S(1)} %get-tuple-element.551) | copy-start | bytes 484
  511.8 475.7 %all-gather.17.cloned.1.call-start = ((), (), s32[]{:S(2)}) async-start(), calls=%async_computation.6 | async-start | bytes 10649600 | tf_op jit(solution)/shard_map/all_gather | solution.py:20
  522.5 5.4 copy-start.5
  525.6 3.4 copy-start.18
  556.9 2.8 copy-start.40
  599.9 2.4 copy-start.41
  605.7 4.7 copy-start.11
  605.8 266.9 %copy-start.20 = (f32[1,8,8192]{2,1,0:T(8,128)}, f32[1,8,8192]{2,1,0:T(8,128)S(1)}, u32[]{:S(2)}) copy-start(f32[1,8,8192]{2,1,0:T(8,128)S(1)} %squeeze.187) | copy-start | bytes 786436
  870.3 2.3 copy-start.39
  878.2 11.3 collective-permute-start.2
  881.4 15.3 %collective-permute-start.3 = (f32[5,2,8192]{2,1,0:T(2,128)S(1)}, f32[5,2,8192]{2,1,0:T(2,128)S(1)}, u32[]{:S(2)}, u32[]{:S(2)}) collective-permute-start(f32[5,2,8192]{2,1,0:T(2,128)S(1)} %get-tuple-element.525), channel_id=1, source_target_pairs={{2,0},{4,2},{6,4},{8,6},{10,8},{12,10},{14,12},{16,14},{18,16},{20... | collective-permute-start | bytes 983048 | tf_op jit(solution)/shard_map/ppermute | solution.py:43
  896.7 5.0 copy-start.50
  901.6 346.4 %all-gather.19.cloned.1.call-start = ((), (), s32[]{:S(2)}) async-start(), calls=%async_computation.7 | async-start | bytes 10649600 | tf_op jit(solution)/shard_map/all_gather | solution.py:20
  1140.3 5.5 copy-start.49
  1176.3 2.5 copy-start.33
  1176.3 2.7 copy-start.38
  1290.0 122.0 %copy-start.9 = (f32[5,8,8192]{2,1,0:T(8,128)S(1)}, f32[5,8,8192]{2,1,0:T(8,128)}, u32[]{:S(2)}) copy-start(f32[5,8,8192]{2,1,0:T(8,128)} %copy-done.8) | copy-start | bytes 3932164
  1301.6 110.5 %copy-start.43 = (f32[5,8]{1,0:T(8,128)S(1)}, f32[5,8]{1,0:T(8,128)}, u32[]{:S(2)}) copy-start(f32[5,8]{1,0:T(8,128)} %copy-done.42) | copy-start | bytes 484
  (36 other events, 52.4 us)
Sparse Core Ops, SparseCore 0:
  48.6 111.5 all-gather.12
  511.9 144.9 all-gather.14
  901.7 85.7 all-gather.16
  1144.9 84.9 all-gather.18
where the time goes:
time: 1450 us; the launch traced here: 1420 us
  other arithmetic  492 us (34%)
  local copies, waits for them, and re-layouts  367 us (25%)
  blocking collectives  330 us (23%)
  waiting for transfers between devices  158 us (11%)
  matrix products  32.4 us (2%)
  starting transfers between devices  21.6 us (1%)
  between operations  16.2 us (1%)
    unnamed x1, blocking collectives  304 us
    select_n x252, other arithmetic, lap(): jnp.where(position < mine, new, old)  279 us
    all_gather x4, other arithmetic, entering(): pieces = jax.tree.map(lambda part: lax.all_gather(part, axis), value)  169 us
    all_gather x4, waiting for transfers between devices, entering(): pieces = jax.tree.map(lambda part: lax.all_gather(part, axis), value)  131 us
    mul x252, local copies, waits for them, and re-layouts, affine_combine(): return (nearer[0] * earlier[0], nearer[0][:, None] * earlier[1] + nearer[1])  131 us
    all_gather x8, local copies, waits for them, and re-layouts, entering(): pieces = jax.tree.map(lambda part: lax.all_gather(part, axis), value)  61.9 us
    unnamed x132, local copies, waits for them, and re-layouts  53.3 us
    rev x4, local copies, waits for them, and re-layouts, entering(): pieces = jax.tree.map(lambda part: part[::-1], pieces)  36.3 us
  transfers between devices with their start and end apart: 8, of which 6 were waited for; matrix products, arithmetic and copies ran while one was open for 12% of the time, Pallas kernels for 0%

commit v1 on v0

v1 whole, which is shorter than its diff:
```python
import functools

import jax
import jax.numpy as jnp
import numpy as np
from jax import lax
from jax.sharding import PartitionSpec as P

GAMMA_GAS = 1.4
PRANDTL = 0.72
VISCOSITY = 0.25
ALPHA_FILTER = 0.499
ALPHA_SLOPE = 0.498
STRETCH = 1.2
STREAM_STEP = 1.0
SPAN_STEP = 0.5
HIGHEST = lax.Precision.HIGHEST


def slope_weights():
    near_weight = (2.0 + ALPHA_SLOPE) / 3.0
    far_weight = (4.0 * ALPHA_SLOPE - 1.0) / 12.0
    return (near_weight, far_weight)


def system_rows(system_kind, points):
    lower = np.zeros(points)
    middle = np.ones(points)
    upper = np.zeros(points)
    weights = np.zeros((7, points))
    if system_kind == "slope":
        near_weight, far_weight = slope_weights()
        lower[:] = ALPHA_SLOPE
        upper[:] = ALPHA_SLOPE
        weights[1] = -far_weight
        weights[2] = -near_weight
        weights[4] = near_weight
        weights[5] = far_weight
        for edge_row in (1, points - 2):
            lower[edge_row] = 0.25
            upper[edge_row] = 0.25
            weights[:, edge_row] = 0.0
            weights[2, edge_row] = -0.75
            weights[4, edge_row] = 0.75
        lower[0] = 0.0
        upper[0] = 2.0
        weights[:, 0] = 0.0
        weights[3, 0] = -2.5
        weights[4, 0] = 2.0
        weights[5, 0] = 0.5
        lower[points - 1] = 2.0
        upper[points - 1] = 0.0
        weights[:, points - 1] = 0.0
        weights[3, points - 1] = 2.5
        weights[2, points - 1] = -2.0
        weights[1, points - 1] = -0.5
    else:
        strength = ALPHA_FILTER
        lower[:] = strength
        upper[:] = strength
        weights[3] = 11.0 / 16.0 + 5.0 * strength / 8.0
        weights[2] = 15.0 / 64.0 + 17.0 * strength / 32.0
        weights[4] = weights[2]
        weights[1] = -3.0 / 32.0 + 3.0 * strength / 16.0
        weights[5] = weights[1]
        weights[0] = 1.0 / 64.0 - strength / 32.0
        weights[6] = weights[0]
        for edge_row in (2, points - 3):
            weights[:, edge_row] = 0.0
            weights[3, edge_row] = 5.0 / 8.0 + 3.0 * strength / 4.0
            weights[2, edge_row] = 0.25 + strength / 2.0
            weights[4, edge_row] = 0.25 + strength / 2.0
            weights[1, edge_row] = -1.0 / 16.0 + strength / 8.0
            weights[5, edge_row] = -1.0 / 16.0 + strength / 8.0
        for edge_row in (1, points - 2):
            weights[:, edge_row] = 0.0
            weights[3, edge_row] = 0.5 + strength
            weights[2, edge_row] = 0.25 + strength / 2.0
            weights[4, edge_row] = 0.25 + strength / 2.0
        for edge_row in (0, points - 1):
            lower[edge_row] = 0.0
            upper[edge_row] = 0.0
            weights[:, edge_row] = 0.0
            weights[3, edge_row] = 1.0
    return (lower, middle, upper, weights)


def inverse_metric(points):
    places = 2.0 * np.arange(points) / (points - 1) - 1.0
    growth = np.exp(STRETCH * places)
    cosh_values = 0.5 * (growth + 1.0 / growth)
    edge_growth = np.exp(STRETCH)
    tanh_value = (edge_growth - 1.0 / edge_growth) / (edge_growth + 1.0 / edge_growth)
    return tanh_value * cosh_values**2 / (0.64 * STRETCH)


def periodic_matrix(points, spacing):
    near_weight, far_weight = slope_weights()
    wave_numbers = np.arange(1, points // 2)
    angles = 2.0 * np.pi * wave_numbers / points
    modified = (2.0 * near_weight * np.sin(angles) + 2.0 * far_weight * np.sin(2.0 * angles)) / (
        1.0 + 2.0 * ALPHA_SLOPE * np.cos(angles)
    )
    phases = np.arange(points)[:, None] * wave_numbers[None, :] % points
    circulant = -2.0 / (points * spacing) * (np.sin(2.0 * np.pi * phases / points) @ modified)
    shifts = (np.arange(points)[:, None] - np.arange(points)[None, :]) % points
    return circulant[shifts].T


@functools.lru_cache(maxsize=None)
def wall_tables(kind, points, rows, pad):
    lower, middle, upper, weights = system_rows(kind, points)
    system = np.diag(middle) + np.diag(lower[1:], -1) + np.diag(upper[:-1], 1)
    inv = np.linalg.inv(system)
    stencil = np.zeros((points, points + 6))
    for row in range(points):
        for offset in range(-3, 4):
            if weights[3 + offset, row] != 0.0:
                assert abs(offset) <= pad and 0 <= row + offset < points
                stencil[row, row + offset + 3] = weights[3 + offset, row]
    scale = inverse_metric(points) if kind == "slope" else np.ones(points)
    blocks = points // rows
    combine = np.zeros((blocks, rows + 2, rows + 2 * pad))
    rise_gain = np.zeros((blocks, rows))
    fall_gain = np.zeros((blocks, rows))
    rise_step = np.zeros(blocks)
    fall_step = np.zeros(blocks)
    for block in range(blocks):
        lo, hi = block * rows, block * rows + rows
        own = slice(lo, hi)
        rise_part = np.zeros(rows)
        fall_part = np.zeros(rows)
        alpha = np.zeros(rows)
        beta = np.zeros(rows)
        if block > 0:
            ref = hi if block < blocks - 1 else lo
            alpha = inv[own, lo - 1] / inv[ref, lo - 1]
            rise_step[block] = inv[ref, lo - 1] / inv[lo, lo - 1]
            fall_part = inv[lo - 1, own]
        if block < blocks - 1:
            ref = lo - 1 if block > 0 else hi - 1
            beta = inv[own, hi] / inv[ref, hi]
            fall_step[block] = inv[ref, hi] / inv[hi - 1, hi]
            rise_part = inv[hi, own]
        local = inv[own, own] - np.outer(alpha, rise_part) - np.outer(beta, fall_part)
        rows_stencil = stencil[own, lo - pad + 3 : hi + pad + 3]
        outside = stencil[own].copy()
        outside[:, lo - pad + 3 : hi + pad + 3] = 0.0
        assert not outside.any()
        combine[block, :rows] = scale[own, None] * (local @ rows_stencil)
        combine[block, rows] = rise_part @ rows_stencil
        combine[block, rows + 1] = fall_part @ rows_stencil
        rise_gain[block] = scale[own] * alpha
        fall_gain[block] = scale[own] * beta
    rounds = []
    shift = 1
    while shift < blocks:
        rise = np.zeros(blocks)
        fall = np.zeros(blocks)
        for block in range(blocks):
            if block - shift >= 0:
                rise[block] = np.prod(rise_step[block - shift + 1 : block + 1])
            if block + shift <= blocks - 1:
                fall[block] = np.prod(fall_step[block : block + shift])
        rounds.append((shift, rise, fall))
        shift *= 2
    return combine, rise_gain, fall_gain, rounds


def wall_apply(padded, kinds, rows, pad, position):
    count = lax.axis_size("gy")
    points = rows * count
    parts = [wall_tables(kind, points, rows, pad) for kind in kinds]
    pick = lambda table: lax.dynamic_index_in_dim(
        jnp.asarray(np.stack(table, axis=1), jnp.float32), position, 0, keepdims=False
    )
    combine = pick([part[0] for part in parts])
    rise_gain = pick([part[1] for part in parts])
    fall_gain = pick([part[2] for part in parts])
    summed = None
    for tap in range(rows + 2 * pad):
        term = combine[:, :, tap, None, None] * padded[:, None, tap]
        summed = term if summed is None else summed + term
    rise = summed[:, rows]
    fall = summed[:, rows + 1]
    for level, (shift, _, _) in enumerate(parts[0][3]):
        rise_coef = pick([part[3][level][1] for part in parts])
        fall_coef = pick([part[3][level][2] for part in parts])
        up_pairs = [(i, i + shift) for i in range(count - shift)]
        down_pairs = [(i + shift, i) for i in range(count - shift)]
        from_below = lax.ppermute(rise, "gy", up_pairs)
        from_above = lax.ppermute(fall, "gy", down_pairs)
        rise = rise + rise_coef[:, None, None] * from_below
        fall = fall + fall_coef[:, None, None] * from_above
    return (
        summed[:, :rows]
        + rise_gain[:, :, None, None] * rise[:, None]
        + fall_gain[:, :, None, None] * fall[:, None]
    )


def halo(block, width):
    count = lax.axis_size("gy")
    up_pairs = [(i, i + 1) for i in range(count - 1)]
    down_pairs = [(i + 1, i) for i in range(count - 1)]
    below = lax.ppermute(block[:, block.shape[1] - width :], "gy", up_pairs)
    above = lax.ppermute(block[:, :width], "gy", down_pairs)
    return jnp.concatenate([below, block, above], axis=1)


def stream_slope(fields, stream_matrix):
    flat_rows = fields.reshape(-1, stream_matrix.shape[0])
    return jnp.dot(
        flat_rows, stream_matrix, precision=HIGHEST, preferred_element_type=jnp.float32
    ).reshape(fields.shape)


def span_slope(fields, own_block, other_block):
    other = lax.ppermute(fields, "pa", [(0, 1), (1, 0)])
    return jnp.einsum("fyzx,zw->fywx", fields, own_block, precision=HIGHEST) + jnp.einsum(
        "fyzx,zw->fywx", other, other_block, precision=HIGHEST
    )


def flux_along(direction, momentum, energy, speed, push, gradients):
    divergence = gradients[0][0] + gradients[1][1] + gradients[2][2]
    conduct = VISCOSITY * GAMMA_GAS / ((GAMMA_GAS - 1.0) * PRANDTL)
    rows_out = [momentum[direction]]
    energy_flux = (energy + push) * speed[direction]
    for component in range(3):
        stress = VISCOSITY * (gradients[direction][component] + gradients[component][direction])
        if component == direction:
            stress = stress - 2.0 / 3.0 * VISCOSITY * divergence
            rows_out.append(momentum[component] * speed[direction] + push - stress)
        else:
            rows_out.append(momentum[component] * speed[direction] - stress)
        energy_flux = energy_flux - speed[component] * stress
    energy_flux = energy_flux - conduct * gradients[direction][3]
    rows_out.append(energy_flux)
    return jnp.stack(rows_out)


def per_device(mass_per_volume, mass_flux_vector, total_heat_content):
    rows, span_own, stream_cells = mass_per_volume.shape
    count = lax.axis_size("gy")
    points = rows * count
    position = lax.axis_index("gy")
    span_total = span_own * lax.axis_size("pa")
    stream_matrix = jnp.asarray(periodic_matrix(stream_cells, STREAM_STEP), jnp.float32)
    span_full = periodic_matrix(span_total, SPAN_STEP)
    own_block = jnp.asarray(span_full[:span_own, :span_own], jnp.float32)
    other_block = jnp.asarray(span_full[span_own : 2 * span_own, :span_own], jnp.float32)

    state = jnp.concatenate(
        [mass_per_volume[None], mass_flux_vector, total_heat_content[None]], axis=0
    )
    padded = halo(state, 3)
    global_rows = position * rows - 3 + jnp.arange(rows + 6)
    inside = ((global_rows >= 0) & (global_rows < points))[:, None, None]
    density = jnp.where(inside, padded[0], 1.0)
    speed_pad = padded[1:4] / density[None]
    kinetic = 0.5 * jnp.sum(speed_pad * padded[1:4], axis=0)
    push_pad = (GAMMA_GAS - 1.0) * (padded[4] - kinetic)
    warmth_pad = push_pad / density
    basic_pad = jnp.concatenate([speed_pad, warmth_pad[None]], axis=0)

    wall_grad = wall_apply(basic_pad, ["slope"] * 4, rows, 3, position)
    smoothed = wall_apply(padded, ["smooth"] * 5, rows, 3, position)

    basic = basic_pad[:, 3 : 3 + rows]
    speed = basic[:3]
    push = push_pad[3 : 3 + rows]
    grad_stream = stream_slope(basic, stream_matrix)
    grad_span = span_slope(basic, own_block, other_block)
    gradients = [grad_stream, wall_grad, grad_span]
    momentum = mass_flux_vector
    energy = total_heat_content

    flux_wall = flux_along(1, momentum, energy, speed, push, gradients)
    wall_term = wall_apply(halo(flux_wall, 2), ["slope"] * 5, rows, 2, position)
    stream_term = stream_slope(
        flux_along(0, momentum, energy, speed, push, gradients), stream_matrix
    )
    span_term = span_slope(
        flux_along(2, momentum, energy, speed, push, gradients), own_block, other_block
    )
    time_rate = -(stream_term + wall_term + span_term)
    own_rows = position * rows + jnp.arange(rows)
    at_wall = ((own_rows == 0) | (own_rows == points - 1))[None, :, None, None]
    held = jnp.where(at_wall, 0.0, time_rate[1:4])
    time_rate = jnp.concatenate([time_rate[:1], held, time_rate[4:]], axis=0)
    return (time_rate, smoothed)


def solution(mesh):
    placed = (P("gy", "pa", None), P(None, "gy", "pa", None), P("gy", "pa", None))
    return jax.shard_map(
        per_device,
        mesh=mesh,
        in_specs=placed,
        out_specs=(P(None, "gy", "pa", None), P(None, "gy", "pa", None)),
        check_vma=False,
    )
```

time: 1450 us -> 252 us (0.17); the launches traced: 1420 us -> 250 us
  other arithmetic: 492 us -> 14.2 us
  local copies, waits for them, and re-layouts: 367 us -> 28.6 us
  blocking collectives: 330 us -> 0 us
  starting transfers between devices: 21.6 us -> 127 us
  waiting for transfers between devices: 158 us -> 71.3 us
  matrix products: 32.4 us -> 7.31 us
  between operations: 16.2 us -> 1.65 us
    unnamed x1 -> x0, blocking collectives: 304 us -> none
    select_n x254 -> x2, other arithmetic: 280 us -> 0.26 us  [the longest x1 0.16 us: per_device(): held = jnp.where(at_wall, 0.0, time_rate[1:4])]
    all_gather x4 -> x0, other arithmetic: 169 us -> none  [entering(): pieces = jax.tree.map(lambda part: lax.all_gather(part, axis), value)]
    all_gather x4 -> x0, waiting for transfers between devices: 131 us -> none  [entering(): pieces = jax.tree.map(lambda part: lax.all_gather(part, axis), value)]
    mul x267 -> x42, local copies, waits for them, and re-layouts: 140 us -> 23.3 us  [the longest x18 12.6 us: wall_apply(): rise = rise + rise_coef[:, None, None] * from_below]
    ppermute x4 -> x42, starting transfers between devices: 11.7 us -> 127 us  [the longest x18 61.5 us: wall_apply(): from_below = lax.ppermute(rise, 'gy', up_pairs)]
    all_gather x8 -> x0, local copies, waits for them, and re-layouts: 61.9 us -> none  [entering(): pieces = jax.tree.map(lambda part: lax.all_gather(part, axis), value)]
    unnamed x132 -> x17, local copies, waits for them, and re-layouts: 53.3 us -> 1.73 us
  transfers between devices with their start and end apart: 8 -> 42, of which waited for: 6 -> 15; matrix products, arithmetic and copies ran while one was open for 12% -> 15% of each run, Pallas kernels for 0% -> 0%
where the time goes in v1:
time: 252 us; the launch traced here: 250 us
  starting transfers between devices  127 us (50%)
  waiting for transfers between devices  71.3 us (28%)
  local copies, waits for them, and re-layouts  28.6 us (11%)
  other arithmetic  14.2 us (6%)
  matrix products  7.31 us (3%)
    ppermute x18, starting transfers between devices, wall_apply(): from_below = lax.ppermute(rise, 'gy', up_pairs)  61.5 us
    ppermute x18, waiting for transfers between devices, wall_apply(): from_above = lax.ppermute(fall, 'gy', down_pairs)  58 us
    ppermute x18, starting transfers between devices, wall_apply(): from_above = lax.ppermute(fall, 'gy', down_pairs)  44.5 us
    ppermute x2, starting transfers between devices, halo(): below = lax.ppermute(block[:, block.shape[1] - width:], 'gy', up_pairs)  16.1 us
    mul x18, local copies, waits for them, and re-layouts, wall_apply(): rise = rise + rise_coef[:, None, None] * from_below  12.6 us
    ppermute x2, waiting for transfers between devices, halo(): above = lax.ppermute(block[:, :width], 'gy', down_pairs)  8.59 us
    mul x12, local copies, waits for them, and re-layouts, wall_apply(): fall = fall + fall_coef[:, None, None] * from_above  8.29 us
  transfers between devices with their start and end apart: 42, of which 15 were waited for; matrix products, arithmetic and copies ran while one was open for 15% of the time, Pallas kernels for 0%

profile of v1, /device:TPU:30, one launch (start us, length us, event | category | flops | bytes accessed | tf_op | source)
XLA Modules:
  0.0 249.7 jit_solution(2241715749417399676)
XLA Ops:
  3.0 3.4 %collective-permute-start = (f32[5,3,64,128]{3,2,1,0:T(8,128)}, f32[5,3,64,128]{3,2,1,0:T(8,128)S(1)}, u32[]{:S(2)}, u32[]{:S(2)}) collective-permute-start(f32[5,3,64,128]{3,2,1,0:T(8,128)} %get-tuple-element.62), channel_id=1, source_target_pairs={{0,2},{2,4},{4,6},{6,8},{8,10},{10,12},{12,14},{14,16},{16,18},{18... | collective-permute-start | bytes 1474568 | tf_op jit(solution)/shard_map/ppermute | solution.py:206
  37.9 7.6 %collective-permute-start.30 = (f32[5,64,128]{2,1,0:T(8,128)S(1)}, f32[5,64,128]{2,1,0:T(8,128)S(1)}, u32[]{:S(2)}, u32[]{:S(2)}) collective-permute-start(f32[5,64,128]{2,1,0:T(8,128)S(1)} %get-tuple-element.32), channel_id=1, source_target_pairs={{0,2},{2,4},{4,6},{6,8},{8,10},{10,12},{12,14},{14,16},{16,18},{18... | collective-permute-start | bytes 491528 | tf_op jit(solution)/shard_map/ppermute | solution.py:191
  48.8 8.1 %collective-permute-start.2 = (f32[4,64,128]{2,1,0:T(8,128)S(1)}, f32[4,64,128]{2,1,0:T(8,128)S(1)}, u32[]{:S(2)}, u32[]{:S(2)}) collective-permute-start(f32[4,64,128]{2,1,0:T(8,128)S(1)} %get-tuple-element.60), channel_id=1, source_target_pairs={{0,2},{2,4},{4,6},{6,8},{8,10},{10,12},{12,14},{14,16},{16,18},{18... | collective-permute-start | bytes 393224 | tf_op jit(solution)/shard_map/ppermute | solution.py:191
  60.1 8.8 %collective-permute-done.8 = f32[4,64,128]{2,1,0:T(8,128)S(1)} collective-permute-done((f32[4,64,128]{2,1,0:T(8,128)S(1)}, f32[4,64,128]{2,1,0:T(8,128)S(1)}, u32[]{:S(2)}, u32[]{:S(2)}) %collective-permute-start.8) | collective-permute-done | bytes 131104 | tf_op jit(solution)/shard_map/ppermute | solution.py:192
  70.9 5.4 %collective-permute-start.9 = (f32[4,64,128]{2,1,0:T(8,128)S(1)}, f32[4,64,128]{2,1,0:T(8,128)S(1)}, u32[]{:S(2)}, u32[]{:S(2)}) collective-permute-start(f32[4,64,128]{2,1,0:T(8,128)S(1)} %get-tuple-element.59), channel_id=1, source_target_pairs={{4,0},{6,2},{8,4},{10,6},{12,8},{14,10},{16,12},{18,14},{20,16},{2... | collective-permute-start | bytes 393224 | tf_op jit(solution)/shard_map/ppermute | solution.py:192
  76.5 4.9 %collective-permute-start.31 = (f32[5,64,128]{2,1,0:T(8,128)S(1)}, f32[5,64,128]{2,1,0:T(8,128)S(1)}, u32[]{:S(2)}, u32[]{:S(2)}) collective-permute-start(f32[5,64,128]{2,1,0:T(8,128)S(1)} %get-tuple-element.30), channel_id=1, source_target_pairs={{0,4},{2,6},{4,8},{6,10},{8,12},{10,14},{12,16},{14,18},{16,20},{1... | collective-permute-start | bytes 491528 | tf_op jit(solution)/shard_map/ppermute | solution.py:191
  86.0 3.9 %collective-permute-start.10 = (f32[4,64,128]{2,1,0:T(8,128)S(1)}, f32[4,64,128]{2,1,0:T(8,128)S(1)}, u32[]{:S(2)}, u32[]{:S(2)}) collective-permute-start(f32[4,64,128]{2,1,0:T(8,128)S(1)} %multiply_add_fusion.31), channel_id=1, source_target_pairs={{8,0},{10,2},{12,4},{14,6},{16,8},{18,10},{20,12},{22,14},{24,16},... | collective-permute-start | bytes 393224 | tf_op jit(solution)/shard_map/ppermute | solution.py:192
  90.0 4.1 %collective-permute-start.32 = (f32[5,64,128]{2,1,0:T(8,128)S(1)}, f32[5,64,128]{2,1,0:T(8,128)S(1)}, u32[]{:S(2)}, u32[]{:S(2)}) collective-permute-start(f32[5,64,128]{2,1,0:T(8,128)S(1)} %multiply_add_fusion.13), channel_id=1, source_target_pairs={{0,8},{2,10},{4,12},{6,14},{8,16},{10,18},{12,20},{14,22},{16,24},... | collective-permute-start | bytes 491528 | tf_op jit(solution)/shard_map/ppermute | solution.py:191
  99.7 4.0 %collective-permute-start.11 = (f32[4,64,128]{2,1,0:T(8,128)S(1)}, f32[4,64,128]{2,1,0:T(8,128)S(1)}, u32[]{:S(2)}, u32[]{:S(2)}) collective-permute-start(f32[4,64,128]{2,1,0:T(8,128)S(1)} %multiply_add_fusion.30), channel_id=1, source_target_pairs={{16,0},{18,2},{20,4},{22,6},{24,8},{26,10},{28,12},{30,14},{32,16}... | collective-permute-start | bytes 393224 | tf_op jit(solution)/shard_map/ppermute | solution.py:192
  103.8 4.3 %collective-permute-start.33 = (f32[5,64,128]{2,1,0:T(8,128)S(1)}, f32[5,64,128]{2,1,0:T(8,128)S(1)}, u32[]{:S(2)}, u32[]{:S(2)}) collective-permute-start(f32[5,64,128]{2,1,0:T(8,128)S(1)} %multiply_add_fusion.12), channel_id=1, source_target_pairs={{0,16},{2,18},{4,20},{6,22},{8,24},{10,26},{12,28},{14,30},{16,32}... | collective-permute-start | bytes 491528 | tf_op jit(solution)/shard_map/ppermute | solution.py:191
  116.7 4.6 %collective-permute-start.34 = (f32[5,64,128]{2,1,0:T(8,128)S(1)}, f32[5,64,128]{2,1,0:T(8,128)S(1)}, u32[]{:S(2)}, u32[]{:S(2)}) collective-permute-start(f32[5,64,128]{2,1,0:T(8,128)S(1)} %multiply_add_fusion.11), channel_id=1, source_target_pairs={{0,32},{2,34},{4,36},{6,38},{8,40},{10,42},{12,44},{14,46},{16,48}... | collective-permute-start | bytes 491528 | tf_op jit(solution)/shard_map/ppermute | solution.py:191
  122.7 6.2 %collective-permute-start.7 = (f32[4,64,128]{2,1,0:T(8,128)S(1)}, f32[4,64,128]{2,1,0:T(8,128)S(1)}, u32[]{:S(2)}, u32[]{:S(2)}) collective-permute-start(f32[4,64,128]{2,1,0:T(8,128)S(1)} %multiply_add_fusion.34), channel_id=1, source_target_pairs={{0,64},{2,66},{4,68},{6,70},{8,72},{10,74},{12,76},{14,78},{16,80}... | collective-permute-start | bytes 393224 | tf_op jit(solution)/shard_map/ppermute | solution.py:191
  131.5 5.9 %collective-permute-done.13 = f32[4,64,128]{2,1,0:T(8,128)S(1)} collective-permute-done((f32[4,64,128]{2,1,0:T(8,128)S(1)}, f32[4,64,128]{2,1,0:T(8,128)S(1)}, u32[]{:S(2)}, u32[]{:S(2)}) %collective-permute-start.13) | collective-permute-done | bytes 131104 | tf_op jit(solution)/shard_map/ppermute | solution.py:192
  143.3 5.9 %collective-permute-done.41 = f32[5,64,128]{2,1,0:T(8,128)S(1)} collective-permute-done((f32[5,64,128]{2,1,0:T(8,128)S(1)}, f32[5,64,128]{2,1,0:T(8,128)S(1)}, u32[]{:S(2)}, u32[]{:S(2)}) %collective-permute-start.41) | collective-permute-done | bytes 163872 | tf_op jit(solution)/shard_map/ppermute | solution.py:192
  154.4 12.7 %collective-permute-start.15 = (f32[5,2,64,128]{3,2,1,0:T(8,128)S(1)}, f32[5,2,64,128]{3,2,1,0:T(8,128)S(1)}, u32[]{:S(2)}, u32[]{:S(2)}) collective-permute-start(f32[5,2,64,128]{3,2,1,0:T(8,128)S(1)} %get-tuple-element.48), channel_id=1, source_target_pairs={{0,2},{2,4},{4,6},{6,8},{8,10},{10,12},{12,14},{14,16},{16,18},{18... | collective-permute-start | bytes 983048 | tf_op jit(solution)/shard_map/ppermute | solution.py:206
  171.7 8.6 %collective-permute-done.16 = f32[5,2,64,128]{3,2,1,0:T(8,128)S(1)} collective-permute-done((f32[5,2,64,128]{3,2,1,0:T(8,128)S(1)}, f32[5,2,64,128]{3,2,1,0:T(8,128)S(1)}, u32[]{:S(2)}, u32[]{:S(2)}) %collective-permute-start.16) | collective-permute-done | bytes 327712 | tf_op jit(solution)/shard_map/ppermute | solution.py:207
  183.7 3.9 %collective-permute-start.23 = (f32[5,64,128]{2,1,0:T(8,128)S(1)}, f32[5,64,128]{2,1,0:T(8,128)S(1)}, u32[]{:S(2)}, u32[]{:S(2)}) collective-permute-start(f32[5,64,128]{2,1,0:T(8,128)S(1)} %get-tuple-element.37), channel_id=1, source_target_pairs={{2,0},{4,2},{6,4},{8,6},{10,8},{12,10},{14,12},{16,14},{18,16},{20... | collective-permute-start | bytes 491528 | tf_op jit(solution)/shard_map/ppermute | solution.py:192
  189.0 6.1 %collective-permute-done.23 = f32[5,64,128]{2,1,0:T(8,128)S(1)} collective-permute-done((f32[5,64,128]{2,1,0:T(8,128)S(1)}, f32[5,64,128]{2,1,0:T(8,128)S(1)}, u32[]{:S(2)}, u32[]{:S(2)}) %collective-permute-start.23) | collective-permute-done | bytes 163872 | tf_op jit(solution)/shard_map/ppermute | solution.py:192
  198.5 5.4 %collective-permute-start.24 = (f32[5,64,128]{2,1,0:T(8,128)S(1)}, f32[5,64,128]{2,1,0:T(8,128)S(1)}, u32[]{:S(2)}, u32[]{:S(2)}) collective-permute-start(f32[5,64,128]{2,1,0:T(8,128)S(1)} %get-tuple-element.35), channel_id=1, source_target_pairs={{4,0},{6,2},{8,4},{10,6},{12,8},{14,10},{16,12},{18,14},{20,16},{2... | collective-permute-start | bytes 491528 | tf_op jit(solution)/shard_map/ppermute | solution.py:192
  206.0 4.2 %collective-permute-done.24 = f32[5,64,128]{2,1,0:T(8,128)S(1)} collective-permute-done((f32[5,64,128]{2,1,0:T(8,128)S(1)}, f32[5,64,128]{2,1,0:T(8,128)S(1)}, u32[]{:S(2)}, u32[]{:S(2)}) %collective-permute-start.24) | collective-permute-done | bytes 163872 | tf_op jit(solution)/shard_map/ppermute | solution.py:192
  214.3 6.4 %collective-permute-done.25 = f32[5,64,128]{2,1,0:T(8,128)S(1)} collective-permute-done((f32[5,64,128]{2,1,0:T(8,128)S(1)}, f32[5,64,128]{2,1,0:T(8,128)S(1)}, u32[]{:S(2)}, u32[]{:S(2)}) %collective-permute-start.25) | collective-permute-done | bytes 163872 | tf_op jit(solution)/shard_map/ppermute | solution.py:192
  224.1 6.4 %collective-permute-done.26 = f32[5,64,128]{2,1,0:T(8,128)S(1)} collective-permute-done((f32[5,64,128]{2,1,0:T(8,128)S(1)}, f32[5,64,128]{2,1,0:T(8,128)S(1)}, u32[]{:S(2)}, u32[]{:S(2)}) %collective-permute-start.26) | collective-permute-done | bytes 163872 | tf_op jit(solution)/shard_map/ppermute | solution.py:192
  234.0 3.8 %collective-permute-done.27 = f32[5,64,128]{2,1,0:T(8,128)S(1)} collective-permute-done((f32[5,64,128]{2,1,0:T(8,128)S(1)}, f32[5,64,128]{2,1,0:T(8,128)S(1)}, u32[]{:S(2)}, u32[]{:S(2)}) %collective-permute-start.27) | collective-permute-done | bytes 163872 | tf_op jit(solution)/shard_map/ppermute | solution.py:192
  239.3 7.3 %collective-permute-done.28 = f32[5,64,128]{2,1,0:T(8,128)S(1)} collective-permute-done((f32[5,64,128]{2,1,0:T(8,128)S(1)}, f32[5,64,128]{2,1,0:T(8,128)S(1)}, u32[]{:S(2)}, u32[]{:S(2)}) %collective-permute-start.28) | collective-permute-done | bytes 163872 | tf_op jit(solution)/shard_map/ppermute | solution.py:192
  (195 shorter events, 106.0 us)
Async XLA Ops:
  3.0 32.1 %collective-permute-start = (f32[5,3,64,128]{3,2,1,0:T(8,128)}, f32[5,3,64,128]{3,2,1,0:T(8,128)S(1)}, u32[]{:S(2)}, u32[]{:S(2)}) collective-permute-start(f32[5,3,64,128]{3,2,1,0:T(8,128)} %get-tuple-element.62), channel_id=1, source_target_pairs={{0,2},{2,4},{4,6},{6,8},{8,10},{10,12},{12,14},{14,16},{16,18},{18... | collective-permute-start | bytes 1474568 | tf_op jit(solution)/shard_map/ppermute | solution.py:206
  6.4 28.8 %collective-permute-start.1 = (f32[5,3,64,128]{3,2,1,0:T(8,128)}, f32[5,3,64,128]{3,2,1,0:T(8,128)S(1)}, u32[]{:S(2)}, u32[]{:S(2)}) collective-permute-start(f32[5,3,64,128]{3,2,1,0:T(8,128)} %get-tuple-element.63), channel_id=1, source_target_pairs={{2,0},{4,2},{6,4},{8,6},{10,8},{12,10},{14,12},{16,14},{18,16},{20... | collective-permute-start | bytes 1474568 | tf_op jit(solution)/shard_map/ppermute | solution.py:207
  37.9 38.5 %collective-permute-start.30 = (f32[5,64,128]{2,1,0:T(8,128)S(1)}, f32[5,64,128]{2,1,0:T(8,128)S(1)}, u32[]{:S(2)}, u32[]{:S(2)}) collective-permute-start(f32[5,64,128]{2,1,0:T(8,128)S(1)} %get-tuple-element.32), channel_id=1, source_target_pairs={{0,2},{2,4},{4,6},{6,8},{8,10},{10,12},{12,14},{14,16},{16,18},{18... | collective-permute-start | bytes 491528 | tf_op jit(solution)/shard_map/ppermute | solution.py:191
  45.5 30.9 %collective-permute-start.36 = (f32[5,64,128]{2,1,0:T(8,128)S(1)}, f32[5,64,128]{2,1,0:T(8,128)S(1)}, u32[]{:S(2)}, u32[]{:S(2)}) collective-permute-start(f32[5,64,128]{2,1,0:T(8,128)S(1)} %get-tuple-element.33), channel_id=1, source_target_pairs={{2,0},{4,2},{6,4},{8,6},{10,8},{12,10},{14,12},{16,14},{18,16},{20... | collective-permute-start | bytes 491528 | tf_op jit(solution)/shard_map/ppermute | solution.py:192
  57.0 11.9 %collective-permute-start.8 = (f32[4,64,128]{2,1,0:T(8,128)S(1)}, f32[4,64,128]{2,1,0:T(8,128)S(1)}, u32[]{:S(2)}, u32[]{:S(2)}) collective-permute-start(f32[4,64,128]{2,1,0:T(8,128)S(1)} %get-tuple-element.61), channel_id=1, source_target_pairs={{2,0},{4,2},{6,4},{8,6},{10,8},{12,10},{14,12},{16,14},{18,16},{20... | collective-permute-start | bytes 393224 | tf_op jit(solution)/shard_map/ppermute | solution.py:192
  58.9 91.9 %collective-permute-start.14 = (f32[4,8,64,128]{3,2,1,0:T(8,128)S(1)}, f32[4,8,64,128]{3,2,1,0:T(8,128)S(1)}, u32[]{:S(2)}, u32[]{:S(2)}) collective-permute-start(f32[4,8,64,128]{3,2,1,0:T(8,128)S(1)} %fusion.9), channel_id=1, source_target_pairs={{0,1},{1,0},{2,3},{3,2},{4,5},{5,4},{6,7},{7,6},{8,9},{9,8},{10,11... | collective-permute-start | bytes 3145736 | tf_op jit(solution)/shard_map/ppermute | solution.py:219
  69.0 14.9 %collective-permute-start.3 = (f32[4,64,128]{2,1,0:T(8,128)S(1)}, f32[4,64,128]{2,1,0:T(8,128)S(1)}, u32[]{:S(2)}, u32[]{:S(2)}) collective-permute-start(f32[4,64,128]{2,1,0:T(8,128)S(1)} %get-tuple-element.58), channel_id=1, source_target_pairs={{0,4},{2,6},{4,8},{6,10},{8,12},{10,14},{12,16},{14,18},{16,20},{1... | collective-permute-start | bytes 393224 | tf_op jit(solution)/shard_map/ppermute | solution.py:191
  70.9 15.0 %collective-permute-start.9 = (f32[4,64,128]{2,1,0:T(8,128)S(1)}, f32[4,64,128]{2,1,0:T(8,128)S(1)}, u32[]{:S(2)}, u32[]{:S(2)}) collective-permute-start(f32[4,64,128]{2,1,0:T(8,128)S(1)} %get-tuple-element.59), channel_id=1, source_target_pairs={{4,0},{6,2},{8,4},{10,6},{12,8},{14,10},{16,12},{18,14},{20,16},{2... | collective-permute-start | bytes 393224 | tf_op jit(solution)/shard_map/ppermute | solution.py:192
  76.5 13.4 %collective-permute-start.31 = (f32[5,64,128]{2,1,0:T(8,128)S(1)}, f32[5,64,128]{2,1,0:T(8,128)S(1)}, u32[]{:S(2)}, u32[]{:S(2)}) collective-permute-start(f32[5,64,128]{2,1,0:T(8,128)S(1)} %get-tuple-element.30), channel_id=1, source_target_pairs={{0,4},{2,6},{4,8},{6,10},{8,12},{10,14},{12,16},{14,18},{16,20},{1... | collective-permute-start | bytes 491528 | tf_op jit(solution)/shard_map/ppermute | solution.py:191
  81.4 12.7 %collective-permute-start.37 = (f32[5,64,128]{2,1,0:T(8,128)S(1)}, f32[5,64,128]{2,1,0:T(8,128)S(1)}, u32[]{:S(2)}, u32[]{:S(2)}) collective-permute-start(f32[5,64,128]{2,1,0:T(8,128)S(1)} %get-tuple-element.31), channel_id=1, source_target_pairs={{4,0},{6,2},{8,4},{10,6},{12,8},{14,10},{16,12},{18,14},{20,16},{2... | collective-permute-start | bytes 491528 | tf_op jit(solution)/shard_map/ppermute | solution.py:192
  84.0 12.2 %collective-permute-start.4 = (f32[4,64,128]{2,1,0:T(8,128)S(1)}, f32[4,64,128]{2,1,0:T(8,128)S(1)}, u32[]{:S(2)}, u32[]{:S(2)}) collective-permute-start(f32[4,64,128]{2,1,0:T(8,128)S(1)} %multiply_add_fusion.37), channel_id=1, source_target_pairs={{0,8},{2,10},{4,12},{6,14},{8,16},{10,18},{12,20},{14,22},{16,24},... | collective-permute-start | bytes 393224 | tf_op jit(solution)/shard_map/ppermute | solution.py:191
  86.0 13.6 %collective-permute-start.10 = (f32[4,64,128]{2,1,0:T(8,128)S(1)}, f32[4,64,128]{2,1,0:T(8,128)S(1)}, u32[]{:S(2)}, u32[]{:S(2)}) collective-permute-start(f32[4,64,128]{2,1,0:T(8,128)S(1)} %multiply_add_fusion.31), channel_id=1, source_target_pairs={{8,0},{10,2},{12,4},{14,6},{16,8},{18,10},{20,12},{22,14},{24,16},... | collective-permute-start | bytes 393224 | tf_op jit(solution)/shard_map/ppermute | solution.py:192
  90.0 13.7 %collective-permute-start.32 = (f32[5,64,128]{2,1,0:T(8,128)S(1)}, f32[5,64,128]{2,1,0:T(8,128)S(1)}, u32[]{:S(2)}, u32[]{:S(2)}) collective-permute-start(f32[5,64,128]{2,1,0:T(8,128)S(1)} %multiply_add_fusion.13), channel_id=1, source_target_pairs={{0,8},{2,10},{4,12},{6,14},{8,16},{10,18},{12,20},{14,22},{16,24},... | collective-permute-start | bytes 491528 | tf_op jit(solution)/shard_map/ppermute | solution.py:191
  94.2 16.9 %collective-permute-start.38 = (f32[5,64,128]{2,1,0:T(8,128)S(1)}, f32[5,64,128]{2,1,0:T(8,128)S(1)}, u32[]{:S(2)}, u32[]{:S(2)}) collective-permute-start(f32[5,64,128]{2,1,0:T(8,128)S(1)} %multiply_add_fusion.7), channel_id=1, source_target_pairs={{8,0},{10,2},{12,4},{14,6},{16,8},{18,10},{20,12},{22,14},{24,16},... | collective-permute-start | bytes 491528 | tf_op jit(solution)/shard_map/ppermute | solution.py:192
  96.2 16.9 %collective-permute-start.5 = (f32[4,64,128]{2,1,0:T(8,128)S(1)}, f32[4,64,128]{2,1,0:T(8,128)S(1)}, u32[]{:S(2)}, u32[]{:S(2)}) collective-permute-start(f32[4,64,128]{2,1,0:T(8,128)S(1)} %multiply_add_fusion.36), channel_id=1, source_target_pairs={{0,16},{2,18},{4,20},{6,22},{8,24},{10,26},{12,28},{14,30},{16,32}... | collective-permute-start | bytes 393224 | tf_op jit(solution)/shard_map/ppermute | solution.py:191
  99.7 15.5 %collective-permute-start.11 = (f32[4,64,128]{2,1,0:T(8,128)S(1)}, f32[4,64,128]{2,1,0:T(8,128)S(1)}, u32[]{:S(2)}, u32[]{:S(2)}) collective-permute-start(f32[4,64,128]{2,1,0:T(8,128)S(1)} %multiply_add_fusion.30), channel_id=1, source_target_pairs={{16,0},{18,2},{20,4},{22,6},{24,8},{26,10},{28,12},{30,14},{32,16}... | collective-permute-start | bytes 393224 | tf_op jit(solution)/shard_map/ppermute | solution.py:192
  103.8 12.8 %collective-permute-start.33 = (f32[5,64,128]{2,1,0:T(8,128)S(1)}, f32[5,64,128]{2,1,0:T(8,128)S(1)}, u32[]{:S(2)}, u32[]{:S(2)}) collective-permute-start(f32[5,64,128]{2,1,0:T(8,128)S(1)} %multiply_add_fusion.12), channel_id=1, source_target_pairs={{0,16},{2,18},{4,20},{6,22},{8,24},{10,26},{12,28},{14,30},{16,32}... | collective-permute-start | bytes 491528 | tf_op jit(solution)/shard_map/ppermute | solution.py:191
  115.3 13.7 %collective-permute-start.12 = (f32[4,64,128]{2,1,0:T(8,128)S(1)}, f32[4,64,128]{2,1,0:T(8,128)S(1)}, u32[]{:S(2)}, u32[]{:S(2)}) collective-permute-start(f32[4,64,128]{2,1,0:T(8,128)S(1)} %multiply_add_fusion.29), channel_id=1, source_target_pairs={{32,0},{34,2},{36,4},{38,6},{40,8},{42,10},{44,12},{46,14},{48,16}... | collective-permute-start | bytes 393224 | tf_op jit(solution)/shard_map/ppermute | solution.py:192
  116.7 22.2 %collective-permute-start.34 = (f32[5,64,128]{2,1,0:T(8,128)S(1)}, f32[5,64,128]{2,1,0:T(8,128)S(1)}, u32[]{:S(2)}, u32[]{:S(2)}) collective-permute-start(f32[5,64,128]{2,1,0:T(8,128)S(1)} %multiply_add_fusion.11), channel_id=1, source_target_pairs={{0,32},{2,34},{4,36},{6,38},{8,40},{10,42},{12,44},{14,46},{16,48}... | collective-permute-start | bytes 491528 | tf_op jit(solution)/shard_map/ppermute | solution.py:191
  121.3 19.1 %collective-permute-start.40 = (f32[5,64,128]{2,1,0:T(8,128)S(1)}, f32[5,64,128]{2,1,0:T(8,128)S(1)}, u32[]{:S(2)}, u32[]{:S(2)}) collective-permute-start(f32[5,64,128]{2,1,0:T(8,128)S(1)} %multiply_add_fusion.5), channel_id=1, source_target_pairs={{32,0},{34,2},{36,4},{38,6},{40,8},{42,10},{44,12},{46,14},{48,16}... | collective-permute-start | bytes 491528 | tf_op jit(solution)/shard_map/ppermute | solution.py:192
  154.4 17.3 %collective-permute-start.15 = (f32[5,2,64,128]{3,2,1,0:T(8,128)S(1)}, f32[5,2,64,128]{3,2,1,0:T(8,128)S(1)}, u32[]{:S(2)}, u32[]{:S(2)}) collective-permute-start(f32[5,2,64,128]{3,2,1,0:T(8,128)S(1)} %get-tuple-element.48), channel_id=1, source_target_pairs={{0,2},{2,4},{4,6},{6,8},{8,10},{10,12},{12,14},{14,16},{16,18},{18... | collective-permute-start | bytes 983048 | tf_op jit(solution)/shard_map/ppermute | solution.py:206
  167.1 13.2 %collective-permute-start.16 = (f32[5,2,64,128]{3,2,1,0:T(8,128)S(1)}, f32[5,2,64,128]{3,2,1,0:T(8,128)S(1)}, u32[]{:S(2)}, u32[]{:S(2)}) collective-permute-start(f32[5,2,64,128]{3,2,1,0:T(8,128)S(1)} %get-tuple-element.49), channel_id=1, source_target_pairs={{2,0},{4,2},{6,4},{8,6},{10,8},{12,10},{14,12},{16,14},{18,16},{20... | collective-permute-start | bytes 983048 | tf_op jit(solution)/shard_map/ppermute | solution.py:207
  169.5 77.3 %collective-permute-start.29 = (f32[5,8,64,128]{3,2,1,0:T(8,128)S(1)}, f32[5,8,64,128]{3,2,1,0:T(8,128)S(1)}, u32[]{:S(2)}, u32[]{:S(2)}) collective-permute-start(f32[5,8,64,128]{3,2,1,0:T(8,128)S(1)} %fusion.16), channel_id=1, source_target_pairs={{0,1},{1,0},{2,3},{3,2},{4,5},{5,4},{6,7},{7,6},{8,9},{9,8},{10,11... | collective-permute-start | bytes 3932168 | tf_op jit(solution)/shard_map/ppermute | solution.py:219
  198.5 11.7 %collective-permute-start.24 = (f32[5,64,128]{2,1,0:T(8,128)S(1)}, f32[5,64,128]{2,1,0:T(8,128)S(1)}, u32[]{:S(2)}, u32[]{:S(2)}) collective-permute-start(f32[5,64,128]{2,1,0:T(8,128)S(1)} %get-tuple-element.35), channel_id=1, source_target_pairs={{4,0},{6,2},{8,4},{10,6},{12,8},{14,10},{16,12},{18,14},{20,16},{2... | collective-permute-start | bytes 491528 | tf_op jit(solution)/shard_map/ppermute | solution.py:192
  (26 other events, 192.0 us)

commit v2 on v1

--- a/solution.py
+++ b/solution.py
@@ -167,36 +167,53 @@
     return combine, rise_gain, fall_gain, rounds
 
 
-def wall_apply(padded, kinds, rows, pad, position):
+def wall_apply(groups, rows, pad, position):
     count = lax.axis_size("gy")
     points = rows * count
-    parts = [wall_tables(kind, points, rows, pad) for kind in kinds]
+    tables = [wall_tables(kind, points, rows, pad) for _, kind in groups]
     pick = lambda table: lax.dynamic_index_in_dim(
-        jnp.asarray(np.stack(table, axis=1), jnp.float32), position, 0, keepdims=False
-    )
-    combine = pick([part[0] for part in parts])
-    rise_gain = pick([part[1] for part in parts])
-    fall_gain = pick([part[2] for part in parts])
-    summed = None
-    for tap in range(rows + 2 * pad):
-        term = combine[:, :, tap, None, None] * padded[:, None, tap]
-        summed = term if summed is None else summed + term
-    rise = summed[:, rows]
-    fall = summed[:, rows + 1]
-    for level, (shift, _, _) in enumerate(parts[0][3]):
-        rise_coef = pick([part[3][level][1] for part in parts])
-        fall_coef = pick([part[3][level][2] for part in parts])
+        jnp.asarray(table, jnp.float32), position, 0, keepdims=False
+    )
+
+    def taps(padded, combine):
+        summed = None
+        for tap in range(rows + 2 * pad):
+            term = combine[:, tap, None, None] * padded[:, None, tap]
+            summed = term if summed is None else summed + term
+        return summed
+
+    partials = [
+        taps(padded, pick(table[0])[rows:]) for (padded, _), table in zip(groups, tables)
+    ]
+    sizes = [padded.shape[0] for padded, _ in groups]
+    rise = jnp.concatenate([part[:, 0] for part in partials], axis=0)
+    fall = jnp.concatenate([part[:, 1] for part in partials], axis=0)
+    for level, (shift, _, _) in enumerate(tables[0][3]):
+        rise_coef = pick(
+            np.concatenate([np.repeat(t[3][level][1][:, None], n, 1) for t, n in zip(tables, sizes)], 1)
+        )
+        fall_coef = pick(
+            np.concatenate([np.repeat(t[3][level][2][:, None], n, 1) for t, n in zip(tables, sizes)], 1)
+        )
         up_pairs = [(i, i + shift) for i in range(count - shift)]
         down_pairs = [(i + shift, i) for i in range(count - shift)]
         from_below = lax.ppermute(rise, "gy", up_pairs)
         from_above = lax.ppermute(fall, "gy", down_pairs)
         rise = rise + rise_coef[:, None, None] * from_below
         fall = fall + fall_coef[:, None, None] * from_above
-    return (
-        summed[:, :rows]
-        + rise_gain[:, :, None, None] * rise[:, None]
-        + fall_gain[:, :, None, None] * fall[:, None]
-    )
+    results = []
+    first = 0
+    for (padded, _), table, size in zip(groups, tables, sizes):
+        local = taps(padded, pick(table[0])[:rows])
+        rise_gain = pick(table[1])
+        fall_gain = pick(table[2])
+        results.append(
+            local
+            + rise_gain[None, :, None, None] * rise[first : first + size, None]
+            + fall_gain[None, :, None, None] * fall[first : first + size, None]
+        )
+        first += size
+    return results
 
 
 def halo(block, width):
@@ -264,8 +281,9 @@
     warmth_pad = push_pad / density
     basic_pad = jnp.concatenate([speed_pad, warmth_pad[None]], axis=0)
 
-    wall_grad = wall_apply(basic_pad, ["slope"] * 4, rows, 3, position)
-    smoothed = wall_apply(padded, ["smooth"] * 5, rows, 3, position)
+    wall_grad, smoothed = wall_apply(
+        [(basic_pad, "slope"), (padded, "smooth")], rows, 3, position
+    )
 
     basic = basic_pad[:, 3 : 3 + rows]
     speed = basic[:3]
@@ -277,7 +295,7 @@
     energy = total_heat_content
 
     flux_wall = flux_along(1, momentum, energy, speed, push, gradients)
-    wall_term = wall_apply(halo(flux_wall, 2), ["slope"] * 5, rows, 2, position)
+    (wall_term,) = wall_apply([(halo(flux_wall, 2), "slope")], rows, 2, position)
     stream_term = stream_slope(
         flux_along(0, momentum, energy, speed, push, gradients), stream_matrix
     )

time: 252 us -> 218 us (0.87)
  starting transfers between devices: 127 us -> 76 us
  waiting for transfers between devices: 71.3 us -> 92.7 us
  local copies, waits for them, and re-layouts: 28.6 us -> 24.9 us
    ppermute x18 -> x12, waiting for transfers between devices: 58 us -> 83.8 us  [wall_apply(): from_above = lax.ppermute(fall, 'gy', down_pairs)]
    ppermute x18 -> x12, starting transfers between devices: 61.5 us -> 38.1 us  [wall_apply(): from_below = lax.ppermute(rise, 'gy', up_pairs)]
    ppermute x18 -> x12, starting transfers between devices: 44.5 us -> 26 us  [wall_apply(): from_above = lax.ppermute(fall, 'gy', down_pairs)]
    ppermute x2, starting transfers between devices: 16.1 us -> 5.49 us  [halo(): below = lax.ppermute(block[:, block.shape[1] - width:], 'gy', up_pairs)]
    slice x0 -> x17, local copies, waits for them, and re-layouts: none -> 6.41 us  [the longest x6 2.31 us: taps(): term = combine[:, tap, None, None] * padded[:, None, tap]]
    mul x18 -> x11, local copies, waits for them, and re-layouts: 12.6 us -> 7.66 us  [wall_apply(): rise = rise + rise_coef[:, None, None] * from_below]
    ppermute x2, waiting for transfers between devices: 8.59 us -> 5.4 us  [halo(): above = lax.ppermute(block[:, :width], 'gy', down_pairs)]
    mul x12 -> x10, local copies, waits for them, and re-layouts: 8.29 us -> 6.94 us  [wall_apply(): fall = fall + fall_coef[:, None, None] * from_above]
  transfers between devices with their start and end apart: 42 -> 30, of which waited for: 15 -> 16; matrix products, arithmetic and copies ran while one was open for 15% -> 15% of each run, Pallas kernels for 0% -> 0%
where the time goes in v2:
time: 218 us; the launch traced here: 216 us
  waiting for transfers between devices  92.7 us (43%)
  starting transfers between devices  76 us (35%)
  local copies, waits for them, and re-layouts  24.9 us (11%)
  other arithmetic  12.8 us (6%)
  matrix products  8.53 us (4%)
    ppermute x12, waiting for transfers between devices, wall_apply(): from_above = lax.ppermute(fall, 'gy', down_pairs)  83.8 us
    ppermute x12, starting transfers between devices, wall_apply(): from_below = lax.ppermute(rise, 'gy', up_pairs)  38.1 us
    ppermute x12, starting transfers between devices, wall_apply(): from_above = lax.ppermute(fall, 'gy', down_pairs)  26 us
    mul x11, local copies, waits for them, and re-layouts, wall_apply(): rise = rise + rise_coef[:, None, None] * from_below  7.66 us
    mul x10, local copies, waits for them, and re-layouts, wall_apply(): fall = fall + fall_coef[:, None, None] * from_above  6.94 us
    ppermute x2, starting transfers between devices, halo(): above = lax.ppermute(block[:, :width], 'gy', down_pairs)  6.18 us
    ppermute x2, starting transfers between devices, halo(): below = lax.ppermute(block[:, block.shape[1] - width:], 'gy', up_pairs)  5.49 us
    ppermute x2, waiting for transfers between devices, halo(): above = lax.ppermute(block[:, :width], 'gy', down_pairs)  5.4 us
  transfers between devices with their start and end apart: 30, of which 16 were waited for; matrix products, arithmetic and copies ran while one was open for 15% of the time, Pallas kernels for 0%

profile of v2, /device:TPU:30, one launch (start us, length us, event | category | flops | bytes accessed | tf_op | source)
XLA Modules:
  0.0 216.4 jit_solution(5688965687063487392)
XLA Ops:
  3.0 3.4 %collective-permute-start = (f32[5,3,64,128]{3,2,1,0:T(8,128)}, f32[5,3,64,128]{3,2,1,0:T(8,128)S(1)}, u32[]{:S(2)}, u32[]{:S(2)}) collective-permute-start(f32[5,3,64,128]{3,2,1,0:T(8,128)} %get-tuple-element.130), channel_id=1, source_target_pairs={{0,2},{2,4},{4,6},{6,8},{8,10},{10,12},{12,14},{14,16},{16,18},{18... | collective-permute-start | bytes 1474568 | tf_op jit(solution)/shard_map/ppermute | solution.py:223
  32.8 7.6 %collective-permute-start.2 = (f32[9,64,128]{2,1,0:T(8,128)S(1)}, f32[9,64,128]{2,1,0:T(8,128)S(1)}, u32[]{:S(2)}, u32[]{:S(2)}) collective-permute-start(f32[9,64,128]{2,1,0:T(8,128)S(1)} %pad_maximum_fusion.10), channel_id=1, source_target_pairs={{0,2},{2,4},{4,6},{6,8},{8,10},{10,12},{12,14},{14,16},{16,18},{18... | collective-permute-start | bytes 884744 | tf_op jit(solution)/shard_map/ppermute | solution.py:200
  43.3 2.8 %collective-permute-done.2 = f32[9,64,128]{2,1,0:T(8,128)S(1)} collective-permute-done((f32[9,64,128]{2,1,0:T(8,128)S(1)}, f32[9,64,128]{2,1,0:T(8,128)S(1)}, u32[]{:S(2)}, u32[]{:S(2)}) %collective-permute-start.2) | collective-permute-done | bytes 294944 | tf_op jit(solution)/shard_map/ppermute | solution.py:200
  46.2 4.1 %collective-permute-start.3 = (f32[9,64,128]{2,1,0:T(8,128)S(1)}, f32[9,64,128]{2,1,0:T(8,128)S(1)}, u32[]{:S(2)}, u32[]{:S(2)}) collective-permute-start(f32[9,64,128]{2,1,0:T(8,128)S(1)} %multiply_add_fusion.15), channel_id=1, source_target_pairs={{0,4},{2,6},{4,8},{6,10},{8,12},{10,14},{12,16},{14,18},{16,20},{1... | collective-permute-start | bytes 884744 | tf_op jit(solution)/shard_map/ppermute | solution.py:200
  50.3 11.2 %collective-permute-done.8 = f32[9,64,128]{2,1,0:T(8,128)S(1)} collective-permute-done((f32[9,64,128]{2,1,0:T(8,128)S(1)}, f32[9,64,128]{2,1,0:T(8,128)S(1)}, u32[]{:S(2)}, u32[]{:S(2)}) %collective-permute-start.8) | collective-permute-done | bytes 294944 | tf_op jit(solution)/shard_map/ppermute | solution.py:201
  67.1 8.4 %collective-permute-done.9 = f32[9,64,128]{2,1,0:T(8,128)S(1)} collective-permute-done((f32[9,64,128]{2,1,0:T(8,128)S(1)}, f32[9,64,128]{2,1,0:T(8,128)S(1)}, u32[]{:S(2)}, u32[]{:S(2)}) %collective-permute-start.9) | collective-permute-done | bytes 294944 | tf_op jit(solution)/shard_map/ppermute | solution.py:201
  79.6 12.8 %collective-permute-done.10 = f32[9,64,128]{2,1,0:T(8,128)S(1)} collective-permute-done((f32[9,64,128]{2,1,0:T(8,128)S(1)}, f32[9,64,128]{2,1,0:T(8,128)S(1)}, u32[]{:S(2)}, u32[]{:S(2)}) %collective-permute-start.10) | collective-permute-done | bytes 294944 | tf_op jit(solution)/shard_map/ppermute | solution.py:201
  94.6 3.8 %collective-permute-start.6 = (f32[9,64,128]{2,1,0:T(8,128)S(1)}, f32[9,64,128]{2,1,0:T(8,128)S(1)}, u32[]{:S(2)}, u32[]{:S(2)}) collective-permute-start(f32[9,64,128]{2,1,0:T(8,128)S(1)} %multiply_add_fusion.12), channel_id=1, source_target_pairs={{0,32},{2,34},{4,36},{6,38},{8,40},{10,42},{12,44},{14,46},{16,48}... | collective-permute-start | bytes 884744 | tf_op jit(solution)/shard_map/ppermute | solution.py:200
  98.4 5.1 %collective-permute-done.11 = f32[9,64,128]{2,1,0:T(8,128)S(1)} collective-permute-done((f32[9,64,128]{2,1,0:T(8,128)S(1)}, f32[9,64,128]{2,1,0:T(8,128)S(1)}, u32[]{:S(2)}, u32[]{:S(2)}) %collective-permute-start.11) | collective-permute-done | bytes 294944 | tf_op jit(solution)/shard_map/ppermute | solution.py:201
  106.2 6.5 %collective-permute-start.7 = (f32[9,64,128]{2,1,0:T(8,128)S(1)}, f32[9,64,128]{2,1,0:T(8,128)S(1)}, u32[]{:S(2)}, u32[]{:S(2)}) collective-permute-start(f32[9,64,128]{2,1,0:T(8,128)S(1)} %multiply_add_fusion.11), channel_id=1, source_target_pairs={{0,64},{2,66},{4,68},{6,70},{8,72},{10,74},{12,76},{14,78},{16,80}... | collective-permute-start | bytes 884744 | tf_op jit(solution)/shard_map/ppermute | solution.py:200
  117.0 7.2 %collective-permute-done.13 = f32[9,64,128]{2,1,0:T(8,128)S(1)} collective-permute-done((f32[9,64,128]{2,1,0:T(8,128)S(1)}, f32[9,64,128]{2,1,0:T(8,128)S(1)}, u32[]{:S(2)}, u32[]{:S(2)}) %collective-permute-start.13) | collective-permute-done | bytes 294944 | tf_op jit(solution)/shard_map/ppermute | solution.py:201
  129.4 3.7 %collective-permute-start.16 = (f32[5,2,64,128]{3,2,1,0:T(8,128)S(1)}, f32[5,2,64,128]{3,2,1,0:T(8,128)S(1)}, u32[]{:S(2)}, u32[]{:S(2)}) collective-permute-start(f32[5,2,64,128]{3,2,1,0:T(8,128)S(1)} %get-tuple-element.113), channel_id=1, source_target_pairs={{2,0},{4,2},{6,4},{8,6},{10,8},{12,10},{14,12},{16,14},{18,16},{20... | collective-permute-start | bytes 983048 | tf_op jit(solution)/shard_map/ppermute | solution.py:224
  134.1 2.9 %multiply_add_fusion = f32[5,8,64,128]{3,2,1,0:T(8,128)} fusion(f32[5,64,128]{2,1,0:T(8,128)S(1)} %slice-done.1, f32[8]{0:T(128)S(1)} %get-tuple-element.162, f32[5,64,128]{2,1,0:T(8,128)S(1)} %slice-done, f32[8]{0:T(128)S(1)} %get-tuple-element.163, f32[5,64,128]{2,1,0:T(8,128)S(1)} %get-tuple-element.144, f32[8]{0:T(128)S(1)} %get-tuple-element.3, ...), kind=kLoop, calls=%fused_computation.42 | loop fusion | flops 10158080 | bytes 3932672 | tf_op jit(solution)/shard_map/add | solution.py:211
  137.2 5.4 %collective-permute-done.16 = f32[5,2,64,128]{3,2,1,0:T(8,128)S(1)} collective-permute-done((f32[5,2,64,128]{3,2,1,0:T(8,128)S(1)}, f32[5,2,64,128]{3,2,1,0:T(8,128)S(1)}, u32[]{:S(2)}, u32[]{:S(2)}) %collective-permute-start.16) | collective-permute-done | bytes 327712 | tf_op jit(solution)/shard_map/ppermute | solution.py:224
  144.9 3.9 %collective-permute-start.23 = (f32[5,64,128]{2,1,0:T(8,128)S(1)}, f32[5,64,128]{2,1,0:T(8,128)S(1)}, u32[]{:S(2)}, u32[]{:S(2)}) collective-permute-start(f32[5,64,128]{2,1,0:T(8,128)S(1)} %get-tuple-element.149), channel_id=1, source_target_pairs={{2,0},{4,2},{6,4},{8,6},{10,8},{12,10},{14,12},{16,14},{18,16},{20... | collective-permute-start | bytes 491528 | tf_op jit(solution)/shard_map/ppermute | solution.py:201
  150.2 7.9 %collective-permute-done.23 = f32[5,64,128]{2,1,0:T(8,128)S(1)} collective-permute-done((f32[5,64,128]{2,1,0:T(8,128)S(1)}, f32[5,64,128]{2,1,0:T(8,128)S(1)}, u32[]{:S(2)}, u32[]{:S(2)}) %collective-permute-start.23) | collective-permute-done | bytes 163872 | tf_op jit(solution)/shard_map/ppermute | solution.py:201
  161.4 5.4 %collective-permute-start.24 = (f32[5,64,128]{2,1,0:T(8,128)S(1)}, f32[5,64,128]{2,1,0:T(8,128)S(1)}, u32[]{:S(2)}, u32[]{:S(2)}) collective-permute-start(f32[5,64,128]{2,1,0:T(8,128)S(1)} %get-tuple-element.147), channel_id=1, source_target_pairs={{4,0},{6,2},{8,4},{10,6},{12,8},{14,10},{16,12},{18,14},{20,16},{2... | collective-permute-start | bytes 491528 | tf_op jit(solution)/shard_map/ppermute | solution.py:201
  168.9 4.2 %collective-permute-done.24 = f32[5,64,128]{2,1,0:T(8,128)S(1)} collective-permute-done((f32[5,64,128]{2,1,0:T(8,128)S(1)}, f32[5,64,128]{2,1,0:T(8,128)S(1)}, u32[]{:S(2)}, u32[]{:S(2)}) %collective-permute-start.24) | collective-permute-done | bytes 163872 | tf_op jit(solution)/shard_map/ppermute | solution.py:201
  177.2 8.9 %collective-permute-done.25 = f32[5,64,128]{2,1,0:T(8,128)S(1)} collective-permute-done((f32[5,64,128]{2,1,0:T(8,128)S(1)}, f32[5,64,128]{2,1,0:T(8,128)S(1)}, u32[]{:S(2)}, u32[]{:S(2)}) %collective-permute-start.25) | collective-permute-done | bytes 163872 | tf_op jit(solution)/shard_map/ppermute | solution.py:201
  189.5 6.4 %collective-permute-done.26 = f32[5,64,128]{2,1,0:T(8,128)S(1)} collective-permute-done((f32[5,64,128]{2,1,0:T(8,128)S(1)}, f32[5,64,128]{2,1,0:T(8,128)S(1)}, u32[]{:S(2)}, u32[]{:S(2)}) %collective-permute-start.26) | collective-permute-done | bytes 163872 | tf_op jit(solution)/shard_map/ppermute | solution.py:201
  197.4 2.6 %collective-permute-start.22 = (f32[5,64,128]{2,1,0:T(8,128)S(1)}, f32[5,64,128]{2,1,0:T(8,128)S(1)}, u32[]{:S(2)}, u32[]{:S(2)}) collective-permute-start(f32[5,64,128]{2,1,0:T(8,128)S(1)} %multiply_add_fusion.24), channel_id=1, source_target_pairs={{0,64},{2,66},{4,68},{6,70},{8,72},{10,74},{12,76},{14,78},{16,80}... | collective-permute-start | bytes 491528 | tf_op jit(solution)/shard_map/ppermute | solution.py:200
  200.1 3.2 %collective-permute-done.27 = f32[5,64,128]{2,1,0:T(8,128)S(1)} collective-permute-done((f32[5,64,128]{2,1,0:T(8,128)S(1)}, f32[5,64,128]{2,1,0:T(8,128)S(1)}, u32[]{:S(2)}, u32[]{:S(2)}) %collective-permute-start.27) | collective-permute-done | bytes 163872 | tf_op jit(solution)/shard_map/ppermute | solution.py:201
  204.7 7.3 %collective-permute-done.28 = f32[5,64,128]{2,1,0:T(8,128)S(1)} collective-permute-done((f32[5,64,128]{2,1,0:T(8,128)S(1)}, f32[5,64,128]{2,1,0:T(8,128)S(1)}, u32[]{:S(2)}, u32[]{:S(2)}) %collective-permute-start.28) | collective-permute-done | bytes 163872 | tf_op jit(solution)/shard_map/ppermute | solution.py:201
  212.1 2.9 %fusion.3 = f32[5,8,64,128]{3,2,1,0:T(8,128)S(1)} fusion(f32[5,8,128,64]{2,3,1,0:T(8,128)S(1)} %fusion.108, f32[5,8,64,128]{3,2,1,0:T(8,128)S(1)} %collective-permute-done.29, f32[64,64,1,1]{0,1,3,2:T(8,128)S(1)} %copy-done.8, f32[5,8,64,128]{3,2,1,0:T(8,128)S(1)} %fusion.107, f32[5,64,128]{2,1,0:T(8,128)S(1)} %multiply_add_fusion.17, ...), kind=kOutput, calls=%fused_computation.36 | convolution fusion | flops 261816320 | bytes 7553472 | tf_op jit(solution)/shard_map/fyzx,zw->fywx/dot_general | solution.py:237
  (166 shorter events, 77.1 us)
Async XLA Ops:
  3.0 27.1 %collective-permute-start = (f32[5,3,64,128]{3,2,1,0:T(8,128)}, f32[5,3,64,128]{3,2,1,0:T(8,128)S(1)}, u32[]{:S(2)}, u32[]{:S(2)}) collective-permute-start(f32[5,3,64,128]{3,2,1,0:T(8,128)} %get-tuple-element.130), channel_id=1, source_target_pairs={{0,2},{2,4},{4,6},{6,8},{8,10},{10,12},{12,14},{14,16},{16,18},{18... | collective-permute-start | bytes 1474568 | tf_op jit(solution)/shard_map/ppermute | solution.py:223
  6.4 23.7 %collective-permute-start.1 = (f32[5,3,64,128]{3,2,1,0:T(8,128)}, f32[5,3,64,128]{3,2,1,0:T(8,128)S(1)}, u32[]{:S(2)}, u32[]{:S(2)}) collective-permute-start(f32[5,3,64,128]{3,2,1,0:T(8,128)} %get-tuple-element.131), channel_id=1, source_target_pairs={{2,0},{4,2},{6,4},{8,6},{10,8},{12,10},{14,12},{16,14},{18,16},{20... | collective-permute-start | bytes 1474568 | tf_op jit(solution)/shard_map/ppermute | solution.py:224
  32.8 13.3 %collective-permute-start.2 = (f32[9,64,128]{2,1,0:T(8,128)S(1)}, f32[9,64,128]{2,1,0:T(8,128)S(1)}, u32[]{:S(2)}, u32[]{:S(2)}) collective-permute-start(f32[9,64,128]{2,1,0:T(8,128)S(1)} %pad_maximum_fusion.10), channel_id=1, source_target_pairs={{0,2},{2,4},{4,6},{6,8},{8,10},{10,12},{12,14},{14,16},{16,18},{18... | collective-permute-start | bytes 884744 | tf_op jit(solution)/shard_map/ppermute | solution.py:200
  41.1 20.3 %collective-permute-start.8 = (f32[9,64,128]{2,1,0:T(8,128)S(1)}, f32[9,64,128]{2,1,0:T(8,128)S(1)}, u32[]{:S(2)}, u32[]{:S(2)}) collective-permute-start(f32[9,64,128]{2,1,0:T(8,128)S(1)} %pad_maximum_fusion.11), channel_id=1, source_target_pairs={{2,0},{4,2},{6,4},{8,6},{10,8},{12,10},{14,12},{16,14},{18,16},{20... | collective-permute-start | bytes 884744 | tf_op jit(solution)/shard_map/ppermute | solution.py:201
  43.2 61.8 %collective-permute-start.14 = (f32[4,8,64,128]{3,2,1,0:T(8,128)S(1)}, f32[4,8,64,128]{3,2,1,0:T(8,128)S(1)}, u32[]{:S(2)}, u32[]{:S(2)}) collective-permute-start(f32[4,8,64,128]{3,2,1,0:T(8,128)S(1)} %fusion.6), channel_id=1, source_target_pairs={{0,1},{1,0},{2,3},{3,2},{4,5},{5,4},{6,7},{7,6},{8,9},{9,8},{10,11... | collective-permute-start | bytes 3145736 | tf_op jit(solution)/shard_map/ppermute | solution.py:236
  46.2 18.3 %collective-permute-start.3 = (f32[9,64,128]{2,1,0:T(8,128)S(1)}, f32[9,64,128]{2,1,0:T(8,128)S(1)}, u32[]{:S(2)}, u32[]{:S(2)}) collective-permute-start(f32[9,64,128]{2,1,0:T(8,128)S(1)} %multiply_add_fusion.15), channel_id=1, source_target_pairs={{0,4},{2,6},{4,8},{6,10},{8,12},{10,14},{12,16},{14,18},{16,20},{1... | collective-permute-start | bytes 884744 | tf_op jit(solution)/shard_map/ppermute | solution.py:200
  61.6 13.9 %collective-permute-start.9 = (f32[9,64,128]{2,1,0:T(8,128)S(1)}, f32[9,64,128]{2,1,0:T(8,128)S(1)}, u32[]{:S(2)}, u32[]{:S(2)}) collective-permute-start(f32[9,64,128]{2,1,0:T(8,128)S(1)} %multiply_add_fusion.9), channel_id=1, source_target_pairs={{4,0},{6,2},{8,4},{10,6},{12,8},{14,10},{16,12},{18,14},{20,16},{2... | collective-permute-start | bytes 884744 | tf_op jit(solution)/shard_map/ppermute | solution.py:201
  64.6 12.9 %collective-permute-start.4 = (f32[9,64,128]{2,1,0:T(8,128)S(1)}, f32[9,64,128]{2,1,0:T(8,128)S(1)}, u32[]{:S(2)}, u32[]{:S(2)}) collective-permute-start(f32[9,64,128]{2,1,0:T(8,128)S(1)} %multiply_add_fusion.14), channel_id=1, source_target_pairs={{0,8},{2,10},{4,12},{6,14},{8,16},{10,18},{12,20},{14,22},{16,24},... | collective-permute-start | bytes 884744 | tf_op jit(solution)/shard_map/ppermute | solution.py:200
  75.5 16.9 %collective-permute-start.10 = (f32[9,64,128]{2,1,0:T(8,128)S(1)}, f32[9,64,128]{2,1,0:T(8,128)S(1)}, u32[]{:S(2)}, u32[]{:S(2)}) collective-permute-start(f32[9,64,128]{2,1,0:T(8,128)S(1)} %multiply_add_fusion.8), channel_id=1, source_target_pairs={{8,0},{10,2},{12,4},{14,6},{16,8},{18,10},{20,12},{22,14},{24,16},... | collective-permute-start | bytes 884744 | tf_op jit(solution)/shard_map/ppermute | solution.py:201
  77.7 16.8 %collective-permute-start.5 = (f32[9,64,128]{2,1,0:T(8,128)S(1)}, f32[9,64,128]{2,1,0:T(8,128)S(1)}, u32[]{:S(2)}, u32[]{:S(2)}) collective-permute-start(f32[9,64,128]{2,1,0:T(8,128)S(1)} %multiply_add_fusion.13), channel_id=1, source_target_pairs={{0,16},{2,18},{4,20},{6,22},{8,24},{10,26},{12,28},{14,30},{16,32}... | collective-permute-start | bytes 884744 | tf_op jit(solution)/shard_map/ppermute | solution.py:200
  92.5 11.0 %collective-permute-start.11 = (f32[9,64,128]{2,1,0:T(8,128)S(1)}, f32[9,64,128]{2,1,0:T(8,128)S(1)}, u32[]{:S(2)}, u32[]{:S(2)}) collective-permute-start(f32[9,64,128]{2,1,0:T(8,128)S(1)} %multiply_add_fusion.7), channel_id=1, source_target_pairs={{16,0},{18,2},{20,4},{22,6},{24,8},{26,10},{28,12},{30,14},{32,16}... | collective-permute-start | bytes 884744 | tf_op jit(solution)/shard_map/ppermute | solution.py:201
  94.6 11.5 %collective-permute-start.6 = (f32[9,64,128]{2,1,0:T(8,128)S(1)}, f32[9,64,128]{2,1,0:T(8,128)S(1)}, u32[]{:S(2)}, u32[]{:S(2)}) collective-permute-start(f32[9,64,128]{2,1,0:T(8,128)S(1)} %multiply_add_fusion.12), channel_id=1, source_target_pairs={{0,32},{2,34},{4,36},{6,38},{8,40},{10,42},{12,44},{14,46},{16,48}... | collective-permute-start | bytes 884744 | tf_op jit(solution)/shard_map/ppermute | solution.py:200
  103.6 10.4 %collective-permute-start.12 = (f32[9,64,128]{2,1,0:T(8,128)S(1)}, f32[9,64,128]{2,1,0:T(8,128)S(1)}, u32[]{:S(2)}, u32[]{:S(2)}) collective-permute-start(f32[9,64,128]{2,1,0:T(8,128)S(1)} %multiply_add_fusion.6), channel_id=1, source_target_pairs={{32,0},{34,2},{36,4},{38,6},{40,8},{42,10},{44,12},{46,14},{48,16}... | collective-permute-start | bytes 884744 | tf_op jit(solution)/shard_map/ppermute | solution.py:201
  106.2 10.7 %collective-permute-start.7 = (f32[9,64,128]{2,1,0:T(8,128)S(1)}, f32[9,64,128]{2,1,0:T(8,128)S(1)}, u32[]{:S(2)}, u32[]{:S(2)}) collective-permute-start(f32[9,64,128]{2,1,0:T(8,128)S(1)} %multiply_add_fusion.11), channel_id=1, source_target_pairs={{0,64},{2,66},{4,68},{6,70},{8,72},{10,74},{12,76},{14,78},{16,80}... | collective-permute-start | bytes 884744 | tf_op jit(solution)/shard_map/ppermute | solution.py:200
  114.1 10.1 %collective-permute-start.13 = (f32[9,64,128]{2,1,0:T(8,128)S(1)}, f32[9,64,128]{2,1,0:T(8,128)S(1)}, u32[]{:S(2)}, u32[]{:S(2)}) collective-permute-start(f32[9,64,128]{2,1,0:T(8,128)S(1)} %multiply_add_fusion.5), channel_id=1, source_target_pairs={{64,0},{66,2},{68,4},{70,6},{72,8},{74,10},{76,12},{78,14},{80,16}... | collective-permute-start | bytes 884744 | tf_op jit(solution)/shard_map/ppermute | solution.py:201
  127.3 9.9 %collective-permute-start.15 = (f32[5,2,64,128]{3,2,1,0:T(8,128)S(1)}, f32[5,2,64,128]{3,2,1,0:T(8,128)S(1)}, u32[]{:S(2)}, u32[]{:S(2)}) collective-permute-start(f32[5,2,64,128]{3,2,1,0:T(8,128)S(1)} %get-tuple-element.112), channel_id=1, source_target_pairs={{0,2},{2,4},{4,6},{6,8},{8,10},{10,12},{12,14},{14,16},{16,18},{18... | collective-permute-start | bytes 983048 | tf_op jit(solution)/shard_map/ppermute | solution.py:223
  129.4 13.2 %collective-permute-start.16 = (f32[5,2,64,128]{3,2,1,0:T(8,128)S(1)}, f32[5,2,64,128]{3,2,1,0:T(8,128)S(1)}, u32[]{:S(2)}, u32[]{:S(2)}) collective-permute-start(f32[5,2,64,128]{3,2,1,0:T(8,128)S(1)} %get-tuple-element.113), channel_id=1, source_target_pairs={{2,0},{4,2},{6,4},{8,6},{10,8},{12,10},{14,12},{16,14},{18,16},{20... | collective-permute-start | bytes 983048 | tf_op jit(solution)/shard_map/ppermute | solution.py:224
  133.4 78.7 %collective-permute-start.29 = (f32[5,8,64,128]{3,2,1,0:T(8,128)S(1)}, f32[5,8,64,128]{3,2,1,0:T(8,128)S(1)}, u32[]{:S(2)}, u32[]{:S(2)}) collective-permute-start(f32[5,8,64,128]{3,2,1,0:T(8,128)S(1)} %fusion.12), channel_id=1, source_target_pairs={{0,1},{1,0},{2,3},{3,2},{4,5},{5,4},{6,7},{7,6},{8,9},{9,8},{10,11... | collective-permute-start | bytes 3932168 | tf_op jit(solution)/shard_map/ppermute | solution.py:236
  144.9 13.2 %collective-permute-start.23 = (f32[5,64,128]{2,1,0:T(8,128)S(1)}, f32[5,64,128]{2,1,0:T(8,128)S(1)}, u32[]{:S(2)}, u32[]{:S(2)}) collective-permute-start(f32[5,64,128]{2,1,0:T(8,128)S(1)} %get-tuple-element.149), channel_id=1, source_target_pairs={{2,0},{4,2},{6,4},{8,6},{10,8},{12,10},{14,12},{16,14},{18,16},{20... | collective-permute-start | bytes 491528 | tf_op jit(solution)/shard_map/ppermute | solution.py:201
  161.4 11.7 %collective-permute-start.24 = (f32[5,64,128]{2,1,0:T(8,128)S(1)}, f32[5,64,128]{2,1,0:T(8,128)S(1)}, u32[]{:S(2)}, u32[]{:S(2)}) collective-permute-start(f32[5,64,128]{2,1,0:T(8,128)S(1)} %get-tuple-element.147), channel_id=1, source_target_pairs={{4,0},{6,2},{8,4},{10,6},{12,8},{14,10},{16,12},{18,14},{20,16},{2... | collective-permute-start | bytes 491528 | tf_op jit(solution)/shard_map/ppermute | solution.py:201
  173.2 12.9 %collective-permute-start.25 = (f32[5,64,128]{2,1,0:T(8,128)S(1)}, f32[5,64,128]{2,1,0:T(8,128)S(1)}, u32[]{:S(2)}, u32[]{:S(2)}) collective-permute-start(f32[5,64,128]{2,1,0:T(8,128)S(1)} %multiply_add_fusion.21), channel_id=1, source_target_pairs={{8,0},{10,2},{12,4},{14,6},{16,8},{18,10},{20,12},{22,14},{24,16},... | collective-permute-start | bytes 491528 | tf_op jit(solution)/shard_map/ppermute | solution.py:201
  175.3 12.9 %collective-permute-start.20 = (f32[5,64,128]{2,1,0:T(8,128)S(1)}, f32[5,64,128]{2,1,0:T(8,128)S(1)}, u32[]{:S(2)}, u32[]{:S(2)}) collective-permute-start(f32[5,64,128]{2,1,0:T(8,128)S(1)} %multiply_add_fusion.26), channel_id=1, source_target_pairs={{0,16},{2,18},{4,20},{6,22},{8,24},{10,26},{12,28},{14,30},{16,32}... | collective-permute-start | bytes 491528 | tf_op jit(solution)/shard_map/ppermute | solution.py:200
  186.2 9.7 %collective-permute-start.26 = (f32[5,64,128]{2,1,0:T(8,128)S(1)}, f32[5,64,128]{2,1,0:T(8,128)S(1)}, u32[]{:S(2)}, u32[]{:S(2)}) collective-permute-start(f32[5,64,128]{2,1,0:T(8,128)S(1)} %multiply_add_fusion.20), channel_id=1, source_target_pairs={{16,0},{18,2},{20,4},{22,6},{24,8},{26,10},{28,12},{30,14},{32,16}... | collective-permute-start | bytes 491528 | tf_op jit(solution)/shard_map/ppermute | solution.py:201
  188.2 9.1 %collective-permute-start.21 = (f32[5,64,128]{2,1,0:T(8,128)S(1)}, f32[5,64,128]{2,1,0:T(8,128)S(1)}, u32[]{:S(2)}, u32[]{:S(2)}) collective-permute-start(f32[5,64,128]{2,1,0:T(8,128)S(1)} %multiply_add_fusion.25), channel_id=1, source_target_pairs={{0,32},{2,34},{4,36},{6,38},{8,40},{10,42},{12,44},{14,46},{16,48}... | collective-permute-start | bytes 491528 | tf_op jit(solution)/shard_map/ppermute | solution.py:200
  (17 other events, 137.7 us)

commit v3 on v2

--- a/solution.py
+++ b/solution.py
@@ -152,28 +152,78 @@
         combine[block, rows + 1] = fall_part @ rows_stencil
         rise_gain[block] = scale[own] * alpha
         fall_gain[block] = scale[own] * beta
+    return combine, rise_gain, fall_gain, rise_step, fall_step
+
+
+def scan_rounds(blocks):
     rounds = []
-    shift = 1
-    while shift < blocks:
-        rise = np.zeros(blocks)
-        fall = np.zeros(blocks)
-        for block in range(blocks):
-            if block - shift >= 0:
-                rise[block] = np.prod(rise_step[block - shift + 1 : block + 1])
-            if block + shift <= blocks - 1:
-                fall[block] = np.prod(fall_step[block : block + shift])
-        rounds.append((shift, rise, fall))
-        shift *= 2
-    return combine, rise_gain, fall_gain, rounds
-
-
-def wall_apply(groups, rows, pad, position):
+    stride = 1
+    while stride < blocks:
+        radix = min(4, -(-blocks // stride))
+        rounds.append((stride, list(range(1, radix))))
+        stride *= radix
+    return rounds
+
+
+def scan_coefs(rise_step, fall_step, shift):
+    blocks = rise_step.shape[0]
+    rise = np.zeros(blocks)
+    fall = np.zeros(blocks)
+    for block in range(blocks):
+        if block - shift >= 0:
+            rise[block] = np.prod(rise_step[block - shift + 1 : block + 1])
+        if block + shift <= blocks - 1:
+            fall[block] = np.prod(fall_step[block : block + shift])
+    return rise, fall
+
+
+class TableBank:
+    def __init__(self):
+        self.parts = []
+        self.width = 0
+
+    def add(self, table):
+        table = np.asarray(table, np.float64)
+        handle = (self.width, table.shape[1:])
+        self.parts.append(table.reshape(table.shape[0], -1))
+        self.width += self.parts[-1].shape[1]
+        return handle
+
+    def lookup(self, position):
+        whole = jnp.asarray(np.concatenate(self.parts, axis=1), jnp.float32)
+        self.row = lax.dynamic_index_in_dim(whole, position, 0, keepdims=False)
+
+    def get(self, handle):
+        start, shape = handle
+        return self.row[start : start + int(np.prod(shape))].reshape(shape)
+
+
+def plan_wall(bank, kinds_sizes, points, rows, pad):
+    tables = [wall_tables(kind, points, rows, pad) for kind, _ in kinds_sizes]
+    groups = [
+        (bank.add(table[0]), bank.add(table[1]), bank.add(table[2])) for table in tables
+    ]
+    blocks = points // rows
+    rounds = []
+    for stride, multiples in scan_rounds(blocks):
+        entries = []
+        for multiple in multiples:
+            shift = stride * multiple
+            coefs = [scan_coefs(table[3], table[4], shift) for table in tables]
+            rise = np.concatenate(
+                [np.repeat(c[0][:, None], n, 1) for c, (_, n) in zip(coefs, kinds_sizes)], 1
+            )
+            fall = np.concatenate(
+                [np.repeat(c[1][:, None], n, 1) for c, (_, n) in zip(coefs, kinds_sizes)], 1
+            )
+            entries.append((shift, bank.add(rise), bank.add(fall)))
+        rounds.append(entries)
+    return groups, rounds
+
+
+def wall_apply(bank, plan, padded_groups, rows, pad):
     count = lax.axis_size("gy")
-    points = rows * count
-    tables = [wall_tables(kind, points, rows, pad) for _, kind in groups]
-    pick = lambda table: lax.dynamic_index_in_dim(
-        jnp.asarray(table, jnp.float32), position, 0, keepdims=False
-    )
+    groups, rounds = plan
 
     def taps(padded, combine):
         summed = None
@@ -183,30 +233,28 @@
         return summed
 
     partials = [
-        taps(padded, pick(table[0])[rows:]) for (padded, _), table in zip(groups, tables)
+        taps(padded, bank.get(handles[0])[rows:])
+        for padded, handles in zip(padded_groups, groups)
     ]
-    sizes = [padded.shape[0] for padded, _ in groups]
+    sizes = [padded.shape[0] for padded in padded_groups]
     rise = jnp.concatenate([part[:, 0] for part in partials], axis=0)
     fall = jnp.concatenate([part[:, 1] for part in partials], axis=0)
-    for level, (shift, _, _) in enumerate(tables[0][3]):
-        rise_coef = pick(
-            np.concatenate([np.repeat(t[3][level][1][:, None], n, 1) for t, n in zip(tables, sizes)], 1)
-        )
-        fall_coef = pick(
-            np.concatenate([np.repeat(t[3][level][2][:, None], n, 1) for t, n in zip(tables, sizes)], 1)
-        )
-        up_pairs = [(i, i + shift) for i in range(count - shift)]
-        down_pairs = [(i + shift, i) for i in range(count - shift)]
-        from_below = lax.ppermute(rise, "gy", up_pairs)
-        from_above = lax.ppermute(fall, "gy", down_pairs)
-        rise = rise + rise_coef[:, None, None] * from_below
-        fall = fall + fall_coef[:, None, None] * from_above
+    for entries in rounds:
+        rise_next, fall_next = rise, fall
+        for shift, rise_handle, fall_handle in entries:
+            up_pairs = [(i, i + shift) for i in range(count - shift)]
+            down_pairs = [(i + shift, i) for i in range(count - shift)]
+            from_below = lax.ppermute(rise, "gy", up_pairs)
+            from_above = lax.ppermute(fall, "gy", down_pairs)
+            rise_next = rise_next + bank.get(rise_handle)[:, None, None] * from_below
+            fall_next = fall_next + bank.get(fall_handle)[:, None, None] * from_above
+        rise, fall = rise_next, fall_next
     results = []
     first = 0
-    for (padded, _), table, size in zip(groups, tables, sizes):
-        local = taps(padded, pick(table[0])[:rows])
-        rise_gain = pick(table[1])
-        fall_gain = pick(table[2])
+    for padded, handles, size in zip(padded_groups, groups, sizes):
+        local = taps(padded, bank.get(handles[0])[:rows])
+        rise_gain = bank.get(handles[1])
+        fall_gain = bank.get(handles[2])
         results.append(
             local
             + rise_gain[None, :, None, None] * rise[first : first + size, None]
@@ -268,6 +316,11 @@
     own_block = jnp.asarray(span_full[:span_own, :span_own], jnp.float32)
     other_block = jnp.asarray(span_full[span_own : 2 * span_own, :span_own], jnp.float32)
 
+    bank = TableBank()
+    first_plan = plan_wall(bank, [("slope", 4), ("smooth", 5)], points, rows, 3)
+    second_plan = plan_wall(bank, [("slope", 5)], points, rows, 2)
+    bank.lookup(position)
+
     state = jnp.concatenate(
         [mass_per_volume[None], mass_flux_vector, total_heat_content[None]], axis=0
     )
@@ -281,9 +334,7 @@
     warmth_pad = push_pad / density
     basic_pad = jnp.concatenate([speed_pad, warmth_pad[None]], axis=0)
 
-    wall_grad, smoothed = wall_apply(
-        [(basic_pad, "slope"), (padded, "smooth")], rows, 3, position
-    )
+    wall_grad, smoothed = wall_apply(bank, first_plan, [basic_pad, padded], rows, 3)
 
     basic = basic_pad[:, 3 : 3 + rows]
     speed = basic[:3]
@@ -295,7 +346,7 @@
     energy = total_heat_content
 
     flux_wall = flux_along(1, momentum, energy, speed, push, gradients)
-    (wall_term,) = wall_apply([(halo(flux_wall, 2), "slope")], rows, 2, position)
+    (wall_term,) = wall_apply(bank, second_plan, [halo(flux_wall, 2)], rows, 2)
     stream_term = stream_slope(
         flux_along(0, momentum, energy, speed, push, gradients), stream_matrix
     )

time: 218 us -> 225 us (1.032)
  starting transfers between devices: 76 us -> 118 us
  waiting for transfers between devices: 92.7 us -> 67.1 us
  local copies, waits for them, and re-layouts: 24.9 us -> 13.1 us
    ppermute x12 -> x18, waiting for transfers between devices: 83.8 us -> 41.4 us  [wall_apply(): from_above = lax.ppermute(fall, 'gy', down_pairs)]
    ppermute x12 -> x18, starting transfers between devices: 26 us -> 57.2 us  [wall_apply(): from_above = lax.ppermute(fall, 'gy', down_pairs)]
    ppermute x2, waiting for transfers between devices: 5.4 us -> 17 us  [halo(): above = lax.ppermute(block[:, :width], 'gy', down_pairs)]
    mul x22 -> x4, local copies, waits for them, and re-layouts: 15.3 us -> 3.97 us  [wall_apply(): rise_next = rise_next + bank.get(rise_handle)[:, None, None] * from_below]
    ppermute x12 -> x18, starting transfers between devices: 38.1 us -> 49.1 us  [wall_apply(): from_below = lax.ppermute(rise, 'gy', up_pairs)]
    ppermute x2, waiting for transfers between devices: 0.01 us -> 2.63 us  [halo(): below = lax.ppermute(block[:, block.shape[1] - width:], 'gy', up_pairs)]
    ppermute x12 -> x18, waiting for transfers between devices: 3.41 us -> 5.99 us  [wall_apply(): from_below = lax.ppermute(rise, 'gy', up_pairs)]
  transfers between devices with their start and end apart: 30 -> 42, of which waited for: 16 -> 14; matrix products, arithmetic and copies ran while one was open for 15% -> 9% of each run, Pallas kernels for 0% -> 0%
where the time goes in v3:
time: 225 us; the launch traced here: 221 us
  starting transfers between devices  118 us (52%)
  waiting for transfers between devices  67.1 us (30%)
  local copies, waits for them, and re-layouts  13.1 us (6%)
  other arithmetic  12.3 us (5%)
  matrix products  8.53 us (4%)
    ppermute x18, starting transfers between devices, wall_apply(): from_above = lax.ppermute(fall, 'gy', down_pairs)  57.2 us
    ppermute x18, starting transfers between devices, wall_apply(): from_below = lax.ppermute(rise, 'gy', up_pairs)  49.1 us
    ppermute x18, waiting for transfers between devices, wall_apply(): from_above = lax.ppermute(fall, 'gy', down_pairs)  41.4 us
    ppermute x2, waiting for transfers between devices, halo(): above = lax.ppermute(block[:, :width], 'gy', down_pairs)  17 us
    ppermute x2, starting transfers between devices, halo(): above = lax.ppermute(block[:, :width], 'gy', down_pairs)  6.35 us
    ppermute x18, waiting for transfers between devices, wall_apply(): from_below = lax.ppermute(rise, 'gy', up_pairs)  5.99 us
    ppermute x2, starting transfers between devices, halo(): below = lax.ppermute(block[:, block.shape[1] - width:], 'gy', up_pairs)  5.44 us
  transfers between devices with their start and end apart: 42, of which 14 were waited for; matrix products, arithmetic and copies ran while one was open for 9% of the time, Pallas kernels for 0%

profile of v3, /device:TPU:30, one launch (start us, length us, event | category | flops | bytes accessed | tf_op | source)
XLA Modules:
  0.0 221.2 jit_solution(4205933560286139760)
XLA Ops:
  3.0 3.4 %collective-permute-start = (f32[5,3,64,128]{3,2,1,0:T(8,128)}, f32[5,3,64,128]{3,2,1,0:T(8,128)S(1)}, u32[]{:S(2)}, u32[]{:S(2)}) collective-permute-start(f32[5,3,64,128]{3,2,1,0:T(8,128)} %get-tuple-element.134), channel_id=1, source_target_pairs={{0,2},{2,4},{4,6},{6,8},{8,10},{10,12},{12,14},{14,16},{16,18},{18... | collective-permute-start | bytes 1474568 | tf_op jit(solution)/shard_map/ppermute | solution.py:271
  19.1 6.3 %collective-permute-done.1 = f32[5,3,64,128]{3,2,1,0:T(8,128)S(1)} collective-permute-done((f32[5,3,64,128]{3,2,1,0:T(8,128)}, f32[5,3,64,128]{3,2,1,0:T(8,128)S(1)}, u32[]{:S(2)}, u32[]{:S(2)}) %collective-permute-start.1) | collective-permute-done | bytes 491552 | tf_op jit(solution)/shard_map/ppermute | solution.py:272
  34.7 3.7 %collective-permute-start.11 = (f32[9,64,128]{2,1,0:T(8,128)S(1)}, f32[9,64,128]{2,1,0:T(8,128)S(1)}, u32[]{:S(2)}, u32[]{:S(2)}) collective-permute-start(f32[9,64,128]{2,1,0:T(8,128)S(1)} %pad_maximum_fusion.11), channel_id=1, source_target_pairs={{2,0},{4,2},{6,4},{8,6},{10,8},{12,10},{14,12},{16,14},{18,16},{20... | collective-permute-start | bytes 884744 | tf_op jit(solution)/shard_map/ppermute | solution.py:248
  38.4 5.4 %collective-permute-start.12 = (f32[9,64,128]{2,1,0:T(8,128)S(1)}, f32[9,64,128]{2,1,0:T(8,128)S(1)}, u32[]{:S(2)}, u32[]{:S(2)}) collective-permute-start(f32[9,64,128]{2,1,0:T(8,128)S(1)} %pad_maximum_fusion.11), channel_id=1, source_target_pairs={{4,0},{6,2},{8,4},{10,6},{12,8},{14,10},{16,12},{18,14},{20,16},{2... | collective-permute-start | bytes 884744 | tf_op jit(solution)/shard_map/ppermute | solution.py:248
  43.8 5.6 %collective-permute-start.13 = (f32[9,64,128]{2,1,0:T(8,128)S(1)}, f32[9,64,128]{2,1,0:T(8,128)S(1)}, u32[]{:S(2)}, u32[]{:S(2)}) collective-permute-start(f32[9,64,128]{2,1,0:T(8,128)S(1)} %pad_maximum_fusion.11), channel_id=1, source_target_pairs={{6,0},{8,2},{10,4},{12,6},{14,8},{16,10},{18,12},{20,14},{22,16},{... | collective-permute-start | bytes 884744 | tf_op jit(solution)/shard_map/ppermute | solution.py:248
  49.6 3.5 %collective-permute-start.5 = (f32[9,64,128]{2,1,0:T(8,128)S(1)}, f32[9,64,128]{2,1,0:T(8,128)S(1)}, u32[]{:S(2)}, u32[]{:S(2)}) collective-permute-start(f32[9,64,128]{2,1,0:T(8,128)S(1)} %multiply_add_fusion.9), channel_id=1, source_target_pairs={{0,8},{2,10},{4,12},{6,14},{8,16},{10,18},{12,20},{14,22},{16,24},... | collective-permute-start | bytes 884744 | tf_op jit(solution)/shard_map/ppermute | solution.py:247
  55.2 6.0 %collective-permute-start.7 = (f32[9,64,128]{2,1,0:T(8,128)S(1)}, f32[9,64,128]{2,1,0:T(8,128)S(1)}, u32[]{:S(2)}, u32[]{:S(2)}) collective-permute-start(f32[9,64,128]{2,1,0:T(8,128)S(1)} %multiply_add_fusion.9), channel_id=1, source_target_pairs={{0,24},{2,26},{4,28},{6,30},{8,32},{10,34},{12,36},{14,38},{16,40}... | collective-permute-start | bytes 884744 | tf_op jit(solution)/shard_map/ppermute | solution.py:247
  65.3 4.4 %collective-permute-start.14 = (f32[9,64,128]{2,1,0:T(8,128)S(1)}, f32[9,64,128]{2,1,0:T(8,128)S(1)}, u32[]{:S(2)}, u32[]{:S(2)}) collective-permute-start(f32[9,64,128]{2,1,0:T(8,128)S(1)} %multiply_add_fusion.6), channel_id=1, source_target_pairs={{8,0},{10,2},{12,4},{14,6},{16,8},{18,10},{20,12},{22,14},{24,16},... | collective-permute-start | bytes 884744 | tf_op jit(solution)/shard_map/ppermute | solution.py:248
  73.5 4.2 %collective-permute-done.7 = f32[9,64,128]{2,1,0:T(8,128)S(1)} collective-permute-done((f32[9,64,128]{2,1,0:T(8,128)S(1)}, f32[9,64,128]{2,1,0:T(8,128)S(1)}, u32[]{:S(2)}, u32[]{:S(2)}) %collective-permute-start.7) | collective-permute-done | bytes 294944 | tf_op jit(solution)/shard_map/ppermute | solution.py:247
  77.9 4.5 %collective-permute-start.10 = (f32[9,64,128]{2,1,0:T(8,128)S(1)}, f32[9,64,128]{2,1,0:T(8,128)S(1)}, u32[]{:S(2)}, u32[]{:S(2)}) collective-permute-start(f32[9,64,128]{2,1,0:T(8,128)S(1)} %multiply_add_fusion.8), channel_id=1, source_target_pairs={{0,96},{2,98},{4,100},{6,102},{8,104},{10,106},{12,108},{14,110},{... | collective-permute-start | bytes 884744 | tf_op jit(solution)/shard_map/ppermute | solution.py:247
  83.8 10.8 %collective-permute-done.14 = f32[9,64,128]{2,1,0:T(8,128)S(1)} collective-permute-done((f32[9,64,128]{2,1,0:T(8,128)S(1)}, f32[9,64,128]{2,1,0:T(8,128)S(1)}, u32[]{:S(2)}, u32[]{:S(2)}) %collective-permute-start.14) | collective-permute-done | bytes 294944 | tf_op jit(solution)/shard_map/ppermute | solution.py:248
  94.6 7.4 %collective-permute-start.9 = (f32[9,64,128]{2,1,0:T(8,128)S(1)}, f32[9,64,128]{2,1,0:T(8,128)S(1)}, u32[]{:S(2)}, u32[]{:S(2)}) collective-permute-start(f32[9,64,128]{2,1,0:T(8,128)S(1)} %multiply_add_fusion.8), channel_id=1, source_target_pairs={{0,64},{2,66},{4,68},{6,70},{8,72},{10,74},{12,76},{14,78},{16,80}... | collective-permute-start | bytes 884744 | tf_op jit(solution)/shard_map/ppermute | solution.py:247
  108.3 4.1 %collective-permute-done.17 = f32[9,64,128]{2,1,0:T(8,128)S(1)} collective-permute-done((f32[9,64,128]{2,1,0:T(8,128)S(1)}, f32[9,64,128]{2,1,0:T(8,128)S(1)}, u32[]{:S(2)}, u32[]{:S(2)}) %collective-permute-start.17) | collective-permute-done | bytes 294944 | tf_op jit(solution)/shard_map/ppermute | solution.py:248
  115.3 6.2 %collective-permute-done.19 = f32[9,64,128]{2,1,0:T(8,128)S(1)} collective-permute-done((f32[9,64,128]{2,1,0:T(8,128)S(1)}, f32[9,64,128]{2,1,0:T(8,128)S(1)}, u32[]{:S(2)}, u32[]{:S(2)}) %collective-permute-start.19) | collective-permute-done | bytes 294944 | tf_op jit(solution)/shard_map/ppermute | solution.py:248
  132.5 3.9 %collective-permute-start.22 = (f32[5,2,64,128]{3,2,1,0:T(8,128)S(1)}, f32[5,2,64,128]{3,2,1,0:T(8,128)S(1)}, u32[]{:S(2)}, u32[]{:S(2)}) collective-permute-start(f32[5,2,64,128]{3,2,1,0:T(8,128)S(1)} %get-tuple-element.117), channel_id=1, source_target_pairs={{2,0},{4,2},{6,4},{8,6},{10,8},{12,10},{14,12},{16,14},{18,16},{20... | collective-permute-start | bytes 983048 | tf_op jit(solution)/shard_map/ppermute | solution.py:272
  139.3 10.8 %collective-permute-done.22 = f32[5,2,64,128]{3,2,1,0:T(8,128)S(1)} collective-permute-done((f32[5,2,64,128]{3,2,1,0:T(8,128)S(1)}, f32[5,2,64,128]{3,2,1,0:T(8,128)S(1)}, u32[]{:S(2)}, u32[]{:S(2)}) %collective-permute-start.22) | collective-permute-done | bytes 327712 | tf_op jit(solution)/shard_map/ppermute | solution.py:272
  157.4 3.9 %collective-permute-start.32 = (f32[5,64,128]{2,1,0:T(8,128)S(1)}, f32[5,64,128]{2,1,0:T(8,128)S(1)}, u32[]{:S(2)}, u32[]{:S(2)}) collective-permute-start(f32[5,64,128]{2,1,0:T(8,128)S(1)} %get-tuple-element.153), channel_id=1, source_target_pairs={{2,0},{4,2},{6,4},{8,6},{10,8},{12,10},{14,12},{16,14},{18,16},{20... | collective-permute-start | bytes 491528 | tf_op jit(solution)/shard_map/ppermute | solution.py:248
  161.4 6.0 %collective-permute-start.33 = (f32[5,64,128]{2,1,0:T(8,128)S(1)}, f32[5,64,128]{2,1,0:T(8,128)S(1)}, u32[]{:S(2)}, u32[]{:S(2)}) collective-permute-start(f32[5,64,128]{2,1,0:T(8,128)S(1)} %get-tuple-element.153), channel_id=1, source_target_pairs={{4,0},{6,2},{8,4},{10,6},{12,8},{14,10},{16,12},{18,14},{20,16},{2... | collective-permute-start | bytes 491528 | tf_op jit(solution)/shard_map/ppermute | solution.py:248
  167.4 5.4 %collective-permute-start.34 = (f32[5,64,128]{2,1,0:T(8,128)S(1)}, f32[5,64,128]{2,1,0:T(8,128)S(1)}, u32[]{:S(2)}, u32[]{:S(2)}) collective-permute-start(f32[5,64,128]{2,1,0:T(8,128)S(1)} %get-tuple-element.153), channel_id=1, source_target_pairs={{6,0},{8,2},{10,4},{12,6},{14,8},{16,10},{18,12},{20,14},{22,16},{... | collective-permute-start | bytes 491528 | tf_op jit(solution)/shard_map/ppermute | solution.py:248
  173.3 5.3 %collective-permute-done.34 = f32[5,64,128]{2,1,0:T(8,128)S(1)} collective-permute-done((f32[5,64,128]{2,1,0:T(8,128)S(1)}, f32[5,64,128]{2,1,0:T(8,128)S(1)}, u32[]{:S(2)}, u32[]{:S(2)}) %collective-permute-start.34) | collective-permute-done | bytes 163872 | tf_op jit(solution)/shard_map/ppermute | solution.py:248
  185.9 3.3 %collective-permute-start.35 = (f32[5,64,128]{2,1,0:T(8,128)S(1)}, f32[5,64,128]{2,1,0:T(8,128)S(1)}, u32[]{:S(2)}, u32[]{:S(2)}) collective-permute-start(f32[5,64,128]{2,1,0:T(8,128)S(1)} %get-tuple-element.151), channel_id=1, source_target_pairs={{8,0},{10,2},{12,4},{14,6},{16,8},{18,10},{20,12},{22,14},{24,16},... | collective-permute-start | bytes 491528 | tf_op jit(solution)/shard_map/ppermute | solution.py:248
  189.2 6.0 %collective-permute-start.36 = (f32[5,64,128]{2,1,0:T(8,128)S(1)}, f32[5,64,128]{2,1,0:T(8,128)S(1)}, u32[]{:S(2)}, u32[]{:S(2)}) collective-permute-start(f32[5,64,128]{2,1,0:T(8,128)S(1)} %get-tuple-element.151), channel_id=1, source_target_pairs={{16,0},{18,2},{20,4},{22,6},{24,8},{26,10},{28,12},{30,14},{32,16}... | collective-permute-start | bytes 491528 | tf_op jit(solution)/shard_map/ppermute | solution.py:248
  197.3 3.6 %collective-permute-start.29 = (f32[5,64,128]{2,1,0:T(8,128)S(1)}, f32[5,64,128]{2,1,0:T(8,128)S(1)}, u32[]{:S(2)}, u32[]{:S(2)}) collective-permute-start(f32[5,64,128]{2,1,0:T(8,128)S(1)} %multiply_add_fusion.15), channel_id=1, source_target_pairs={{0,32},{2,34},{4,36},{6,38},{8,40},{10,42},{12,44},{14,46},{16,48}... | collective-permute-start | bytes 491528 | tf_op jit(solution)/shard_map/ppermute | solution.py:247
  207.7 3.2 %collective-permute-done.38 = f32[5,64,128]{2,1,0:T(8,128)S(1)} collective-permute-done((f32[5,64,128]{2,1,0:T(8,128)S(1)}, f32[5,64,128]{2,1,0:T(8,128)S(1)}, u32[]{:S(2)}, u32[]{:S(2)}) %collective-permute-start.38) | collective-permute-done | bytes 163872 | tf_op jit(solution)/shard_map/ppermute | solution.py:248
  (165 shorter events, 92.6 us)
Async XLA Ops:
  3.0 16.1 %collective-permute-start = (f32[5,3,64,128]{3,2,1,0:T(8,128)}, f32[5,3,64,128]{3,2,1,0:T(8,128)S(1)}, u32[]{:S(2)}, u32[]{:S(2)}) collective-permute-start(f32[5,3,64,128]{3,2,1,0:T(8,128)} %get-tuple-element.134), channel_id=1, source_target_pairs={{0,2},{2,4},{4,6},{6,8},{8,10},{10,12},{12,14},{14,16},{16,18},{18... | collective-permute-start | bytes 1474568 | tf_op jit(solution)/shard_map/ppermute | solution.py:271
  6.4 19.0 %collective-permute-start.1 = (f32[5,3,64,128]{3,2,1,0:T(8,128)}, f32[5,3,64,128]{3,2,1,0:T(8,128)S(1)}, u32[]{:S(2)}, u32[]{:S(2)}) collective-permute-start(f32[5,3,64,128]{3,2,1,0:T(8,128)} %get-tuple-element.135), channel_id=1, source_target_pairs={{2,0},{4,2},{6,4},{8,6},{10,8},{12,10},{14,12},{16,14},{18,16},{20... | collective-permute-start | bytes 1474568 | tf_op jit(solution)/shard_map/ppermute | solution.py:272
  27.2 16.7 %collective-permute-start.2 = (f32[9,64,128]{2,1,0:T(8,128)S(1)}, f32[9,64,128]{2,1,0:T(8,128)S(1)}, u32[]{:S(2)}, u32[]{:S(2)}) collective-permute-start(f32[9,64,128]{2,1,0:T(8,128)S(1)} %pad_maximum_fusion.10), channel_id=1, source_target_pairs={{0,2},{2,4},{4,6},{6,8},{8,10},{10,12},{12,14},{14,16},{16,18},{18... | collective-permute-start | bytes 884744 | tf_op jit(solution)/shard_map/ppermute | solution.py:247
  29.4 20.0 %collective-permute-start.3 = (f32[9,64,128]{2,1,0:T(8,128)S(1)}, f32[9,64,128]{2,1,0:T(8,128)S(1)}, u32[]{:S(2)}, u32[]{:S(2)}) collective-permute-start(f32[9,64,128]{2,1,0:T(8,128)S(1)} %pad_maximum_fusion.10), channel_id=1, source_target_pairs={{0,4},{2,6},{4,8},{6,10},{8,12},{10,14},{12,16},{14,18},{16,20},{1... | collective-permute-start | bytes 884744 | tf_op jit(solution)/shard_map/ppermute | solution.py:247
  31.4 18.1 %collective-permute-start.4 = (f32[9,64,128]{2,1,0:T(8,128)S(1)}, f32[9,64,128]{2,1,0:T(8,128)S(1)}, u32[]{:S(2)}, u32[]{:S(2)}) collective-permute-start(f32[9,64,128]{2,1,0:T(8,128)S(1)} %pad_maximum_fusion.10), channel_id=1, source_target_pairs={{0,6},{2,8},{4,10},{6,12},{8,14},{10,16},{12,18},{14,20},{16,22},{... | collective-permute-start | bytes 884744 | tf_op jit(solution)/shard_map/ppermute | solution.py:247
  34.7 20.5 %collective-permute-start.11 = (f32[9,64,128]{2,1,0:T(8,128)S(1)}, f32[9,64,128]{2,1,0:T(8,128)S(1)}, u32[]{:S(2)}, u32[]{:S(2)}) collective-permute-start(f32[9,64,128]{2,1,0:T(8,128)S(1)} %pad_maximum_fusion.11), channel_id=1, source_target_pairs={{2,0},{4,2},{6,4},{8,6},{10,8},{12,10},{14,12},{16,14},{18,16},{20... | collective-permute-start | bytes 884744 | tf_op jit(solution)/shard_map/ppermute | solution.py:248
  38.4 26.8 %collective-permute-start.12 = (f32[9,64,128]{2,1,0:T(8,128)S(1)}, f32[9,64,128]{2,1,0:T(8,128)S(1)}, u32[]{:S(2)}, u32[]{:S(2)}) collective-permute-start(f32[9,64,128]{2,1,0:T(8,128)S(1)} %pad_maximum_fusion.11), channel_id=1, source_target_pairs={{4,0},{6,2},{8,4},{10,6},{12,8},{14,10},{16,12},{18,14},{20,16},{2... | collective-permute-start | bytes 884744 | tf_op jit(solution)/shard_map/ppermute | solution.py:248
  43.8 21.3 %collective-permute-start.13 = (f32[9,64,128]{2,1,0:T(8,128)S(1)}, f32[9,64,128]{2,1,0:T(8,128)S(1)}, u32[]{:S(2)}, u32[]{:S(2)}) collective-permute-start(f32[9,64,128]{2,1,0:T(8,128)S(1)} %pad_maximum_fusion.11), channel_id=1, source_target_pairs={{6,0},{8,2},{10,4},{12,6},{14,8},{16,10},{18,12},{20,14},{22,16},{... | collective-permute-start | bytes 884744 | tf_op jit(solution)/shard_map/ppermute | solution.py:248
  49.6 22.0 %collective-permute-start.5 = (f32[9,64,128]{2,1,0:T(8,128)S(1)}, f32[9,64,128]{2,1,0:T(8,128)S(1)}, u32[]{:S(2)}, u32[]{:S(2)}) collective-permute-start(f32[9,64,128]{2,1,0:T(8,128)S(1)} %multiply_add_fusion.9), channel_id=1, source_target_pairs={{0,8},{2,10},{4,12},{6,14},{8,16},{10,18},{12,20},{14,22},{16,24},... | collective-permute-start | bytes 884744 | tf_op jit(solution)/shard_map/ppermute | solution.py:247
  53.1 20.4 %collective-permute-start.6 = (f32[9,64,128]{2,1,0:T(8,128)S(1)}, f32[9,64,128]{2,1,0:T(8,128)S(1)}, u32[]{:S(2)}, u32[]{:S(2)}) collective-permute-start(f32[9,64,128]{2,1,0:T(8,128)S(1)} %multiply_add_fusion.9), channel_id=1, source_target_pairs={{0,16},{2,18},{4,20},{6,22},{8,24},{10,26},{12,28},{14,30},{16,32}... | collective-permute-start | bytes 884744 | tf_op jit(solution)/shard_map/ppermute | solution.py:247
  55.2 22.6 %collective-permute-start.7 = (f32[9,64,128]{2,1,0:T(8,128)S(1)}, f32[9,64,128]{2,1,0:T(8,128)S(1)}, u32[]{:S(2)}, u32[]{:S(2)}) collective-permute-start(f32[9,64,128]{2,1,0:T(8,128)S(1)} %multiply_add_fusion.9), channel_id=1, source_target_pairs={{0,24},{2,26},{4,28},{6,30},{8,32},{10,34},{12,36},{14,38},{16,40}... | collective-permute-start | bytes 884744 | tf_op jit(solution)/shard_map/ppermute | solution.py:247
  65.3 29.3 %collective-permute-start.14 = (f32[9,64,128]{2,1,0:T(8,128)S(1)}, f32[9,64,128]{2,1,0:T(8,128)S(1)}, u32[]{:S(2)}, u32[]{:S(2)}) collective-permute-start(f32[9,64,128]{2,1,0:T(8,128)S(1)} %multiply_add_fusion.6), channel_id=1, source_target_pairs={{8,0},{10,2},{12,4},{14,6},{16,8},{18,10},{20,12},{22,14},{24,16},... | collective-permute-start | bytes 884744 | tf_op jit(solution)/shard_map/ppermute | solution.py:248
  69.6 32.4 %collective-permute-start.15 = (f32[9,64,128]{2,1,0:T(8,128)S(1)}, f32[9,64,128]{2,1,0:T(8,128)S(1)}, u32[]{:S(2)}, u32[]{:S(2)}) collective-permute-start(f32[9,64,128]{2,1,0:T(8,128)S(1)} %multiply_add_fusion.6), channel_id=1, source_target_pairs={{16,0},{18,2},{20,4},{22,6},{24,8},{26,10},{28,12},{30,14},{32,16}... | collective-permute-start | bytes 884744 | tf_op jit(solution)/shard_map/ppermute | solution.py:248
  71.6 30.4 %collective-permute-start.16 = (f32[9,64,128]{2,1,0:T(8,128)S(1)}, f32[9,64,128]{2,1,0:T(8,128)S(1)}, u32[]{:S(2)}, u32[]{:S(2)}) collective-permute-start(f32[9,64,128]{2,1,0:T(8,128)S(1)} %multiply_add_fusion.6), channel_id=1, source_target_pairs={{24,0},{26,2},{28,4},{30,6},{32,8},{34,10},{36,12},{38,14},{40,16}... | collective-permute-start | bytes 884744 | tf_op jit(solution)/shard_map/ppermute | solution.py:248
  77.9 26.9 %collective-permute-start.10 = (f32[9,64,128]{2,1,0:T(8,128)S(1)}, f32[9,64,128]{2,1,0:T(8,128)S(1)}, u32[]{:S(2)}, u32[]{:S(2)}) collective-permute-start(f32[9,64,128]{2,1,0:T(8,128)S(1)} %multiply_add_fusion.8), channel_id=1, source_target_pairs={{0,96},{2,98},{4,100},{6,102},{8,104},{10,106},{12,108},{14,110},{... | collective-permute-start | bytes 884744 | tf_op jit(solution)/shard_map/ppermute | solution.py:247
  82.5 23.6 %collective-permute-start.8 = (f32[9,64,128]{2,1,0:T(8,128)S(1)}, f32[9,64,128]{2,1,0:T(8,128)S(1)}, u32[]{:S(2)}, u32[]{:S(2)}) collective-permute-start(f32[9,64,128]{2,1,0:T(8,128)S(1)} %multiply_add_fusion.8), channel_id=1, source_target_pairs={{0,32},{2,34},{4,36},{6,38},{8,40},{10,42},{12,44},{14,46},{16,48}... | collective-permute-start | bytes 884744 | tf_op jit(solution)/shard_map/ppermute | solution.py:247
  104.8 16.8 %collective-permute-start.19 = (f32[9,64,128]{2,1,0:T(8,128)S(1)}, f32[9,64,128]{2,1,0:T(8,128)S(1)}, u32[]{:S(2)}, u32[]{:S(2)}) collective-permute-start(f32[9,64,128]{2,1,0:T(8,128)S(1)} %multiply_add_fusion.5), channel_id=1, source_target_pairs={{96,0},{98,2},{100,4},{102,6},{104,8},{106,10},{108,12},{110,14},{... | collective-permute-start | bytes 884744 | tf_op jit(solution)/shard_map/ppermute | solution.py:248
  106.2 17.1 %collective-permute-start.20 = (f32[4,8,64,128]{3,2,1,0:T(8,128)S(1)}, f32[4,8,64,128]{3,2,1,0:T(8,128)S(1)}, u32[]{:S(2)}, u32[]{:S(2)}) collective-permute-start(f32[4,8,64,128]{3,2,1,0:T(8,128)S(1)} %fusion.6), channel_id=1, source_target_pairs={{0,1},{1,0},{2,3},{3,2},{4,5},{5,4},{6,7},{7,6},{8,9},{9,8},{10,11... | collective-permute-start | bytes 3145736 | tf_op jit(solution)/shard_map/ppermute | solution.py:284
  132.5 17.5 %collective-permute-start.22 = (f32[5,2,64,128]{3,2,1,0:T(8,128)S(1)}, f32[5,2,64,128]{3,2,1,0:T(8,128)S(1)}, u32[]{:S(2)}, u32[]{:S(2)}) collective-permute-start(f32[5,2,64,128]{3,2,1,0:T(8,128)S(1)} %get-tuple-element.117), channel_id=1, source_target_pairs={{2,0},{4,2},{6,4},{8,6},{10,8},{12,10},{14,12},{16,14},{18,16},{20... | collective-permute-start | bytes 983048 | tf_op jit(solution)/shard_map/ppermute | solution.py:272
  150.4 17.0 %collective-permute-start.23 = (f32[5,64,128]{2,1,0:T(8,128)S(1)}, f32[5,64,128]{2,1,0:T(8,128)S(1)}, u32[]{:S(2)}, u32[]{:S(2)}) collective-permute-start(f32[5,64,128]{2,1,0:T(8,128)S(1)} %get-tuple-element.152), channel_id=1, source_target_pairs={{0,2},{2,4},{4,6},{6,8},{8,10},{10,12},{12,14},{14,16},{16,18},{18... | collective-permute-start | bytes 491528 | tf_op jit(solution)/shard_map/ppermute | solution.py:247
  153.6 19.6 %collective-permute-start.24 = (f32[5,64,128]{2,1,0:T(8,128)S(1)}, f32[5,64,128]{2,1,0:T(8,128)S(1)}, u32[]{:S(2)}, u32[]{:S(2)}) collective-permute-start(f32[5,64,128]{2,1,0:T(8,128)S(1)} %get-tuple-element.152), channel_id=1, source_target_pairs={{0,4},{2,6},{4,8},{6,10},{8,12},{10,14},{12,16},{14,18},{16,20},{1... | collective-permute-start | bytes 491528 | tf_op jit(solution)/shard_map/ppermute | solution.py:247
  155.5 17.7 %collective-permute-start.25 = (f32[5,64,128]{2,1,0:T(8,128)S(1)}, f32[5,64,128]{2,1,0:T(8,128)S(1)}, u32[]{:S(2)}, u32[]{:S(2)}) collective-permute-start(f32[5,64,128]{2,1,0:T(8,128)S(1)} %get-tuple-element.152), channel_id=1, source_target_pairs={{0,6},{2,8},{4,10},{6,12},{8,14},{10,16},{12,18},{14,20},{16,22},{... | collective-permute-start | bytes 491528 | tf_op jit(solution)/shard_map/ppermute | solution.py:247
  157.4 15.8 %collective-permute-start.32 = (f32[5,64,128]{2,1,0:T(8,128)S(1)}, f32[5,64,128]{2,1,0:T(8,128)S(1)}, u32[]{:S(2)}, u32[]{:S(2)}) collective-permute-start(f32[5,64,128]{2,1,0:T(8,128)S(1)} %get-tuple-element.153), channel_id=1, source_target_pairs={{2,0},{4,2},{6,4},{8,6},{10,8},{12,10},{14,12},{16,14},{18,16},{20... | collective-permute-start | bytes 491528 | tf_op jit(solution)/shard_map/ppermute | solution.py:248
  173.1 43.8 %collective-permute-start.41 = (f32[5,8,64,128]{3,2,1,0:T(8,128)S(1)}, f32[5,8,64,128]{3,2,1,0:T(8,128)S(1)}, u32[]{:S(2)}, u32[]{:S(2)}) collective-permute-start(f32[5,8,64,128]{3,2,1,0:T(8,128)S(1)} %fusion.12), channel_id=1, source_target_pairs={{0,1},{1,0},{2,3},{3,2},{4,5},{5,4},{6,7},{7,6},{8,9},{9,8},{10,11... | collective-permute-start | bytes 3932168 | tf_op jit(solution)/shard_map/ppermute | solution.py:284
  (29 other events, 262.2 us)

commit v4 on v3

--- a/solution.py
+++ b/solution.py
@@ -15,6 +15,8 @@
 STREAM_STEP = 1.0
 SPAN_STEP = 0.5
 HIGHEST = lax.Precision.HIGHEST
+LEVEL_AXES = ("gx", "gm", "gz")
+WALL_AXES = ("gz", "gm", "gx")
 
 
 def slope_weights():
@@ -155,26 +157,39 @@
     return combine, rise_gain, fall_gain, rise_step, fall_step
 
 
-def scan_rounds(blocks):
-    rounds = []
+def level_tables(rise_step, fall_step, sizes):
+    blocks = rise_step.shape[0]
+
+    def rise_weight(source, target):
+        return np.prod(rise_step[source + 1 : target + 1]) if source <= target else 0.0
+
+    def fall_weight(source, target):
+        return np.prod(fall_step[target:source]) if source >= target else 0.0
+
+    levels = []
     stride = 1
-    while stride < blocks:
-        radix = min(4, -(-blocks // stride))
-        rounds.append((stride, list(range(1, radix))))
-        stride *= radix
-    return rounds
-
-
-def scan_coefs(rise_step, fall_step, shift):
-    blocks = rise_step.shape[0]
-    rise = np.zeros(blocks)
-    fall = np.zeros(blocks)
-    for block in range(blocks):
-        if block - shift >= 0:
-            rise[block] = np.prod(rise_step[block - shift + 1 : block + 1])
-        if block + shift <= blocks - 1:
-            fall[block] = np.prod(fall_step[block : block + shift])
-    return rise, fall
+    for level, size in enumerate(sizes):
+        span = stride * size
+        rise_own = np.zeros((blocks, size))
+        rise_total = np.zeros((blocks, size))
+        fall_own = np.zeros((blocks, size))
+        fall_total = np.zeros((blocks, size))
+        for block in range(blocks):
+            base = block // span * span
+            mine = block // stride % size
+            last, first = base + span - 1, base
+            for member in range(size):
+                group_first = base + member * stride
+                group_last = group_first + stride - 1
+                if level == 0 or member < mine:
+                    rise_own[block, member] = rise_weight(group_last, block)
+                if level == 0 or member > mine:
+                    fall_own[block, member] = fall_weight(group_first, block)
+                rise_total[block, member] = rise_weight(group_last, last)
+                fall_total[block, member] = fall_weight(group_first, first)
+        levels.append((rise_own, rise_total, fall_own, fall_total))
+        stride = span
+    return levels
 
 
 class TableBank:
@@ -198,32 +213,30 @@
         return self.row[start : start + int(np.prod(shape))].reshape(shape)
 
 
-def plan_wall(bank, kinds_sizes, points, rows, pad):
+def plan_wall(bank, kinds_sizes, points, rows, pad, sizes):
     tables = [wall_tables(kind, points, rows, pad) for kind, _ in kinds_sizes]
     groups = [
         (bank.add(table[0]), bank.add(table[1]), bank.add(table[2])) for table in tables
     ]
-    blocks = points // rows
-    rounds = []
-    for stride, multiples in scan_rounds(blocks):
-        entries = []
-        for multiple in multiples:
-            shift = stride * multiple
-            coefs = [scan_coefs(table[3], table[4], shift) for table in tables]
-            rise = np.concatenate(
-                [np.repeat(c[0][:, None], n, 1) for c, (_, n) in zip(coefs, kinds_sizes)], 1
+    per_kind = [level_tables(table[3], table[4], sizes) for table in tables]
+    levels = []
+    for level in range(len(sizes)):
+        handles = []
+        for part in range(4):
+            joined = np.concatenate(
+                [
+                    np.repeat(kind_levels[level][part][:, :, None], n, 2)
+                    for kind_levels, (_, n) in zip(per_kind, kinds_sizes)
+                ],
+                2,
             )
-            fall = np.concatenate(
-                [np.repeat(c[1][:, None], n, 1) for c, (_, n) in zip(coefs, kinds_sizes)], 1
-            )
-            entries.append((shift, bank.add(rise), bank.add(fall)))
-        rounds.append(entries)
-    return groups, rounds
+            handles.append(bank.add(joined))
+        levels.append(handles)
+    return groups, levels
 
 
 def wall_apply(bank, plan, padded_groups, rows, pad):
-    count = lax.axis_size("gy")
-    groups, rounds = plan
+    groups, levels = plan
 
     def taps(padded, combine):
         summed = None
@@ -237,18 +250,18 @@
         for padded, handles in zip(padded_groups, groups)
     ]
     sizes = [padded.shape[0] for padded in padded_groups]
-    rise = jnp.concatenate([part[:, 0] for part in partials], axis=0)
-    fall = jnp.concatenate([part[:, 1] for part in partials], axis=0)
-    for entries in rounds:
-        rise_next, fall_next = rise, fall
-        for shift, rise_handle, fall_handle in entries:
-            up_pairs = [(i, i + shift) for i in range(count - shift)]
-            down_pairs = [(i + shift, i) for i in range(count - shift)]
-            from_below = lax.ppermute(rise, "gy", up_pairs)
-            from_above = lax.ppermute(fall, "gy", down_pairs)
-            rise_next = rise_next + bank.get(rise_handle)[:, None, None] * from_below
-            fall_next = fall_next + bank.get(fall_handle)[:, None, None] * from_above
-        rise, fall = rise_next, fall_next
+    rise_total = jnp.concatenate([part[:, 0] for part in partials], axis=0)
+    fall_total = jnp.concatenate([part[:, 1] for part in partials], axis=0)
+    rise = fall = None
+    for axis, handles in zip(LEVEL_AXES, levels):
+        gathered = lax.all_gather(jnp.stack([rise_total, fall_total]), axis)
+        weights = [bank.get(handle)[:, :, None, None] for handle in handles]
+        rise_part = jnp.sum(weights[0] * gathered[:, 0], axis=0)
+        fall_part = jnp.sum(weights[2] * gathered[:, 1], axis=0)
+        rise = rise_part if rise is None else rise + rise_part
+        fall = fall_part if fall is None else fall + fall_part
+        rise_total = jnp.sum(weights[1] * gathered[:, 0], axis=0)
+        fall_total = jnp.sum(weights[3] * gathered[:, 1], axis=0)
     results = []
     first = 0
     for padded, handles, size in zip(padded_groups, groups, sizes):
@@ -264,12 +277,11 @@
     return results
 
 
-def halo(block, width):
-    count = lax.axis_size("gy")
+def halo(block, width, count):
     up_pairs = [(i, i + 1) for i in range(count - 1)]
     down_pairs = [(i + 1, i) for i in range(count - 1)]
-    below = lax.ppermute(block[:, block.shape[1] - width :], "gy", up_pairs)
-    above = lax.ppermute(block[:, :width], "gy", down_pairs)
+    below = lax.ppermute(block[:, block.shape[1] - width :], WALL_AXES, up_pairs)
+    above = lax.ppermute(block[:, :width], WALL_AXES, down_pairs)
     return jnp.concatenate([below, block, above], axis=1)
 
 
@@ -305,11 +317,11 @@
     return jnp.stack(rows_out)
 
 
-def per_device(mass_per_volume, mass_flux_vector, total_heat_content):
+def per_device(level_sizes, mass_per_volume, mass_flux_vector, total_heat_content):
     rows, span_own, stream_cells = mass_per_volume.shape
-    count = lax.axis_size("gy")
+    count = int(np.prod(level_sizes))
     points = rows * count
-    position = lax.axis_index("gy")
+    position = lax.axis_index(WALL_AXES)
     span_total = span_own * lax.axis_size("pa")
     stream_matrix = jnp.asarray(periodic_matrix(stream_cells, STREAM_STEP), jnp.float32)
     span_full = periodic_matrix(span_total, SPAN_STEP)
@@ -317,14 +329,16 @@
     other_block = jnp.asarray(span_full[span_own : 2 * span_own, :span_own], jnp.float32)
 
     bank = TableBank()
-    first_plan = plan_wall(bank, [("slope", 4), ("smooth", 5)], points, rows, 3)
-    second_plan = plan_wall(bank, [("slope", 5)], points, rows, 2)
+    first_plan = plan_wall(
+        bank, [("slope", 4), ("smooth", 5)], points, rows, 3, level_sizes
+    )
+    second_plan = plan_wall(bank, [("slope", 5)], points, rows, 2, level_sizes)
     bank.lookup(position)
 
     state = jnp.concatenate(
         [mass_per_volume[None], mass_flux_vector, total_heat_content[None]], axis=0
     )
-    padded = halo(state, 3)
+    padded = halo(state, 3, count)
     global_rows = position * rows - 3 + jnp.arange(rows + 6)
     inside = ((global_rows >= 0) & (global_rows < points))[:, None, None]
     density = jnp.where(inside, padded[0], 1.0)
@@ -346,7 +360,7 @@
     energy = total_heat_content
 
     flux_wall = flux_along(1, momentum, energy, speed, push, gradients)
-    (wall_term,) = wall_apply(bank, second_plan, [halo(flux_wall, 2)], rows, 2)
+    (wall_term,) = wall_apply(bank, second_plan, [halo(flux_wall, 2, count)], rows, 2)
     stream_term = stream_slope(
         flux_along(0, momentum, energy, speed, push, gradients), stream_matrix
     )
@@ -362,11 +376,22 @@
 
 
 def solution(mesh):
-    placed = (P("gy", "pa", None), P(None, "gy", "pa", None), P("gy", "pa", None))
+    rows_devices = mesh.shape["gy"]
+    fast = int(np.gcd(rows_devices, 4))
+    middle = int(np.gcd(rows_devices // fast, 4))
+    slow = rows_devices // fast // middle
+    split = jax.sharding.Mesh(
+        mesh.devices.reshape(slow, middle, fast, mesh.shape["pa"]), WALL_AXES + ("pa",)
+    )
+    placed = (
+        P(WALL_AXES, "pa", None),
+        P(None, WALL_AXES, "pa", None),
+        P(WALL_AXES, "pa", None),
+    )
     return jax.shard_map(
-        per_device,
-        mesh=mesh,
+        functools.partial(per_device, (fast, middle, slow)),
+        mesh=split,
         in_specs=placed,
-        out_specs=(P(None, "gy", "pa", None), P(None, "gy", "pa", None)),
+        out_specs=(P(None, WALL_AXES, "pa", None), P(None, WALL_AXES, "pa", None)),
         check_vma=False,
     )

time: 225 us -> 281 us (1.25)
  waiting for transfers between devices: 67.1 us -> 174 us
  starting transfers between devices: 118 us -> 12.2 us
  other arithmetic: 12.3 us -> 39.1 us
  between operations: 1.72 us -> 15.9 us
  local copies, waits for them, and re-layouts: 13.1 us -> 23 us
  matrix products: 8.53 us -> 14.8 us
    all_gather x0 -> x6, waiting for transfers between devices: none -> 148 us  [wall_apply(): gathered = lax.all_gather(jnp.stack([rise_total, fall_total]), axis)]
    ppermute x40 -> x4, starting transfers between devices: 118 us -> 11.7 us  [the longest x2 5.97 us: halo(): above = lax.ppermute(block[:, :width], WALL_AXES, down_pairs)]
    ppermute x40 -> x4, waiting for transfers between devices: 67.1 us -> 26 us  [the longest x2 13.8 us: halo(): above = lax.ppermute(block[:, :width], WALL_AXES, down_pairs)]
    reduce_sum x0 -> x6, other arithmetic: none -> 14.4 us  [wall_apply(): rise_part = jnp.sum(weights[0] * gathered[:, 0], axis=0)]
    unnamed x19 -> x237, local copies, waits for them, and re-layouts: 0.72 us -> 7.1 us
    another operation x0 -> x7, other arithmetic: none -> 4.87 us  [wall_apply(): gathered = lax.all_gather(jnp.stack([rise_total, fall_total]), axis)]
    dot_general x2, matrix products: 2.18 us -> 5.98 us  [stream_slope(): jnp.dot(flat_rows, stream_matrix, precision=HIGHEST, preferred_element_ty...]
  transfers between devices with their start and end apart: 42 -> 12, of which waited for: 14 -> 10; matrix products, arithmetic and copies ran while one was open for 9% -> 12% of each run, Pallas kernels for 0% -> 0%
where the time goes in v4:
time: 281 us; the launch traced here: 280 us
  waiting for transfers between devices  174 us (62%)
  other arithmetic  39.1 us (14%)
  local copies, waits for them, and re-layouts  23 us (8%)
  between operations  15.9 us (6%)
  matrix products  14.8 us (5%)
  starting transfers between devices  12.2 us (4%)
    all_gather x6, waiting for transfers between devices, wall_apply(): gathered = lax.all_gather(jnp.stack([rise_total, fall_total]), axis)  148 us
    reduce_sum x6, other arithmetic, wall_apply(): rise_part = jnp.sum(weights[0] * gathered[:, 0], axis=0)  14.4 us
    ppermute x2, waiting for transfers between devices, halo(): above = lax.ppermute(block[:, :width], WALL_AXES, down_pairs)  13.8 us
    ppermute x2, waiting for transfers between devices, halo(): below = lax.ppermute(block[:, block.shape[1] - width:], WALL_AXES, up_pairs)  12.2 us
    unnamed x237, local copies, waits for them, and re-layouts  7.1 us
    dot_general x2, matrix products, stream_slope(): jnp.dot(flat_rows, stream_matrix, precision=HIGHEST, preferred_element_ty...  5.98 us
    ppermute x2, starting transfers between devices, halo(): above = lax.ppermute(block[:, :width], WALL_AXES, down_pairs)  5.97 us
    ppermute x2, starting transfers between devices, halo(): below = lax.ppermute(block[:, block.shape[1] - width:], WALL_AXES, up_pairs)  5.7 us
  transfers between devices with their start and end apart: 12, of which 10 were waited for; matrix products, arithmetic and copies ran while one was open for 12% of the time, Pallas kernels for 0%

profile of v4, /device:TPU:30, one launch (start us, length us, event | category | flops | bytes accessed | tf_op | source)
XLA Modules:
  0.0 279.5 jit_solution(11913821809780021820)
XLA Ops:
  9.4 3.4 %collective-permute-start = (f32[5,3,64,128]{3,2,1,0:T(8,128)}, f32[5,3,64,128]{3,2,1,0:T(8,128)S(1)}, u32[]{:S(2)}, u32[]{:S(2)}) collective-permute-start(f32[5,3,64,128]{3,2,1,0:T(8,128)} %get-tuple-element.175), channel_id=1, source_target_pairs={{0,2},{2,4},{4,6},{6,8},{8,10},{10,12},{12,14},{14,16},{16,18},{18... | collective-permute-start | bytes 1474568 | tf_op jit(solution)/shard_map/ppermute | solution.py:283
  12.8 2.4 collective-permute-start.1
  17.3 7.2 %collective-permute-done = f32[5,3,64,128]{3,2,1,0:T(8,128)S(1)} collective-permute-done((f32[5,3,64,128]{3,2,1,0:T(8,128)}, f32[5,3,64,128]{3,2,1,0:T(8,128)S(1)}, u32[]{:S(2)}, u32[]{:S(2)}) %collective-permute-start) | collective-permute-done | bytes 491552 | tf_op jit(solution)/shard_map/ppermute | solution.py:283
  24.5 7.2 %collective-permute-done.1 = f32[5,3,64,128]{3,2,1,0:T(8,128)} collective-permute-done((f32[5,3,64,128]{3,2,1,0:T(8,128)S(1)}, f32[5,3,64,128]{3,2,1,0:T(8,128)}, u32[]{:S(2)}, u32[]{:S(2)}) %collective-permute-start.1) | collective-permute-done | bytes 491552 | tf_op jit(solution)/shard_map/ppermute | solution.py:284
  41.8 31.1 %all-gather.13.cloned.1.call-done = f32[8,9,64,128]{3,2,1,0:T(8,128)} async-done(((f32[2,9,64,128]{3,2,1,0:T(8,128)}), f32[8,9,64,128]{3,2,1,0:T(8,128)}) %all-gather.13.cloned.1.call-update) | async-done | bytes 2359312 | tf_op jit(solution)/shard_map/all_gather | solution.py:257
  73.0 3.0 %multiply_reduce_fusion.8 = (f32[9,64,128]{2,1,0:T(8,128)}, f32[9,64,128]{2,1,0:T(8,128)}, f32[9,64,128]{2,1,0:T(8,128)S(1)}, f32[9,64,128]{2,1,0:T(8,128)S(1)}) fusion(f32[4,2,9,64,128]{4,3,2,1,0:T(8,128)} %bitcast.418, f32[4,9]{1,0:T(4,128)S(1)} %mul.1821, f32[4,9]{1,0:T(4,128)S(1)} %mul.1972, f32[4,9]{1,0:T(4,128)S(1)} %mul.1952, f32[4,9]{1,0:T(4,128)S(1)} %mul.1955), kind=kLoop, calls=%fused_computation.62 | loop fusion | flops 2064384 | bytes 3539520 | tf_op jit(solution)/shard_map/reduce_sum | solution.py:259
  77.2 32.8 %all-gather.15.cloned.1.call-done = f32[8,9,64,128]{3,2,1,0:T(8,128)} async-done(((f32[2,9,64,128]{3,2,1,0:T(8,128)}), f32[8,9,64,128]{3,2,1,0:T(8,128)}) %all-gather.15.cloned.1.call-update) | async-done | bytes 2359312 | tf_op jit(solution)/shard_map/all_gather | solution.py:257
  110.0 3.0 %multiply_reduce_fusion.5 = (f32[9,64,128]{2,1,0:T(8,128)}, f32[9,64,128]{2,1,0:T(8,128)}, f32[9,64,128]{2,1,0:T(8,128)S(1)}, f32[9,64,128]{2,1,0:T(8,128)S(1)}) fusion(f32[4,2,9,64,128]{4,3,2,1,0:T(8,128)} %bitcast.419, f32[4,9]{1,0:T(4,128)S(1)} %mul.1950, f32[4,9]{1,0:T(4,128)S(1)} %mul.1975, f32[4,9]{1,0:T(4,128)S(1)} %mul.1961, f32[4,9]{1,0:T(4,128)S(1)} %mul.1964), kind=kLoop, calls=%fused_computation.59 | loop fusion | flops 2064384 | bytes 3539520 | tf_op jit(solution)/shard_map/reduce_sum | solution.py:259
  122.5 2.2 fusion.79
  125.6 2.3 fusion.80
  130.9 18.3 %all-gather.17.cloned.1.call-done = f32[8,9,64,128]{3,2,1,0:T(8,128)} async-done(((f32[2,9,64,128]{3,2,1,0:T(8,128)}), f32[8,9,64,128]{3,2,1,0:T(8,128)}) %all-gather.17.cloned.1.call-update) | async-done | bytes 2359312 | tf_op jit(solution)/shard_map/all_gather | solution.py:257
  161.0 2.3 collective-permute-start.3
  163.7 3.5 %collective-permute-start.4 = (f32[5,2,64,128]{3,2,1,0:T(8,128)S(1)}, f32[5,2,64,128]{3,2,1,0:T(8,128)S(1)}, u32[]{:S(2)}, u32[]{:S(2)}) collective-permute-start(f32[5,2,64,128]{3,2,1,0:T(8,128)S(1)} %get-tuple-element.158), channel_id=1, source_target_pairs={{2,0},{4,2},{6,4},{8,6},{10,8},{12,10},{14,12},{16,14},{18,16},{20... | collective-permute-start | bytes 983048 | tf_op jit(solution)/shard_map/ppermute | solution.py:284
  167.3 5.0 %collective-permute-done.3 = f32[5,2,64,128]{3,2,1,0:T(8,128)S(1)} collective-permute-done((f32[5,2,64,128]{3,2,1,0:T(8,128)S(1)}, f32[5,2,64,128]{3,2,1,0:T(8,128)S(1)}, u32[]{:S(2)}, u32[]{:S(2)}) %collective-permute-start.3) | collective-permute-done | bytes 327712 | tf_op jit(solution)/shard_map/ppermute | solution.py:283
  172.4 6.6 %collective-permute-done.4 = f32[5,2,64,128]{3,2,1,0:T(8,128)S(1)} collective-permute-done((f32[5,2,64,128]{3,2,1,0:T(8,128)S(1)}, f32[5,2,64,128]{3,2,1,0:T(8,128)S(1)}, u32[]{:S(2)}, u32[]{:S(2)}) %collective-permute-start.4) | collective-permute-done | bytes 327712 | tf_op jit(solution)/shard_map/ppermute | solution.py:284
  182.0 21.9 %all-gather.19.cloned.1.call-done = f32[8,5,64,128]{3,2,1,0:T(8,128)} async-done(((f32[2,5,64,128]{3,2,1,0:T(8,128)}), f32[8,5,64,128]{3,2,1,0:T(8,128)}) %all-gather.19.cloned.1.call-update) | async-done | bytes 1310736 | tf_op jit(solution)/shard_map/all_gather | solution.py:257
  203.9 2.3 multiply_reduce_fusion.16
  207.4 25.2 %all-gather.21.cloned.1.call-done = f32[8,5,64,128]{3,2,1,0:T(8,128)} async-done(((f32[2,5,64,128]{3,2,1,0:T(8,128)}), f32[8,5,64,128]{3,2,1,0:T(8,128)}) %all-gather.21.cloned.1.call-update) | async-done | bytes 1310736 | tf_op jit(solution)/shard_map/all_gather | solution.py:257
  232.6 2.4 multiply_reduce_fusion.13
  238.3 2.8 %multiply_add_fusion = f32[5,8,64,128]{3,2,1,0:T(8,128)} fusion(f32[5,64,128]{2,1,0:T(8,128)S(1)} %slice-done.1, f32[8]{0:T(128)S(1)} %copy-done.114, f32[5,64,128]{2,1,0:T(8,128)S(1)} %slice-done, f32[8]{0:T(128)S(1)} %copy-done.113, f32[5,64,128]{2,1,0:T(8,128)S(1)} %copy-done.34, f32[8]{0:T(128)S(1)} %get-tuple-element.47, ...), kind=kLoop, calls=%fused_computation.43 | loop fusion | flops 10158080 | bytes 3932672 | tf_op jit(solution)/shard_map/add | solution.py:272
  241.2 2.6 fusion.81
  243.8 19.0 %all-gather.23.cloned.1.call-done = f32[8,5,64,128]{3,2,1,0:T(8,128)} async-done(((f32[2,5,64,128]{3,2,1,0:T(8,128)}), f32[8,5,64,128]{3,2,1,0:T(8,128)}) %all-gather.23.cloned.1.call-update) | async-done | bytes 1310736 | tf_op jit(solution)/shard_map/all_gather | solution.py:257
  264.8 3.8 %convolution_add_fusion.1 = f32[5,8,64,128]{3,2,1,0:T(8,128)S(1)} fusion(f32[5,8,64,128]{3,2,1,0:T(8,128)} %copy-done.96, f32[128,128,1,1]{1,0,3,2:T(8,128)S(1)} %copy-done.117, f32[5,64,128]{2,1,0:T(8,128)S(1)} %add_add_fusion.2, f32[8]{0:T(128)S(1)} %copy-done.115, f32[5,64,128]{2,1,0:T(8,128)S(1)} %add_add_fusion.3, f32[8]{0:T(128)S(1)} %copy-done.116, ...), kind=kOutput, calls=%fused_computation.34 | convolution fusion | flops 512491520 | bytes 4981184 | tf_op jit(solution)/shard_map/dot_general | solution.py:290
  268.6 2.7 fusion.3
  (351 shorter events, 50.3 us)
Async XLA Ops:
  7.2 65.8 %all-gather.13.cloned.1.call-start = ((), (), s32[]{:S(2)}) async-start(), calls=%async_computation | async-start | bytes 2949120 | tf_op jit(solution)/shard_map/all_gather | solution.py:257
  9.4 15.1 %collective-permute-start = (f32[5,3,64,128]{3,2,1,0:T(8,128)}, f32[5,3,64,128]{3,2,1,0:T(8,128)S(1)}, u32[]{:S(2)}, u32[]{:S(2)}) collective-permute-start(f32[5,3,64,128]{3,2,1,0:T(8,128)} %get-tuple-element.175), channel_id=1, source_target_pairs={{0,2},{2,4},{4,6},{6,8},{8,10},{10,12},{12,14},{14,16},{16,18},{18... | collective-permute-start | bytes 1474568 | tf_op jit(solution)/shard_map/ppermute | solution.py:283
  12.8 18.9 %collective-permute-start.1 = (f32[5,3,64,128]{3,2,1,0:T(8,128)S(1)}, f32[5,3,64,128]{3,2,1,0:T(8,128)}, u32[]{:S(2)}, u32[]{:S(2)}) collective-permute-start(f32[5,3,64,128]{3,2,1,0:T(8,128)S(1)} %get-tuple-element.176), channel_id=1, source_target_pairs={{2,0},{4,2},{6,4},{8,6},{10,8},{12,10},{14,12},{16,14},{18,16},{20... | collective-permute-start | bytes 1474568 | tf_op jit(solution)/shard_map/ppermute | solution.py:284
  17.1 14.7 %copy-start = (f32[3,8,64,128]{3,2,1,0:T(8,128)S(1)}, f32[3,8,64,128]{3,2,1,0:T(8,128)}, u32[]{:S(2)}) copy-start(f32[3,8,64,128]{3,2,1,0:T(8,128)} %param.8) | copy-start | bytes 2359300
  17.1 14.7 %copy-start.1 = (f32[8,64,128]{2,1,0:T(8,128)S(1)}, f32[8,64,128]{2,1,0:T(8,128)}, u32[]{:S(2)}) copy-start(f32[8,64,128]{2,1,0:T(8,128)} %param.9) | copy-start | bytes 786436
  17.1 14.6 %copy-start.4 = (f32[8,64,128]{2,1,0:T(8,128)S(1)}, f32[8,64,128]{2,1,0:T(8,128)}, u32[]{:S(2)}) copy-start(f32[8,64,128]{2,1,0:T(8,128)} %param.7) | copy-start | bytes 786436
  17.2 21.6 %copy-start.9 = (f32[5,64,128]{2,1,0:T(8,128)}, f32[5,64,128]{2,1,0:T(8,128)S(1)}, u32[]{:S(2)}) copy-start(f32[5,64,128]{2,1,0:T(8,128)S(1)} %get-tuple-element.167) | copy-start | bytes 491524
  17.2 21.6 %copy-start.11 = (f32[5,64,128]{2,1,0:T(8,128)}, f32[5,64,128]{2,1,0:T(8,128)S(1)}, u32[]{:S(2)}) copy-start(f32[5,64,128]{2,1,0:T(8,128)S(1)} %get-tuple-element.168) | copy-start | bytes 491524
  17.2 21.6 %copy-start.13 = (f32[5,64,128]{2,1,0:T(8,128)}, f32[5,64,128]{2,1,0:T(8,128)S(1)}, u32[]{:S(2)}) copy-start(f32[5,64,128]{2,1,0:T(8,128)S(1)} %get-tuple-element.169) | copy-start | bytes 491524
  17.2 21.6 %copy-start.15 = (f32[5,64,128]{2,1,0:T(8,128)}, f32[5,64,128]{2,1,0:T(8,128)S(1)}, u32[]{:S(2)}) copy-start(f32[5,64,128]{2,1,0:T(8,128)S(1)} %get-tuple-element.170) | copy-start | bytes 491524
  17.2 21.6 %copy-start.17 = (f32[5,64,128]{2,1,0:T(8,128)}, f32[5,64,128]{2,1,0:T(8,128)S(1)}, u32[]{:S(2)}) copy-start(f32[5,64,128]{2,1,0:T(8,128)S(1)} %get-tuple-element.171) | copy-start | bytes 491524
  17.2 21.6 %copy-start.19 = (f32[5,64,128]{2,1,0:T(8,128)}, f32[5,64,128]{2,1,0:T(8,128)S(1)}, u32[]{:S(2)}) copy-start(f32[5,64,128]{2,1,0:T(8,128)S(1)} %get-tuple-element.172) | copy-start | bytes 491524
  17.3 21.6 %copy-start.21 = (f32[5,64,128]{2,1,0:T(8,128)}, f32[5,64,128]{2,1,0:T(8,128)S(1)}, u32[]{:S(2)}) copy-start(f32[5,64,128]{2,1,0:T(8,128)S(1)} %get-tuple-element.173) | copy-start | bytes 491524
  17.3 21.6 %copy-start.23 = (f32[5,64,128]{2,1,0:T(8,128)}, f32[5,64,128]{2,1,0:T(8,128)S(1)}, u32[]{:S(2)}) copy-start(f32[5,64,128]{2,1,0:T(8,128)S(1)} %get-tuple-element.174) | copy-start | bytes 491524
  40.5 69.5 %all-gather.15.cloned.1.call-start = ((), (), s32[]{:S(2)}) async-start(), calls=%async_computation.1 | async-start | bytes 2949120 | tf_op jit(solution)/shard_map/all_gather | solution.py:257
  76.8 72.4 %all-gather.17.cloned.1.call-start = ((), (), s32[]{:S(2)}) async-start(), calls=%async_computation.2 | async-start | bytes 2949120 | tf_op jit(solution)/shard_map/all_gather | solution.py:257
  113.9 90.0 %all-gather.19.cloned.1.call-start = ((), (), s32[]{:S(2)}) async-start(), calls=%async_computation.3 | async-start | bytes 1638400 | tf_op jit(solution)/shard_map/all_gather | solution.py:257
  117.3 8.3 %collective-permute-start.2 = (f32[4,8,64,128]{3,2,1,0:T(8,128)}, f32[4,8,64,128]{3,2,1,0:T(8,128)}, u32[]{:S(2)}, u32[]{:S(2)}) collective-permute-start(f32[4,8,64,128]{3,2,1,0:T(8,128)} %fusion.10), channel_id=1, source_target_pairs={{0,1},{1,0},{2,3},{3,2},{4,5},{5,4},{6,7},{7,6},{8,9},{9,8},{10,11... | collective-permute-start | bytes 3145736 | tf_op jit(solution)/shard_map/ppermute | solution.py:296
  161.0 11.3 %collective-permute-start.3 = (f32[5,2,64,128]{3,2,1,0:T(8,128)S(1)}, f32[5,2,64,128]{3,2,1,0:T(8,128)S(1)}, u32[]{:S(2)}, u32[]{:S(2)}) collective-permute-start(f32[5,2,64,128]{3,2,1,0:T(8,128)S(1)} %get-tuple-element.157), channel_id=1, source_target_pairs={{0,2},{2,4},{4,6},{6,8},{8,10},{10,12},{12,14},{14,16},{16,18},{18... | collective-permute-start | bytes 983048 | tf_op jit(solution)/shard_map/ppermute | solution.py:283
  163.7 15.3 %collective-permute-start.4 = (f32[5,2,64,128]{3,2,1,0:T(8,128)S(1)}, f32[5,2,64,128]{3,2,1,0:T(8,128)S(1)}, u32[]{:S(2)}, u32[]{:S(2)}) collective-permute-start(f32[5,2,64,128]{3,2,1,0:T(8,128)S(1)} %get-tuple-element.158), channel_id=1, source_target_pairs={{2,0},{4,2},{6,4},{8,6},{10,8},{12,10},{14,12},{16,14},{18,16},{20... | collective-permute-start | bytes 983048 | tf_op jit(solution)/shard_map/ppermute | solution.py:284
  167.3 12.0 %copy-start.72 = (f32[5,64,128]{2,1,0:T(8,128)}, f32[5,64,128]{2,1,0:T(8,128)S(1)}, u32[]{:S(2)}) copy-start(f32[5,64,128]{2,1,0:T(8,128)S(1)} %get-tuple-element.164) | copy-start | bytes 491524
  180.5 52.1 %all-gather.21.cloned.1.call-start = ((), (), s32[]{:S(2)}) async-start(), calls=%async_computation.4 | async-start | bytes 1638400 | tf_op jit(solution)/shard_map/all_gather | solution.py:257
  207.0 55.8 %all-gather.23.cloned.1.call-start = ((), (), s32[]{:S(2)}) async-start(), calls=%async_computation.5 | async-start | bytes 1638400 | tf_op jit(solution)/shard_map/all_gather | solution.py:257
  237.8 30.7 %collective-permute-start.5 = (f32[5,8,64,128]{3,2,1,0:T(8,128)}, f32[5,8,64,128]{3,2,1,0:T(8,128)}, u32[]{:S(2)}, u32[]{:S(2)}) collective-permute-start(f32[5,8,64,128]{3,2,1,0:T(8,128)} %get-tuple-element.139), channel_id=1, source_target_pairs={{0,1},{1,0},{2,3},{3,2},{4,5},{5,4},{6,7},{7,6},{8,9},{9,8},{10,11... | collective-permute-start | bytes 3932168 | tf_op jit(solution)/shard_map/ppermute | solution.py:296
  (108 other events, 246.7 us)
Sparse Core Ops, SparseCore 0:
  40.6 32.2 all-gather.12
  76.9 33.0 all-gather.14
  114.0 35.1 all-gather.16
  180.6 23.2 all-gather.18
  207.1 25.4 all-gather.20
  236.1 26.6 all-gather.22

commit v5 on v3

--- a/solution.py
+++ b/solution.py
@@ -159,7 +159,7 @@
     rounds = []
     stride = 1
     while stride < blocks:
-        radix = min(4, -(-blocks // stride))
+        radix = min(2, -(-blocks // stride))
         rounds.append((stride, list(range(1, radix))))
         stride *= radix
     return rounds
@@ -239,16 +239,24 @@
     sizes = [padded.shape[0] for padded in padded_groups]
     rise = jnp.concatenate([part[:, 0] for part in partials], axis=0)
     fall = jnp.concatenate([part[:, 1] for part in partials], axis=0)
+    core = lax.axis_index("pa")
+    first_core = core == 0
+    swap = [(0, 1), (1, 0)]
+    sent = lax.ppermute(jnp.where(first_core, fall, rise), "pa", swap)
+    kept = jnp.where(first_core, rise, fall)
+    carry = jnp.where(first_core, jnp.stack([kept, sent]), jnp.stack([sent, kept]))
     for entries in rounds:
-        rise_next, fall_next = rise, fall
+        update = carry
         for shift, rise_handle, fall_handle in entries:
-            up_pairs = [(i, i + shift) for i in range(count - shift)]
-            down_pairs = [(i + shift, i) for i in range(count - shift)]
-            from_below = lax.ppermute(rise, "gy", up_pairs)
-            from_above = lax.ppermute(fall, "gy", down_pairs)
-            rise_next = rise_next + bank.get(rise_handle)[:, None, None] * from_below
-            fall_next = fall_next + bank.get(fall_handle)[:, None, None] * from_above
-        rise, fall = rise_next, fall_next
+            pairs = [(2 * i, 2 * (i + shift)) for i in range(count - shift)]
+            pairs += [(2 * (i + shift) + 1, 2 * i + 1) for i in range(count - shift)]
+            arrived = lax.ppermute(carry, ("gy", "pa"), pairs)
+            coef = jnp.where(first_core, bank.get(rise_handle), bank.get(fall_handle))
+            update = update + coef[None, :, None, None] * arrived
+        carry = update
+    back = lax.ppermute(jnp.where(first_core, carry[1], carry[0]), "pa", swap)
+    rise = jnp.where(first_core, carry[0], back)
+    fall = jnp.where(first_core, back, carry[1])
     results = []
     first = 0
     for padded, handles, size in zip(padded_groups, groups, sizes):

time: 225 us -> 241 us (1.071)
  starting transfers between devices: 118 us -> 68.2 us
  waiting for transfers between devices: 67.1 us -> 114 us
  other arithmetic: 12.3 us -> 24.5 us
  local copies, waits for them, and re-layouts: 13.1 us -> 19 us
    ppermute x36 -> x16, starting transfers between devices: 106 us -> 55.8 us  [the longest x12 52.4 us: wall_apply(): arrived = lax.ppermute(carry, ('gy', 'pa'), pairs)]
    ppermute x36 -> x16, waiting for transfers between devices: 47.4 us -> 86.3 us  [the longest x12 83.4 us: wall_apply(): arrived = lax.ppermute(carry, ('gy', 'pa'), pairs)]
    ppermute x2, waiting for transfers between devices: 2.63 us -> 12.5 us  [halo(): below = lax.ppermute(block[:, block.shape[1] - width:], 'gy', up_pairs)]
    unnamed x19 -> x223, local copies, waits for them, and re-layouts: 0.72 us -> 5.28 us
    select_n x0 -> x11, other arithmetic: none -> 3.99 us  [the longest x2 2.84 us: wall_apply(): coef = jnp.where(first_core, bank.get(rise_handle), bank.get(fall_handle))]
    mul x4 -> x0, local copies, waits for them, and re-layouts: 3.97 us -> none  [wall_apply(): rise_next = rise_next + bank.get(rise_handle)[:, None, None] * from_below]
    add x11 -> x12, other arithmetic: 1.52 us -> 5.32 us  [wall_apply(): update = update + coef[None, :, None, None] * arrived]
    slice x5, local copies, waits for them, and re-layouts: 1.82 us -> 4.3 us  [wall_apply(): local = taps(padded, bank.get(handles[0])[:rows])]
  transfers between devices with their start and end apart: 42 -> 22, of which waited for: 14 -> 17; matrix products, arithmetic and copies ran while one was open for 9% -> 10% of each run, Pallas kernels for 0% -> 0%
where the time goes in v5:
time: 241 us; the launch traced here: 237 us
  waiting for transfers between devices  114 us (47%)
  starting transfers between devices  68.2 us (28%)
  other arithmetic  24.5 us (10%)
  local copies, waits for them, and re-layouts  19 us (8%)
  matrix products  8.4 us (3%)
  between operations  2.57 us (1%)
    ppermute x12, waiting for transfers between devices, wall_apply(): arrived = lax.ppermute(carry, ('gy', 'pa'), pairs)  83.4 us
    ppermute x12, starting transfers between devices, wall_apply(): arrived = lax.ppermute(carry, ('gy', 'pa'), pairs)  52.4 us
    ppermute x2, waiting for transfers between devices, halo(): above = lax.ppermute(block[:, :width], 'gy', down_pairs)  15.4 us
    ppermute x2, waiting for transfers between devices, halo(): below = lax.ppermute(block[:, block.shape[1] - width:], 'gy', up_pairs)  12.5 us
    ppermute x2, starting transfers between devices, halo(): below = lax.ppermute(block[:, block.shape[1] - width:], 'gy', up_pairs)  7.12 us
    add x12, other arithmetic, wall_apply(): update = update + coef[None, :, None, None] * arrived  5.32 us
    unnamed x223, local copies, waits for them, and re-layouts  5.28 us
  transfers between devices with their start and end apart: 22, of which 17 were waited for; matrix products, arithmetic and copies ran while one was open for 10% of the time, Pallas kernels for 0%

profile of v5, /device:TPU:30, one launch (start us, length us, event | category | flops | bytes accessed | tf_op | source)
XLA Modules:
  0.0 236.9 jit_solution(5127744185955723264)
XLA Ops:
  3.1 3.4 %collective-permute-start = (f32[5,3,64,128]{3,2,1,0:T(8,128)}, f32[5,3,64,128]{3,2,1,0:T(8,128)S(1)}, u32[]{:S(2)}, u32[]{:S(2)}) collective-permute-start(f32[5,3,64,128]{3,2,1,0:T(8,128)} %get-tuple-element.134), channel_id=1, source_target_pairs={{0,2},{2,4},{4,6},{6,8},{8,10},{10,12},{12,14},{14,16},{16,18},{18... | collective-permute-start | bytes 1474568 | tf_op jit(solution)/shard_map/ppermute | solution.py:279
  11.0 7.2 %collective-permute-done = f32[5,3,64,128]{3,2,1,0:T(8,128)S(1)} collective-permute-done((f32[5,3,64,128]{3,2,1,0:T(8,128)}, f32[5,3,64,128]{3,2,1,0:T(8,128)S(1)}, u32[]{:S(2)}, u32[]{:S(2)}) %collective-permute-start) | collective-permute-done | bytes 491552 | tf_op jit(solution)/shard_map/ppermute | solution.py:279
  18.1 7.5 %collective-permute-done.1 = f32[5,3,64,128]{3,2,1,0:T(8,128)} collective-permute-done((f32[5,3,64,128]{3,2,1,0:T(8,128)}, f32[5,3,64,128]{3,2,1,0:T(8,128)}, u32[]{:S(2)}, u32[]{:S(2)}) %collective-permute-start.1) | collective-permute-done | bytes 491552 | tf_op jit(solution)/shard_map/ppermute | solution.py:280
  39.1 9.1 %collective-permute-done.3 = f32[2,9,64,128]{3,2,1,0:T(8,128)} collective-permute-done((f32[2,9,64,128]{3,2,1,0:T(8,128)}, f32[2,9,64,128]{3,2,1,0:T(8,128)}, u32[]{:S(2)}, u32[]{:S(2)}) %collective-permute-start.3) | collective-permute-done | bytes 589856 | tf_op jit(solution)/shard_map/ppermute | solution.py:253
  51.3 15.6 %collective-permute-done.4 = f32[2,9,64,128]{3,2,1,0:T(8,128)S(1)} collective-permute-done((f32[2,9,64,128]{3,2,1,0:T(8,128)S(1)}, f32[2,9,64,128]{3,2,1,0:T(8,128)S(1)}, u32[]{:S(2)}, u32[]{:S(2)}) %collective-permute-start.4) | collective-permute-done | bytes 589856 | tf_op jit(solution)/shard_map/ppermute | solution.py:253
  68.9 9.8 %collective-permute-done.5 = f32[2,9,64,128]{3,2,1,0:T(8,128)S(1)} collective-permute-done((f32[2,9,64,128]{3,2,1,0:T(8,128)S(1)}, f32[2,9,64,128]{3,2,1,0:T(8,128)S(1)}, u32[]{:S(2)}, u32[]{:S(2)}) %collective-permute-start.5) | collective-permute-done | bytes 589856 | tf_op jit(solution)/shard_map/ppermute | solution.py:253
  78.9 4.5 %collective-permute-start.6 = (f32[2,9,64,128]{3,2,1,0:T(8,128)S(1)}, f32[2,9,64,128]{3,2,1,0:T(8,128)}, u32[]{:S(2)}, u32[]{:S(2)}) collective-permute-start(f32[2,9,64,128]{3,2,1,0:T(8,128)S(1)} %multiply_add_fusion.5), channel_id=1, source_target_pairs={{0,16},{2,18},{4,20},{6,22},{8,24},{10,26},{12,28},{14,30},{16,32}... | collective-permute-start | bytes 1769480 | tf_op jit(solution)/shard_map/ppermute | solution.py:253
  85.7 9.9 %collective-permute-done.6 = f32[2,9,64,128]{3,2,1,0:T(8,128)} collective-permute-done((f32[2,9,64,128]{3,2,1,0:T(8,128)S(1)}, f32[2,9,64,128]{3,2,1,0:T(8,128)}, u32[]{:S(2)}, u32[]{:S(2)}) %collective-permute-start.6) | collective-permute-done | bytes 589856 | tf_op jit(solution)/shard_map/ppermute | solution.py:253
  96.9 6.5 %collective-permute-start.7 = (f32[2,9,64,128]{3,2,1,0:T(8,128)S(1)}, f32[2,9,64,128]{3,2,1,0:T(8,128)S(1)}, u32[]{:S(2)}, u32[]{:S(2)}) collective-permute-start(f32[2,9,64,128]{3,2,1,0:T(8,128)S(1)} %multiply_add_fusion.4), channel_id=1, source_target_pairs={{0,32},{2,34},{4,36},{6,38},{8,40},{10,42},{12,44},{14,46},{16,48}... | collective-permute-start | bytes 1769480 | tf_op jit(solution)/shard_map/ppermute | solution.py:253
  105.5 5.3 %collective-permute-done.7 = f32[2,9,64,128]{3,2,1,0:T(8,128)S(1)} collective-permute-done((f32[2,9,64,128]{3,2,1,0:T(8,128)S(1)}, f32[2,9,64,128]{3,2,1,0:T(8,128)S(1)}, u32[]{:S(2)}, u32[]{:S(2)}) %collective-permute-start.7) | collective-permute-done | bytes 589856 | tf_op jit(solution)/shard_map/ppermute | solution.py:253
  110.9 6.4 %collective-permute-start.8 = (f32[2,9,64,128]{3,2,1,0:T(8,128)S(1)}, f32[2,9,64,128]{3,2,1,0:T(8,128)S(1)}, u32[]{:S(2)}, u32[]{:S(2)}) collective-permute-start(f32[2,9,64,128]{3,2,1,0:T(8,128)S(1)} %multiply_add_fusion.3), channel_id=1, source_target_pairs={{0,64},{2,66},{4,68},{6,70},{8,72},{10,74},{12,76},{14,78},{16,80}... | collective-permute-start | bytes 1769480 | tf_op jit(solution)/shard_map/ppermute | solution.py:253
  118.4 6.2 %collective-permute-done.8 = f32[2,9,64,128]{3,2,1,0:T(8,128)S(1)} collective-permute-done((f32[2,9,64,128]{3,2,1,0:T(8,128)S(1)}, f32[2,9,64,128]{3,2,1,0:T(8,128)S(1)}, u32[]{:S(2)}, u32[]{:S(2)}) %collective-permute-start.8) | collective-permute-done | bytes 589856 | tf_op jit(solution)/shard_map/ppermute | solution.py:253
  134.3 3.7 %collective-permute-start.11 = (f32[5,2,64,128]{3,2,1,0:T(8,128)S(1)}, f32[5,2,64,128]{3,2,1,0:T(8,128)S(1)}, u32[]{:S(2)}, u32[]{:S(2)}) collective-permute-start(f32[5,2,64,128]{3,2,1,0:T(8,128)S(1)} %get-tuple-element.116), channel_id=1, source_target_pairs={{0,2},{2,4},{4,6},{6,8},{8,10},{10,12},{12,14},{14,16},{16,18},{18... | collective-permute-start | bytes 983048 | tf_op jit(solution)/shard_map/ppermute | solution.py:279
  140.7 5.3 %collective-permute-done.11 = f32[5,2,64,128]{3,2,1,0:T(8,128)S(1)} collective-permute-done((f32[5,2,64,128]{3,2,1,0:T(8,128)S(1)}, f32[5,2,64,128]{3,2,1,0:T(8,128)S(1)}, u32[]{:S(2)}, u32[]{:S(2)}) %collective-permute-start.11) | collective-permute-done | bytes 327712 | tf_op jit(solution)/shard_map/ppermute | solution.py:279
  146.1 8.0 %collective-permute-done.12 = f32[5,2,64,128]{3,2,1,0:T(8,128)S(1)} collective-permute-done((f32[5,2,64,128]{3,2,1,0:T(8,128)S(1)}, f32[5,2,64,128]{3,2,1,0:T(8,128)S(1)}, u32[]{:S(2)}, u32[]{:S(2)}) %collective-permute-start.12) | collective-permute-done | bytes 327712 | tf_op jit(solution)/shard_map/ppermute | solution.py:280
  159.9 5.3 %collective-permute-done.14 = f32[2,5,64,128]{3,2,1,0:T(8,128)S(1)} collective-permute-done((f32[2,5,64,128]{3,2,1,0:T(8,128)S(1)}, f32[2,5,64,128]{3,2,1,0:T(8,128)S(1)}, u32[]{:S(2)}, u32[]{:S(2)}) %collective-permute-start.14) | collective-permute-done | bytes 327712 | tf_op jit(solution)/shard_map/ppermute | solution.py:253
  167.2 8.8 %collective-permute-done.15 = f32[2,5,64,128]{3,2,1,0:T(8,128)S(1)} collective-permute-done((f32[2,5,64,128]{3,2,1,0:T(8,128)S(1)}, f32[2,5,64,128]{3,2,1,0:T(8,128)S(1)}, u32[]{:S(2)}, u32[]{:S(2)}) %collective-permute-start.15) | collective-permute-done | bytes 327712 | tf_op jit(solution)/shard_map/ppermute | solution.py:253
  178.1 7.0 %collective-permute-done.16 = f32[2,5,64,128]{3,2,1,0:T(8,128)S(1)} collective-permute-done((f32[2,5,64,128]{3,2,1,0:T(8,128)S(1)}, f32[2,5,64,128]{3,2,1,0:T(8,128)S(1)}, u32[]{:S(2)}, u32[]{:S(2)}) %collective-permute-start.16) | collective-permute-done | bytes 327712 | tf_op jit(solution)/shard_map/ppermute | solution.py:253
  192.3 4.5 %collective-permute-done.17 = f32[2,5,64,128]{3,2,1,0:T(8,128)} collective-permute-done((f32[2,5,64,128]{3,2,1,0:T(8,128)}, f32[2,5,64,128]{3,2,1,0:T(8,128)}, u32[]{:S(2)}, u32[]{:S(2)}) %collective-permute-start.17) | collective-permute-done | bytes 327712 | tf_op jit(solution)/shard_map/ppermute | solution.py:253
  197.9 7.8 %collective-permute-start.18 = (f32[2,5,64,128]{3,2,1,0:T(8,128)S(1)}, f32[2,5,64,128]{3,2,1,0:T(8,128)S(1)}, u32[]{:S(2)}, u32[]{:S(2)}) collective-permute-start(f32[2,5,64,128]{3,2,1,0:T(8,128)S(1)} %multiply_add_fusion.10), channel_id=1, source_target_pairs={{0,32},{2,34},{4,36},{6,38},{8,40},{10,42},{12,44},{14,46},{16,48}... | collective-permute-start | bytes 983048 | tf_op jit(solution)/shard_map/ppermute | solution.py:253
  210.4 13.1 %collective-permute-start.19 = (f32[2,5,64,128]{3,2,1,0:T(8,128)S(1)}, f32[2,5,64,128]{3,2,1,0:T(8,128)S(1)}, u32[]{:S(2)}, u32[]{:S(2)}) collective-permute-start(f32[2,5,64,128]{3,2,1,0:T(8,128)S(1)} %multiply_add_fusion.9), channel_id=1, source_target_pairs={{0,64},{2,66},{4,68},{6,70},{8,72},{10,74},{12,76},{14,78},{16,80}... | collective-permute-start | bytes 983048 | tf_op jit(solution)/shard_map/ppermute | solution.py:253
  223.6 2.9 %multiply_add_fusion = f32[5,8,64,128]{3,2,1,0:T(8,128)} fusion(f32[5,64,128]{2,1,0:T(8,128)S(1)} %slice.1064, f32[8]{0:T(128)S(1)} %copy-done.108, f32[5,64,128]{2,1,0:T(8,128)S(1)} %slice.1063, f32[8]{0:T(128)S(1)} %copy-done.107, f32[5,64,128]{2,1,0:T(8,128)S(1)} %copy-done.44, f32[8]{0:T(128)S(1)} %get-tuple-element.7, f32[5,64,128]{2,1,0:T(8,128)S(1)} %copy-done.46, ...), kind=kLoop, calls=%fused_computation.40 | loop fusion | flops 10158080 | bytes 3932672 | tf_op jit(solution)/shard_map/add | solution.py:267
  228.1 3.1 %collective-permute-start.20 = (f32[5,64,128]{2,1,0:T(8,128)S(1)}, f32[5,64,128]{2,1,0:T(8,128)S(1)}, u32[]{:S(2)}, u32[]{:S(2)}) collective-permute-start(f32[5,64,128]{2,1,0:T(8,128)S(1)} %fusion.39), channel_id=1, source_target_pairs={{0,1},{1,0},{2,3},{3,2},{4,5},{5,4},{6,7},{7,6},{8,9},{9,8},{10,11... | collective-permute-start | bytes 491528 | tf_op jit(solution)/shard_map/ppermute | solution.py:257
  232.7 2.8 %add_negate_fusion = f32[5,8,64,128]{3,2,1,0:T(8,128)S(1)} fusion(f32[5,8,64,128]{3,2,1,0:T(8,128)S(1)} %fusion.89, f32[5,64,128]{2,1,0:T(8,128)S(1)} %get-tuple-element.147, f32[8]{0:T(128)S(1)} %copy-done.110, f32[5,64,128]{2,1,0:T(8,128)S(1)} %get-tuple-element.146, f32[8]{0:T(128)S(1)} %copy-done.109, f32[5,64,128]{2,1,0:T(8,128)S(1)} %copy-done.102, ...), kind=kOutput, calls=%fused_computation.41 | convolution fusion | flops 261816320 | bytes 7553472 | tf_op jit(solution)/shard_map/fyzx,zw->fywx/dot_general | solution.py:293
  (332 shorter events, 70.7 us)
Async XLA Ops:
  3.1 15.1 %collective-permute-start = (f32[5,3,64,128]{3,2,1,0:T(8,128)}, f32[5,3,64,128]{3,2,1,0:T(8,128)S(1)}, u32[]{:S(2)}, u32[]{:S(2)}) collective-permute-start(f32[5,3,64,128]{3,2,1,0:T(8,128)} %get-tuple-element.134), channel_id=1, source_target_pairs={{0,2},{2,4},{4,6},{6,8},{8,10},{10,12},{12,14},{14,16},{16,18},{18... | collective-permute-start | bytes 1474568 | tf_op jit(solution)/shard_map/ppermute | solution.py:279
  6.5 19.1 %collective-permute-start.1 = (f32[5,3,64,128]{3,2,1,0:T(8,128)}, f32[5,3,64,128]{3,2,1,0:T(8,128)}, u32[]{:S(2)}, u32[]{:S(2)}) collective-permute-start(f32[5,3,64,128]{3,2,1,0:T(8,128)} %get-tuple-element.135), channel_id=1, source_target_pairs={{2,0},{4,2},{6,4},{8,6},{10,8},{12,10},{14,12},{16,14},{18,16},{20... | collective-permute-start | bytes 1474568 | tf_op jit(solution)/shard_map/ppermute | solution.py:280
  10.9 21.8 %copy-start.19 = (f32[5,64,128]{2,1,0:T(8,128)}, f32[5,64,128]{2,1,0:T(8,128)S(1)}, u32[]{:S(2)}) copy-start(f32[5,64,128]{2,1,0:T(8,128)S(1)} %get-tuple-element.126) | copy-start | bytes 491524
  10.9 21.8 %copy-start.21 = (f32[5,64,128]{2,1,0:T(8,128)}, f32[5,64,128]{2,1,0:T(8,128)S(1)}, u32[]{:S(2)}) copy-start(f32[5,64,128]{2,1,0:T(8,128)S(1)} %get-tuple-element.127) | copy-start | bytes 491524
  33.6 1.7 collective-permute-start.2
  36.1 12.1 %collective-permute-start.3 = (f32[2,9,64,128]{3,2,1,0:T(8,128)}, f32[2,9,64,128]{3,2,1,0:T(8,128)}, u32[]{:S(2)}, u32[]{:S(2)}) collective-permute-start(f32[2,9,64,128]{3,2,1,0:T(8,128)} %maximum_select_fusion), channel_id=1, source_target_pairs={{0,2},{2,4},{4,6},{6,8},{8,10},{10,12},{12,14},{14,16},{16,18},{18... | collective-permute-start | bytes 1769480 | tf_op jit(solution)/shard_map/ppermute | solution.py:253
  49.4 17.5 %collective-permute-start.4 = (f32[2,9,64,128]{3,2,1,0:T(8,128)S(1)}, f32[2,9,64,128]{3,2,1,0:T(8,128)S(1)}, u32[]{:S(2)}, u32[]{:S(2)}) collective-permute-start(f32[2,9,64,128]{3,2,1,0:T(8,128)S(1)} %multiply_add_fusion.7), channel_id=1, source_target_pairs={{0,4},{2,6},{4,8},{6,10},{8,12},{10,14},{12,16},{14,18},{16,20},{1... | collective-permute-start | bytes 1769480 | tf_op jit(solution)/shard_map/ppermute | solution.py:253
  67.0 11.8 %collective-permute-start.5 = (f32[2,9,64,128]{3,2,1,0:T(8,128)S(1)}, f32[2,9,64,128]{3,2,1,0:T(8,128)S(1)}, u32[]{:S(2)}, u32[]{:S(2)}) collective-permute-start(f32[2,9,64,128]{3,2,1,0:T(8,128)S(1)} %multiply_add_fusion.6), channel_id=1, source_target_pairs={{0,8},{2,10},{4,12},{6,14},{8,16},{10,18},{12,20},{14,22},{16,24},... | collective-permute-start | bytes 1769480 | tf_op jit(solution)/shard_map/ppermute | solution.py:253
  78.9 16.7 %collective-permute-start.6 = (f32[2,9,64,128]{3,2,1,0:T(8,128)S(1)}, f32[2,9,64,128]{3,2,1,0:T(8,128)}, u32[]{:S(2)}, u32[]{:S(2)}) collective-permute-start(f32[2,9,64,128]{3,2,1,0:T(8,128)S(1)} %multiply_add_fusion.5), channel_id=1, source_target_pairs={{0,16},{2,18},{4,20},{6,22},{8,24},{10,26},{12,28},{14,30},{16,32}... | collective-permute-start | bytes 1769480 | tf_op jit(solution)/shard_map/ppermute | solution.py:253
  96.9 13.9 %collective-permute-start.7 = (f32[2,9,64,128]{3,2,1,0:T(8,128)S(1)}, f32[2,9,64,128]{3,2,1,0:T(8,128)S(1)}, u32[]{:S(2)}, u32[]{:S(2)}) collective-permute-start(f32[2,9,64,128]{3,2,1,0:T(8,128)S(1)} %multiply_add_fusion.4), channel_id=1, source_target_pairs={{0,32},{2,34},{4,36},{6,38},{8,40},{10,42},{12,44},{14,46},{16,48}... | collective-permute-start | bytes 1769480 | tf_op jit(solution)/shard_map/ppermute | solution.py:253
  105.4 19.7 %collective-permute-start.10 = (f32[4,8,64,128]{3,2,1,0:T(8,128)S(1)}, f32[4,8,64,128]{3,2,1,0:T(8,128)S(1)}, u32[]{:S(2)}, u32[]{:S(2)}) collective-permute-start(f32[4,8,64,128]{3,2,1,0:T(8,128)S(1)} %fusion.4), channel_id=1, source_target_pairs={{0,1},{1,0},{2,3},{3,2},{4,5},{5,4},{6,7},{7,6},{8,9},{9,8},{10,11... | collective-permute-start | bytes 3145736 | tf_op jit(solution)/shard_map/ppermute | solution.py:292
  110.9 13.7 %collective-permute-start.8 = (f32[2,9,64,128]{3,2,1,0:T(8,128)S(1)}, f32[2,9,64,128]{3,2,1,0:T(8,128)S(1)}, u32[]{:S(2)}, u32[]{:S(2)}) collective-permute-start(f32[2,9,64,128]{3,2,1,0:T(8,128)S(1)} %multiply_add_fusion.3), channel_id=1, source_target_pairs={{0,64},{2,66},{4,68},{6,70},{8,72},{10,74},{12,76},{14,78},{16,80}... | collective-permute-start | bytes 1769480 | tf_op jit(solution)/shard_map/ppermute | solution.py:253
  124.8 2.9 %collective-permute-start.9 = (f32[9,64,128]{2,1,0:T(8,128)S(1)}, f32[9,64,128]{2,1,0:T(8,128)S(1)}, u32[]{:S(2)}, u32[]{:S(2)}) collective-permute-start(f32[9,64,128]{2,1,0:T(8,128)S(1)} %fusion.8), channel_id=1, source_target_pairs={{0,1},{1,0},{2,3},{3,2},{4,5},{5,4},{6,7},{7,6},{8,9},{9,8},{10,11... | collective-permute-start | bytes 884744 | tf_op jit(solution)/shard_map/ppermute | solution.py:257
  134.3 11.7 %collective-permute-start.11 = (f32[5,2,64,128]{3,2,1,0:T(8,128)S(1)}, f32[5,2,64,128]{3,2,1,0:T(8,128)S(1)}, u32[]{:S(2)}, u32[]{:S(2)}) collective-permute-start(f32[5,2,64,128]{3,2,1,0:T(8,128)S(1)} %get-tuple-element.116), channel_id=1, source_target_pairs={{0,2},{2,4},{4,6},{6,8},{8,10},{10,12},{12,14},{14,16},{16,18},{18... | collective-permute-start | bytes 983048 | tf_op jit(solution)/shard_map/ppermute | solution.py:279
  138.4 15.7 %collective-permute-start.12 = (f32[5,2,64,128]{3,2,1,0:T(8,128)S(1)}, f32[5,2,64,128]{3,2,1,0:T(8,128)S(1)}, u32[]{:S(2)}, u32[]{:S(2)}) collective-permute-start(f32[5,2,64,128]{3,2,1,0:T(8,128)S(1)} %get-tuple-element.117), channel_id=1, source_target_pairs={{2,0},{4,2},{6,4},{8,6},{10,8},{12,10},{14,12},{16,14},{18,16},{20... | collective-permute-start | bytes 983048 | tf_op jit(solution)/shard_map/ppermute | solution.py:280
  154.8 1.4 collective-permute-start.13
  156.2 9.0 %collective-permute-start.14 = (f32[2,5,64,128]{3,2,1,0:T(8,128)S(1)}, f32[2,5,64,128]{3,2,1,0:T(8,128)S(1)}, u32[]{:S(2)}, u32[]{:S(2)}) collective-permute-start(f32[2,5,64,128]{3,2,1,0:T(8,128)S(1)} %maximum_select_fusion.2), channel_id=1, source_target_pairs={{0,2},{2,4},{4,6},{6,8},{8,10},{10,12},{12,14},{14,16},{16,18},{18... | collective-permute-start | bytes 983048 | tf_op jit(solution)/shard_map/ppermute | solution.py:253
  165.3 10.8 %collective-permute-start.15 = (f32[2,5,64,128]{3,2,1,0:T(8,128)S(1)}, f32[2,5,64,128]{3,2,1,0:T(8,128)S(1)}, u32[]{:S(2)}, u32[]{:S(2)}) collective-permute-start(f32[2,5,64,128]{3,2,1,0:T(8,128)S(1)} %multiply_add_fusion.13), channel_id=1, source_target_pairs={{0,4},{2,6},{4,8},{6,10},{8,12},{10,14},{12,16},{14,18},{16,20},{1... | collective-permute-start | bytes 983048 | tf_op jit(solution)/shard_map/ppermute | solution.py:253
  176.2 9.0 %collective-permute-start.16 = (f32[2,5,64,128]{3,2,1,0:T(8,128)S(1)}, f32[2,5,64,128]{3,2,1,0:T(8,128)S(1)}, u32[]{:S(2)}, u32[]{:S(2)}) collective-permute-start(f32[2,5,64,128]{3,2,1,0:T(8,128)S(1)} %multiply_add_fusion.12), channel_id=1, source_target_pairs={{0,8},{2,10},{4,12},{6,14},{8,16},{10,18},{12,20},{14,22},{16,24},... | collective-permute-start | bytes 983048 | tf_op jit(solution)/shard_map/ppermute | solution.py:253
  186.0 10.8 %collective-permute-start.17 = (f32[2,5,64,128]{3,2,1,0:T(8,128)}, f32[2,5,64,128]{3,2,1,0:T(8,128)}, u32[]{:S(2)}, u32[]{:S(2)}) collective-permute-start(f32[2,5,64,128]{3,2,1,0:T(8,128)} %multiply_add_fusion.11), channel_id=1, source_target_pairs={{0,16},{2,18},{4,20},{6,22},{8,24},{10,26},{12,28},{14,30},{16,32}... | collective-permute-start | bytes 983048 | tf_op jit(solution)/shard_map/ppermute | solution.py:253
  197.9 12.3 %collective-permute-start.18 = (f32[2,5,64,128]{3,2,1,0:T(8,128)S(1)}, f32[2,5,64,128]{3,2,1,0:T(8,128)S(1)}, u32[]{:S(2)}, u32[]{:S(2)}) collective-permute-start(f32[2,5,64,128]{3,2,1,0:T(8,128)S(1)} %multiply_add_fusion.10), channel_id=1, source_target_pairs={{0,32},{2,34},{4,36},{6,38},{8,40},{10,42},{12,44},{14,46},{16,48}... | collective-permute-start | bytes 983048 | tf_op jit(solution)/shard_map/ppermute | solution.py:253
  207.9 24.6 %collective-permute-start.21 = (f32[5,8,64,128]{3,2,1,0:T(8,128)}, f32[5,8,64,128]{3,2,1,0:T(8,128)S(1)}, u32[]{:S(2)}, u32[]{:S(2)}) collective-permute-start(f32[5,8,64,128]{3,2,1,0:T(8,128)} %fusion.13), channel_id=1, source_target_pairs={{0,1},{1,0},{2,3},{3,2},{4,5},{5,4},{6,7},{7,6},{8,9},{9,8},{10,11... | collective-permute-start | bytes 3932168 | tf_op jit(solution)/shard_map/ppermute | solution.py:292
  210.4 17.4 %collective-permute-start.19 = (f32[2,5,64,128]{3,2,1,0:T(8,128)S(1)}, f32[2,5,64,128]{3,2,1,0:T(8,128)S(1)}, u32[]{:S(2)}, u32[]{:S(2)}) collective-permute-start(f32[2,5,64,128]{3,2,1,0:T(8,128)S(1)} %multiply_add_fusion.9), channel_id=1, source_target_pairs={{0,64},{2,66},{4,68},{6,70},{8,72},{10,74},{12,76},{14,78},{16,80}... | collective-permute-start | bytes 983048 | tf_op jit(solution)/shard_map/ppermute | solution.py:253
  228.1 4.4 %collective-permute-start.20 = (f32[5,64,128]{2,1,0:T(8,128)S(1)}, f32[5,64,128]{2,1,0:T(8,128)S(1)}, u32[]{:S(2)}, u32[]{:S(2)}) collective-permute-start(f32[5,64,128]{2,1,0:T(8,128)S(1)} %fusion.39), channel_id=1, source_target_pairs={{0,1},{1,0},{2,3},{3,2},{4,5},{5,4},{6,7},{7,6},{8,9},{9,8},{10,11... | collective-permute-start | bytes 491528 | tf_op jit(solution)/shard_map/ppermute | solution.py:257
  (109 other events, 861.3 us)

commit v6 on v3

--- a/solution.py
+++ b/solution.py
@@ -159,7 +159,7 @@
     rounds = []
     stride = 1
     while stride < blocks:
-        radix = min(4, -(-blocks // stride))
+        radix = min(2, -(-blocks // stride))
         rounds.append((stride, list(range(1, radix))))
         stride *= radix
     return rounds

time: 225 us -> 206 us (0.916); the launches traced: 221 us -> 204 us
  starting transfers between devices: 118 us -> 80.7 us
  waiting for transfers between devices: 67.1 us -> 89.5 us
    ppermute x18 -> x12, starting transfers between devices: 57.2 us -> 28 us  [wall_apply(): from_above = lax.ppermute(fall, 'gy', down_pairs)]
    ppermute x18 -> x12, waiting for transfers between devices: 41.4 us -> 69 us  [wall_apply(): from_above = lax.ppermute(fall, 'gy', down_pairs)]
    ppermute x18 -> x12, starting transfers between devices: 49.1 us -> 40.7 us  [wall_apply(): from_below = lax.ppermute(rise, 'gy', up_pairs)]
    ppermute x2, waiting for transfers between devices: 17 us -> 12.4 us  [halo(): above = lax.ppermute(block[:, :width], 'gy', down_pairs)]
    ppermute x2, waiting for transfers between devices: 2.63 us -> 0.01 us  [halo(): below = lax.ppermute(block[:, block.shape[1] - width:], 'gy', up_pairs)]
    ppermute x18 -> x12, waiting for transfers between devices: 5.99 us -> 8.05 us  [wall_apply(): from_below = lax.ppermute(rise, 'gy', up_pairs)]
  transfers between devices with their start and end apart: 42 -> 30, of which waited for: 14 -> 16; matrix products, arithmetic and copies ran while one was open for 9% -> 10% of each run, Pallas kernels for 0% -> 0%
where the time goes in v6:
time: 206 us; the launch traced here: 204 us
  waiting for transfers between devices  89.5 us (43%)
  starting transfers between devices  80.7 us (39%)
  other arithmetic  12.8 us (6%)
  local copies, waits for them, and re-layouts  11.4 us (6%)
  matrix products  8.53 us (4%)
    ppermute x12, waiting for transfers between devices, wall_apply(): from_above = lax.ppermute(fall, 'gy', down_pairs)  69 us
    ppermute x12, starting transfers between devices, wall_apply(): from_below = lax.ppermute(rise, 'gy', up_pairs)  40.7 us
    ppermute x12, starting transfers between devices, wall_apply(): from_above = lax.ppermute(fall, 'gy', down_pairs)  28 us
    ppermute x2, waiting for transfers between devices, halo(): above = lax.ppermute(block[:, :width], 'gy', down_pairs)  12.4 us
    ppermute x12, waiting for transfers between devices, wall_apply(): from_below = lax.ppermute(rise, 'gy', up_pairs)  8.05 us
    ppermute x2, starting transfers between devices, halo(): above = lax.ppermute(block[:, :width], 'gy', down_pairs)  6.36 us
    ppermute x2, starting transfers between devices, halo(): below = lax.ppermute(block[:, block.shape[1] - width:], 'gy', up_pairs)  5.49 us
    add x2, other arithmetic, wall_apply(): local + rise_gain[None, :, None, None] * rise[first:first + size, None]  4.24 us
  transfers between devices with their start and end apart: 30, of which 16 were waited for; matrix products, arithmetic and copies ran while one was open for 10% of the time, Pallas kernels for 0%

profile of v6, /device:TPU:30, one launch (start us, length us, event | category | flops | bytes accessed | tf_op | source)
XLA Modules:
  0.0 204.5 jit_solution(1389090020219726235)
XLA Ops:
  3.0 3.4 %collective-permute-start = (f32[5,3,64,128]{3,2,1,0:T(8,128)}, f32[5,3,64,128]{3,2,1,0:T(8,128)S(1)}, u32[]{:S(2)}, u32[]{:S(2)}) collective-permute-start(f32[5,3,64,128]{3,2,1,0:T(8,128)} %get-tuple-element.134), channel_id=1, source_target_pairs={{0,2},{2,4},{4,6},{6,8},{8,10},{10,12},{12,14},{14,16},{16,18},{18... | collective-permute-start | bytes 1474568 | tf_op jit(solution)/shard_map/ppermute | solution.py:271
  6.4 2.4 %collective-permute-start.1 = (f32[5,3,64,128]{3,2,1,0:T(8,128)}, f32[5,3,64,128]{3,2,1,0:T(8,128)S(1)}, u32[]{:S(2)}, u32[]{:S(2)}) collective-permute-start(f32[5,3,64,128]{3,2,1,0:T(8,128)} %get-tuple-element.135), channel_id=1, source_target_pairs={{2,0},{4,2},{6,4},{8,6},{10,8},{12,10},{14,12},{16,14},{18,16},{20... | collective-permute-start | bytes 1474568 | tf_op jit(solution)/shard_map/ppermute | solution.py:272
  18.2 7.2 %collective-permute-done.1 = f32[5,3,64,128]{3,2,1,0:T(8,128)S(1)} collective-permute-done((f32[5,3,64,128]{3,2,1,0:T(8,128)}, f32[5,3,64,128]{3,2,1,0:T(8,128)S(1)}, u32[]{:S(2)}, u32[]{:S(2)}) %collective-permute-start.1) | collective-permute-done | bytes 491552 | tf_op jit(solution)/shard_map/ppermute | solution.py:272
  29.1 3.9 %collective-permute-start.8 = (f32[9,64,128]{2,1,0:T(8,128)S(1)}, f32[9,64,128]{2,1,0:T(8,128)S(1)}, u32[]{:S(2)}, u32[]{:S(2)}) collective-permute-start(f32[9,64,128]{2,1,0:T(8,128)S(1)} %pad_maximum_fusion.11), channel_id=1, source_target_pairs={{2,0},{4,2},{6,4},{8,6},{10,8},{12,10},{14,12},{16,14},{18,16},{20... | collective-permute-start | bytes 884744 | tf_op jit(solution)/shard_map/ppermute | solution.py:248
  33.3 3.3 %collective-permute-done.2 = f32[9,64,128]{2,1,0:T(8,128)S(1)} collective-permute-done((f32[9,64,128]{2,1,0:T(8,128)S(1)}, f32[9,64,128]{2,1,0:T(8,128)S(1)}, u32[]{:S(2)}, u32[]{:S(2)}) %collective-permute-start.2) | collective-permute-done | bytes 294944 | tf_op jit(solution)/shard_map/ppermute | solution.py:247
  38.6 10.5 %collective-permute-done.8 = f32[9,64,128]{2,1,0:T(8,128)S(1)} collective-permute-done((f32[9,64,128]{2,1,0:T(8,128)S(1)}, f32[9,64,128]{2,1,0:T(8,128)S(1)}, u32[]{:S(2)}, u32[]{:S(2)}) %collective-permute-start.8) | collective-permute-done | bytes 294944 | tf_op jit(solution)/shard_map/ppermute | solution.py:248
  54.2 8.2 %collective-permute-done.9 = f32[9,64,128]{2,1,0:T(8,128)S(1)} collective-permute-done((f32[9,64,128]{2,1,0:T(8,128)S(1)}, f32[9,64,128]{2,1,0:T(8,128)S(1)}, u32[]{:S(2)}, u32[]{:S(2)}) %collective-permute-start.9) | collective-permute-done | bytes 294944 | tf_op jit(solution)/shard_map/ppermute | solution.py:248
  66.5 11.8 %collective-permute-done.10 = f32[9,64,128]{2,1,0:T(8,128)S(1)} collective-permute-done((f32[9,64,128]{2,1,0:T(8,128)S(1)}, f32[9,64,128]{2,1,0:T(8,128)S(1)}, u32[]{:S(2)}, u32[]{:S(2)}) %collective-permute-start.10) | collective-permute-done | bytes 294944 | tf_op jit(solution)/shard_map/ppermute | solution.py:248
  81.8 7.7 %collective-permute-done.11 = f32[9,64,128]{2,1,0:T(8,128)S(1)} collective-permute-done((f32[9,64,128]{2,1,0:T(8,128)S(1)}, f32[9,64,128]{2,1,0:T(8,128)S(1)}, u32[]{:S(2)}, u32[]{:S(2)}) %collective-permute-start.11) | collective-permute-done | bytes 294944 | tf_op jit(solution)/shard_map/ppermute | solution.py:248
  92.1 7.4 %collective-permute-start.7 = (f32[9,64,128]{2,1,0:T(8,128)S(1)}, f32[9,64,128]{2,1,0:T(8,128)S(1)}, u32[]{:S(2)}, u32[]{:S(2)}) collective-permute-start(f32[9,64,128]{2,1,0:T(8,128)S(1)} %multiply_add_fusion.11), channel_id=1, source_target_pairs={{0,64},{2,66},{4,68},{6,70},{8,72},{10,74},{12,76},{14,78},{16,80}... | collective-permute-start | bytes 884744 | tf_op jit(solution)/shard_map/ppermute | solution.py:247
  103.9 7.5 %collective-permute-done.13 = f32[9,64,128]{2,1,0:T(8,128)S(1)} collective-permute-done((f32[9,64,128]{2,1,0:T(8,128)S(1)}, f32[9,64,128]{2,1,0:T(8,128)S(1)}, u32[]{:S(2)}, u32[]{:S(2)}) %collective-permute-start.13) | collective-permute-done | bytes 294944 | tf_op jit(solution)/shard_map/ppermute | solution.py:248
  114.4 2.1 %collective-permute-start.15 = (f32[5,2,64,128]{3,2,1,0:T(8,128)S(1)}, f32[5,2,64,128]{3,2,1,0:T(8,128)S(1)}, u32[]{:S(2)}, u32[]{:S(2)}) collective-permute-start(f32[5,2,64,128]{3,2,1,0:T(8,128)S(1)} %get-tuple-element.116), channel_id=1, source_target_pairs={{0,2},{2,4},{4,6},{6,8},{8,10},{10,12},{12,14},{14,16},{16,18},{18... | collective-permute-start | bytes 983048 | tf_op jit(solution)/shard_map/ppermute | solution.py:271
  116.5 3.9 %collective-permute-start.16 = (f32[5,2,64,128]{3,2,1,0:T(8,128)S(1)}, f32[5,2,64,128]{3,2,1,0:T(8,128)S(1)}, u32[]{:S(2)}, u32[]{:S(2)}) collective-permute-start(f32[5,2,64,128]{3,2,1,0:T(8,128)S(1)} %get-tuple-element.117), channel_id=1, source_target_pairs={{2,0},{4,2},{6,4},{8,6},{10,8},{12,10},{14,12},{16,14},{18,16},{20... | collective-permute-start | bytes 983048 | tf_op jit(solution)/shard_map/ppermute | solution.py:272
  121.4 2.9 %multiply_add_fusion = f32[5,8,64,128]{3,2,1,0:T(8,128)} fusion(f32[5,64,128]{2,1,0:T(8,128)S(1)} %slice-done.1, f32[8]{0:T(128)S(1)} %get-tuple-element.167, f32[5,64,128]{2,1,0:T(8,128)S(1)} %slice-done, f32[8]{0:T(128)S(1)} %get-tuple-element.162, f32[5,64,128]{2,1,0:T(8,128)S(1)} %get-tuple-element.148, f32[8]{0:T(128)S(1)} %get-tuple-element.7, ...), kind=kLoop, calls=%fused_computation.42 | loop fusion | flops 10158080 | bytes 3932672 | tf_op jit(solution)/shard_map/add | solution.py:259
  124.5 5.2 %collective-permute-done.16 = f32[5,2,64,128]{3,2,1,0:T(8,128)S(1)} collective-permute-done((f32[5,2,64,128]{3,2,1,0:T(8,128)S(1)}, f32[5,2,64,128]{3,2,1,0:T(8,128)S(1)}, u32[]{:S(2)}, u32[]{:S(2)}) %collective-permute-start.16) | collective-permute-done | bytes 327712 | tf_op jit(solution)/shard_map/ppermute | solution.py:272
  132.0 3.9 %collective-permute-start.23 = (f32[5,64,128]{2,1,0:T(8,128)S(1)}, f32[5,64,128]{2,1,0:T(8,128)S(1)}, u32[]{:S(2)}, u32[]{:S(2)}) collective-permute-start(f32[5,64,128]{2,1,0:T(8,128)S(1)} %get-tuple-element.153), channel_id=1, source_target_pairs={{2,0},{4,2},{6,4},{8,6},{10,8},{12,10},{14,12},{16,14},{18,16},{20... | collective-permute-start | bytes 491528 | tf_op jit(solution)/shard_map/ppermute | solution.py:248
  137.3 7.9 %collective-permute-done.23 = f32[5,64,128]{2,1,0:T(8,128)S(1)} collective-permute-done((f32[5,64,128]{2,1,0:T(8,128)S(1)}, f32[5,64,128]{2,1,0:T(8,128)S(1)}, u32[]{:S(2)}, u32[]{:S(2)}) %collective-permute-start.23) | collective-permute-done | bytes 163872 | tf_op jit(solution)/shard_map/ppermute | solution.py:248
  148.6 5.4 %collective-permute-start.24 = (f32[5,64,128]{2,1,0:T(8,128)S(1)}, f32[5,64,128]{2,1,0:T(8,128)S(1)}, u32[]{:S(2)}, u32[]{:S(2)}) collective-permute-start(f32[5,64,128]{2,1,0:T(8,128)S(1)} %get-tuple-element.151), channel_id=1, source_target_pairs={{4,0},{6,2},{8,4},{10,6},{12,8},{14,10},{16,12},{18,14},{20,16},{2... | collective-permute-start | bytes 491528 | tf_op jit(solution)/shard_map/ppermute | solution.py:248
  156.1 4.2 %collective-permute-done.24 = f32[5,64,128]{2,1,0:T(8,128)S(1)} collective-permute-done((f32[5,64,128]{2,1,0:T(8,128)S(1)}, f32[5,64,128]{2,1,0:T(8,128)S(1)}, u32[]{:S(2)}, u32[]{:S(2)}) %collective-permute-start.24) | collective-permute-done | bytes 163872 | tf_op jit(solution)/shard_map/ppermute | solution.py:248
  164.3 5.4 %collective-permute-done.25 = f32[5,64,128]{2,1,0:T(8,128)S(1)} collective-permute-done((f32[5,64,128]{2,1,0:T(8,128)S(1)}, f32[5,64,128]{2,1,0:T(8,128)S(1)}, u32[]{:S(2)}, u32[]{:S(2)}) %collective-permute-start.25) | collective-permute-done | bytes 163872 | tf_op jit(solution)/shard_map/ppermute | solution.py:248
  171.8 7.7 %collective-permute-start.21 = (f32[5,64,128]{2,1,0:T(8,128)S(1)}, f32[5,64,128]{2,1,0:T(8,128)S(1)}, u32[]{:S(2)}, u32[]{:S(2)}) collective-permute-start(f32[5,64,128]{2,1,0:T(8,128)S(1)} %multiply_add_fusion.25), channel_id=1, source_target_pairs={{0,32},{2,34},{4,36},{6,38},{8,40},{10,42},{12,44},{14,46},{16,48}... | collective-permute-start | bytes 491528 | tf_op jit(solution)/shard_map/ppermute | solution.py:247
  182.5 8.9 %collective-permute-start.22 = (f32[5,64,128]{2,1,0:T(8,128)S(1)}, f32[5,64,128]{2,1,0:T(8,128)S(1)}, u32[]{:S(2)}, u32[]{:S(2)}) collective-permute-start(f32[5,64,128]{2,1,0:T(8,128)S(1)} %multiply_add_fusion.24), channel_id=1, source_target_pairs={{0,64},{2,66},{4,68},{6,70},{8,72},{10,74},{12,76},{14,78},{16,80}... | collective-permute-start | bytes 491528 | tf_op jit(solution)/shard_map/ppermute | solution.py:247
  194.2 5.9 %collective-permute-done.28 = f32[5,64,128]{2,1,0:T(8,128)S(1)} collective-permute-done((f32[5,64,128]{2,1,0:T(8,128)S(1)}, f32[5,64,128]{2,1,0:T(8,128)S(1)}, u32[]{:S(2)}, u32[]{:S(2)}) %collective-permute-start.28) | collective-permute-done | bytes 163872 | tf_op jit(solution)/shard_map/ppermute | solution.py:248
  200.2 2.9 %fusion.3 = f32[5,8,64,128]{3,2,1,0:T(8,128)S(1)} fusion(f32[5,8,128,64]{2,3,1,0:T(8,128)S(1)} %fusion.74, f32[5,8,64,128]{3,2,1,0:T(8,128)S(1)} %collective-permute-done.29, f32[64,64,1,1]{0,1,3,2:T(8,128)S(1)} %copy-done.8, f32[5,8,64,128]{3,2,1,0:T(8,128)S(1)} %fusion.73, f32[5,64,128]{2,1,0:T(8,128)S(1)} %multiply_add_fusion.17, ...), kind=kOutput, calls=%fused_computation.36 | convolution fusion | flops 261816320 | bytes 7553472 | tf_op jit(solution)/shard_map/fyzx,zw->fywx/dot_general | solution.py:285
  (151 shorter events, 63.3 us)
Async XLA Ops:
  3.0 15.2 %collective-permute-start = (f32[5,3,64,128]{3,2,1,0:T(8,128)}, f32[5,3,64,128]{3,2,1,0:T(8,128)S(1)}, u32[]{:S(2)}, u32[]{:S(2)}) collective-permute-start(f32[5,3,64,128]{3,2,1,0:T(8,128)} %get-tuple-element.134), channel_id=1, source_target_pairs={{0,2},{2,4},{4,6},{6,8},{8,10},{10,12},{12,14},{14,16},{16,18},{18... | collective-permute-start | bytes 1474568 | tf_op jit(solution)/shard_map/ppermute | solution.py:271
  6.4 19.0 %collective-permute-start.1 = (f32[5,3,64,128]{3,2,1,0:T(8,128)}, f32[5,3,64,128]{3,2,1,0:T(8,128)S(1)}, u32[]{:S(2)}, u32[]{:S(2)}) collective-permute-start(f32[5,3,64,128]{3,2,1,0:T(8,128)} %get-tuple-element.135), channel_id=1, source_target_pairs={{2,0},{4,2},{6,4},{8,6},{10,8},{12,10},{14,12},{16,14},{18,16},{20... | collective-permute-start | bytes 1474568 | tf_op jit(solution)/shard_map/ppermute | solution.py:272
  27.2 9.5 %collective-permute-start.2 = (f32[9,64,128]{2,1,0:T(8,128)S(1)}, f32[9,64,128]{2,1,0:T(8,128)S(1)}, u32[]{:S(2)}, u32[]{:S(2)}) collective-permute-start(f32[9,64,128]{2,1,0:T(8,128)S(1)} %pad_maximum_fusion.10), channel_id=1, source_target_pairs={{0,2},{2,4},{4,6},{6,8},{8,10},{10,12},{12,14},{14,16},{16,18},{18... | collective-permute-start | bytes 884744 | tf_op jit(solution)/shard_map/ppermute | solution.py:247
  29.1 20.0 %collective-permute-start.8 = (f32[9,64,128]{2,1,0:T(8,128)S(1)}, f32[9,64,128]{2,1,0:T(8,128)S(1)}, u32[]{:S(2)}, u32[]{:S(2)}) collective-permute-start(f32[9,64,128]{2,1,0:T(8,128)S(1)} %pad_maximum_fusion.11), channel_id=1, source_target_pairs={{2,0},{4,2},{6,4},{8,6},{10,8},{12,10},{14,12},{16,14},{18,16},{20... | collective-permute-start | bytes 884744 | tf_op jit(solution)/shard_map/ppermute | solution.py:248
  33.2 57.7 %collective-permute-start.14 = (f32[4,8,64,128]{3,2,1,0:T(8,128)S(1)}, f32[4,8,64,128]{3,2,1,0:T(8,128)S(1)}, u32[]{:S(2)}, u32[]{:S(2)}) collective-permute-start(f32[4,8,64,128]{3,2,1,0:T(8,128)S(1)} %fusion.6), channel_id=1, source_target_pairs={{0,1},{1,0},{2,3},{3,2},{4,5},{5,4},{6,7},{7,6},{8,9},{9,8},{10,11... | collective-permute-start | bytes 3145736 | tf_op jit(solution)/shard_map/ppermute | solution.py:284
  36.7 15.4 %collective-permute-start.3 = (f32[9,64,128]{2,1,0:T(8,128)S(1)}, f32[9,64,128]{2,1,0:T(8,128)S(1)}, u32[]{:S(2)}, u32[]{:S(2)}) collective-permute-start(f32[9,64,128]{2,1,0:T(8,128)S(1)} %multiply_add_fusion.15), channel_id=1, source_target_pairs={{0,4},{2,6},{4,8},{6,10},{8,12},{10,14},{12,16},{14,18},{16,20},{1... | collective-permute-start | bytes 884744 | tf_op jit(solution)/shard_map/ppermute | solution.py:247
  49.2 13.1 %collective-permute-start.9 = (f32[9,64,128]{2,1,0:T(8,128)S(1)}, f32[9,64,128]{2,1,0:T(8,128)S(1)}, u32[]{:S(2)}, u32[]{:S(2)}) collective-permute-start(f32[9,64,128]{2,1,0:T(8,128)S(1)} %multiply_add_fusion.9), channel_id=1, source_target_pairs={{4,0},{6,2},{8,4},{10,6},{12,8},{14,10},{16,12},{18,14},{20,16},{2... | collective-permute-start | bytes 884744 | tf_op jit(solution)/shard_map/ppermute | solution.py:248
  52.3 12.2 %collective-permute-start.4 = (f32[9,64,128]{2,1,0:T(8,128)S(1)}, f32[9,64,128]{2,1,0:T(8,128)S(1)}, u32[]{:S(2)}, u32[]{:S(2)}) collective-permute-start(f32[9,64,128]{2,1,0:T(8,128)S(1)} %multiply_add_fusion.14), channel_id=1, source_target_pairs={{0,8},{2,10},{4,12},{6,14},{8,16},{10,18},{12,20},{14,22},{16,24},... | collective-permute-start | bytes 884744 | tf_op jit(solution)/shard_map/ppermute | solution.py:247
  62.5 15.8 %collective-permute-start.10 = (f32[9,64,128]{2,1,0:T(8,128)S(1)}, f32[9,64,128]{2,1,0:T(8,128)S(1)}, u32[]{:S(2)}, u32[]{:S(2)}) collective-permute-start(f32[9,64,128]{2,1,0:T(8,128)S(1)} %multiply_add_fusion.8), channel_id=1, source_target_pairs={{8,0},{10,2},{12,4},{14,6},{16,8},{18,10},{20,12},{22,14},{24,16},... | collective-permute-start | bytes 884744 | tf_op jit(solution)/shard_map/ppermute | solution.py:248
  64.6 15.8 %collective-permute-start.5 = (f32[9,64,128]{2,1,0:T(8,128)S(1)}, f32[9,64,128]{2,1,0:T(8,128)S(1)}, u32[]{:S(2)}, u32[]{:S(2)}) collective-permute-start(f32[9,64,128]{2,1,0:T(8,128)S(1)} %multiply_add_fusion.13), channel_id=1, source_target_pairs={{0,16},{2,18},{4,20},{6,22},{8,24},{10,26},{12,28},{14,30},{16,32}... | collective-permute-start | bytes 884744 | tf_op jit(solution)/shard_map/ppermute | solution.py:247
  78.4 11.1 %collective-permute-start.11 = (f32[9,64,128]{2,1,0:T(8,128)S(1)}, f32[9,64,128]{2,1,0:T(8,128)S(1)}, u32[]{:S(2)}, u32[]{:S(2)}) collective-permute-start(f32[9,64,128]{2,1,0:T(8,128)S(1)} %multiply_add_fusion.7), channel_id=1, source_target_pairs={{16,0},{18,2},{20,4},{22,6},{24,8},{26,10},{28,12},{30,14},{32,16}... | collective-permute-start | bytes 884744 | tf_op jit(solution)/shard_map/ppermute | solution.py:248
  80.5 11.6 %collective-permute-start.6 = (f32[9,64,128]{2,1,0:T(8,128)S(1)}, f32[9,64,128]{2,1,0:T(8,128)S(1)}, u32[]{:S(2)}, u32[]{:S(2)}) collective-permute-start(f32[9,64,128]{2,1,0:T(8,128)S(1)} %multiply_add_fusion.12), channel_id=1, source_target_pairs={{0,32},{2,34},{4,36},{6,38},{8,40},{10,42},{12,44},{14,46},{16,48}... | collective-permute-start | bytes 884744 | tf_op jit(solution)/shard_map/ppermute | solution.py:247
  89.6 10.0 %collective-permute-start.12 = (f32[9,64,128]{2,1,0:T(8,128)S(1)}, f32[9,64,128]{2,1,0:T(8,128)S(1)}, u32[]{:S(2)}, u32[]{:S(2)}) collective-permute-start(f32[9,64,128]{2,1,0:T(8,128)S(1)} %multiply_add_fusion.6), channel_id=1, source_target_pairs={{32,0},{34,2},{36,4},{38,6},{40,8},{42,10},{44,12},{46,14},{48,16}... | collective-permute-start | bytes 884744 | tf_op jit(solution)/shard_map/ppermute | solution.py:248
  92.1 11.6 %collective-permute-start.7 = (f32[9,64,128]{2,1,0:T(8,128)S(1)}, f32[9,64,128]{2,1,0:T(8,128)S(1)}, u32[]{:S(2)}, u32[]{:S(2)}) collective-permute-start(f32[9,64,128]{2,1,0:T(8,128)S(1)} %multiply_add_fusion.11), channel_id=1, source_target_pairs={{0,64},{2,66},{4,68},{6,70},{8,72},{10,74},{12,76},{14,78},{16,80}... | collective-permute-start | bytes 884744 | tf_op jit(solution)/shard_map/ppermute | solution.py:247
  99.7 11.7 %collective-permute-start.13 = (f32[9,64,128]{2,1,0:T(8,128)S(1)}, f32[9,64,128]{2,1,0:T(8,128)S(1)}, u32[]{:S(2)}, u32[]{:S(2)}) collective-permute-start(f32[9,64,128]{2,1,0:T(8,128)S(1)} %multiply_add_fusion.5), channel_id=1, source_target_pairs={{64,0},{66,2},{68,4},{70,6},{72,8},{74,10},{76,12},{78,14},{80,16}... | collective-permute-start | bytes 884744 | tf_op jit(solution)/shard_map/ppermute | solution.py:248
  114.4 10.0 %collective-permute-start.15 = (f32[5,2,64,128]{3,2,1,0:T(8,128)S(1)}, f32[5,2,64,128]{3,2,1,0:T(8,128)S(1)}, u32[]{:S(2)}, u32[]{:S(2)}) collective-permute-start(f32[5,2,64,128]{3,2,1,0:T(8,128)S(1)} %get-tuple-element.116), channel_id=1, source_target_pairs={{0,2},{2,4},{4,6},{6,8},{8,10},{10,12},{12,14},{14,16},{16,18},{18... | collective-permute-start | bytes 983048 | tf_op jit(solution)/shard_map/ppermute | solution.py:271
  116.5 13.2 %collective-permute-start.16 = (f32[5,2,64,128]{3,2,1,0:T(8,128)S(1)}, f32[5,2,64,128]{3,2,1,0:T(8,128)S(1)}, u32[]{:S(2)}, u32[]{:S(2)}) collective-permute-start(f32[5,2,64,128]{3,2,1,0:T(8,128)S(1)} %get-tuple-element.117), channel_id=1, source_target_pairs={{2,0},{4,2},{6,4},{8,6},{10,8},{12,10},{14,12},{16,14},{18,16},{20... | collective-permute-start | bytes 983048 | tf_op jit(solution)/shard_map/ppermute | solution.py:272
  120.7 79.5 %collective-permute-start.29 = (f32[5,8,64,128]{3,2,1,0:T(8,128)S(1)}, f32[5,8,64,128]{3,2,1,0:T(8,128)S(1)}, u32[]{:S(2)}, u32[]{:S(2)}) collective-permute-start(f32[5,8,64,128]{3,2,1,0:T(8,128)S(1)} %fusion.12), channel_id=1, source_target_pairs={{0,1},{1,0},{2,3},{3,2},{4,5},{5,4},{6,7},{7,6},{8,9},{9,8},{10,11... | collective-permute-start | bytes 3932168 | tf_op jit(solution)/shard_map/ppermute | solution.py:284
  132.0 13.2 %collective-permute-start.23 = (f32[5,64,128]{2,1,0:T(8,128)S(1)}, f32[5,64,128]{2,1,0:T(8,128)S(1)}, u32[]{:S(2)}, u32[]{:S(2)}) collective-permute-start(f32[5,64,128]{2,1,0:T(8,128)S(1)} %get-tuple-element.153), channel_id=1, source_target_pairs={{2,0},{4,2},{6,4},{8,6},{10,8},{12,10},{14,12},{16,14},{18,16},{20... | collective-permute-start | bytes 491528 | tf_op jit(solution)/shard_map/ppermute | solution.py:248
  148.6 11.7 %collective-permute-start.24 = (f32[5,64,128]{2,1,0:T(8,128)S(1)}, f32[5,64,128]{2,1,0:T(8,128)S(1)}, u32[]{:S(2)}, u32[]{:S(2)}) collective-permute-start(f32[5,64,128]{2,1,0:T(8,128)S(1)} %get-tuple-element.151), channel_id=1, source_target_pairs={{4,0},{6,2},{8,4},{10,6},{12,8},{14,10},{16,12},{18,14},{20,16},{2... | collective-permute-start | bytes 491528 | tf_op jit(solution)/shard_map/ppermute | solution.py:248
  169.8 9.8 %collective-permute-start.26 = (f32[5,64,128]{2,1,0:T(8,128)S(1)}, f32[5,64,128]{2,1,0:T(8,128)S(1)}, u32[]{:S(2)}, u32[]{:S(2)}) collective-permute-start(f32[5,64,128]{2,1,0:T(8,128)S(1)} %multiply_add_fusion.20), channel_id=1, source_target_pairs={{16,0},{18,2},{20,4},{22,6},{24,8},{26,10},{28,12},{30,14},{32,16}... | collective-permute-start | bytes 491528 | tf_op jit(solution)/shard_map/ppermute | solution.py:248
  171.8 10.6 %collective-permute-start.21 = (f32[5,64,128]{2,1,0:T(8,128)S(1)}, f32[5,64,128]{2,1,0:T(8,128)S(1)}, u32[]{:S(2)}, u32[]{:S(2)}) collective-permute-start(f32[5,64,128]{2,1,0:T(8,128)S(1)} %multiply_add_fusion.25), channel_id=1, source_target_pairs={{0,32},{2,34},{4,36},{6,38},{8,40},{10,42},{12,44},{14,46},{16,48}... | collective-permute-start | bytes 491528 | tf_op jit(solution)/shard_map/ppermute | solution.py:247
  179.7 11.7 %collective-permute-start.27 = (f32[5,64,128]{2,1,0:T(8,128)S(1)}, f32[5,64,128]{2,1,0:T(8,128)S(1)}, u32[]{:S(2)}, u32[]{:S(2)}) collective-permute-start(f32[5,64,128]{2,1,0:T(8,128)S(1)} %multiply_add_fusion.19), channel_id=1, source_target_pairs={{32,0},{34,2},{36,4},{38,6},{40,8},{42,10},{44,12},{46,14},{48,16}... | collective-permute-start | bytes 491528 | tf_op jit(solution)/shard_map/ppermute | solution.py:248
  182.5 11.7 %collective-permute-start.22 = (f32[5,64,128]{2,1,0:T(8,128)S(1)}, f32[5,64,128]{2,1,0:T(8,128)S(1)}, u32[]{:S(2)}, u32[]{:S(2)}) collective-permute-start(f32[5,64,128]{2,1,0:T(8,128)S(1)} %multiply_add_fusion.24), channel_id=1, source_target_pairs={{0,64},{2,66},{4,68},{6,70},{8,72},{10,74},{12,76},{14,78},{16,80}... | collective-permute-start | bytes 491528 | tf_op jit(solution)/shard_map/ppermute | solution.py:247
  (17 other events, 140.3 us)

commit v7 on v6

--- a/solution.py
+++ b/solution.py
@@ -108,7 +108,8 @@
 
 
 @functools.lru_cache(maxsize=None)
-def wall_tables(kind, points, rows, pad):
+def wall_tables(kind, points, rows, pad, extra=0):
+    assert extra == 0 or kind == "slope"
     lower, middle, upper, weights = system_rows(kind, points)
     system = np.diag(middle) + np.diag(lower[1:], -1) + np.diag(upper[:-1], 1)
     inv = np.linalg.inv(system)
@@ -120,38 +121,53 @@
                 stencil[row, row + offset + 3] = weights[3 + offset, row]
     scale = inverse_metric(points) if kind == "slope" else np.ones(points)
     blocks = points // rows
-    combine = np.zeros((blocks, rows + 2, rows + 2 * pad))
-    rise_gain = np.zeros((blocks, rows))
-    fall_gain = np.zeros((blocks, rows))
+    outputs = rows + 2 * extra
+    combine = np.zeros((blocks, outputs + 2, rows + 2 * pad))
+    rise_gain = np.zeros((blocks, outputs))
+    fall_gain = np.zeros((blocks, outputs))
     rise_step = np.zeros(blocks)
     fall_step = np.zeros(blocks)
     for block in range(blocks):
         lo, hi = block * rows, block * rows + rows
         own = slice(lo, hi)
+        window = slice(lo - pad + 3, hi + pad + 3)
         rise_part = np.zeros(rows)
         fall_part = np.zeros(rows)
-        alpha = np.zeros(rows)
-        beta = np.zeros(rows)
+        rise_ref = hi if block < blocks - 1 else lo
+        fall_ref = lo - 1 if block > 0 else hi - 1
         if block > 0:
-            ref = hi if block < blocks - 1 else lo
-            alpha = inv[own, lo - 1] / inv[ref, lo - 1]
-            rise_step[block] = inv[ref, lo - 1] / inv[lo, lo - 1]
+            rise_step[block] = inv[rise_ref, lo - 1] / inv[lo, lo - 1]
             fall_part = inv[lo - 1, own]
         if block < blocks - 1:
-            ref = lo - 1 if block > 0 else hi - 1
-            beta = inv[own, hi] / inv[ref, hi]
-            fall_step[block] = inv[ref, hi] / inv[hi - 1, hi]
+            fall_step[block] = inv[fall_ref, hi] / inv[hi - 1, hi]
             rise_part = inv[hi, own]
-        local = inv[own, own] - np.outer(alpha, rise_part) - np.outer(beta, fall_part)
-        rows_stencil = stencil[own, lo - pad + 3 : hi + pad + 3]
-        outside = stencil[own].copy()
-        outside[:, lo - pad + 3 : hi + pad + 3] = 0.0
-        assert not outside.any()
-        combine[block, :rows] = scale[own, None] * (local @ rows_stencil)
-        combine[block, rows] = rise_part @ rows_stencil
-        combine[block, rows + 1] = fall_part @ rows_stencil
-        rise_gain[block] = scale[own] * alpha
-        fall_gain[block] = scale[own] * beta
+        for out, row in enumerate(range(lo - extra, hi + extra)):
+            if row < 0 or row >= points:
+                continue
+            alpha = beta = 0.0
+            if block > 0 or row >= hi:
+                column = lo - 1 if lo <= row < hi else min(row, rise_ref) - 1
+                alpha = inv[row, column] / inv[rise_ref, column]
+            if block < blocks - 1:
+                column = hi if row < hi else row + 1
+                beta = inv[row, column] / inv[fall_ref, column]
+            coef = np.zeros(points + 6)
+            coef += (inv[row, own] - alpha * rise_part - beta * fall_part) @ stencil[own]
+            if row == lo - 2:
+                model = inv[row, row - 1] / inv[lo - 1, row - 1] * inv[lo - 1, lo - 1]
+                coef += (inv[row, lo - 1] - model) * stencil[lo - 1]
+            if row == hi + 1:
+                model = inv[row, row + 1] / inv[hi, row + 1] * inv[hi, hi]
+                coef += (inv[row, hi] - model) * stencil[hi]
+            outside = coef.copy()
+            outside[window] = 0.0
+            assert not outside.any()
+            combine[block, out] = scale[row] * coef[window]
+            rise_gain[block, out] = scale[row] * alpha
+            fall_gain[block, out] = scale[row] * beta
+        rows_stencil = stencil[own, window]
+        combine[block, outputs] = rise_part @ rows_stencil
+        combine[block, outputs + 1] = fall_part @ rows_stencil
     return combine, rise_gain, fall_gain, rise_step, fall_step
 
 
@@ -198,10 +214,14 @@
         return self.row[start : start + int(np.prod(shape))].reshape(shape)
 
 
-def plan_wall(bank, kinds_sizes, points, rows, pad):
-    tables = [wall_tables(kind, points, rows, pad) for kind, _ in kinds_sizes]
+def plan_wall(bank, kinds_sizes, points, rows, pad, extras):
+    tables = [
+        wall_tables(kind, points, rows, pad, extra)
+        for (kind, _), extra in zip(kinds_sizes, extras)
+    ]
     groups = [
-        (bank.add(table[0]), bank.add(table[1]), bank.add(table[2])) for table in tables
+        (bank.add(table[0]), bank.add(table[1]), bank.add(table[2]), table[1].shape[1])
+        for table in tables
     ]
     blocks = points // rows
     rounds = []
@@ -233,7 +253,7 @@
         return summed
 
     partials = [
-        taps(padded, bank.get(handles[0])[rows:])
+        taps(padded, bank.get(handles[0])[handles[3] :])
         for padded, handles in zip(padded_groups, groups)
     ]
     sizes = [padded.shape[0] for padded in padded_groups]
@@ -252,7 +272,7 @@
     results = []
     first = 0
     for padded, handles, size in zip(padded_groups, groups, sizes):
-        local = taps(padded, bank.get(handles[0])[:rows])
+        local = taps(padded, bank.get(handles[0])[: handles[3]])
         rise_gain = bank.get(handles[1])
         fall_gain = bank.get(handles[2])
         results.append(
@@ -317,8 +337,8 @@
     other_block = jnp.asarray(span_full[span_own : 2 * span_own, :span_own], jnp.float32)
 
     bank = TableBank()
-    first_plan = plan_wall(bank, [("slope", 4), ("smooth", 5)], points, rows, 3)
-    second_plan = plan_wall(bank, [("slope", 5)], points, rows, 2)
+    first_plan = plan_wall(bank, [("slope", 4), ("smooth", 5)], points, rows, 3, (2, 0))
+    second_plan = plan_wall(bank, [("slope", 5)], points, rows, 2, (0,))
     bank.lookup(position)
 
     state = jnp.concatenate(
@@ -336,17 +356,20 @@
 
     wall_grad, smoothed = wall_apply(bank, first_plan, [basic_pad, padded], rows, 3)
 
-    basic = basic_pad[:, 3 : 3 + rows]
+    basic = basic_pad[:, 1 : rows + 5]
     speed = basic[:3]
-    push = push_pad[3 : 3 + rows]
+    push = push_pad[1 : rows + 5]
+    momentum = padded[1:4, 1 : rows + 5]
+    energy = padded[4, 1 : rows + 5]
     grad_stream = stream_slope(basic, stream_matrix)
     grad_span = span_slope(basic, own_block, other_block)
     gradients = [grad_stream, wall_grad, grad_span]
-    momentum = mass_flux_vector
-    energy = total_heat_content
-
     flux_wall = flux_along(1, momentum, energy, speed, push, gradients)
-    (wall_term,) = wall_apply(bank, second_plan, [halo(flux_wall, 2)], rows, 2)
+    (wall_term,) = wall_apply(bank, second_plan, [flux_wall], rows, 2)
+    own = slice(2, 2 + rows)
+    gradients = [[part[own] for part in grad] for grad in gradients]
+    speed, push = speed[:, own], push[own]
+    momentum, energy = mass_flux_vector, total_heat_content
     stream_term = stream_slope(
         flux_along(0, momentum, energy, speed, push, gradients), stream_matrix
     )

time: 206 us -> 195 us (0.947)
  the two profiles are of different devices: /device:TPU:30 before, /device:TPU:28 now
where the time goes in v7:
time: 195 us; the launch traced here: 194 us
  starting transfers between devices  85.3 us (44%)
  waiting for transfers between devices  67.9 us (35%)
  local copies, waits for them, and re-layouts  14.7 us (8%)
  other arithmetic  14.3 us (7%)
  matrix products  9.93 us (5%)
    ppermute x12, waiting for transfers between devices, wall_apply(): from_above = lax.ppermute(fall, 'gy', down_pairs)  59.4 us
    ppermute x12, starting transfers between devices, wall_apply(): from_below = lax.ppermute(rise, 'gy', up_pairs)  58.6 us
    ppermute x12, starting transfers between devices, wall_apply(): from_above = lax.ppermute(fall, 'gy', down_pairs)  20.7 us
    ppermute x12, waiting for transfers between devices, wall_apply(): from_below = lax.ppermute(rise, 'gy', up_pairs)  8.32 us
    add x2, other arithmetic, wall_apply(): local + rise_gain[None, :, None, None] * rise[first:first + size, None]  4.83 us
    dot_general x2, matrix products, span_slope(): jnp.einsum('fyzx,zw->fywx', other, other_block, precision=HIGHEST)  4.4 us
  transfers between devices with their start and end apart: 28, of which 16 were waited for; matrix products, arithmetic and copies ran while one was open for 13% of the time, Pallas kernels for 0%

profile of v7, /device:TPU:28, one launch (start us, length us, event | category | flops | bytes accessed | tf_op | source)
XLA Modules:
  0.0 193.7 jit_solution(5876680714707415147)
XLA Ops:
  3.0 3.1 %collective-permute-start = (f32[5,3,64,128]{3,2,1,0:T(8,128)}, f32[5,3,64,128]{3,2,1,0:T(8,128)S(1)}, u32[]{:S(2)}, u32[]{:S(2)}) collective-permute-start(f32[5,3,64,128]{3,2,1,0:T(8,128)} %get-tuple-element.119), channel_id=1, source_target_pairs={{0,2},{2,4},{4,6},{6,8},{8,10},{10,12},{12,14},{14,16},{16,18},{18... | collective-permute-start | bytes 1474568 | tf_op jit(solution)/shard_map/ppermute | solution.py:291
  6.1 2.7 %collective-permute-start.1 = (f32[5,3,64,128]{3,2,1,0:T(8,128)}, f32[5,3,64,128]{3,2,1,0:T(8,128)S(1)}, u32[]{:S(2)}, u32[]{:S(2)}) collective-permute-start(f32[5,3,64,128]{3,2,1,0:T(8,128)} %get-tuple-element.120), channel_id=1, source_target_pairs={{2,0},{4,2},{6,4},{8,6},{10,8},{12,10},{14,12},{16,14},{18,16},{20... | collective-permute-start | bytes 1474568 | tf_op jit(solution)/shard_map/ppermute | solution.py:292
  23.6 6.9 %collective-permute-start.2 = (f32[9,64,128]{2,1,0:T(8,128)S(1)}, f32[9,64,128]{2,1,0:T(8,128)S(1)}, u32[]{:S(2)}, u32[]{:S(2)}) collective-permute-start(f32[9,64,128]{2,1,0:T(8,128)S(1)} %pad_maximum_fusion.7), channel_id=1, source_target_pairs={{0,2},{2,4},{4,6},{6,8},{8,10},{10,12},{12,14},{14,16},{16,18},{18... | collective-permute-start | bytes 884744 | tf_op jit(solution)/shard_map/ppermute | solution.py:267
  35.7 10.0 %collective-permute-start.3 = (f32[9,64,128]{2,1,0:T(8,128)S(1)}, f32[9,64,128]{2,1,0:T(8,128)S(1)}, u32[]{:S(2)}, u32[]{:S(2)}) collective-permute-start(f32[9,64,128]{2,1,0:T(8,128)S(1)} %multiply_add_fusion.15), channel_id=1, source_target_pairs={{0,4},{2,6},{4,8},{6,10},{8,12},{10,14},{12,16},{14,18},{16,20},{1... | collective-permute-start | bytes 884744 | tf_op jit(solution)/shard_map/ppermute | solution.py:267
  47.8 5.3 %collective-permute-done.3 = f32[9,64,128]{2,1,0:T(8,128)S(1)} collective-permute-done((f32[9,64,128]{2,1,0:T(8,128)S(1)}, f32[9,64,128]{2,1,0:T(8,128)S(1)}, u32[]{:S(2)}, u32[]{:S(2)}) %collective-permute-start.3) | collective-permute-done | bytes 294944 | tf_op jit(solution)/shard_map/ppermute | solution.py:267
  53.2 2.7 %collective-permute-start.4 = (f32[9,64,128]{2,1,0:T(8,128)S(1)}, f32[9,64,128]{2,1,0:T(8,128)S(1)}, u32[]{:S(2)}, u32[]{:S(2)}) collective-permute-start(f32[9,64,128]{2,1,0:T(8,128)S(1)} %multiply_add_fusion.14), channel_id=1, source_target_pairs={{0,8},{2,10},{4,12},{6,14},{8,16},{10,18},{12,20},{14,22},{16,24},... | collective-permute-start | bytes 884744 | tf_op jit(solution)/shard_map/ppermute | solution.py:267
  55.9 3.3 %collective-permute-done.9 = f32[9,64,128]{2,1,0:T(8,128)S(1)} collective-permute-done((f32[9,64,128]{2,1,0:T(8,128)S(1)}, f32[9,64,128]{2,1,0:T(8,128)S(1)}, u32[]{:S(2)}, u32[]{:S(2)}) %collective-permute-start.9) | collective-permute-done | bytes 294944 | tf_op jit(solution)/shard_map/ppermute | solution.py:268
  62.0 2.6 %collective-permute-start.5 = (f32[9,64,128]{2,1,0:T(8,128)S(1)}, f32[9,64,128]{2,1,0:T(8,128)S(1)}, u32[]{:S(2)}, u32[]{:S(2)}) collective-permute-start(f32[9,64,128]{2,1,0:T(8,128)S(1)} %multiply_add_fusion.13), channel_id=1, source_target_pairs={{0,16},{2,18},{4,20},{6,22},{8,24},{10,26},{12,28},{14,30},{16,32}... | collective-permute-start | bytes 884744 | tf_op jit(solution)/shard_map/ppermute | solution.py:267
  64.6 14.4 %collective-permute-done.10 = f32[9,64,128]{2,1,0:T(8,128)S(1)} collective-permute-done((f32[9,64,128]{2,1,0:T(8,128)S(1)}, f32[9,64,128]{2,1,0:T(8,128)S(1)}, u32[]{:S(2)}, u32[]{:S(2)}) %collective-permute-start.10) | collective-permute-done | bytes 294944 | tf_op jit(solution)/shard_map/ppermute | solution.py:268
  81.3 3.7 %collective-permute-start.6 = (f32[9,64,128]{2,1,0:T(8,128)S(1)}, f32[9,64,128]{2,1,0:T(8,128)S(1)}, u32[]{:S(2)}, u32[]{:S(2)}) collective-permute-start(f32[9,64,128]{2,1,0:T(8,128)S(1)} %multiply_add_fusion.12), channel_id=1, source_target_pairs={{0,32},{2,34},{4,36},{6,38},{8,40},{10,42},{12,44},{14,46},{16,48}... | collective-permute-start | bytes 884744 | tf_op jit(solution)/shard_map/ppermute | solution.py:267
  85.0 5.3 %collective-permute-done.11 = f32[9,64,128]{2,1,0:T(8,128)S(1)} collective-permute-done((f32[9,64,128]{2,1,0:T(8,128)S(1)}, f32[9,64,128]{2,1,0:T(8,128)S(1)}, u32[]{:S(2)}, u32[]{:S(2)}) %collective-permute-start.11) | collective-permute-done | bytes 294944 | tf_op jit(solution)/shard_map/ppermute | solution.py:268
  91.9 6.4 %collective-permute-start.7 = (f32[9,64,128]{2,1,0:T(8,128)S(1)}, f32[9,64,128]{2,1,0:T(8,128)S(1)}, u32[]{:S(2)}, u32[]{:S(2)}) collective-permute-start(f32[9,64,128]{2,1,0:T(8,128)S(1)} %multiply_add_fusion.11), channel_id=1, source_target_pairs={{0,64},{2,66},{4,68},{6,70},{8,72},{10,74},{12,76},{14,78},{16,80}... | collective-permute-start | bytes 884744 | tf_op jit(solution)/shard_map/ppermute | solution.py:267
  105.3 5.2 %collective-permute-done.13 = f32[9,64,128]{2,1,0:T(8,128)S(1)} collective-permute-done((f32[9,64,128]{2,1,0:T(8,128)S(1)}, f32[9,64,128]{2,1,0:T(8,128)S(1)}, u32[]{:S(2)}, u32[]{:S(2)}) %collective-permute-start.13) | collective-permute-done | bytes 294944 | tf_op jit(solution)/shard_map/ppermute | solution.py:268
  114.4 5.2 %collective-permute-start.15 = (f32[5,64,128]{2,1,0:T(8,128)S(1)}, f32[5,64,128]{2,1,0:T(8,128)S(1)}, u32[]{:S(2)}, u32[]{:S(2)}) collective-permute-start(f32[5,64,128]{2,1,0:T(8,128)S(1)} %get-tuple-element.131), channel_id=1, source_target_pairs={{0,2},{2,4},{4,6},{6,8},{8,10},{10,12},{12,14},{14,16},{16,18},{18... | collective-permute-start | bytes 491528 | tf_op jit(solution)/shard_map/ppermute | solution.py:267
  123.5 2.8 %multiply_add_fusion.1 = f32[5,8,64,128]{3,2,1,0:T(8,128)} fusion(f32[5,64,128]{2,1,0:T(8,128)S(1)} %slice-done.1, f32[8]{0:T(128)S(1)} %get-tuple-element.140, f32[5,64,128]{2,1,0:T(8,128)S(1)} %slice-done, f32[8]{0:T(128)S(1)} %get-tuple-element.137, f32[5,64,128]{2,1,0:T(8,128)S(1)} %get-tuple-element.127, f32[8]{0:T(128)S(1)} %get-tuple-element.5, ...), kind=kLoop, calls=%fused_computation.43 | loop fusion | flops 10158080 | bytes 3932672 | tf_op jit(solution)/shard_map/add | solution.py:279
  127.7 7.2 %collective-permute-start.16 = (f32[5,64,128]{2,1,0:T(8,128)S(1)}, f32[5,64,128]{2,1,0:T(8,128)S(1)}, u32[]{:S(2)}, u32[]{:S(2)}) collective-permute-start(f32[5,64,128]{2,1,0:T(8,128)S(1)} %get-tuple-element.129), channel_id=1, source_target_pairs={{0,4},{2,6},{4,8},{6,10},{8,12},{10,14},{12,16},{14,18},{16,20},{1... | collective-permute-start | bytes 491528 | tf_op jit(solution)/shard_map/ppermute | solution.py:267
  138.8 3.2 %collective-permute-start.17 = (f32[5,64,128]{2,1,0:T(8,128)S(1)}, f32[5,64,128]{2,1,0:T(8,128)S(1)}, u32[]{:S(2)}, u32[]{:S(2)}) collective-permute-start(f32[5,64,128]{2,1,0:T(8,128)S(1)} %multiply_add_fusion.27), channel_id=1, source_target_pairs={{0,8},{2,10},{4,12},{6,14},{8,16},{10,18},{12,20},{14,22},{16,24},... | collective-permute-start | bytes 491528 | tf_op jit(solution)/shard_map/ppermute | solution.py:267
  142.1 6.9 %collective-permute-done.22 = f32[5,64,128]{2,1,0:T(8,128)S(1)} collective-permute-done((f32[5,64,128]{2,1,0:T(8,128)S(1)}, f32[5,64,128]{2,1,0:T(8,128)S(1)}, u32[]{:S(2)}, u32[]{:S(2)}) %collective-permute-start.22) | collective-permute-done | bytes 163872 | tf_op jit(solution)/shard_map/ppermute | solution.py:268
  153.0 9.1 %collective-permute-done.23 = f32[5,64,128]{2,1,0:T(8,128)S(1)} collective-permute-done((f32[5,64,128]{2,1,0:T(8,128)S(1)}, f32[5,64,128]{2,1,0:T(8,128)S(1)}, u32[]{:S(2)}, u32[]{:S(2)}) %collective-permute-start.23) | collective-permute-done | bytes 163872 | tf_op jit(solution)/shard_map/ppermute | solution.py:268
  164.1 2.6 %collective-permute-start.19 = (f32[5,64,128]{2,1,0:T(8,128)S(1)}, f32[5,64,128]{2,1,0:T(8,128)S(1)}, u32[]{:S(2)}, u32[]{:S(2)}) collective-permute-start(f32[5,64,128]{2,1,0:T(8,128)S(1)} %multiply_add_fusion.25), channel_id=1, source_target_pairs={{0,32},{2,34},{4,36},{6,38},{8,40},{10,42},{12,44},{14,46},{16,48}... | collective-permute-start | bytes 491528 | tf_op jit(solution)/shard_map/ppermute | solution.py:267
  166.8 4.9 %collective-permute-done.24 = f32[5,64,128]{2,1,0:T(8,128)S(1)} collective-permute-done((f32[5,64,128]{2,1,0:T(8,128)S(1)}, f32[5,64,128]{2,1,0:T(8,128)S(1)}, u32[]{:S(2)}, u32[]{:S(2)}) %collective-permute-start.24) | collective-permute-done | bytes 163872 | tf_op jit(solution)/shard_map/ppermute | solution.py:268
  173.2 6.1 %collective-permute-start.20 = (f32[5,64,128]{2,1,0:T(8,128)S(1)}, f32[5,64,128]{2,1,0:T(8,128)S(1)}, u32[]{:S(2)}, u32[]{:S(2)}) collective-permute-start(f32[5,64,128]{2,1,0:T(8,128)S(1)} %multiply_add_fusion.24), channel_id=1, source_target_pairs={{0,64},{2,66},{4,68},{6,70},{8,72},{10,74},{12,76},{14,78},{16,80}... | collective-permute-start | bytes 491528 | tf_op jit(solution)/shard_map/ppermute | solution.py:267
  182.3 7.1 %collective-permute-done.26 = f32[5,64,128]{2,1,0:T(8,128)S(1)} collective-permute-done((f32[5,64,128]{2,1,0:T(8,128)S(1)}, f32[5,64,128]{2,1,0:T(8,128)S(1)}, u32[]{:S(2)}, u32[]{:S(2)}) %collective-permute-start.26) | collective-permute-done | bytes 163872 | tf_op jit(solution)/shard_map/ppermute | solution.py:268
  189.4 2.8 %fusion.4 = f32[5,8,64,128]{3,2,1,0:T(8,128)S(1)} fusion(f32[5,8,128,64]{2,3,1,0:T(8,128)S(1)} %fusion.90, f32[5,8,64,128]{3,2,1,0:T(8,128)S(1)} %collective-permute-done.27, f32[64,64,1,1]{0,1,3,2:T(8,128)S(1)} %copy-done.8, f32[5,8,64,128]{3,2,1,0:T(8,128)S(1)} %fusion.89, f32[5,64,128]{2,1,0:T(8,128)S(1)} %multiply_add_fusion.17, ...), kind=kOutput, calls=%fused_computation.39 | convolution fusion | flops 261816320 | bytes 7553472 | tf_op jit(solution)/shard_map/fyzx,zw->fywx/dot_general | solution.py:305
  (163 shorter events, 62.5 us)
Async XLA Ops:
  3.0 17.7 %collective-permute-start = (f32[5,3,64,128]{3,2,1,0:T(8,128)}, f32[5,3,64,128]{3,2,1,0:T(8,128)S(1)}, u32[]{:S(2)}, u32[]{:S(2)}) collective-permute-start(f32[5,3,64,128]{3,2,1,0:T(8,128)} %get-tuple-element.119), channel_id=1, source_target_pairs={{0,2},{2,4},{4,6},{6,8},{8,10},{10,12},{12,14},{14,16},{16,18},{18... | collective-permute-start | bytes 1474568 | tf_op jit(solution)/shard_map/ppermute | solution.py:291
  6.1 14.8 %collective-permute-start.1 = (f32[5,3,64,128]{3,2,1,0:T(8,128)}, f32[5,3,64,128]{3,2,1,0:T(8,128)S(1)}, u32[]{:S(2)}, u32[]{:S(2)}) collective-permute-start(f32[5,3,64,128]{3,2,1,0:T(8,128)} %get-tuple-element.120), channel_id=1, source_target_pairs={{2,0},{4,2},{6,4},{8,6},{10,8},{12,10},{14,12},{16,14},{18,16},{20... | collective-permute-start | bytes 1474568 | tf_op jit(solution)/shard_map/ppermute | solution.py:292
  23.6 11.9 %collective-permute-start.2 = (f32[9,64,128]{2,1,0:T(8,128)S(1)}, f32[9,64,128]{2,1,0:T(8,128)S(1)}, u32[]{:S(2)}, u32[]{:S(2)}) collective-permute-start(f32[9,64,128]{2,1,0:T(8,128)S(1)} %pad_maximum_fusion.7), channel_id=1, source_target_pairs={{0,2},{2,4},{4,6},{6,8},{8,10},{10,12},{12,14},{14,16},{16,18},{18... | collective-permute-start | bytes 884744 | tf_op jit(solution)/shard_map/ppermute | solution.py:267
  30.5 15.2 %collective-permute-start.8 = (f32[9,64,128]{2,1,0:T(8,128)S(1)}, f32[9,64,128]{2,1,0:T(8,128)S(1)}, u32[]{:S(2)}, u32[]{:S(2)}) collective-permute-start(f32[9,64,128]{2,1,0:T(8,128)S(1)} %pad_maximum_fusion.8), channel_id=1, source_target_pairs={{2,0},{4,2},{6,4},{8,6},{10,8},{12,10},{14,12},{16,14},{18,16},{20... | collective-permute-start | bytes 884744 | tf_op jit(solution)/shard_map/ppermute | solution.py:268
  32.5 69.4 %collective-permute-start.14 = (f32[4,12,64,128]{3,2,1,0:T(8,128)S(1)}, f32[4,12,64,128]{3,2,1,0:T(8,128)S(1)}, u32[]{:S(2)}, u32[]{:S(2)}) collective-permute-start(f32[4,12,64,128]{3,2,1,0:T(8,128)S(1)} %fusion.1), channel_id=1, source_target_pairs={{0,1},{1,0},{2,3},{3,2},{4,5},{5,4},{6,7},{7,6},{8,9},{9,8},{10,11... | collective-permute-start | bytes 4718600 | tf_op jit(solution)/shard_map/ppermute | solution.py:304
  35.7 17.5 %collective-permute-start.3 = (f32[9,64,128]{2,1,0:T(8,128)S(1)}, f32[9,64,128]{2,1,0:T(8,128)S(1)}, u32[]{:S(2)}, u32[]{:S(2)}) collective-permute-start(f32[9,64,128]{2,1,0:T(8,128)S(1)} %multiply_add_fusion.15), channel_id=1, source_target_pairs={{0,4},{2,6},{4,8},{6,10},{8,12},{10,14},{12,16},{14,18},{16,20},{1... | collective-permute-start | bytes 884744 | tf_op jit(solution)/shard_map/ppermute | solution.py:267
  45.8 13.4 %collective-permute-start.9 = (f32[9,64,128]{2,1,0:T(8,128)S(1)}, f32[9,64,128]{2,1,0:T(8,128)S(1)}, u32[]{:S(2)}, u32[]{:S(2)}) collective-permute-start(f32[9,64,128]{2,1,0:T(8,128)S(1)} %multiply_add_fusion.9), channel_id=1, source_target_pairs={{4,0},{6,2},{8,4},{10,6},{12,8},{14,10},{16,12},{18,14},{20,16},{2... | collective-permute-start | bytes 884744 | tf_op jit(solution)/shard_map/ppermute | solution.py:268
  59.3 19.8 %collective-permute-start.10 = (f32[9,64,128]{2,1,0:T(8,128)S(1)}, f32[9,64,128]{2,1,0:T(8,128)S(1)}, u32[]{:S(2)}, u32[]{:S(2)}) collective-permute-start(f32[9,64,128]{2,1,0:T(8,128)S(1)} %multiply_add_fusion.8), channel_id=1, source_target_pairs={{8,0},{10,2},{12,4},{14,6},{16,8},{18,10},{20,12},{22,14},{24,16},... | collective-permute-start | bytes 884744 | tf_op jit(solution)/shard_map/ppermute | solution.py:268
  62.0 19.2 %collective-permute-start.5 = (f32[9,64,128]{2,1,0:T(8,128)S(1)}, f32[9,64,128]{2,1,0:T(8,128)S(1)}, u32[]{:S(2)}, u32[]{:S(2)}) collective-permute-start(f32[9,64,128]{2,1,0:T(8,128)S(1)} %multiply_add_fusion.13), channel_id=1, source_target_pairs={{0,16},{2,18},{4,20},{6,22},{8,24},{10,26},{12,28},{14,30},{16,32}... | collective-permute-start | bytes 884744 | tf_op jit(solution)/shard_map/ppermute | solution.py:267
  79.2 11.1 %collective-permute-start.11 = (f32[9,64,128]{2,1,0:T(8,128)S(1)}, f32[9,64,128]{2,1,0:T(8,128)S(1)}, u32[]{:S(2)}, u32[]{:S(2)}) collective-permute-start(f32[9,64,128]{2,1,0:T(8,128)S(1)} %multiply_add_fusion.7), channel_id=1, source_target_pairs={{16,0},{18,2},{20,4},{22,6},{24,8},{26,10},{28,12},{30,14},{32,16}... | collective-permute-start | bytes 884744 | tf_op jit(solution)/shard_map/ppermute | solution.py:268
  81.3 10.5 %collective-permute-start.6 = (f32[9,64,128]{2,1,0:T(8,128)S(1)}, f32[9,64,128]{2,1,0:T(8,128)S(1)}, u32[]{:S(2)}, u32[]{:S(2)}) collective-permute-start(f32[9,64,128]{2,1,0:T(8,128)S(1)} %multiply_add_fusion.12), channel_id=1, source_target_pairs={{0,32},{2,34},{4,36},{6,38},{8,40},{10,42},{12,44},{14,46},{16,48}... | collective-permute-start | bytes 884744 | tf_op jit(solution)/shard_map/ppermute | solution.py:267
  90.4 9.9 %collective-permute-start.12 = (f32[9,64,128]{2,1,0:T(8,128)S(1)}, f32[9,64,128]{2,1,0:T(8,128)S(1)}, u32[]{:S(2)}, u32[]{:S(2)}) collective-permute-start(f32[9,64,128]{2,1,0:T(8,128)S(1)} %multiply_add_fusion.6), channel_id=1, source_target_pairs={{32,0},{34,2},{36,4},{38,6},{40,8},{42,10},{44,12},{46,14},{48,16}... | collective-permute-start | bytes 884744 | tf_op jit(solution)/shard_map/ppermute | solution.py:268
  91.9 13.3 %collective-permute-start.7 = (f32[9,64,128]{2,1,0:T(8,128)S(1)}, f32[9,64,128]{2,1,0:T(8,128)S(1)}, u32[]{:S(2)}, u32[]{:S(2)}) collective-permute-start(f32[9,64,128]{2,1,0:T(8,128)S(1)} %multiply_add_fusion.11), channel_id=1, source_target_pairs={{0,64},{2,66},{4,68},{6,70},{8,72},{10,74},{12,76},{14,78},{16,80}... | collective-permute-start | bytes 884744 | tf_op jit(solution)/shard_map/ppermute | solution.py:267
  100.4 10.1 %collective-permute-start.13 = (f32[9,64,128]{2,1,0:T(8,128)S(1)}, f32[9,64,128]{2,1,0:T(8,128)S(1)}, u32[]{:S(2)}, u32[]{:S(2)}) collective-permute-start(f32[9,64,128]{2,1,0:T(8,128)S(1)} %multiply_add_fusion.5), channel_id=1, source_target_pairs={{64,0},{66,2},{68,4},{70,6},{72,8},{74,10},{76,12},{78,14},{80,16}... | collective-permute-start | bytes 884744 | tf_op jit(solution)/shard_map/ppermute | solution.py:268
  114.4 13.2 %collective-permute-start.15 = (f32[5,64,128]{2,1,0:T(8,128)S(1)}, f32[5,64,128]{2,1,0:T(8,128)S(1)}, u32[]{:S(2)}, u32[]{:S(2)}) collective-permute-start(f32[5,64,128]{2,1,0:T(8,128)S(1)} %get-tuple-element.131), channel_id=1, source_target_pairs={{0,2},{2,4},{4,6},{6,8},{8,10},{10,12},{12,14},{14,16},{16,18},{18... | collective-permute-start | bytes 491528 | tf_op jit(solution)/shard_map/ppermute | solution.py:267
  122.4 67.0 %collective-permute-start.27 = (f32[5,8,64,128]{3,2,1,0:T(8,128)S(1)}, f32[5,8,64,128]{3,2,1,0:T(8,128)S(1)}, u32[]{:S(2)}, u32[]{:S(2)}) collective-permute-start(f32[5,8,64,128]{3,2,1,0:T(8,128)S(1)} %fusion.34), channel_id=1, source_target_pairs={{0,1},{1,0},{2,3},{3,2},{4,5},{5,4},{6,7},{7,6},{8,9},{9,8},{10,11... | collective-permute-start | bytes 3932168 | tf_op jit(solution)/shard_map/ppermute | solution.py:304
  127.7 11.1 %collective-permute-start.16 = (f32[5,64,128]{2,1,0:T(8,128)S(1)}, f32[5,64,128]{2,1,0:T(8,128)S(1)}, u32[]{:S(2)}, u32[]{:S(2)}) collective-permute-start(f32[5,64,128]{2,1,0:T(8,128)S(1)} %get-tuple-element.129), channel_id=1, source_target_pairs={{0,4},{2,6},{4,8},{6,10},{8,12},{10,14},{12,16},{14,18},{16,20},{1... | collective-permute-start | bytes 491528 | tf_op jit(solution)/shard_map/ppermute | solution.py:267
  136.2 12.7 %collective-permute-start.22 = (f32[5,64,128]{2,1,0:T(8,128)S(1)}, f32[5,64,128]{2,1,0:T(8,128)S(1)}, u32[]{:S(2)}, u32[]{:S(2)}) collective-permute-start(f32[5,64,128]{2,1,0:T(8,128)S(1)} %get-tuple-element.130), channel_id=1, source_target_pairs={{4,0},{6,2},{8,4},{10,6},{12,8},{14,10},{16,12},{18,14},{20,16},{2... | collective-permute-start | bytes 491528 | tf_op jit(solution)/shard_map/ppermute | solution.py:268
  138.8 12.1 %collective-permute-start.17 = (f32[5,64,128]{2,1,0:T(8,128)S(1)}, f32[5,64,128]{2,1,0:T(8,128)S(1)}, u32[]{:S(2)}, u32[]{:S(2)}) collective-permute-start(f32[5,64,128]{2,1,0:T(8,128)S(1)} %multiply_add_fusion.27), channel_id=1, source_target_pairs={{0,8},{2,10},{4,12},{6,14},{8,16},{10,18},{12,20},{14,22},{16,24},... | collective-permute-start | bytes 491528 | tf_op jit(solution)/shard_map/ppermute | solution.py:267
  149.0 13.0 %collective-permute-start.23 = (f32[5,64,128]{2,1,0:T(8,128)S(1)}, f32[5,64,128]{2,1,0:T(8,128)S(1)}, u32[]{:S(2)}, u32[]{:S(2)}) collective-permute-start(f32[5,64,128]{2,1,0:T(8,128)S(1)} %multiply_add_fusion.21), channel_id=1, source_target_pairs={{8,0},{10,2},{12,4},{14,6},{16,8},{18,10},{20,12},{22,14},{24,16},... | collective-permute-start | bytes 491528 | tf_op jit(solution)/shard_map/ppermute | solution.py:268
  151.0 13.0 %collective-permute-start.18 = (f32[5,64,128]{2,1,0:T(8,128)S(1)}, f32[5,64,128]{2,1,0:T(8,128)S(1)}, u32[]{:S(2)}, u32[]{:S(2)}) collective-permute-start(f32[5,64,128]{2,1,0:T(8,128)S(1)} %multiply_add_fusion.26), channel_id=1, source_target_pairs={{0,16},{2,18},{4,20},{6,22},{8,24},{10,26},{12,28},{14,30},{16,32}... | collective-permute-start | bytes 491528 | tf_op jit(solution)/shard_map/ppermute | solution.py:267
  162.1 9.6 %collective-permute-start.24 = (f32[5,64,128]{2,1,0:T(8,128)S(1)}, f32[5,64,128]{2,1,0:T(8,128)S(1)}, u32[]{:S(2)}, u32[]{:S(2)}) collective-permute-start(f32[5,64,128]{2,1,0:T(8,128)S(1)} %multiply_add_fusion.20), channel_id=1, source_target_pairs={{16,0},{18,2},{20,4},{22,6},{24,8},{26,10},{28,12},{30,14},{32,16}... | collective-permute-start | bytes 491528 | tf_op jit(solution)/shard_map/ppermute | solution.py:268
  164.1 9.0 %collective-permute-start.19 = (f32[5,64,128]{2,1,0:T(8,128)S(1)}, f32[5,64,128]{2,1,0:T(8,128)S(1)}, u32[]{:S(2)}, u32[]{:S(2)}) collective-permute-start(f32[5,64,128]{2,1,0:T(8,128)S(1)} %multiply_add_fusion.25), channel_id=1, source_target_pairs={{0,32},{2,34},{4,36},{6,38},{8,40},{10,42},{12,44},{14,46},{16,48}... | collective-permute-start | bytes 491528 | tf_op jit(solution)/shard_map/ppermute | solution.py:267
  173.2 9.0 %collective-permute-start.20 = (f32[5,64,128]{2,1,0:T(8,128)S(1)}, f32[5,64,128]{2,1,0:T(8,128)S(1)}, u32[]{:S(2)}, u32[]{:S(2)}) collective-permute-start(f32[5,64,128]{2,1,0:T(8,128)S(1)} %multiply_add_fusion.24), channel_id=1, source_target_pairs={{0,64},{2,66},{4,68},{6,70},{8,72},{10,74},{12,76},{14,78},{16,80}... | collective-permute-start | bytes 491528 | tf_op jit(solution)/shard_map/ppermute | solution.py:267
  (15 other events, 92.3 us)

commit v8 on v7

--- a/solution.py
+++ b/solution.py
@@ -168,6 +168,32 @@
         rows_stencil = stencil[own, window]
         combine[block, outputs] = rise_part @ rows_stencil
         combine[block, outputs + 1] = fall_part @ rows_stencil
+    rise_rows = combine[:, outputs].copy()
+    fall_rows = combine[:, outputs + 1].copy()
+    bottom = slice(pad, 2 * pad)
+    top = slice(rows, rows + pad)
+    below, above = slice(0, pad), slice(rows + pad, rows + 2 * pad)
+    for block in range(blocks):
+        rise_own = np.zeros(rows + 2 * pad)
+        fall_own = np.zeros(rows + 2 * pad)
+        rise_own[pad : pad + rows] = rise_rows[block, pad : pad + rows]
+        fall_own[pad : pad + rows] = fall_rows[block, pad : pad + rows]
+        rise_left = np.zeros(rows + 2 * pad)
+        fall_left = np.zeros(rows + 2 * pad)
+        if block + 1 < blocks:
+            rise_own[top] += rise_rows[block + 1, below] / rise_step[block + 1]
+            rise_left[top] -= rise_rows[block + 1, below] / rise_step[block + 1]
+            fall_own[top] += fall_step[block] * fall_rows[block + 1, below]
+        if block > 0:
+            rise_own[bottom] += rise_step[block] * rise_rows[block - 1, above]
+            fall_own[bottom] += fall_rows[block - 1, above] / fall_step[block - 1]
+            fall_left[bottom] -= fall_rows[block - 1, above] / fall_step[block - 1]
+        rise_left[above] += rise_rows[block, above]
+        fall_left[below] += fall_rows[block, below]
+        combine[block, :outputs] += np.outer(rise_gain[block], rise_left)
+        combine[block, :outputs] += np.outer(fall_gain[block], fall_left)
+        combine[block, outputs] = rise_own
+        combine[block, outputs + 1] = fall_own
     return combine, rise_gain, fall_gain, rise_step, fall_step
 
 
@@ -241,20 +267,20 @@
     return groups, rounds
 
 
-def wall_apply(bank, plan, padded_groups, rows, pad):
+def wall_apply(bank, plan, padded_groups, own_groups, rows, pad):
     count = lax.axis_size("gy")
     groups, rounds = plan
 
     def taps(padded, combine):
         summed = None
-        for tap in range(rows + 2 * pad):
+        for tap in range(combine.shape[1]):
             term = combine[:, tap, None, None] * padded[:, None, tap]
             summed = term if summed is None else summed + term
         return summed
 
     partials = [
-        taps(padded, bank.get(handles[0])[handles[3] :])
-        for padded, handles in zip(padded_groups, groups)
+        taps(own, bank.get(handles[0])[handles[3] :, pad : pad + rows])
+        for own, handles in zip(own_groups, groups)
     ]
     sizes = [padded.shape[0] for padded in padded_groups]
     rise = jnp.concatenate([part[:, 0] for part in partials], axis=0)
@@ -354,7 +380,13 @@
     warmth_pad = push_pad / density
     basic_pad = jnp.concatenate([speed_pad, warmth_pad[None]], axis=0)
 
-    wall_grad, smoothed = wall_apply(bank, first_plan, [basic_pad, padded], rows, 3)
+    speed_own = mass_flux_vector / mass_per_volume[None]
+    kinetic_own = 0.5 * jnp.sum(speed_own * mass_flux_vector, axis=0)
+    push_own = (GAMMA_GAS - 1.0) * (total_heat_content - kinetic_own)
+    basic_own = jnp.concatenate([speed_own, (push_own / mass_per_volume)[None]], axis=0)
+    wall_grad, smoothed = wall_apply(
+        bank, first_plan, [basic_pad, padded], [basic_own, state], rows, 3
+    )
 
     basic = basic_pad[:, 1 : rows + 5]
     speed = basic[:3]
@@ -365,7 +397,7 @@
     grad_span = span_slope(basic, own_block, other_block)
     gradients = [grad_stream, wall_grad, grad_span]
     flux_wall = flux_along(1, momentum, energy, speed, push, gradients)
-    (wall_term,) = wall_apply(bank, second_plan, [flux_wall], rows, 2)
+    (wall_term,) = wall_apply(bank, second_plan, [flux_wall], [flux_wall[:, 2 : 2 + rows]], rows, 2)
     own = slice(2, 2 + rows)
     gradients = [[part[own] for part in grad] for grad in gradients]
     speed, push = speed[:, own], push[own]

time: 195 us -> 211 us (1.082)
  the two profiles are of different devices: /device:TPU:28 before, /device:TPU:30 now
where the time goes in v8:
time: 211 us; the launch traced here: 208 us
  starting transfers between devices  85.1 us (40%)
  waiting for transfers between devices  61.7 us (29%)
  local copies, waits for them, and re-layouts  29.5 us (14%)
  other arithmetic  19.4 us (9%)
  matrix products  9.98 us (5%)
  between operations  2.37 us (1%)
    ppermute x12, starting transfers between devices, wall_apply(): from_below = lax.ppermute(rise, 'gy', up_pairs)  47.7 us
    ppermute x12, waiting for transfers between devices, wall_apply(): from_above = lax.ppermute(fall, 'gy', down_pairs)  47.2 us
    ppermute x12, starting transfers between devices, wall_apply(): from_above = lax.ppermute(fall, 'gy', down_pairs)  27.6 us
    ppermute x12, waiting for transfers between devices, wall_apply(): from_below = lax.ppermute(rise, 'gy', up_pairs)  14.5 us
    unnamed x198, local copies, waits for them, and re-layouts  14.3 us
    ppermute x1, starting transfers between devices, halo(): below = lax.ppermute(block[:, block.shape[1] - width:], 'gy', up_pairs)  7.75 us
    add x2, other arithmetic, wall_apply(): local + rise_gain[None, :, None, None] * rise[first:first + size, None]  4.88 us
    dot_general x2, matrix products, span_slope(): jnp.einsum('fyzx,zw->fywx', other, other_block, precision=HIGHEST)  4.47 us
  transfers between devices with their start and end apart: 28, of which 16 were waited for; matrix products, arithmetic and copies ran while one was open for 18% of the time, Pallas kernels for 0%

profile of v8, /device:TPU:30, one launch (start us, length us, event | category | flops | bytes accessed | tf_op | source)
XLA Modules:
  0.0 208.1 jit_solution(1396992130991810835)
XLA Ops:
  11.0 3.4 %collective-permute-start.2 = (f32[9,64,128]{2,1,0:T(8,128)}, f32[9,64,128]{2,1,0:T(8,128)}, u32[]{:S(2)}, u32[]{:S(2)}) collective-permute-start(f32[9,64,128]{2,1,0:T(8,128)} %pad_maximum_fusion.7), channel_id=1, source_target_pairs={{0,2},{2,4},{4,6},{6,8},{8,10},{10,12},{12,14},{14,16},{16,18},{18... | collective-permute-start | bytes 884744 | tf_op jit(solution)/shard_map/ppermute | solution.py:293
  18.6 7.7 %collective-permute-start = (f32[5,3,64,128]{3,2,1,0:T(8,128)}, f32[5,3,64,128]{3,2,1,0:T(8,128)S(1)}, u32[]{:S(2)}, u32[]{:S(2)}) collective-permute-start(f32[5,3,64,128]{3,2,1,0:T(8,128)} %get-tuple-element.85), channel_id=1, source_target_pairs={{0,2},{2,4},{4,6},{6,8},{8,10},{10,12},{12,14},{14,16},{16,18},{18... | collective-permute-start | bytes 1474568 | tf_op jit(solution)/shard_map/ppermute | solution.py:317
  49.1 3.4 %collective-permute-start.3 = (f32[9,64,128]{2,1,0:T(8,128)S(1)}, f32[9,64,128]{2,1,0:T(8,128)S(1)}, u32[]{:S(2)}, u32[]{:S(2)}) collective-permute-start(f32[9,64,128]{2,1,0:T(8,128)S(1)} %multiply_add_fusion.15), channel_id=1, source_target_pairs={{0,4},{2,6},{4,8},{6,10},{8,12},{10,14},{12,16},{14,18},{16,20},{1... | collective-permute-start | bytes 884744 | tf_op jit(solution)/shard_map/ppermute | solution.py:293
  53.6 4.0 %collective-permute-start.9 = (f32[9,64,128]{2,1,0:T(8,128)S(1)}, f32[9,64,128]{2,1,0:T(8,128)S(1)}, u32[]{:S(2)}, u32[]{:S(2)}) collective-permute-start(f32[9,64,128]{2,1,0:T(8,128)S(1)} %multiply_add_fusion.9), channel_id=1, source_target_pairs={{4,0},{6,2},{8,4},{10,6},{12,8},{14,10},{16,12},{18,14},{20,16},{2... | collective-permute-start | bytes 884744 | tf_op jit(solution)/shard_map/ppermute | solution.py:294
  64.5 3.1 %collective-permute-done.9 = f32[9,64,128]{2,1,0:T(8,128)S(1)} collective-permute-done((f32[9,64,128]{2,1,0:T(8,128)S(1)}, f32[9,64,128]{2,1,0:T(8,128)S(1)}, u32[]{:S(2)}, u32[]{:S(2)}) %collective-permute-start.9) | collective-permute-done | bytes 294944 | tf_op jit(solution)/shard_map/ppermute | solution.py:294
  67.7 2.5 %collective-permute-start.10 = (f32[9,64,128]{2,1,0:T(8,128)S(1)}, f32[9,64,128]{2,1,0:T(8,128)S(1)}, u32[]{:S(2)}, u32[]{:S(2)}) collective-permute-start(f32[9,64,128]{2,1,0:T(8,128)S(1)} %multiply_add_fusion.8), channel_id=1, source_target_pairs={{8,0},{10,2},{12,4},{14,6},{16,8},{18,10},{20,12},{22,14},{24,16},... | collective-permute-start | bytes 884744 | tf_op jit(solution)/shard_map/ppermute | solution.py:294
  75.2 3.3 %collective-permute-done.10 = f32[9,64,128]{2,1,0:T(8,128)S(1)} collective-permute-done((f32[9,64,128]{2,1,0:T(8,128)S(1)}, f32[9,64,128]{2,1,0:T(8,128)S(1)}, u32[]{:S(2)}, u32[]{:S(2)}) %collective-permute-start.10) | collective-permute-done | bytes 294944 | tf_op jit(solution)/shard_map/ppermute | solution.py:294
  80.5 3.0 %collective-permute-done.5 = f32[9,64,128]{2,1,0:T(8,128)S(1)} collective-permute-done((f32[9,64,128]{2,1,0:T(8,128)S(1)}, f32[9,64,128]{2,1,0:T(8,128)S(1)}, u32[]{:S(2)}, u32[]{:S(2)}) %collective-permute-start.5) | collective-permute-done | bytes 294944 | tf_op jit(solution)/shard_map/ppermute | solution.py:293
  83.6 10.4 %collective-permute-start.6 = (f32[9,64,128]{2,1,0:T(8,128)S(1)}, f32[9,64,128]{2,1,0:T(8,128)S(1)}, u32[]{:S(2)}, u32[]{:S(2)}) collective-permute-start(f32[9,64,128]{2,1,0:T(8,128)S(1)} %multiply_add_fusion.12), channel_id=1, source_target_pairs={{0,32},{2,34},{4,36},{6,38},{8,40},{10,42},{12,44},{14,46},{16,48}... | collective-permute-start | bytes 884744 | tf_op jit(solution)/shard_map/ppermute | solution.py:293
  95.5 5.4 %collective-permute-done.6 = f32[9,64,128]{2,1,0:T(8,128)S(1)} collective-permute-done((f32[9,64,128]{2,1,0:T(8,128)S(1)}, f32[9,64,128]{2,1,0:T(8,128)S(1)}, u32[]{:S(2)}, u32[]{:S(2)}) %collective-permute-start.6) | collective-permute-done | bytes 294944 | tf_op jit(solution)/shard_map/ppermute | solution.py:293
  100.9 6.6 %collective-permute-start.7 = (f32[9,64,128]{2,1,0:T(8,128)S(1)}, f32[9,64,128]{2,1,0:T(8,128)S(1)}, u32[]{:S(2)}, u32[]{:S(2)}) collective-permute-start(f32[9,64,128]{2,1,0:T(8,128)S(1)} %multiply_add_fusion.11), channel_id=1, source_target_pairs={{0,64},{2,66},{4,68},{6,70},{8,72},{10,74},{12,76},{14,78},{16,80}... | collective-permute-start | bytes 884744 | tf_op jit(solution)/shard_map/ppermute | solution.py:293
  111.9 6.0 %collective-permute-done.13 = f32[9,64,128]{2,1,0:T(8,128)S(1)} collective-permute-done((f32[9,64,128]{2,1,0:T(8,128)S(1)}, f32[9,64,128]{2,1,0:T(8,128)S(1)}, u32[]{:S(2)}, u32[]{:S(2)}) %collective-permute-start.13) | collective-permute-done | bytes 294944 | tf_op jit(solution)/shard_map/ppermute | solution.py:294
  121.8 2.9 %multiply_add_fusion.1 = f32[5,8,64,128]{3,2,1,0:T(8,128)} fusion(f32[5,64,128]{2,1,0:T(8,128)S(1)} %slice-done.1, f32[8]{0:T(128)S(1)} %copy-done.67, f32[5,64,128]{2,1,0:T(8,128)S(1)} %slice-done, f32[8]{0:T(128)S(1)} %copy-done.66, f32[5,64,128]{2,1,0:T(8,128)S(1)} %get-tuple-element.103, f32[8]{0:T(128)S(1)} %copy-done.53, ...), kind=kLoop, calls=%fused_computation.57 | loop fusion | flops 10158080 | bytes 3932672 | tf_op jit(solution)/shard_map/add | solution.py:305
  129.3 8.8 %collective-permute-start.15 = (f32[5,64,128]{2,1,0:T(8,128)S(1)}, f32[5,64,128]{2,1,0:T(8,128)S(1)}, u32[]{:S(2)}, u32[]{:S(2)}) collective-permute-start(f32[5,64,128]{2,1,0:T(8,128)S(1)} %get-tuple-element.107), channel_id=1, source_target_pairs={{0,2},{2,4},{4,6},{6,8},{8,10},{10,12},{12,14},{14,16},{16,18},{18... | collective-permute-start | bytes 491528 | tf_op jit(solution)/shard_map/ppermute | solution.py:293
  143.4 6.2 %collective-permute-done.21 = f32[5,64,128]{2,1,0:T(8,128)S(1)} collective-permute-done((f32[5,64,128]{2,1,0:T(8,128)S(1)}, f32[5,64,128]{2,1,0:T(8,128)S(1)}, u32[]{:S(2)}, u32[]{:S(2)}) %collective-permute-start.21) | collective-permute-done | bytes 163872 | tf_op jit(solution)/shard_map/ppermute | solution.py:294
  153.1 5.4 %collective-permute-start.22 = (f32[5,64,128]{2,1,0:T(8,128)S(1)}, f32[5,64,128]{2,1,0:T(8,128)S(1)}, u32[]{:S(2)}, u32[]{:S(2)}) collective-permute-start(f32[5,64,128]{2,1,0:T(8,128)S(1)} %get-tuple-element.106), channel_id=1, source_target_pairs={{4,0},{6,2},{8,4},{10,6},{12,8},{14,10},{16,12},{18,14},{20,16},{2... | collective-permute-start | bytes 491528 | tf_op jit(solution)/shard_map/ppermute | solution.py:294
  160.9 4.0 %collective-permute-done.22 = f32[5,64,128]{2,1,0:T(8,128)S(1)} collective-permute-done((f32[5,64,128]{2,1,0:T(8,128)S(1)}, f32[5,64,128]{2,1,0:T(8,128)S(1)}, u32[]{:S(2)}, u32[]{:S(2)}) %collective-permute-start.22) | collective-permute-done | bytes 163872 | tf_op jit(solution)/shard_map/ppermute | solution.py:294
  167.0 2.8 %collective-permute-start.18 = (f32[5,64,128]{2,1,0:T(8,128)S(1)}, f32[5,64,128]{2,1,0:T(8,128)S(1)}, u32[]{:S(2)}, u32[]{:S(2)}) collective-permute-start(f32[5,64,128]{2,1,0:T(8,128)S(1)} %multiply_add_fusion.26), channel_id=1, source_target_pairs={{0,16},{2,18},{4,20},{6,22},{8,24},{10,26},{12,28},{14,30},{16,32}... | collective-permute-start | bytes 491528 | tf_op jit(solution)/shard_map/ppermute | solution.py:293
  169.7 8.0 %collective-permute-done.23 = f32[5,64,128]{2,1,0:T(8,128)S(1)} collective-permute-done((f32[5,64,128]{2,1,0:T(8,128)S(1)}, f32[5,64,128]{2,1,0:T(8,128)S(1)}, u32[]{:S(2)}, u32[]{:S(2)}) %collective-permute-start.23) | collective-permute-done | bytes 163872 | tf_op jit(solution)/shard_map/ppermute | solution.py:294
  181.3 6.1 %collective-permute-done.24 = f32[5,64,128]{2,1,0:T(8,128)S(1)} collective-permute-done((f32[5,64,128]{2,1,0:T(8,128)S(1)}, f32[5,64,128]{2,1,0:T(8,128)S(1)}, u32[]{:S(2)}, u32[]{:S(2)}) %collective-permute-start.24) | collective-permute-done | bytes 163872 | tf_op jit(solution)/shard_map/ppermute | solution.py:294
  189.0 2.7 %collective-permute-start.20 = (f32[5,64,128]{2,1,0:T(8,128)S(1)}, f32[5,64,128]{2,1,0:T(8,128)S(1)}, u32[]{:S(2)}, u32[]{:S(2)}) collective-permute-start(f32[5,64,128]{2,1,0:T(8,128)S(1)} %multiply_add_fusion.24), channel_id=1, source_target_pairs={{0,64},{2,66},{4,68},{6,70},{8,72},{10,74},{12,76},{14,78},{16,80}... | collective-permute-start | bytes 491528 | tf_op jit(solution)/shard_map/ppermute | solution.py:293
  191.7 3.1 %collective-permute-done.25 = f32[5,64,128]{2,1,0:T(8,128)S(1)} collective-permute-done((f32[5,64,128]{2,1,0:T(8,128)S(1)}, f32[5,64,128]{2,1,0:T(8,128)S(1)}, u32[]{:S(2)}, u32[]{:S(2)}) %collective-permute-start.25) | collective-permute-done | bytes 163872 | tf_op jit(solution)/shard_map/ppermute | solution.py:294
  196.3 7.3 %collective-permute-done.26 = f32[5,64,128]{2,1,0:T(8,128)S(1)} collective-permute-done((f32[5,64,128]{2,1,0:T(8,128)S(1)}, f32[5,64,128]{2,1,0:T(8,128)S(1)}, u32[]{:S(2)}, u32[]{:S(2)}) %collective-permute-start.26) | collective-permute-done | bytes 163872 | tf_op jit(solution)/shard_map/ppermute | solution.py:294
  203.8 2.9 %fusion.4 = f32[5,8,64,128]{3,2,1,0:T(8,128)S(1)} fusion(f32[5,8,128,64]{2,3,1,0:T(8,128)S(1)} %fusion.107, f32[5,8,64,128]{3,2,1,0:T(8,128)S(1)} %collective-permute-done.27, f32[64,64,1,1]{0,1,3,2:T(8,128)S(1)} %copy-done.33, f32[5,8,64,128]{3,2,1,0:T(8,128)S(1)} %fusion.106, f32[5,64,128]{2,1,0:T(8,128)S(1)} %multiply_add_fusion.17, ...), kind=kOutput, calls=%fused_computation.53 | convolution fusion | flops 261816320 | bytes 7553472 | tf_op jit(solution)/shard_map/fyzx,zw->fywx/dot_general | solution.py:331
  (331 shorter events, 86.9 us)
Async XLA Ops:
  11.0 37.0 %collective-permute-start.2 = (f32[9,64,128]{2,1,0:T(8,128)}, f32[9,64,128]{2,1,0:T(8,128)}, u32[]{:S(2)}, u32[]{:S(2)}) collective-permute-start(f32[9,64,128]{2,1,0:T(8,128)} %pad_maximum_fusion.7), channel_id=1, source_target_pairs={{0,2},{2,4},{4,6},{6,8},{8,10},{10,12},{12,14},{14,16},{16,18},{18... | collective-permute-start | bytes 884744 | tf_op jit(solution)/shard_map/ppermute | solution.py:293
  15.2 37.3 %collective-permute-start.8 = (f32[9,64,128]{2,1,0:T(8,128)}, f32[9,64,128]{2,1,0:T(8,128)}, u32[]{:S(2)}, u32[]{:S(2)}) collective-permute-start(f32[9,64,128]{2,1,0:T(8,128)} %pad_maximum_fusion.8), channel_id=1, source_target_pairs={{2,0},{4,2},{6,4},{8,6},{10,8},{12,10},{14,12},{16,14},{18,16},{20... | collective-permute-start | bytes 884744 | tf_op jit(solution)/shard_map/ppermute | solution.py:294
  18.6 38.9 %collective-permute-start = (f32[5,3,64,128]{3,2,1,0:T(8,128)}, f32[5,3,64,128]{3,2,1,0:T(8,128)S(1)}, u32[]{:S(2)}, u32[]{:S(2)}) collective-permute-start(f32[5,3,64,128]{3,2,1,0:T(8,128)} %get-tuple-element.85), channel_id=1, source_target_pairs={{0,2},{2,4},{4,6},{6,8},{8,10},{10,12},{12,14},{14,16},{16,18},{18... | collective-permute-start | bytes 1474568 | tf_op jit(solution)/shard_map/ppermute | solution.py:317
  26.4 31.2 %collective-permute-start.1 = (f32[5,3,64,128]{3,2,1,0:T(8,128)}, f32[5,3,64,128]{3,2,1,0:T(8,128)S(1)}, u32[]{:S(2)}, u32[]{:S(2)}) collective-permute-start(f32[5,3,64,128]{3,2,1,0:T(8,128)} %get-tuple-element.86), channel_id=1, source_target_pairs={{2,0},{4,2},{6,4},{8,6},{10,8},{12,10},{14,12},{16,14},{18,16},{20... | collective-permute-start | bytes 1474568 | tf_op jit(solution)/shard_map/ppermute | solution.py:318
  49.1 13.3 %collective-permute-start.3 = (f32[9,64,128]{2,1,0:T(8,128)S(1)}, f32[9,64,128]{2,1,0:T(8,128)S(1)}, u32[]{:S(2)}, u32[]{:S(2)}) collective-permute-start(f32[9,64,128]{2,1,0:T(8,128)S(1)} %multiply_add_fusion.15), channel_id=1, source_target_pairs={{0,4},{2,6},{4,8},{6,10},{8,12},{10,14},{12,16},{14,18},{16,20},{1... | collective-permute-start | bytes 884744 | tf_op jit(solution)/shard_map/ppermute | solution.py:293
  53.6 14.0 %collective-permute-start.9 = (f32[9,64,128]{2,1,0:T(8,128)S(1)}, f32[9,64,128]{2,1,0:T(8,128)S(1)}, u32[]{:S(2)}, u32[]{:S(2)}) collective-permute-start(f32[9,64,128]{2,1,0:T(8,128)S(1)} %multiply_add_fusion.9), channel_id=1, source_target_pairs={{4,0},{6,2},{8,4},{10,6},{12,8},{14,10},{16,12},{18,14},{20,16},{2... | collective-permute-start | bytes 884744 | tf_op jit(solution)/shard_map/ppermute | solution.py:294
  59.1 65.6 %collective-permute-start.14 = (f32[4,12,64,128]{3,2,1,0:T(8,128)S(1)}, f32[4,12,64,128]{3,2,1,0:T(8,128)S(1)}, u32[]{:S(2)}, u32[]{:S(2)}) collective-permute-start(f32[4,12,64,128]{3,2,1,0:T(8,128)S(1)} %fusion.1), channel_id=1, source_target_pairs={{0,1},{1,0},{2,3},{3,2},{4,5},{5,4},{6,7},{7,6},{8,9},{9,8},{10,11... | collective-permute-start | bytes 4718600 | tf_op jit(solution)/shard_map/ppermute | solution.py:330
  62.6 10.1 %collective-permute-start.4 = (f32[9,64,128]{2,1,0:T(8,128)S(1)}, f32[9,64,128]{2,1,0:T(8,128)S(1)}, u32[]{:S(2)}, u32[]{:S(2)}) collective-permute-start(f32[9,64,128]{2,1,0:T(8,128)S(1)} %multiply_add_fusion.14), channel_id=1, source_target_pairs={{0,8},{2,10},{4,12},{6,14},{8,16},{10,18},{12,20},{14,22},{16,24},... | collective-permute-start | bytes 884744 | tf_op jit(solution)/shard_map/ppermute | solution.py:293
  67.7 10.7 %collective-permute-start.10 = (f32[9,64,128]{2,1,0:T(8,128)S(1)}, f32[9,64,128]{2,1,0:T(8,128)S(1)}, u32[]{:S(2)}, u32[]{:S(2)}) collective-permute-start(f32[9,64,128]{2,1,0:T(8,128)S(1)} %multiply_add_fusion.8), channel_id=1, source_target_pairs={{8,0},{10,2},{12,4},{14,6},{16,8},{18,10},{20,12},{22,14},{24,16},... | collective-permute-start | bytes 884744 | tf_op jit(solution)/shard_map/ppermute | solution.py:294
  72.8 10.7 %collective-permute-start.5 = (f32[9,64,128]{2,1,0:T(8,128)S(1)}, f32[9,64,128]{2,1,0:T(8,128)S(1)}, u32[]{:S(2)}, u32[]{:S(2)}) collective-permute-start(f32[9,64,128]{2,1,0:T(8,128)S(1)} %multiply_add_fusion.13), channel_id=1, source_target_pairs={{0,16},{2,18},{4,20},{6,22},{8,24},{10,26},{12,28},{14,30},{16,32}... | collective-permute-start | bytes 884744 | tf_op jit(solution)/shard_map/ppermute | solution.py:293
  78.5 15.4 %collective-permute-start.11 = (f32[9,64,128]{2,1,0:T(8,128)S(1)}, f32[9,64,128]{2,1,0:T(8,128)S(1)}, u32[]{:S(2)}, u32[]{:S(2)}) collective-permute-start(f32[9,64,128]{2,1,0:T(8,128)S(1)} %multiply_add_fusion.7), channel_id=1, source_target_pairs={{16,0},{18,2},{20,4},{22,6},{24,8},{26,10},{28,12},{30,14},{32,16}... | collective-permute-start | bytes 884744 | tf_op jit(solution)/shard_map/ppermute | solution.py:294
  83.6 17.3 %collective-permute-start.6 = (f32[9,64,128]{2,1,0:T(8,128)S(1)}, f32[9,64,128]{2,1,0:T(8,128)S(1)}, u32[]{:S(2)}, u32[]{:S(2)}) collective-permute-start(f32[9,64,128]{2,1,0:T(8,128)S(1)} %multiply_add_fusion.12), channel_id=1, source_target_pairs={{0,32},{2,34},{4,36},{6,38},{8,40},{10,42},{12,44},{14,46},{16,48}... | collective-permute-start | bytes 884744 | tf_op jit(solution)/shard_map/ppermute | solution.py:293
  94.1 13.6 %collective-permute-start.12 = (f32[9,64,128]{2,1,0:T(8,128)S(1)}, f32[9,64,128]{2,1,0:T(8,128)S(1)}, u32[]{:S(2)}, u32[]{:S(2)}) collective-permute-start(f32[9,64,128]{2,1,0:T(8,128)S(1)} %multiply_add_fusion.6), channel_id=1, source_target_pairs={{32,0},{34,2},{36,4},{38,6},{40,8},{42,10},{44,12},{46,14},{48,16}... | collective-permute-start | bytes 884744 | tf_op jit(solution)/shard_map/ppermute | solution.py:294
  100.9 10.8 %collective-permute-start.7 = (f32[9,64,128]{2,1,0:T(8,128)S(1)}, f32[9,64,128]{2,1,0:T(8,128)S(1)}, u32[]{:S(2)}, u32[]{:S(2)}) collective-permute-start(f32[9,64,128]{2,1,0:T(8,128)S(1)} %multiply_add_fusion.11), channel_id=1, source_target_pairs={{0,64},{2,66},{4,68},{6,70},{8,72},{10,74},{12,76},{14,78},{16,80}... | collective-permute-start | bytes 884744 | tf_op jit(solution)/shard_map/ppermute | solution.py:293
  107.8 10.1 %collective-permute-start.13 = (f32[9,64,128]{2,1,0:T(8,128)S(1)}, f32[9,64,128]{2,1,0:T(8,128)S(1)}, u32[]{:S(2)}, u32[]{:S(2)}) collective-permute-start(f32[9,64,128]{2,1,0:T(8,128)S(1)} %multiply_add_fusion.5), channel_id=1, source_target_pairs={{64,0},{66,2},{68,4},{70,6},{72,8},{74,10},{76,12},{78,14},{80,16}... | collective-permute-start | bytes 884744 | tf_op jit(solution)/shard_map/ppermute | solution.py:294
  129.3 14.1 %collective-permute-start.15 = (f32[5,64,128]{2,1,0:T(8,128)S(1)}, f32[5,64,128]{2,1,0:T(8,128)S(1)}, u32[]{:S(2)}, u32[]{:S(2)}) collective-permute-start(f32[5,64,128]{2,1,0:T(8,128)S(1)} %get-tuple-element.107), channel_id=1, source_target_pairs={{0,2},{2,4},{4,6},{6,8},{8,10},{10,12},{12,14},{14,16},{16,18},{18... | collective-permute-start | bytes 491528 | tf_op jit(solution)/shard_map/ppermute | solution.py:293
  138.1 11.4 %collective-permute-start.21 = (f32[5,64,128]{2,1,0:T(8,128)S(1)}, f32[5,64,128]{2,1,0:T(8,128)S(1)}, u32[]{:S(2)}, u32[]{:S(2)}) collective-permute-start(f32[5,64,128]{2,1,0:T(8,128)S(1)} %get-tuple-element.108), channel_id=1, source_target_pairs={{2,0},{4,2},{6,4},{8,6},{10,8},{12,10},{14,12},{16,14},{18,16},{20... | collective-permute-start | bytes 491528 | tf_op jit(solution)/shard_map/ppermute | solution.py:294
  141.2 62.4 %collective-permute-start.27 = (f32[5,8,64,128]{3,2,1,0:T(8,128)S(1)}, f32[5,8,64,128]{3,2,1,0:T(8,128)S(1)}, u32[]{:S(2)}, u32[]{:S(2)}) collective-permute-start(f32[5,8,64,128]{3,2,1,0:T(8,128)S(1)} %fusion.34), channel_id=1, source_target_pairs={{0,1},{1,0},{2,3},{3,2},{4,5},{5,4},{6,7},{7,6},{8,9},{9,8},{10,11... | collective-permute-start | bytes 3932168 | tf_op jit(solution)/shard_map/ppermute | solution.py:330
  149.7 9.2 %collective-permute-start.16 = (f32[5,64,128]{2,1,0:T(8,128)S(1)}, f32[5,64,128]{2,1,0:T(8,128)S(1)}, u32[]{:S(2)}, u32[]{:S(2)}) collective-permute-start(f32[5,64,128]{2,1,0:T(8,128)S(1)} %get-tuple-element.105), channel_id=1, source_target_pairs={{0,4},{2,6},{4,8},{6,10},{8,12},{10,14},{12,16},{14,18},{16,20},{1... | collective-permute-start | bytes 491528 | tf_op jit(solution)/shard_map/ppermute | solution.py:293
  153.1 11.7 %collective-permute-start.22 = (f32[5,64,128]{2,1,0:T(8,128)S(1)}, f32[5,64,128]{2,1,0:T(8,128)S(1)}, u32[]{:S(2)}, u32[]{:S(2)}) collective-permute-start(f32[5,64,128]{2,1,0:T(8,128)S(1)} %get-tuple-element.106), channel_id=1, source_target_pairs={{4,0},{6,2},{8,4},{10,6},{12,8},{14,10},{16,12},{18,14},{20,16},{2... | collective-permute-start | bytes 491528 | tf_op jit(solution)/shard_map/ppermute | solution.py:294
  164.9 12.8 %collective-permute-start.23 = (f32[5,64,128]{2,1,0:T(8,128)S(1)}, f32[5,64,128]{2,1,0:T(8,128)S(1)}, u32[]{:S(2)}, u32[]{:S(2)}) collective-permute-start(f32[5,64,128]{2,1,0:T(8,128)S(1)} %multiply_add_fusion.21), channel_id=1, source_target_pairs={{8,0},{10,2},{12,4},{14,6},{16,8},{18,10},{20,12},{22,14},{24,16},... | collective-permute-start | bytes 491528 | tf_op jit(solution)/shard_map/ppermute | solution.py:294
  167.0 12.8 %collective-permute-start.18 = (f32[5,64,128]{2,1,0:T(8,128)S(1)}, f32[5,64,128]{2,1,0:T(8,128)S(1)}, u32[]{:S(2)}, u32[]{:S(2)}) collective-permute-start(f32[5,64,128]{2,1,0:T(8,128)S(1)} %multiply_add_fusion.26), channel_id=1, source_target_pairs={{0,16},{2,18},{4,20},{6,22},{8,24},{10,26},{12,28},{14,30},{16,32}... | collective-permute-start | bytes 491528 | tf_op jit(solution)/shard_map/ppermute | solution.py:293
  177.9 9.6 %collective-permute-start.24 = (f32[5,64,128]{2,1,0:T(8,128)S(1)}, f32[5,64,128]{2,1,0:T(8,128)S(1)}, u32[]{:S(2)}, u32[]{:S(2)}) collective-permute-start(f32[5,64,128]{2,1,0:T(8,128)S(1)} %multiply_add_fusion.20), channel_id=1, source_target_pairs={{16,0},{18,2},{20,4},{22,6},{24,8},{26,10},{28,12},{30,14},{32,16}... | collective-permute-start | bytes 491528 | tf_op jit(solution)/shard_map/ppermute | solution.py:294
  180.0 8.8 %collective-permute-start.19 = (f32[5,64,128]{2,1,0:T(8,128)S(1)}, f32[5,64,128]{2,1,0:T(8,128)S(1)}, u32[]{:S(2)}, u32[]{:S(2)}) collective-permute-start(f32[5,64,128]{2,1,0:T(8,128)S(1)} %multiply_add_fusion.25), channel_id=1, source_target_pairs={{0,32},{2,34},{4,36},{6,38},{8,40},{10,42},{12,44},{14,46},{16,48}... | collective-permute-start | bytes 491528 | tf_op jit(solution)/shard_map/ppermute | solution.py:293
  (89 other events, 677.5 us)

commit v9 on v8

--- a/solution.py
+++ b/solution.py
@@ -246,7 +246,12 @@
         for (kind, _), extra in zip(kinds_sizes, extras)
     ]
     groups = [
-        (bank.add(table[0]), bank.add(table[1]), bank.add(table[2]), table[1].shape[1])
+        (
+            bank.add(table[0].transpose(0, 2, 1)),
+            bank.add(table[1]),
+            bank.add(table[2]),
+            table[1].shape[1],
+        )
         for table in tables
     ]
     blocks = points // rows
@@ -271,15 +276,15 @@
     count = lax.axis_size("gy")
     groups, rounds = plan
 
-    def taps(padded, combine):
+    def taps(padded, by_tap):
         summed = None
-        for tap in range(combine.shape[1]):
-            term = combine[:, tap, None, None] * padded[:, None, tap]
+        for tap in range(by_tap.shape[0]):
+            term = by_tap[tap][:, None, None] * padded[:, None, tap]
             summed = term if summed is None else summed + term
         return summed
 
     partials = [
-        taps(own, bank.get(handles[0])[handles[3] :, pad : pad + rows])
+        taps(own, bank.get(handles[0])[pad : pad + rows, handles[3] :])
         for own, handles in zip(own_groups, groups)
     ]
     sizes = [padded.shape[0] for padded in padded_groups]
@@ -298,7 +303,7 @@
     results = []
     first = 0
     for padded, handles, size in zip(padded_groups, groups, sizes):
-        local = taps(padded, bank.get(handles[0])[: handles[3]])
+        local = taps(padded, bank.get(handles[0])[:, : handles[3]])
         rise_gain = bank.get(handles[1])
         fall_gain = bank.get(handles[2])
         results.append(

time: 211 us -> 199 us (0.943)
  the two profiles are of different devices: /device:TPU:30 before, /device:TPU:28 now
where the time goes in v9:
time: 199 us; the launch traced here: 198 us
  starting transfers between devices  86.7 us (44%)
  waiting for transfers between devices  66.3 us (33%)
  other arithmetic  19 us (10%)
  local copies, waits for them, and re-layouts  14.4 us (7%)
  matrix products  9.97 us (5%)
    ppermute x12, waiting for transfers between devices, wall_apply(): from_above = lax.ppermute(fall, 'gy', down_pairs)  63.2 us
    ppermute x12, starting transfers between devices, wall_apply(): from_below = lax.ppermute(rise, 'gy', up_pairs)  54.6 us
    ppermute x12, starting transfers between devices, wall_apply(): from_above = lax.ppermute(fall, 'gy', down_pairs)  26 us
    unnamed x68, local copies, waits for them, and re-layouts  5.1 us
    add x2, other arithmetic, wall_apply(): local + rise_gain[None, :, None, None] * rise[first:first + size, None]  4.88 us
    dot_general x2, matrix products, span_slope(): jnp.einsum('fyzx,zw->fywx', other, other_block, precision=HIGHEST)  4.46 us
  transfers between devices with their start and end apart: 28, of which 15 were waited for; matrix products, arithmetic and copies ran while one was open for 12% of the time, Pallas kernels for 0%

profile of v9, /device:TPU:28, one launch (start us, length us, event | category | flops | bytes accessed | tf_op | source)
XLA Modules:
  0.0 198.1 jit_solution(17077109348259566242)
XLA Ops:
  9.5 3.1 %collective-permute-start.2 = (f32[9,64,128]{2,1,0:T(8,128)}, f32[9,64,128]{2,1,0:T(8,128)}, u32[]{:S(2)}, u32[]{:S(2)}) collective-permute-start(f32[9,64,128]{2,1,0:T(8,128)} %pad_maximum_fusion.7), channel_id=1, source_target_pairs={{0,2},{2,4},{4,6},{6,8},{8,10},{10,12},{12,14},{14,16},{16,18},{18... | collective-permute-start | bytes 884744 | tf_op jit(solution)/shard_map/ppermute | solution.py:298
  13.4 2.7 %collective-permute-start.8 = (f32[9,64,128]{2,1,0:T(8,128)}, f32[9,64,128]{2,1,0:T(8,128)}, u32[]{:S(2)}, u32[]{:S(2)}) collective-permute-start(f32[9,64,128]{2,1,0:T(8,128)} %pad_maximum_fusion.8), channel_id=1, source_target_pairs={{2,0},{4,2},{6,4},{8,6},{10,8},{12,10},{14,12},{16,14},{18,16},{20... | collective-permute-start | bytes 884744 | tf_op jit(solution)/shard_map/ppermute | solution.py:299
  17.1 3.2 %collective-permute-start = (f32[5,3,64,128]{3,2,1,0:T(8,128)}, f32[5,3,64,128]{3,2,1,0:T(8,128)S(1)}, u32[]{:S(2)}, u32[]{:S(2)}) collective-permute-start(f32[5,3,64,128]{3,2,1,0:T(8,128)} %get-tuple-element.51), channel_id=1, source_target_pairs={{0,2},{2,4},{4,6},{6,8},{8,10},{10,12},{12,14},{14,16},{16,18},{18... | collective-permute-start | bytes 1474568 | tf_op jit(solution)/shard_map/ppermute | solution.py:322
  20.4 2.7 %collective-permute-start.1 = (f32[5,3,64,128]{3,2,1,0:T(8,128)}, f32[5,3,64,128]{3,2,1,0:T(8,128)S(1)}, u32[]{:S(2)}, u32[]{:S(2)}) collective-permute-start(f32[5,3,64,128]{3,2,1,0:T(8,128)} %get-tuple-element.52), channel_id=1, source_target_pairs={{2,0},{4,2},{6,4},{8,6},{10,8},{12,10},{14,12},{16,14},{18,16},{20... | collective-permute-start | bytes 1474568 | tf_op jit(solution)/shard_map/ppermute | solution.py:323
  29.9 11.9 %collective-permute-start.3 = (f32[9,64,128]{2,1,0:T(8,128)S(1)}, f32[9,64,128]{2,1,0:T(8,128)S(1)}, u32[]{:S(2)}, u32[]{:S(2)}) collective-permute-start(f32[9,64,128]{2,1,0:T(8,128)S(1)} %multiply_add_fusion.15), channel_id=1, source_target_pairs={{0,4},{2,6},{4,8},{6,10},{8,12},{10,14},{12,16},{14,18},{16,20},{1... | collective-permute-start | bytes 884744 | tf_op jit(solution)/shard_map/ppermute | solution.py:298
  51.3 5.4 %collective-permute-done.9 = f32[9,64,128]{2,1,0:T(8,128)S(1)} collective-permute-done((f32[9,64,128]{2,1,0:T(8,128)S(1)}, f32[9,64,128]{2,1,0:T(8,128)S(1)}, u32[]{:S(2)}, u32[]{:S(2)}) %collective-permute-start.9) | collective-permute-done | bytes 294944 | tf_op jit(solution)/shard_map/ppermute | solution.py:299
  61.8 15.2 %collective-permute-done.10 = f32[9,64,128]{2,1,0:T(8,128)S(1)} collective-permute-done((f32[9,64,128]{2,1,0:T(8,128)S(1)}, f32[9,64,128]{2,1,0:T(8,128)S(1)}, u32[]{:S(2)}, u32[]{:S(2)}) %collective-permute-start.10) | collective-permute-done | bytes 294944 | tf_op jit(solution)/shard_map/ppermute | solution.py:299
  79.1 3.8 %collective-permute-start.6 = (f32[9,64,128]{2,1,0:T(8,128)S(1)}, f32[9,64,128]{2,1,0:T(8,128)S(1)}, u32[]{:S(2)}, u32[]{:S(2)}) collective-permute-start(f32[9,64,128]{2,1,0:T(8,128)S(1)} %multiply_add_fusion.12), channel_id=1, source_target_pairs={{0,32},{2,34},{4,36},{6,38},{8,40},{10,42},{12,44},{14,46},{16,48}... | collective-permute-start | bytes 884744 | tf_op jit(solution)/shard_map/ppermute | solution.py:298
  83.0 5.2 %collective-permute-done.11 = f32[9,64,128]{2,1,0:T(8,128)S(1)} collective-permute-done((f32[9,64,128]{2,1,0:T(8,128)S(1)}, f32[9,64,128]{2,1,0:T(8,128)S(1)}, u32[]{:S(2)}, u32[]{:S(2)}) %collective-permute-start.11) | collective-permute-done | bytes 294944 | tf_op jit(solution)/shard_map/ppermute | solution.py:299
  89.8 6.4 %collective-permute-start.7 = (f32[9,64,128]{2,1,0:T(8,128)S(1)}, f32[9,64,128]{2,1,0:T(8,128)S(1)}, u32[]{:S(2)}, u32[]{:S(2)}) collective-permute-start(f32[9,64,128]{2,1,0:T(8,128)S(1)} %multiply_add_fusion.11), channel_id=1, source_target_pairs={{0,64},{2,66},{4,68},{6,70},{8,72},{10,74},{12,76},{14,78},{16,80}... | collective-permute-start | bytes 884744 | tf_op jit(solution)/shard_map/ppermute | solution.py:298
  96.2 3.1 %collective-permute-done.12 = f32[9,64,128]{2,1,0:T(8,128)S(1)} collective-permute-done((f32[9,64,128]{2,1,0:T(8,128)S(1)}, f32[9,64,128]{2,1,0:T(8,128)S(1)}, u32[]{:S(2)}, u32[]{:S(2)}) %collective-permute-start.12) | collective-permute-done | bytes 294944 | tf_op jit(solution)/shard_map/ppermute | solution.py:299
  101.1 8.4 %collective-permute-done.13 = f32[9,64,128]{2,1,0:T(8,128)S(1)} collective-permute-done((f32[9,64,128]{2,1,0:T(8,128)S(1)}, f32[9,64,128]{2,1,0:T(8,128)S(1)}, u32[]{:S(2)}, u32[]{:S(2)}) %collective-permute-start.13) | collective-permute-done | bytes 294944 | tf_op jit(solution)/shard_map/ppermute | solution.py:299
  113.3 2.9 %multiply_add_fusion.1 = f32[5,8,64,128]{3,2,1,0:T(8,128)} fusion(f32[5,64,128]{2,1,0:T(8,128)S(1)} %slice-done.1, f32[8]{0:T(128)S(1)} %get-tuple-element.82, f32[5,64,128]{2,1,0:T(8,128)S(1)} %slice-done, f32[8]{0:T(128)S(1)} %get-tuple-element.79, f32[5,64,128]{2,1,0:T(8,128)S(1)} %get-tuple-element.69, f32[8]{0:T(128)S(1)} %get-tuple-element.110, ...), kind=kLoop, calls=%fused_computation.57 | loop fusion | flops 10158080 | bytes 3932672 | tf_op jit(solution)/shard_map/add | solution.py:310
  120.8 5.1 %collective-permute-start.15 = (f32[5,64,128]{2,1,0:T(8,128)S(1)}, f32[5,64,128]{2,1,0:T(8,128)S(1)}, u32[]{:S(2)}, u32[]{:S(2)}) collective-permute-start(f32[5,64,128]{2,1,0:T(8,128)S(1)} %get-tuple-element.73), channel_id=1, source_target_pairs={{0,2},{2,4},{4,6},{6,8},{8,10},{10,12},{12,14},{14,16},{16,18},{18... | collective-permute-start | bytes 491528 | tf_op jit(solution)/shard_map/ppermute | solution.py:298
  133.2 5.0 %collective-permute-start.16 = (f32[5,64,128]{2,1,0:T(8,128)S(1)}, f32[5,64,128]{2,1,0:T(8,128)S(1)}, u32[]{:S(2)}, u32[]{:S(2)}) collective-permute-start(f32[5,64,128]{2,1,0:T(8,128)S(1)} %get-tuple-element.71), channel_id=1, source_target_pairs={{0,4},{2,6},{4,8},{6,10},{8,12},{10,14},{12,16},{14,18},{16,20},{1... | collective-permute-start | bytes 491528 | tf_op jit(solution)/shard_map/ppermute | solution.py:298
  139.5 4.5 %collective-permute-start.22 = (f32[5,64,128]{2,1,0:T(8,128)S(1)}, f32[5,64,128]{2,1,0:T(8,128)S(1)}, u32[]{:S(2)}, u32[]{:S(2)}) collective-permute-start(f32[5,64,128]{2,1,0:T(8,128)S(1)} %get-tuple-element.72), channel_id=1, source_target_pairs={{4,0},{6,2},{8,4},{10,6},{12,8},{14,10},{16,12},{18,14},{20,16},{2... | collective-permute-start | bytes 491528 | tf_op jit(solution)/shard_map/ppermute | solution.py:299
  147.4 4.8 %collective-permute-done.22 = f32[5,64,128]{2,1,0:T(8,128)S(1)} collective-permute-done((f32[5,64,128]{2,1,0:T(8,128)S(1)}, f32[5,64,128]{2,1,0:T(8,128)S(1)}, u32[]{:S(2)}, u32[]{:S(2)}) %collective-permute-start.22) | collective-permute-done | bytes 163872 | tf_op jit(solution)/shard_map/ppermute | solution.py:299
  152.3 3.8 %collective-permute-start.23 = (f32[5,64,128]{2,1,0:T(8,128)S(1)}, f32[5,64,128]{2,1,0:T(8,128)S(1)}, u32[]{:S(2)}, u32[]{:S(2)}) collective-permute-start(f32[5,64,128]{2,1,0:T(8,128)S(1)} %multiply_add_fusion.21), channel_id=1, source_target_pairs={{8,0},{10,2},{12,4},{14,6},{16,8},{18,10},{20,12},{22,14},{24,16},... | collective-permute-start | bytes 491528 | tf_op jit(solution)/shard_map/ppermute | solution.py:299
  158.2 7.2 %collective-permute-done.23 = f32[5,64,128]{2,1,0:T(8,128)S(1)} collective-permute-done((f32[5,64,128]{2,1,0:T(8,128)S(1)}, f32[5,64,128]{2,1,0:T(8,128)S(1)}, u32[]{:S(2)}, u32[]{:S(2)}) %collective-permute-start.23) | collective-permute-done | bytes 163872 | tf_op jit(solution)/shard_map/ppermute | solution.py:299
  167.5 3.9 %collective-permute-start.19 = (f32[5,64,128]{2,1,0:T(8,128)S(1)}, f32[5,64,128]{2,1,0:T(8,128)S(1)}, u32[]{:S(2)}, u32[]{:S(2)}) collective-permute-start(f32[5,64,128]{2,1,0:T(8,128)S(1)} %multiply_add_fusion.25), channel_id=1, source_target_pairs={{0,32},{2,34},{4,36},{6,38},{8,40},{10,42},{12,44},{14,46},{16,48}... | collective-permute-start | bytes 491528 | tf_op jit(solution)/shard_map/ppermute | solution.py:298
  171.4 3.7 %collective-permute-done.24 = f32[5,64,128]{2,1,0:T(8,128)S(1)} collective-permute-done((f32[5,64,128]{2,1,0:T(8,128)S(1)}, f32[5,64,128]{2,1,0:T(8,128)S(1)}, u32[]{:S(2)}, u32[]{:S(2)}) %collective-permute-start.24) | collective-permute-done | bytes 163872 | tf_op jit(solution)/shard_map/ppermute | solution.py:299
  176.5 7.4 %collective-permute-start.20 = (f32[5,64,128]{2,1,0:T(8,128)S(1)}, f32[5,64,128]{2,1,0:T(8,128)S(1)}, u32[]{:S(2)}, u32[]{:S(2)}) collective-permute-start(f32[5,64,128]{2,1,0:T(8,128)S(1)} %multiply_add_fusion.24), channel_id=1, source_target_pairs={{0,64},{2,66},{4,68},{6,70},{8,72},{10,74},{12,76},{14,78},{16,80}... | collective-permute-start | bytes 491528 | tf_op jit(solution)/shard_map/ppermute | solution.py:298
  186.8 6.9 %collective-permute-done.26 = f32[5,64,128]{2,1,0:T(8,128)S(1)} collective-permute-done((f32[5,64,128]{2,1,0:T(8,128)S(1)}, f32[5,64,128]{2,1,0:T(8,128)S(1)}, u32[]{:S(2)}, u32[]{:S(2)}) %collective-permute-start.26) | collective-permute-done | bytes 163872 | tf_op jit(solution)/shard_map/ppermute | solution.py:299
  193.8 2.9 %fusion.4 = f32[5,8,64,128]{3,2,1,0:T(8,128)S(1)} fusion(f32[5,8,128,64]{2,3,1,0:T(8,128)S(1)} %fusion.104, f32[5,8,64,128]{3,2,1,0:T(8,128)S(1)} %collective-permute-done.27, f32[64,64,1,1]{0,1,3,2:T(8,128)S(1)} %copy-done.32, f32[5,8,64,128]{3,2,1,0:T(8,128)S(1)} %fusion.103, f32[5,64,128]{2,1,0:T(8,128)S(1)} %multiply_add_fusion.17, ...), kind=kOutput, calls=%fused_computation.53 | convolution fusion | flops 261816320 | bytes 7553472 | tf_op jit(solution)/shard_map/fyzx,zw->fywx/dot_general | solution.py:336
  (194 shorter events, 67.1 us)
Async XLA Ops:
  9.5 19.3 %collective-permute-start.2 = (f32[9,64,128]{2,1,0:T(8,128)}, f32[9,64,128]{2,1,0:T(8,128)}, u32[]{:S(2)}, u32[]{:S(2)}) collective-permute-start(f32[9,64,128]{2,1,0:T(8,128)} %pad_maximum_fusion.7), channel_id=1, source_target_pairs={{0,2},{2,4},{4,6},{6,8},{8,10},{10,12},{12,14},{14,16},{16,18},{18... | collective-permute-start | bytes 884744 | tf_op jit(solution)/shard_map/ppermute | solution.py:298
  13.4 28.5 %collective-permute-start.8 = (f32[9,64,128]{2,1,0:T(8,128)}, f32[9,64,128]{2,1,0:T(8,128)}, u32[]{:S(2)}, u32[]{:S(2)}) collective-permute-start(f32[9,64,128]{2,1,0:T(8,128)} %pad_maximum_fusion.8), channel_id=1, source_target_pairs={{2,0},{4,2},{6,4},{8,6},{10,8},{12,10},{14,12},{16,14},{18,16},{20... | collective-permute-start | bytes 884744 | tf_op jit(solution)/shard_map/ppermute | solution.py:299
  17.1 27.7 %collective-permute-start = (f32[5,3,64,128]{3,2,1,0:T(8,128)}, f32[5,3,64,128]{3,2,1,0:T(8,128)S(1)}, u32[]{:S(2)}, u32[]{:S(2)}) collective-permute-start(f32[5,3,64,128]{3,2,1,0:T(8,128)} %get-tuple-element.51), channel_id=1, source_target_pairs={{0,2},{2,4},{4,6},{6,8},{8,10},{10,12},{12,14},{14,16},{16,18},{18... | collective-permute-start | bytes 1474568 | tf_op jit(solution)/shard_map/ppermute | solution.py:322
  20.4 24.5 %collective-permute-start.1 = (f32[5,3,64,128]{3,2,1,0:T(8,128)}, f32[5,3,64,128]{3,2,1,0:T(8,128)S(1)}, u32[]{:S(2)}, u32[]{:S(2)}) collective-permute-start(f32[5,3,64,128]{3,2,1,0:T(8,128)} %get-tuple-element.52), channel_id=1, source_target_pairs={{2,0},{4,2},{6,4},{8,6},{10,8},{12,10},{14,12},{16,14},{18,16},{20... | collective-permute-start | bytes 1474568 | tf_op jit(solution)/shard_map/ppermute | solution.py:323
  29.9 19.3 %collective-permute-start.3 = (f32[9,64,128]{2,1,0:T(8,128)S(1)}, f32[9,64,128]{2,1,0:T(8,128)S(1)}, u32[]{:S(2)}, u32[]{:S(2)}) collective-permute-start(f32[9,64,128]{2,1,0:T(8,128)S(1)} %multiply_add_fusion.15), channel_id=1, source_target_pairs={{0,4},{2,6},{4,8},{6,10},{8,12},{10,14},{12,16},{14,18},{16,20},{1... | collective-permute-start | bytes 884744 | tf_op jit(solution)/shard_map/ppermute | solution.py:298
  42.9 13.8 %collective-permute-start.9 = (f32[9,64,128]{2,1,0:T(8,128)S(1)}, f32[9,64,128]{2,1,0:T(8,128)S(1)}, u32[]{:S(2)}, u32[]{:S(2)}) collective-permute-start(f32[9,64,128]{2,1,0:T(8,128)S(1)} %multiply_add_fusion.9), channel_id=1, source_target_pairs={{4,0},{6,2},{8,4},{10,6},{12,8},{14,10},{16,12},{18,14},{20,16},{2... | collective-permute-start | bytes 884744 | tf_op jit(solution)/shard_map/ppermute | solution.py:299
  46.4 69.8 %collective-permute-start.14 = (f32[4,12,64,128]{3,2,1,0:T(8,128)S(1)}, f32[4,12,64,128]{3,2,1,0:T(8,128)S(1)}, u32[]{:S(2)}, u32[]{:S(2)}) collective-permute-start(f32[4,12,64,128]{3,2,1,0:T(8,128)S(1)} %fusion.1), channel_id=1, source_target_pairs={{0,1},{1,0},{2,3},{3,2},{4,5},{5,4},{6,7},{7,6},{8,9},{9,8},{10,11... | collective-permute-start | bytes 4718600 | tf_op jit(solution)/shard_map/ppermute | solution.py:335
  49.4 10.1 %collective-permute-start.4 = (f32[9,64,128]{2,1,0:T(8,128)S(1)}, f32[9,64,128]{2,1,0:T(8,128)S(1)}, u32[]{:S(2)}, u32[]{:S(2)}) collective-permute-start(f32[9,64,128]{2,1,0:T(8,128)S(1)} %multiply_add_fusion.14), channel_id=1, source_target_pairs={{0,8},{2,10},{4,12},{6,14},{8,16},{10,18},{12,20},{14,22},{16,24},... | collective-permute-start | bytes 884744 | tf_op jit(solution)/shard_map/ppermute | solution.py:298
  56.8 20.2 %collective-permute-start.10 = (f32[9,64,128]{2,1,0:T(8,128)S(1)}, f32[9,64,128]{2,1,0:T(8,128)S(1)}, u32[]{:S(2)}, u32[]{:S(2)}) collective-permute-start(f32[9,64,128]{2,1,0:T(8,128)S(1)} %multiply_add_fusion.8), channel_id=1, source_target_pairs={{8,0},{10,2},{12,4},{14,6},{16,8},{18,10},{20,12},{22,14},{24,16},... | collective-permute-start | bytes 884744 | tf_op jit(solution)/shard_map/ppermute | solution.py:299
  59.6 19.5 %collective-permute-start.5 = (f32[9,64,128]{2,1,0:T(8,128)S(1)}, f32[9,64,128]{2,1,0:T(8,128)S(1)}, u32[]{:S(2)}, u32[]{:S(2)}) collective-permute-start(f32[9,64,128]{2,1,0:T(8,128)S(1)} %multiply_add_fusion.13), channel_id=1, source_target_pairs={{0,16},{2,18},{4,20},{6,22},{8,24},{10,26},{12,28},{14,30},{16,32}... | collective-permute-start | bytes 884744 | tf_op jit(solution)/shard_map/ppermute | solution.py:298
  77.1 11.1 %collective-permute-start.11 = (f32[9,64,128]{2,1,0:T(8,128)S(1)}, f32[9,64,128]{2,1,0:T(8,128)S(1)}, u32[]{:S(2)}, u32[]{:S(2)}) collective-permute-start(f32[9,64,128]{2,1,0:T(8,128)S(1)} %multiply_add_fusion.7), channel_id=1, source_target_pairs={{16,0},{18,2},{20,4},{22,6},{24,8},{26,10},{28,12},{30,14},{32,16}... | collective-permute-start | bytes 884744 | tf_op jit(solution)/shard_map/ppermute | solution.py:299
  79.1 10.5 %collective-permute-start.6 = (f32[9,64,128]{2,1,0:T(8,128)S(1)}, f32[9,64,128]{2,1,0:T(8,128)S(1)}, u32[]{:S(2)}, u32[]{:S(2)}) collective-permute-start(f32[9,64,128]{2,1,0:T(8,128)S(1)} %multiply_add_fusion.12), channel_id=1, source_target_pairs={{0,32},{2,34},{4,36},{6,38},{8,40},{10,42},{12,44},{14,46},{16,48}... | collective-permute-start | bytes 884744 | tf_op jit(solution)/shard_map/ppermute | solution.py:298
  88.3 11.1 %collective-permute-start.12 = (f32[9,64,128]{2,1,0:T(8,128)S(1)}, f32[9,64,128]{2,1,0:T(8,128)S(1)}, u32[]{:S(2)}, u32[]{:S(2)}) collective-permute-start(f32[9,64,128]{2,1,0:T(8,128)S(1)} %multiply_add_fusion.6), channel_id=1, source_target_pairs={{32,0},{34,2},{36,4},{38,6},{40,8},{42,10},{44,12},{46,14},{48,16}... | collective-permute-start | bytes 884744 | tf_op jit(solution)/shard_map/ppermute | solution.py:299
  89.8 11.2 %collective-permute-start.7 = (f32[9,64,128]{2,1,0:T(8,128)S(1)}, f32[9,64,128]{2,1,0:T(8,128)S(1)}, u32[]{:S(2)}, u32[]{:S(2)}) collective-permute-start(f32[9,64,128]{2,1,0:T(8,128)S(1)} %multiply_add_fusion.11), channel_id=1, source_target_pairs={{0,64},{2,66},{4,68},{6,70},{8,72},{10,74},{12,76},{14,78},{16,80}... | collective-permute-start | bytes 884744 | tf_op jit(solution)/shard_map/ppermute | solution.py:298
  99.5 10.1 %collective-permute-start.13 = (f32[9,64,128]{2,1,0:T(8,128)S(1)}, f32[9,64,128]{2,1,0:T(8,128)S(1)}, u32[]{:S(2)}, u32[]{:S(2)}) collective-permute-start(f32[9,64,128]{2,1,0:T(8,128)S(1)} %multiply_add_fusion.5), channel_id=1, source_target_pairs={{64,0},{66,2},{68,4},{70,6},{72,8},{74,10},{76,12},{78,14},{80,16}... | collective-permute-start | bytes 884744 | tf_op jit(solution)/shard_map/ppermute | solution.py:299
  120.8 10.1 %collective-permute-start.15 = (f32[5,64,128]{2,1,0:T(8,128)S(1)}, f32[5,64,128]{2,1,0:T(8,128)S(1)}, u32[]{:S(2)}, u32[]{:S(2)}) collective-permute-start(f32[5,64,128]{2,1,0:T(8,128)S(1)} %get-tuple-element.73), channel_id=1, source_target_pairs={{0,2},{2,4},{4,6},{6,8},{8,10},{10,12},{12,14},{14,16},{16,18},{18... | collective-permute-start | bytes 491528 | tf_op jit(solution)/shard_map/ppermute | solution.py:298
  128.7 65.1 %collective-permute-start.27 = (f32[5,8,64,128]{3,2,1,0:T(8,128)S(1)}, f32[5,8,64,128]{3,2,1,0:T(8,128)S(1)}, u32[]{:S(2)}, u32[]{:S(2)}) collective-permute-start(f32[5,8,64,128]{3,2,1,0:T(8,128)S(1)} %fusion.34), channel_id=1, source_target_pairs={{0,1},{1,0},{2,3},{3,2},{4,5},{5,4},{6,7},{7,6},{8,9},{9,8},{10,11... | collective-permute-start | bytes 3932168 | tf_op jit(solution)/shard_map/ppermute | solution.py:335
  133.2 12.2 %collective-permute-start.16 = (f32[5,64,128]{2,1,0:T(8,128)S(1)}, f32[5,64,128]{2,1,0:T(8,128)S(1)}, u32[]{:S(2)}, u32[]{:S(2)}) collective-permute-start(f32[5,64,128]{2,1,0:T(8,128)S(1)} %get-tuple-element.71), channel_id=1, source_target_pairs={{0,4},{2,6},{4,8},{6,10},{8,12},{10,14},{12,16},{14,18},{16,20},{1... | collective-permute-start | bytes 491528 | tf_op jit(solution)/shard_map/ppermute | solution.py:298
  139.5 12.7 %collective-permute-start.22 = (f32[5,64,128]{2,1,0:T(8,128)S(1)}, f32[5,64,128]{2,1,0:T(8,128)S(1)}, u32[]{:S(2)}, u32[]{:S(2)}) collective-permute-start(f32[5,64,128]{2,1,0:T(8,128)S(1)} %get-tuple-element.72), channel_id=1, source_target_pairs={{4,0},{6,2},{8,4},{10,6},{12,8},{14,10},{16,12},{18,14},{20,16},{2... | collective-permute-start | bytes 491528 | tf_op jit(solution)/shard_map/ppermute | solution.py:299
  145.5 10.7 %collective-permute-start.17 = (f32[5,64,128]{2,1,0:T(8,128)S(1)}, f32[5,64,128]{2,1,0:T(8,128)S(1)}, u32[]{:S(2)}, u32[]{:S(2)}) collective-permute-start(f32[5,64,128]{2,1,0:T(8,128)S(1)} %multiply_add_fusion.27), channel_id=1, source_target_pairs={{0,8},{2,10},{4,12},{6,14},{8,16},{10,18},{12,20},{14,22},{16,24},... | collective-permute-start | bytes 491528 | tf_op jit(solution)/shard_map/ppermute | solution.py:298
  152.3 13.0 %collective-permute-start.23 = (f32[5,64,128]{2,1,0:T(8,128)S(1)}, f32[5,64,128]{2,1,0:T(8,128)S(1)}, u32[]{:S(2)}, u32[]{:S(2)}) collective-permute-start(f32[5,64,128]{2,1,0:T(8,128)S(1)} %multiply_add_fusion.21), channel_id=1, source_target_pairs={{8,0},{10,2},{12,4},{14,6},{16,8},{18,10},{20,12},{22,14},{24,16},... | collective-permute-start | bytes 491528 | tf_op jit(solution)/shard_map/ppermute | solution.py:299
  156.3 11.1 %collective-permute-start.18 = (f32[5,64,128]{2,1,0:T(8,128)S(1)}, f32[5,64,128]{2,1,0:T(8,128)S(1)}, u32[]{:S(2)}, u32[]{:S(2)}) collective-permute-start(f32[5,64,128]{2,1,0:T(8,128)S(1)} %multiply_add_fusion.26), channel_id=1, source_target_pairs={{0,16},{2,18},{4,20},{6,22},{8,24},{10,26},{12,28},{14,30},{16,32}... | collective-permute-start | bytes 491528 | tf_op jit(solution)/shard_map/ppermute | solution.py:298
  175.1 9.8 %collective-permute-start.25 = (f32[5,64,128]{2,1,0:T(8,128)S(1)}, f32[5,64,128]{2,1,0:T(8,128)S(1)}, u32[]{:S(2)}, u32[]{:S(2)}) collective-permute-start(f32[5,64,128]{2,1,0:T(8,128)S(1)} %multiply_add_fusion.19), channel_id=1, source_target_pairs={{32,0},{34,2},{36,4},{38,6},{40,8},{42,10},{44,12},{46,14},{48,16}... | collective-permute-start | bytes 491528 | tf_op jit(solution)/shard_map/ppermute | solution.py:299
  176.5 10.2 %collective-permute-start.20 = (f32[5,64,128]{2,1,0:T(8,128)S(1)}, f32[5,64,128]{2,1,0:T(8,128)S(1)}, u32[]{:S(2)}, u32[]{:S(2)}) collective-permute-start(f32[5,64,128]{2,1,0:T(8,128)S(1)} %multiply_add_fusion.24), channel_id=1, source_target_pairs={{0,64},{2,66},{4,68},{6,70},{8,72},{10,74},{12,76},{14,78},{16,80}... | collective-permute-start | bytes 491528 | tf_op jit(solution)/shard_map/ppermute | solution.py:298
  (39 other events, 150.5 us)

commit v10 on v7

--- a/solution.py
+++ b/solution.py
@@ -220,7 +220,12 @@
         for (kind, _), extra in zip(kinds_sizes, extras)
     ]
     groups = [
-        (bank.add(table[0]), bank.add(table[1]), bank.add(table[2]), table[1].shape[1])
+        (
+            bank.add(table[0].transpose(0, 2, 1)),
+            bank.add(table[1]),
+            bank.add(table[2]),
+            table[1].shape[1],
+        )
         for table in tables
     ]
     blocks = points // rows
@@ -245,15 +250,15 @@
     count = lax.axis_size("gy")
     groups, rounds = plan
 
-    def taps(padded, combine):
+    def taps(padded, by_tap):
         summed = None
-        for tap in range(rows + 2 * pad):
-            term = combine[:, tap, None, None] * padded[:, None, tap]
+        for tap in range(by_tap.shape[0]):
+            term = by_tap[tap][:, None, None] * padded[:, None, tap]
             summed = term if summed is None else summed + term
         return summed
 
     partials = [
-        taps(padded, bank.get(handles[0])[handles[3] :])
+        taps(padded, bank.get(handles[0])[:, handles[3] :])
         for padded, handles in zip(padded_groups, groups)
     ]
     sizes = [padded.shape[0] for padded in padded_groups]
@@ -272,7 +277,7 @@
     results = []
     first = 0
     for padded, handles, size in zip(padded_groups, groups, sizes):
-        local = taps(padded, bank.get(handles[0])[: handles[3]])
+        local = taps(padded, bank.get(handles[0])[:, : handles[3]])
         rise_gain = bank.get(handles[1])
         fall_gain = bank.get(handles[2])
         results.append(

time: 195 us -> 195 us (level)
    slice x17 -> x3, local copies, waits for them, and re-layouts: 6.41 us -> 2.31 us  [get(): return self.row[start:start + int(np.prod(shape))].reshape(shape)]
    mul x4 -> x9, local copies, waits for them, and re-layouts: 0.39 us -> 3.07 us  [taps(): term = by_tap[tap][:, None, None] * padded[:, None, tap]]
where the time goes in v10:
time: 195 us; the launch traced here: 194 us
  starting transfers between devices  85.9 us (44%)
  waiting for transfers between devices  67.3 us (35%)
  other arithmetic  14.7 us (8%)
  local copies, waits for them, and re-layouts  13.8 us (7%)
  matrix products  9.96 us (5%)
  between operations  2.07 us (1%)
    ppermute x12, starting transfers between devices, wall_apply(): from_below = lax.ppermute(rise, 'gy', up_pairs)  59.2 us
    ppermute x12, waiting for transfers between devices, wall_apply(): from_above = lax.ppermute(fall, 'gy', down_pairs)  58.2 us
    ppermute x12, starting transfers between devices, wall_apply(): from_above = lax.ppermute(fall, 'gy', down_pairs)  20.7 us
    ppermute x12, waiting for transfers between devices, wall_apply(): from_below = lax.ppermute(rise, 'gy', up_pairs)  8.32 us
    add x2, other arithmetic, wall_apply(): local + rise_gain[None, :, None, None] * rise[first:first + size, None]  4.9 us
    dot_general x2, matrix products, span_slope(): jnp.einsum('fyzx,zw->fywx', other, other_block, precision=HIGHEST)  4.43 us
  transfers between devices with their start and end apart: 28, of which 16 were waited for; matrix products, arithmetic and copies ran while one was open for 13% of the time, Pallas kernels for 0%

profile of v10, /device:TPU:28, one launch (start us, length us, event | category | flops | bytes accessed | tf_op | source)
XLA Modules:
  0.0 193.8 jit_solution(16328025791013682165)
XLA Ops:
  3.0 3.1 %collective-permute-start = (f32[5,3,64,128]{3,2,1,0:T(8,128)}, f32[5,3,64,128]{3,2,1,0:T(8,128)S(1)}, u32[]{:S(2)}, u32[]{:S(2)}) collective-permute-start(f32[5,3,64,128]{3,2,1,0:T(8,128)} %get-tuple-element.51), channel_id=1, source_target_pairs={{0,2},{2,4},{4,6},{6,8},{8,10},{10,12},{12,14},{14,16},{16,18},{18... | collective-permute-start | bytes 1474568 | tf_op jit(solution)/shard_map/ppermute | solution.py:296
  6.1 2.7 %collective-permute-start.1 = (f32[5,3,64,128]{3,2,1,0:T(8,128)}, f32[5,3,64,128]{3,2,1,0:T(8,128)S(1)}, u32[]{:S(2)}, u32[]{:S(2)}) collective-permute-start(f32[5,3,64,128]{3,2,1,0:T(8,128)} %get-tuple-element.52), channel_id=1, source_target_pairs={{2,0},{4,2},{6,4},{8,6},{10,8},{12,10},{14,12},{16,14},{18,16},{20... | collective-permute-start | bytes 1474568 | tf_op jit(solution)/shard_map/ppermute | solution.py:297
  23.5 7.6 %collective-permute-start.2 = (f32[9,64,128]{2,1,0:T(8,128)S(1)}, f32[9,64,128]{2,1,0:T(8,128)S(1)}, u32[]{:S(2)}, u32[]{:S(2)}) collective-permute-start(f32[9,64,128]{2,1,0:T(8,128)S(1)} %pad_maximum_fusion.7), channel_id=1, source_target_pairs={{0,2},{2,4},{4,6},{6,8},{8,10},{10,12},{12,14},{14,16},{16,18},{18... | collective-permute-start | bytes 884744 | tf_op jit(solution)/shard_map/ppermute | solution.py:272
  36.3 8.5 %collective-permute-start.3 = (f32[9,64,128]{2,1,0:T(8,128)S(1)}, f32[9,64,128]{2,1,0:T(8,128)S(1)}, u32[]{:S(2)}, u32[]{:S(2)}) collective-permute-start(f32[9,64,128]{2,1,0:T(8,128)S(1)} %multiply_add_fusion.15), channel_id=1, source_target_pairs={{0,4},{2,6},{4,8},{6,10},{8,12},{10,14},{12,16},{14,18},{16,20},{1... | collective-permute-start | bytes 884744 | tf_op jit(solution)/shard_map/ppermute | solution.py:272
  46.9 5.3 %collective-permute-done.3 = f32[9,64,128]{2,1,0:T(8,128)S(1)} collective-permute-done((f32[9,64,128]{2,1,0:T(8,128)S(1)}, f32[9,64,128]{2,1,0:T(8,128)S(1)}, u32[]{:S(2)}, u32[]{:S(2)}) %collective-permute-start.3) | collective-permute-done | bytes 294944 | tf_op jit(solution)/shard_map/ppermute | solution.py:272
  52.3 2.7 %collective-permute-start.4 = (f32[9,64,128]{2,1,0:T(8,128)S(1)}, f32[9,64,128]{2,1,0:T(8,128)S(1)}, u32[]{:S(2)}, u32[]{:S(2)}) collective-permute-start(f32[9,64,128]{2,1,0:T(8,128)S(1)} %multiply_add_fusion.14), channel_id=1, source_target_pairs={{0,8},{2,10},{4,12},{6,14},{8,16},{10,18},{12,20},{14,22},{16,24},... | collective-permute-start | bytes 884744 | tf_op jit(solution)/shard_map/ppermute | solution.py:272
  55.0 3.3 %collective-permute-done.9 = f32[9,64,128]{2,1,0:T(8,128)S(1)} collective-permute-done((f32[9,64,128]{2,1,0:T(8,128)S(1)}, f32[9,64,128]{2,1,0:T(8,128)S(1)}, u32[]{:S(2)}, u32[]{:S(2)}) %collective-permute-start.9) | collective-permute-done | bytes 294944 | tf_op jit(solution)/shard_map/ppermute | solution.py:273
  61.1 2.2 %collective-permute-start.5 = (f32[9,64,128]{2,1,0:T(8,128)S(1)}, f32[9,64,128]{2,1,0:T(8,128)S(1)}, u32[]{:S(2)}, u32[]{:S(2)}) collective-permute-start(f32[9,64,128]{2,1,0:T(8,128)S(1)} %multiply_add_fusion.13), channel_id=1, source_target_pairs={{0,16},{2,18},{4,20},{6,22},{8,24},{10,26},{12,28},{14,30},{16,32}... | collective-permute-start | bytes 884744 | tf_op jit(solution)/shard_map/ppermute | solution.py:272
  63.3 14.7 %collective-permute-done.10 = f32[9,64,128]{2,1,0:T(8,128)S(1)} collective-permute-done((f32[9,64,128]{2,1,0:T(8,128)S(1)}, f32[9,64,128]{2,1,0:T(8,128)S(1)}, u32[]{:S(2)}, u32[]{:S(2)}) %collective-permute-start.10) | collective-permute-done | bytes 294944 | tf_op jit(solution)/shard_map/ppermute | solution.py:273
  80.2 3.8 %collective-permute-start.6 = (f32[9,64,128]{2,1,0:T(8,128)S(1)}, f32[9,64,128]{2,1,0:T(8,128)S(1)}, u32[]{:S(2)}, u32[]{:S(2)}) collective-permute-start(f32[9,64,128]{2,1,0:T(8,128)S(1)} %multiply_add_fusion.12), channel_id=1, source_target_pairs={{0,32},{2,34},{4,36},{6,38},{8,40},{10,42},{12,44},{14,46},{16,48}... | collective-permute-start | bytes 884744 | tf_op jit(solution)/shard_map/ppermute | solution.py:272
  84.1 5.1 %collective-permute-done.11 = f32[9,64,128]{2,1,0:T(8,128)S(1)} collective-permute-done((f32[9,64,128]{2,1,0:T(8,128)S(1)}, f32[9,64,128]{2,1,0:T(8,128)S(1)}, u32[]{:S(2)}, u32[]{:S(2)}) %collective-permute-start.11) | collective-permute-done | bytes 294944 | tf_op jit(solution)/shard_map/ppermute | solution.py:273
  90.7 6.6 %collective-permute-start.7 = (f32[9,64,128]{2,1,0:T(8,128)S(1)}, f32[9,64,128]{2,1,0:T(8,128)S(1)}, u32[]{:S(2)}, u32[]{:S(2)}) collective-permute-start(f32[9,64,128]{2,1,0:T(8,128)S(1)} %multiply_add_fusion.11), channel_id=1, source_target_pairs={{0,64},{2,66},{4,68},{6,70},{8,72},{10,74},{12,76},{14,78},{16,80}... | collective-permute-start | bytes 884744 | tf_op jit(solution)/shard_map/ppermute | solution.py:272
  103.6 5.2 %collective-permute-done.13 = f32[9,64,128]{2,1,0:T(8,128)S(1)} collective-permute-done((f32[9,64,128]{2,1,0:T(8,128)S(1)}, f32[9,64,128]{2,1,0:T(8,128)S(1)}, u32[]{:S(2)}, u32[]{:S(2)}) %collective-permute-start.13) | collective-permute-done | bytes 294944 | tf_op jit(solution)/shard_map/ppermute | solution.py:273
  113.0 5.9 %collective-permute-start.15 = (f32[5,64,128]{2,1,0:T(8,128)S(1)}, f32[5,64,128]{2,1,0:T(8,128)S(1)}, u32[]{:S(2)}, u32[]{:S(2)}) collective-permute-start(f32[5,64,128]{2,1,0:T(8,128)S(1)} %get-tuple-element.63), channel_id=1, source_target_pairs={{0,2},{2,4},{4,6},{6,8},{8,10},{10,12},{12,14},{14,16},{16,18},{18... | collective-permute-start | bytes 491528 | tf_op jit(solution)/shard_map/ppermute | solution.py:272
  122.9 2.9 %multiply_add_fusion.1 = f32[5,8,64,128]{3,2,1,0:T(8,128)} fusion(f32[5,64,128]{2,1,0:T(8,128)S(1)} %slice-done.1, f32[8]{0:T(128)S(1)} %copy-done.40, f32[5,64,128]{2,1,0:T(8,128)S(1)} %slice-done, f32[8]{0:T(128)S(1)} %copy-done.39, f32[5,64,128]{2,1,0:T(8,128)S(1)} %get-tuple-element.59, f32[8]{0:T(128)S(1)} %copy-done.26, ...), kind=kLoop, calls=%fused_computation.43 | loop fusion | flops 10158080 | bytes 3932672 | tf_op jit(solution)/shard_map/add | solution.py:284
  127.1 7.5 %collective-permute-start.16 = (f32[5,64,128]{2,1,0:T(8,128)S(1)}, f32[5,64,128]{2,1,0:T(8,128)S(1)}, u32[]{:S(2)}, u32[]{:S(2)}) collective-permute-start(f32[5,64,128]{2,1,0:T(8,128)S(1)} %get-tuple-element.61), channel_id=1, source_target_pairs={{0,4},{2,6},{4,8},{6,10},{8,12},{10,14},{12,16},{14,18},{16,20},{1... | collective-permute-start | bytes 491528 | tf_op jit(solution)/shard_map/ppermute | solution.py:272
  138.6 3.2 %collective-permute-start.17 = (f32[5,64,128]{2,1,0:T(8,128)S(1)}, f32[5,64,128]{2,1,0:T(8,128)S(1)}, u32[]{:S(2)}, u32[]{:S(2)}) collective-permute-start(f32[5,64,128]{2,1,0:T(8,128)S(1)} %multiply_add_fusion.27), channel_id=1, source_target_pairs={{0,8},{2,10},{4,12},{6,14},{8,16},{10,18},{12,20},{14,22},{16,24},... | collective-permute-start | bytes 491528 | tf_op jit(solution)/shard_map/ppermute | solution.py:272
  141.8 6.9 %collective-permute-done.22 = f32[5,64,128]{2,1,0:T(8,128)S(1)} collective-permute-done((f32[5,64,128]{2,1,0:T(8,128)S(1)}, f32[5,64,128]{2,1,0:T(8,128)S(1)}, u32[]{:S(2)}, u32[]{:S(2)}) %collective-permute-start.22) | collective-permute-done | bytes 163872 | tf_op jit(solution)/shard_map/ppermute | solution.py:273
  152.7 9.1 %collective-permute-done.23 = f32[5,64,128]{2,1,0:T(8,128)S(1)} collective-permute-done((f32[5,64,128]{2,1,0:T(8,128)S(1)}, f32[5,64,128]{2,1,0:T(8,128)S(1)}, u32[]{:S(2)}, u32[]{:S(2)}) %collective-permute-start.23) | collective-permute-done | bytes 163872 | tf_op jit(solution)/shard_map/ppermute | solution.py:273
  164.0 2.9 %collective-permute-start.19 = (f32[5,64,128]{2,1,0:T(8,128)S(1)}, f32[5,64,128]{2,1,0:T(8,128)S(1)}, u32[]{:S(2)}, u32[]{:S(2)}) collective-permute-start(f32[5,64,128]{2,1,0:T(8,128)S(1)} %multiply_add_fusion.25), channel_id=1, source_target_pairs={{0,32},{2,34},{4,36},{6,38},{8,40},{10,42},{12,44},{14,46},{16,48}... | collective-permute-start | bytes 491528 | tf_op jit(solution)/shard_map/ppermute | solution.py:272
  166.9 4.6 %collective-permute-done.24 = f32[5,64,128]{2,1,0:T(8,128)S(1)} collective-permute-done((f32[5,64,128]{2,1,0:T(8,128)S(1)}, f32[5,64,128]{2,1,0:T(8,128)S(1)}, u32[]{:S(2)}, u32[]{:S(2)}) %collective-permute-start.24) | collective-permute-done | bytes 163872 | tf_op jit(solution)/shard_map/ppermute | solution.py:273
  172.9 6.4 %collective-permute-start.20 = (f32[5,64,128]{2,1,0:T(8,128)S(1)}, f32[5,64,128]{2,1,0:T(8,128)S(1)}, u32[]{:S(2)}, u32[]{:S(2)}) collective-permute-start(f32[5,64,128]{2,1,0:T(8,128)S(1)} %multiply_add_fusion.24), channel_id=1, source_target_pairs={{0,64},{2,66},{4,68},{6,70},{8,72},{10,74},{12,76},{14,78},{16,80}... | collective-permute-start | bytes 491528 | tf_op jit(solution)/shard_map/ppermute | solution.py:272
  182.2 7.1 %collective-permute-done.26 = f32[5,64,128]{2,1,0:T(8,128)S(1)} collective-permute-done((f32[5,64,128]{2,1,0:T(8,128)S(1)}, f32[5,64,128]{2,1,0:T(8,128)S(1)}, u32[]{:S(2)}, u32[]{:S(2)}) %collective-permute-start.26) | collective-permute-done | bytes 163872 | tf_op jit(solution)/shard_map/ppermute | solution.py:273
  189.5 2.9 %fusion.4 = f32[5,8,64,128]{3,2,1,0:T(8,128)S(1)} fusion(f32[5,8,128,64]{2,3,1,0:T(8,128)S(1)} %fusion.89, f32[5,8,64,128]{3,2,1,0:T(8,128)S(1)} %collective-permute-done.27, f32[64,64,1,1]{0,1,3,2:T(8,128)S(1)} %copy-done.9, f32[5,8,64,128]{3,2,1,0:T(8,128)S(1)} %fusion.88, f32[5,64,128]{2,1,0:T(8,128)S(1)} %multiply_add_fusion.17, f32[8]{0:T(128)S(1)} %copy-done.54, ...), kind=kOutput, calls=%fused_computation.39 | convolution fusion | flops 261816320 | bytes 7553472 | tf_op jit(solution)/shard_map/fyzx,zw->fywx/dot_general | solution.py:310
  (237 shorter events, 61.7 us)
Async XLA Ops:
  3.0 17.1 %collective-permute-start = (f32[5,3,64,128]{3,2,1,0:T(8,128)}, f32[5,3,64,128]{3,2,1,0:T(8,128)S(1)}, u32[]{:S(2)}, u32[]{:S(2)}) collective-permute-start(f32[5,3,64,128]{3,2,1,0:T(8,128)} %get-tuple-element.51), channel_id=1, source_target_pairs={{0,2},{2,4},{4,6},{6,8},{8,10},{10,12},{12,14},{14,16},{16,18},{18... | collective-permute-start | bytes 1474568 | tf_op jit(solution)/shard_map/ppermute | solution.py:296
  6.1 14.8 %collective-permute-start.1 = (f32[5,3,64,128]{3,2,1,0:T(8,128)}, f32[5,3,64,128]{3,2,1,0:T(8,128)S(1)}, u32[]{:S(2)}, u32[]{:S(2)}) collective-permute-start(f32[5,3,64,128]{3,2,1,0:T(8,128)} %get-tuple-element.52), channel_id=1, source_target_pairs={{2,0},{4,2},{6,4},{8,6},{10,8},{12,10},{14,12},{16,14},{18,16},{20... | collective-permute-start | bytes 1474568 | tf_op jit(solution)/shard_map/ppermute | solution.py:297
  23.5 12.7 %collective-permute-start.2 = (f32[9,64,128]{2,1,0:T(8,128)S(1)}, f32[9,64,128]{2,1,0:T(8,128)S(1)}, u32[]{:S(2)}, u32[]{:S(2)}) collective-permute-start(f32[9,64,128]{2,1,0:T(8,128)S(1)} %pad_maximum_fusion.7), channel_id=1, source_target_pairs={{0,2},{2,4},{4,6},{6,8},{8,10},{10,12},{12,14},{14,16},{16,18},{18... | collective-permute-start | bytes 884744 | tf_op jit(solution)/shard_map/ppermute | solution.py:272
  31.2 13.6 %collective-permute-start.8 = (f32[9,64,128]{2,1,0:T(8,128)S(1)}, f32[9,64,128]{2,1,0:T(8,128)S(1)}, u32[]{:S(2)}, u32[]{:S(2)}) collective-permute-start(f32[9,64,128]{2,1,0:T(8,128)S(1)} %pad_maximum_fusion.8), channel_id=1, source_target_pairs={{2,0},{4,2},{6,4},{8,6},{10,8},{12,10},{14,12},{16,14},{18,16},{20... | collective-permute-start | bytes 884744 | tf_op jit(solution)/shard_map/ppermute | solution.py:273
  33.1 67.0 %collective-permute-start.14 = (f32[4,12,64,128]{3,2,1,0:T(8,128)S(1)}, f32[4,12,64,128]{3,2,1,0:T(8,128)S(1)}, u32[]{:S(2)}, u32[]{:S(2)}) collective-permute-start(f32[4,12,64,128]{3,2,1,0:T(8,128)S(1)} %fusion.1), channel_id=1, source_target_pairs={{0,1},{1,0},{2,3},{3,2},{4,5},{5,4},{6,7},{7,6},{8,9},{9,8},{10,11... | collective-permute-start | bytes 4718600 | tf_op jit(solution)/shard_map/ppermute | solution.py:309
  36.3 15.9 %collective-permute-start.3 = (f32[9,64,128]{2,1,0:T(8,128)S(1)}, f32[9,64,128]{2,1,0:T(8,128)S(1)}, u32[]{:S(2)}, u32[]{:S(2)}) collective-permute-start(f32[9,64,128]{2,1,0:T(8,128)S(1)} %multiply_add_fusion.15), channel_id=1, source_target_pairs={{0,4},{2,6},{4,8},{6,10},{8,12},{10,14},{12,16},{14,18},{16,20},{1... | collective-permute-start | bytes 884744 | tf_op jit(solution)/shard_map/ppermute | solution.py:272
  44.9 13.4 %collective-permute-start.9 = (f32[9,64,128]{2,1,0:T(8,128)S(1)}, f32[9,64,128]{2,1,0:T(8,128)S(1)}, u32[]{:S(2)}, u32[]{:S(2)}) collective-permute-start(f32[9,64,128]{2,1,0:T(8,128)S(1)} %multiply_add_fusion.9), channel_id=1, source_target_pairs={{4,0},{6,2},{8,4},{10,6},{12,8},{14,10},{16,12},{18,14},{20,16},{2... | collective-permute-start | bytes 884744 | tf_op jit(solution)/shard_map/ppermute | solution.py:273
  58.4 19.6 %collective-permute-start.10 = (f32[9,64,128]{2,1,0:T(8,128)S(1)}, f32[9,64,128]{2,1,0:T(8,128)S(1)}, u32[]{:S(2)}, u32[]{:S(2)}) collective-permute-start(f32[9,64,128]{2,1,0:T(8,128)S(1)} %multiply_add_fusion.8), channel_id=1, source_target_pairs={{8,0},{10,2},{12,4},{14,6},{16,8},{18,10},{20,12},{22,14},{24,16},... | collective-permute-start | bytes 884744 | tf_op jit(solution)/shard_map/ppermute | solution.py:273
  61.1 19.1 %collective-permute-start.5 = (f32[9,64,128]{2,1,0:T(8,128)S(1)}, f32[9,64,128]{2,1,0:T(8,128)S(1)}, u32[]{:S(2)}, u32[]{:S(2)}) collective-permute-start(f32[9,64,128]{2,1,0:T(8,128)S(1)} %multiply_add_fusion.13), channel_id=1, source_target_pairs={{0,16},{2,18},{4,20},{6,22},{8,24},{10,26},{12,28},{14,30},{16,32}... | collective-permute-start | bytes 884744 | tf_op jit(solution)/shard_map/ppermute | solution.py:272
  78.1 11.0 %collective-permute-start.11 = (f32[9,64,128]{2,1,0:T(8,128)S(1)}, f32[9,64,128]{2,1,0:T(8,128)S(1)}, u32[]{:S(2)}, u32[]{:S(2)}) collective-permute-start(f32[9,64,128]{2,1,0:T(8,128)S(1)} %multiply_add_fusion.7), channel_id=1, source_target_pairs={{16,0},{18,2},{20,4},{22,6},{24,8},{26,10},{28,12},{30,14},{32,16}... | collective-permute-start | bytes 884744 | tf_op jit(solution)/shard_map/ppermute | solution.py:273
  80.2 10.4 %collective-permute-start.6 = (f32[9,64,128]{2,1,0:T(8,128)S(1)}, f32[9,64,128]{2,1,0:T(8,128)S(1)}, u32[]{:S(2)}, u32[]{:S(2)}) collective-permute-start(f32[9,64,128]{2,1,0:T(8,128)S(1)} %multiply_add_fusion.12), channel_id=1, source_target_pairs={{0,32},{2,34},{4,36},{6,38},{8,40},{10,42},{12,44},{14,46},{16,48}... | collective-permute-start | bytes 884744 | tf_op jit(solution)/shard_map/ppermute | solution.py:272
  89.3 9.3 %collective-permute-start.12 = (f32[9,64,128]{2,1,0:T(8,128)S(1)}, f32[9,64,128]{2,1,0:T(8,128)S(1)}, u32[]{:S(2)}, u32[]{:S(2)}) collective-permute-start(f32[9,64,128]{2,1,0:T(8,128)S(1)} %multiply_add_fusion.6), channel_id=1, source_target_pairs={{32,0},{34,2},{36,4},{38,6},{40,8},{42,10},{44,12},{46,14},{48,16}... | collective-permute-start | bytes 884744 | tf_op jit(solution)/shard_map/ppermute | solution.py:273
  90.7 12.7 %collective-permute-start.7 = (f32[9,64,128]{2,1,0:T(8,128)S(1)}, f32[9,64,128]{2,1,0:T(8,128)S(1)}, u32[]{:S(2)}, u32[]{:S(2)}) collective-permute-start(f32[9,64,128]{2,1,0:T(8,128)S(1)} %multiply_add_fusion.11), channel_id=1, source_target_pairs={{0,64},{2,66},{4,68},{6,70},{8,72},{10,74},{12,76},{14,78},{16,80}... | collective-permute-start | bytes 884744 | tf_op jit(solution)/shard_map/ppermute | solution.py:272
  98.6 10.1 %collective-permute-start.13 = (f32[9,64,128]{2,1,0:T(8,128)S(1)}, f32[9,64,128]{2,1,0:T(8,128)S(1)}, u32[]{:S(2)}, u32[]{:S(2)}) collective-permute-start(f32[9,64,128]{2,1,0:T(8,128)S(1)} %multiply_add_fusion.5), channel_id=1, source_target_pairs={{64,0},{66,2},{68,4},{70,6},{72,8},{74,10},{76,12},{78,14},{80,16}... | collective-permute-start | bytes 884744 | tf_op jit(solution)/shard_map/ppermute | solution.py:273
  113.0 14.0 %collective-permute-start.15 = (f32[5,64,128]{2,1,0:T(8,128)S(1)}, f32[5,64,128]{2,1,0:T(8,128)S(1)}, u32[]{:S(2)}, u32[]{:S(2)}) collective-permute-start(f32[5,64,128]{2,1,0:T(8,128)S(1)} %get-tuple-element.63), channel_id=1, source_target_pairs={{0,2},{2,4},{4,6},{6,8},{8,10},{10,12},{12,14},{14,16},{16,18},{18... | collective-permute-start | bytes 491528 | tf_op jit(solution)/shard_map/ppermute | solution.py:272
  121.7 67.7 %collective-permute-start.27 = (f32[5,8,64,128]{3,2,1,0:T(8,128)S(1)}, f32[5,8,64,128]{3,2,1,0:T(8,128)S(1)}, u32[]{:S(2)}, u32[]{:S(2)}) collective-permute-start(f32[5,8,64,128]{3,2,1,0:T(8,128)S(1)} %fusion.34), channel_id=1, source_target_pairs={{0,1},{1,0},{2,3},{3,2},{4,5},{5,4},{6,7},{7,6},{8,9},{9,8},{10,11... | collective-permute-start | bytes 3932168 | tf_op jit(solution)/shard_map/ppermute | solution.py:309
  127.1 11.4 %collective-permute-start.16 = (f32[5,64,128]{2,1,0:T(8,128)S(1)}, f32[5,64,128]{2,1,0:T(8,128)S(1)}, u32[]{:S(2)}, u32[]{:S(2)}) collective-permute-start(f32[5,64,128]{2,1,0:T(8,128)S(1)} %get-tuple-element.61), channel_id=1, source_target_pairs={{0,4},{2,6},{4,8},{6,10},{8,12},{10,14},{12,16},{14,18},{16,20},{1... | collective-permute-start | bytes 491528 | tf_op jit(solution)/shard_map/ppermute | solution.py:272
  135.9 12.7 %collective-permute-start.22 = (f32[5,64,128]{2,1,0:T(8,128)S(1)}, f32[5,64,128]{2,1,0:T(8,128)S(1)}, u32[]{:S(2)}, u32[]{:S(2)}) collective-permute-start(f32[5,64,128]{2,1,0:T(8,128)S(1)} %get-tuple-element.62), channel_id=1, source_target_pairs={{4,0},{6,2},{8,4},{10,6},{12,8},{14,10},{16,12},{18,14},{20,16},{2... | collective-permute-start | bytes 491528 | tf_op jit(solution)/shard_map/ppermute | solution.py:273
  138.6 12.1 %collective-permute-start.17 = (f32[5,64,128]{2,1,0:T(8,128)S(1)}, f32[5,64,128]{2,1,0:T(8,128)S(1)}, u32[]{:S(2)}, u32[]{:S(2)}) collective-permute-start(f32[5,64,128]{2,1,0:T(8,128)S(1)} %multiply_add_fusion.27), channel_id=1, source_target_pairs={{0,8},{2,10},{4,12},{6,14},{8,16},{10,18},{12,20},{14,22},{16,24},... | collective-permute-start | bytes 491528 | tf_op jit(solution)/shard_map/ppermute | solution.py:272
  148.7 13.0 %collective-permute-start.23 = (f32[5,64,128]{2,1,0:T(8,128)S(1)}, f32[5,64,128]{2,1,0:T(8,128)S(1)}, u32[]{:S(2)}, u32[]{:S(2)}) collective-permute-start(f32[5,64,128]{2,1,0:T(8,128)S(1)} %multiply_add_fusion.21), channel_id=1, source_target_pairs={{8,0},{10,2},{12,4},{14,6},{16,8},{18,10},{20,12},{22,14},{24,16},... | collective-permute-start | bytes 491528 | tf_op jit(solution)/shard_map/ppermute | solution.py:273
  150.8 13.0 %collective-permute-start.18 = (f32[5,64,128]{2,1,0:T(8,128)S(1)}, f32[5,64,128]{2,1,0:T(8,128)S(1)}, u32[]{:S(2)}, u32[]{:S(2)}) collective-permute-start(f32[5,64,128]{2,1,0:T(8,128)S(1)} %multiply_add_fusion.26), channel_id=1, source_target_pairs={{0,16},{2,18},{4,20},{6,22},{8,24},{10,26},{12,28},{14,30},{16,32}... | collective-permute-start | bytes 491528 | tf_op jit(solution)/shard_map/ppermute | solution.py:272
  161.8 9.6 %collective-permute-start.24 = (f32[5,64,128]{2,1,0:T(8,128)S(1)}, f32[5,64,128]{2,1,0:T(8,128)S(1)}, u32[]{:S(2)}, u32[]{:S(2)}) collective-permute-start(f32[5,64,128]{2,1,0:T(8,128)S(1)} %multiply_add_fusion.20), channel_id=1, source_target_pairs={{16,0},{18,2},{20,4},{22,6},{24,8},{26,10},{28,12},{30,14},{32,16}... | collective-permute-start | bytes 491528 | tf_op jit(solution)/shard_map/ppermute | solution.py:273
  171.5 8.9 %collective-permute-start.25 = (f32[5,64,128]{2,1,0:T(8,128)S(1)}, f32[5,64,128]{2,1,0:T(8,128)S(1)}, u32[]{:S(2)}, u32[]{:S(2)}) collective-permute-start(f32[5,64,128]{2,1,0:T(8,128)S(1)} %multiply_add_fusion.19), channel_id=1, source_target_pairs={{32,0},{34,2},{36,4},{38,6},{40,8},{42,10},{44,12},{46,14},{48,16}... | collective-permute-start | bytes 491528 | tf_op jit(solution)/shard_map/ppermute | solution.py:273
  172.9 9.2 %collective-permute-start.20 = (f32[5,64,128]{2,1,0:T(8,128)S(1)}, f32[5,64,128]{2,1,0:T(8,128)S(1)}, u32[]{:S(2)}, u32[]{:S(2)}) collective-permute-start(f32[5,64,128]{2,1,0:T(8,128)S(1)} %multiply_add_fusion.24), channel_id=1, source_target_pairs={{0,64},{2,66},{4,68},{6,70},{8,72},{10,74},{12,76},{14,78},{16,80}... | collective-permute-start | bytes 491528 | tf_op jit(solution)/shard_map/ppermute | solution.py:272
  (62 other events, 477.9 us)

commit v11 on v10

--- a/solution.py
+++ b/solution.py
@@ -15,6 +15,8 @@
 STREAM_STEP = 1.0
 SPAN_STEP = 0.5
 HIGHEST = lax.Precision.HIGHEST
+LEVEL_AXES = ("gx", "gm", "gz")
+WALL_AXES = ("gz", "gm", "gx")
 
 
 def slope_weights():
@@ -178,7 +180,7 @@
         radix = min(2, -(-blocks // stride))
         rounds.append((stride, list(range(1, radix))))
         stride *= radix
-    return rounds
+    return rounds[::-1]
 
 
 def scan_coefs(rise_step, fall_step, shift):
@@ -193,6 +195,41 @@
     return rise, fall
 
 
+def level_tables(rise_step, fall_step, sizes):
+    blocks = rise_step.shape[0]
+
+    def rise_weight(source, target):
+        return np.prod(rise_step[source + 1 : target + 1]) if source <= target else 0.0
+
+    def fall_weight(source, target):
+        return np.prod(fall_step[target:source]) if source >= target else 0.0
+
+    levels = []
+    stride = 1
+    for level, size in enumerate(sizes):
+        span = stride * size
+        rise_own = np.zeros((blocks, size))
+        rise_total = np.zeros((blocks, size))
+        fall_own = np.zeros((blocks, size))
+        fall_total = np.zeros((blocks, size))
+        for block in range(blocks):
+            base = block // span * span
+            mine = block // stride % size
+            last, first = base + span - 1, base
+            for member in range(size):
+                group_first = base + member * stride
+                group_last = group_first + stride - 1
+                if level == 0 or member < mine:
+                    rise_own[block, member] = rise_weight(group_last, block)
+                if level == 0 or member > mine:
+                    fall_own[block, member] = fall_weight(group_first, block)
+                rise_total[block, member] = rise_weight(group_last, last)
+                fall_total[block, member] = fall_weight(group_first, first)
+        levels.append((rise_own, rise_total, fall_own, fall_total))
+        stride = span
+    return levels
+
+
 class TableBank:
     def __init__(self):
         self.parts = []
@@ -214,7 +251,7 @@
         return self.row[start : start + int(np.prod(shape))].reshape(shape)
 
 
-def plan_wall(bank, kinds_sizes, points, rows, pad, extras):
+def plan_wall(bank, kinds_sizes, points, rows, pad, extras, sizes):
     tables = [
         wall_tables(kind, points, rows, pad, extra)
         for (kind, _), extra in zip(kinds_sizes, extras)
@@ -243,19 +280,58 @@
             )
             entries.append((shift, bank.add(rise), bank.add(fall)))
         rounds.append(entries)
-    return groups, rounds
+    return groups, rounds, sizes
+
+
+def plan_gathered(bank, kind, fields, points, rows, pad, sizes):
+    table = wall_tables(kind, points, rows, pad)
+    handles = (
+        bank.add(table[0].transpose(0, 2, 1)),
+        bank.add(table[1]),
+        bank.add(table[2]),
+        table[1].shape[1],
+    )
+    levels = [
+        [bank.add(np.repeat(part[:, :, None], fields, 2)) for part in level]
+        for level in level_tables(table[3], table[4], sizes)
+    ]
+    return handles, levels
+
+
+def taps(padded, by_tap):
+    summed = None
+    for tap in range(by_tap.shape[0]):
+        term = by_tap[tap][:, None, None] * padded[:, None, tap]
+        summed = term if summed is None else summed + term
+    return summed
+
+
+def gathered_apply(bank, plan, padded):
+    handles, levels = plan
+    outputs = handles[3]
+    partial = taps(padded, bank.get(handles[0])[:, outputs:])
+    rise_total, fall_total = partial[:, 0], partial[:, 1]
+    rise = fall = None
+    for axis, level in zip(LEVEL_AXES, levels):
+        gathered = lax.all_gather(jnp.stack([rise_total, fall_total]), axis)
+        weights = [bank.get(handle)[:, :, None, None] for handle in level]
+        rise_part = jnp.sum(weights[0] * gathered[:, 0], axis=0)
+        fall_part = jnp.sum(weights[2] * gathered[:, 1], axis=0)
+        rise = rise_part if rise is None else rise + rise_part
+        fall = fall_part if fall is None else fall + fall_part
+        rise_total = jnp.sum(weights[1] * gathered[:, 0], axis=0)
+        fall_total = jnp.sum(weights[3] * gathered[:, 1], axis=0)
+    local = taps(padded, bank.get(handles[0])[:, :outputs])
+    return (
+        local
+        + bank.get(handles[1])[None, :, None, None] * rise[:, None]
+        + bank.get(handles[2])[None, :, None, None] * fall[:, None]
+    )
 
 
 def wall_apply(bank, plan, padded_groups, rows, pad):
-    count = lax.axis_size("gy")
-    groups, rounds = plan
-
-    def taps(padded, by_tap):
-        summed = None
-        for tap in range(by_tap.shape[0]):
-            term = by_tap[tap][:, None, None] * padded[:, None, tap]
-            summed = term if summed is None else summed + term
-        return summed
+    count = int(np.prod(plan[2]))
+    groups, rounds, _ = plan
 
     partials = [
         taps(padded, bank.get(handles[0])[:, handles[3] :])
@@ -269,8 +345,8 @@
         for shift, rise_handle, fall_handle in entries:
             up_pairs = [(i, i + shift) for i in range(count - shift)]
             down_pairs = [(i + shift, i) for i in range(count - shift)]
-            from_below = lax.ppermute(rise, "gy", up_pairs)
-            from_above = lax.ppermute(fall, "gy", down_pairs)
+            from_below = lax.ppermute(rise, WALL_AXES, up_pairs)
+            from_above = lax.ppermute(fall, WALL_AXES, down_pairs)
             rise_next = rise_next + bank.get(rise_handle)[:, None, None] * from_below
             fall_next = fall_next + bank.get(fall_handle)[:, None, None] * from_above
         rise, fall = rise_next, fall_next
@@ -289,12 +365,11 @@
     return results
 
 
-def halo(block, width):
-    count = lax.axis_size("gy")
+def halo(block, width, count):
     up_pairs = [(i, i + 1) for i in range(count - 1)]
     down_pairs = [(i + 1, i) for i in range(count - 1)]
-    below = lax.ppermute(block[:, block.shape[1] - width :], "gy", up_pairs)
-    above = lax.ppermute(block[:, :width], "gy", down_pairs)
+    below = lax.ppermute(block[:, block.shape[1] - width :], WALL_AXES, up_pairs)
+    above = lax.ppermute(block[:, :width], WALL_AXES, down_pairs)
     return jnp.concatenate([below, block, above], axis=1)
 
 
@@ -330,11 +405,11 @@
     return jnp.stack(rows_out)
 
 
-def per_device(mass_per_volume, mass_flux_vector, total_heat_content):
+def per_device(level_sizes, mass_per_volume, mass_flux_vector, total_heat_content):
     rows, span_own, stream_cells = mass_per_volume.shape
-    count = lax.axis_size("gy")
+    count = int(np.prod(level_sizes))
     points = rows * count
-    position = lax.axis_index("gy")
+    position = lax.axis_index(WALL_AXES)
     span_total = span_own * lax.axis_size("pa")
     stream_matrix = jnp.asarray(periodic_matrix(stream_cells, STREAM_STEP), jnp.float32)
     span_full = periodic_matrix(span_total, SPAN_STEP)
@@ -342,14 +417,15 @@
     other_block = jnp.asarray(span_full[span_own : 2 * span_own, :span_own], jnp.float32)
 
     bank = TableBank()
-    first_plan = plan_wall(bank, [("slope", 4), ("smooth", 5)], points, rows, 3, (2, 0))
-    second_plan = plan_wall(bank, [("slope", 5)], points, rows, 2, (0,))
+    first_plan = plan_wall(bank, [("slope", 4)], points, rows, 3, (2,), level_sizes)
+    smooth_plan = plan_gathered(bank, "smooth", 5, points, rows, 3, level_sizes)
+    second_plan = plan_wall(bank, [("slope", 5)], points, rows, 2, (0,), level_sizes)
     bank.lookup(position)
 
     state = jnp.concatenate(
         [mass_per_volume[None], mass_flux_vector, total_heat_content[None]], axis=0
     )
-    padded = halo(state, 3)
+    padded = halo(state, 3, count)
     global_rows = position * rows - 3 + jnp.arange(rows + 6)
     inside = ((global_rows >= 0) & (global_rows < points))[:, None, None]
     density = jnp.where(inside, padded[0], 1.0)
@@ -359,7 +435,8 @@
     warmth_pad = push_pad / density
     basic_pad = jnp.concatenate([speed_pad, warmth_pad[None]], axis=0)
 
-    wall_grad, smoothed = wall_apply(bank, first_plan, [basic_pad, padded], rows, 3)
+    smoothed = gathered_apply(bank, smooth_plan, padded)
+    (wall_grad,) = wall_apply(bank, first_plan, [basic_pad], rows, 3)
 
     basic = basic_pad[:, 1 : rows + 5]
     speed = basic[:3]
@@ -390,11 +467,22 @@
 
 
 def solution(mesh):
-    placed = (P("gy", "pa", None), P(None, "gy", "pa", None), P("gy", "pa", None))
+    rows_devices = mesh.shape["gy"]
+    fast = int(np.gcd(rows_devices, 4))
+    middle = int(np.gcd(rows_devices // fast, 4))
+    slow = rows_devices // fast // middle
+    split = jax.sharding.Mesh(
+        mesh.devices.reshape(slow, middle, fast, mesh.shape["pa"]), WALL_AXES + ("pa",)
+    )
+    placed = (
+        P(WALL_AXES, "pa", None),
+        P(None, WALL_AXES, "pa", None),
+        P(WALL_AXES, "pa", None),
+    )
     return jax.shard_map(
-        per_device,
-        mesh=mesh,
+        functools.partial(per_device, (fast, middle, slow)),
+        mesh=split,
         in_specs=placed,
-        out_specs=(P(None, "gy", "pa", None), P(None, "gy", "pa", None)),
+        out_specs=(P(None, WALL_AXES, "pa", None), P(None, WALL_AXES, "pa", None)),
         check_vma=False,
     )

time: 195 us -> 232 us (1.19)
  the two profiles are of different devices: /device:TPU:28 before, /device:TPU:30 now
where the time goes in v11:
time: 232 us; the launch traced here: 230 us
  starting transfers between devices  84.9 us (37%)
  waiting for transfers between devices  53 us (23%)
  other arithmetic  35.1 us (15%)
  local copies, waits for them, and re-layouts  25.3 us (11%)
  between operations  16.6 us (7%)
  matrix products  15.4 us (7%)
    ppermute x12, starting transfers between devices, wall_apply(): from_below = lax.ppermute(rise, WALL_AXES, up_pairs)  53.6 us
    ppermute x12, waiting for transfers between devices, wall_apply(): from_above = lax.ppermute(fall, WALL_AXES, down_pairs)  46.3 us
    ppermute x12, starting transfers between devices, wall_apply(): from_above = lax.ppermute(fall, WALL_AXES, down_pairs)  25.3 us
    dot_general x2, matrix products, span_slope(): jnp.einsum('fyzx,zw->fywx', other, other_block, precision=HIGHEST)  6.24 us
    dot_general x2, matrix products, span_slope(): jnp.einsum('fyzx,zw->fywx', fields, own_block, precision=HIGHEST)  5.3 us
    mul x9, local copies, waits for them, and re-layouts, taps(): term = by_tap[tap][:, None, None] * padded[:, None, tap]  5.01 us
    reduce_sum x3, other arithmetic, gathered_apply(): rise_part = jnp.sum(weights[0] * gathered[:, 0], axis=0)  4.96 us
  transfers between devices with their start and end apart: 31, of which 14 were waited for; matrix products, arithmetic and copies ran while one was open for 25% of the time, Pallas kernels for 0%

profile of v11, /device:TPU:30, one launch (start us, length us, event | category | flops | bytes accessed | tf_op | source)
XLA Modules:
  0.0 230.3 jit_solution(5147353997788234466)
XLA Ops:
  9.4 3.4 %collective-permute-start = (f32[5,3,64,128]{3,2,1,0:T(8,128)}, f32[5,3,64,128]{3,2,1,0:T(8,128)S(1)}, u32[]{:S(2)}, u32[]{:S(2)}) collective-permute-start(f32[5,3,64,128]{3,2,1,0:T(8,128)} %get-tuple-element.71), channel_id=1, source_target_pairs={{0,2},{2,4},{4,6},{6,8},{8,10},{10,12},{12,14},{14,16},{16,18},{18... | collective-permute-start | bytes 1474568 | tf_op jit(solution)/shard_map/ppermute | solution.py:371
  47.2 5.8 %collective-permute-start.2 = (f32[4,64,128]{2,1,0:T(8,128)S(1)}, f32[4,64,128]{2,1,0:T(8,128)S(1)}, u32[]{:S(2)}, u32[]{:S(2)}) collective-permute-start(f32[4,64,128]{2,1,0:T(8,128)S(1)} %get-tuple-element.89), channel_id=1, source_target_pairs={{0,64},{2,66},{4,68},{6,70},{8,72},{10,74},{12,76},{14,78},{16,80}... | collective-permute-start | bytes 393224 | tf_op jit(solution)/shard_map/ppermute | solution.py:348
  56.0 5.4 %collective-permute-done.8 = f32[4,64,128]{2,1,0:T(8,128)S(1)} collective-permute-done((f32[4,64,128]{2,1,0:T(8,128)S(1)}, f32[4,64,128]{2,1,0:T(8,128)S(1)}, u32[]{:S(2)}, u32[]{:S(2)}) %collective-permute-start.8) | collective-permute-done | bytes 131104 | tf_op jit(solution)/shard_map/ppermute | solution.py:349
  61.5 3.7 %collective-permute-start.3 = (f32[4,64,128]{2,1,0:T(8,128)S(1)}, f32[4,64,128]{2,1,0:T(8,128)S(1)}, u32[]{:S(2)}, u32[]{:S(2)}) collective-permute-start(f32[4,64,128]{2,1,0:T(8,128)S(1)} %get-tuple-element.87), channel_id=1, source_target_pairs={{0,32},{2,34},{4,36},{6,38},{8,40},{10,42},{12,44},{14,46},{16,48}... | collective-permute-start | bytes 393224 | tf_op jit(solution)/shard_map/ppermute | solution.py:348
  67.8 4.3 %collective-permute-start.4 = (f32[4,64,128]{2,1,0:T(8,128)S(1)}, f32[4,64,128]{2,1,0:T(8,128)S(1)}, u32[]{:S(2)}, u32[]{:S(2)}) collective-permute-start(f32[4,64,128]{2,1,0:T(8,128)S(1)} %multiply_add_fusion.27), channel_id=1, source_target_pairs={{0,16},{2,18},{4,20},{6,22},{8,24},{10,26},{12,28},{14,30},{16,32}... | collective-permute-start | bytes 393224 | tf_op jit(solution)/shard_map/ppermute | solution.py:348
  72.2 3.1 %collective-permute-start.10 = (f32[4,64,128]{2,1,0:T(8,128)S(1)}, f32[4,64,128]{2,1,0:T(8,128)S(1)}, u32[]{:S(2)}, u32[]{:S(2)}) collective-permute-start(f32[4,64,128]{2,1,0:T(8,128)S(1)} %multiply_add_fusion.21), channel_id=1, source_target_pairs={{16,0},{18,2},{20,4},{22,6},{24,8},{26,10},{28,12},{30,14},{32,16}... | collective-permute-start | bytes 393224 | tf_op jit(solution)/shard_map/ppermute | solution.py:349
  76.2 4.6 %collective-permute-start.5 = (f32[4,64,128]{2,1,0:T(8,128)S(1)}, f32[4,64,128]{2,1,0:T(8,128)S(1)}, u32[]{:S(2)}, u32[]{:S(2)}) collective-permute-start(f32[4,64,128]{2,1,0:T(8,128)S(1)} %multiply_add_fusion.26), channel_id=1, source_target_pairs={{0,8},{2,10},{4,12},{6,14},{8,16},{10,18},{12,20},{14,22},{16,24},... | collective-permute-start | bytes 393224 | tf_op jit(solution)/shard_map/ppermute | solution.py:348
  81.8 2.8 %collective-permute-start.11 = (f32[4,64,128]{2,1,0:T(8,128)S(1)}, f32[4,64,128]{2,1,0:T(8,128)S(1)}, u32[]{:S(2)}, u32[]{:S(2)}) collective-permute-start(f32[4,64,128]{2,1,0:T(8,128)S(1)} %multiply_add_fusion.20), channel_id=1, source_target_pairs={{8,0},{10,2},{12,4},{14,6},{16,8},{18,10},{20,12},{22,14},{24,16},... | collective-permute-start | bytes 393224 | tf_op jit(solution)/shard_map/ppermute | solution.py:349
  84.8 6.0 %collective-permute-start.6 = (f32[4,64,128]{2,1,0:T(8,128)S(1)}, f32[4,64,128]{2,1,0:T(8,128)S(1)}, u32[]{:S(2)}, u32[]{:S(2)}) collective-permute-start(f32[4,64,128]{2,1,0:T(8,128)S(1)} %multiply_add_fusion.25), channel_id=1, source_target_pairs={{0,4},{2,6},{4,8},{6,10},{8,12},{10,14},{12,16},{14,18},{16,20},{1... | collective-permute-start | bytes 393224 | tf_op jit(solution)/shard_map/ppermute | solution.py:348
  91.0 3.3 %collective-permute-start.12 = (f32[4,64,128]{2,1,0:T(8,128)S(1)}, f32[4,64,128]{2,1,0:T(8,128)S(1)}, u32[]{:S(2)}, u32[]{:S(2)}) collective-permute-start(f32[4,64,128]{2,1,0:T(8,128)S(1)} %multiply_add_fusion.19), channel_id=1, source_target_pairs={{4,0},{6,2},{8,4},{10,6},{12,8},{14,10},{16,12},{18,14},{20,16},{2... | collective-permute-start | bytes 393224 | tf_op jit(solution)/shard_map/ppermute | solution.py:349
  94.4 11.6 %collective-permute-start.7 = (f32[4,64,128]{2,1,0:T(8,128)S(1)}, f32[4,64,128]{2,1,0:T(8,128)S(1)}, u32[]{:S(2)}, u32[]{:S(2)}) collective-permute-start(f32[4,64,128]{2,1,0:T(8,128)S(1)} %multiply_add_fusion.24), channel_id=1, source_target_pairs={{0,2},{2,4},{4,6},{6,8},{8,10},{10,12},{12,14},{14,16},{16,18},{18... | collective-permute-start | bytes 393224 | tf_op jit(solution)/shard_map/ppermute | solution.py:348
  106.1 2.9 %collective-permute-start.13 = (f32[4,64,128]{2,1,0:T(8,128)S(1)}, f32[4,64,128]{2,1,0:T(8,128)S(1)}, u32[]{:S(2)}, u32[]{:S(2)}) collective-permute-start(f32[4,64,128]{2,1,0:T(8,128)S(1)} %multiply_add_fusion.18), channel_id=1, source_target_pairs={{2,0},{4,2},{6,4},{8,6},{10,8},{12,10},{14,12},{16,14},{18,16},{20... | collective-permute-start | bytes 393224 | tf_op jit(solution)/shard_map/ppermute | solution.py:349
  109.2 8.0 %collective-permute-done.13 = f32[4,64,128]{2,1,0:T(8,128)S(1)} collective-permute-done((f32[4,64,128]{2,1,0:T(8,128)S(1)}, f32[4,64,128]{2,1,0:T(8,128)S(1)}, u32[]{:S(2)}, u32[]{:S(2)}) %collective-permute-start.13) | collective-permute-done | bytes 131104 | tf_op jit(solution)/shard_map/ppermute | solution.py:349
  126.5 4.5 %collective-permute-start.15 = (f32[5,64,128]{2,1,0:T(8,128)}, f32[5,64,128]{2,1,0:T(8,128)}, u32[]{:S(2)}, u32[]{:S(2)}) collective-permute-start(f32[5,64,128]{2,1,0:T(8,128)} %get-tuple-element.85), channel_id=1, source_target_pairs={{0,64},{2,66},{4,68},{6,70},{8,72},{10,74},{12,76},{14,78},{16,80}... | collective-permute-start | bytes 491528 | tf_op jit(solution)/shard_map/ppermute | solution.py:348
  145.4 3.7 %fusion.93 = f32[5,8,128,64]{2,3,1,0:T(8,128)} fusion(f32[5,8,64,128]{3,2,1,0:T(8,128)} %fusion.38, f32[64,64,1,1]{0,1,3,2:T(8,128)S(1)} %copy-done.61), kind=kOutput, calls=%fused_computation.383 | convolution fusion | flops 251658240 | bytes 2637824 | tf_op jit(solution)/shard_map/fyzx,zw->fywx/dot_general | solution.py:385
  152.8 8.3 %collective-permute-done.22 = f32[5,64,128]{2,1,0:T(8,128)S(1)} collective-permute-done((f32[5,64,128]{2,1,0:T(8,128)S(1)}, f32[5,64,128]{2,1,0:T(8,128)S(1)}, u32[]{:S(2)}, u32[]{:S(2)}) %collective-permute-start.22) | collective-permute-done | bytes 163872 | tf_op jit(solution)/shard_map/ppermute | solution.py:349
  166.7 8.2 %collective-permute-done.23 = f32[5,64,128]{2,1,0:T(8,128)S(1)} collective-permute-done((f32[5,64,128]{2,1,0:T(8,128)S(1)}, f32[5,64,128]{2,1,0:T(8,128)S(1)}, u32[]{:S(2)}, u32[]{:S(2)}) %collective-permute-start.23) | collective-permute-done | bytes 163872 | tf_op jit(solution)/shard_map/ppermute | solution.py:349
  177.0 3.0 %collective-permute-start.19 = (f32[5,64,128]{2,1,0:T(8,128)S(1)}, f32[5,64,128]{2,1,0:T(8,128)}, u32[]{:S(2)}, u32[]{:S(2)}) collective-permute-start(f32[5,64,128]{2,1,0:T(8,128)S(1)} %multiply_add_fusion.13), channel_id=1, source_target_pairs={{0,4},{2,6},{4,8},{6,10},{8,12},{10,14},{12,16},{14,18},{16,20},{1... | collective-permute-start | bytes 491528 | tf_op jit(solution)/shard_map/ppermute | solution.py:348
  180.0 4.8 %collective-permute-done.24 = f32[5,64,128]{2,1,0:T(8,128)S(1)} collective-permute-done((f32[5,64,128]{2,1,0:T(8,128)S(1)}, f32[5,64,128]{2,1,0:T(8,128)S(1)}, u32[]{:S(2)}, u32[]{:S(2)}) %collective-permute-start.24) | collective-permute-done | bytes 163872 | tf_op jit(solution)/shard_map/ppermute | solution.py:349
  190.4 4.9 %collective-permute-start.20 = (f32[5,64,128]{2,1,0:T(8,128)S(1)}, f32[5,64,128]{2,1,0:T(8,128)S(1)}, u32[]{:S(2)}, u32[]{:S(2)}) collective-permute-start(f32[5,64,128]{2,1,0:T(8,128)S(1)} %multiply_add_fusion.12), channel_id=1, source_target_pairs={{0,2},{2,4},{4,6},{6,8},{8,10},{10,12},{12,14},{14,16},{16,18},{18... | collective-permute-start | bytes 491528 | tf_op jit(solution)/shard_map/ppermute | solution.py:348
  199.8 9.5 %collective-permute-done.26 = f32[5,64,128]{2,1,0:T(8,128)S(1)} collective-permute-done((f32[5,64,128]{2,1,0:T(8,128)S(1)}, f32[5,64,128]{2,1,0:T(8,128)S(1)}, u32[]{:S(2)}, u32[]{:S(2)}) %collective-permute-start.26) | collective-permute-done | bytes 163872 | tf_op jit(solution)/shard_map/ppermute | solution.py:349
  209.5 4.7 %fusion.4 = f32[5,8,64,128]{3,2,1,0:T(8,128)S(1)} fusion(f32[5,8,128,64]{2,3,1,0:T(8,128)} %fusion.93, f32[5,8,64,128]{3,2,1,0:T(8,128)} %collective-permute-done.27, f32[64,64,1,1]{0,1,3,2:T(8,128)S(1)} %copy-done.65, f32[5,8,64,128]{3,2,1,0:T(8,128)S(1)} %fusion.92, f32[5,64,128]{2,1,0:T(8,128)S(1)} %multiply_add_fusion.5, f32[8]{0:T(128)S(1)} %copy-done.160, ...), kind=kOutput, calls=%fused_computation.39 | convolution fusion | flops 261816320 | bytes 7553472 | tf_op jit(solution)/shard_map/fyzx,zw->fywx/dot_general | solution.py:385
  215.6 3.0 %all-gather.11.cloned.1.call-done = f32[8,5,64,128]{3,2,1,0:T(8,128)} async-done(((f32[2,5,64,128]{3,2,1,0:T(8,128)}), f32[8,5,64,128]{3,2,1,0:T(8,128)}) %all-gather.11.cloned.1.call-update) | async-done | bytes 1310736 | tf_op jit(solution)/shard_map/all_gather | solution.py:316
  220.9 2.9 %multiply_add_fusion.1 = f32[5,8,64,128]{3,2,1,0:T(8,128)} fusion(f32[5,64,128]{2,1,0:T(8,128)S(1)} %get-tuple-element.215, f32[8]{0:T(128)S(1)} %copy-done.146, f32[5,64,128]{2,1,0:T(8,128)S(1)} %get-tuple-element.216, f32[8]{0:T(128)S(1)} %copy-done.145, f32[5,64,128]{2,1,0:T(8,128)S(1)} %copy-done.32, f32[8]{0:T(128)S(1)} %copy-done.132, ...), kind=kLoop, calls=%fused_computation.43 | loop fusion | flops 10158080 | bytes 3932672 | tf_op jit(solution)/shard_map/add | solution.py:326
  (467 shorter events, 91.5 us)
Async XLA Ops:
  7.2 130.7 %all-gather.7.cloned.1.call-start = ((), (), s32[]{:S(2)}) async-start(), calls=%async_computation | async-start | bytes 1638400 | tf_op jit(solution)/shard_map/all_gather | solution.py:316
  9.4 25.5 %collective-permute-start = (f32[5,3,64,128]{3,2,1,0:T(8,128)}, f32[5,3,64,128]{3,2,1,0:T(8,128)S(1)}, u32[]{:S(2)}, u32[]{:S(2)}) collective-permute-start(f32[5,3,64,128]{3,2,1,0:T(8,128)} %get-tuple-element.71), channel_id=1, source_target_pairs={{0,2},{2,4},{4,6},{6,8},{8,10},{10,12},{12,14},{14,16},{16,18},{18... | collective-permute-start | bytes 1474568 | tf_op jit(solution)/shard_map/ppermute | solution.py:371
  12.8 22.2 %collective-permute-start.1 = (f32[5,3,64,128]{3,2,1,0:T(8,128)S(1)}, f32[5,3,64,128]{3,2,1,0:T(8,128)}, u32[]{:S(2)}, u32[]{:S(2)}) collective-permute-start(f32[5,3,64,128]{3,2,1,0:T(8,128)S(1)} %get-tuple-element.72), channel_id=1, source_target_pairs={{2,0},{4,2},{6,4},{8,6},{10,8},{12,10},{14,12},{16,14},{18,16},{20... | collective-permute-start | bytes 1474568 | tf_op jit(solution)/shard_map/ppermute | solution.py:372
  45.1 141.7 %all-gather.9.cloned.1.call-start = ((), (), s32[]{:S(2)}) async-start(), calls=%async_computation.1 | async-start | bytes 1638400 | tf_op jit(solution)/shard_map/all_gather | solution.py:316
  54.3 65.4 %collective-permute-start.14 = (f32[4,12,64,128]{3,2,1,0:T(8,128)S(1)}, f32[4,12,64,128]{3,2,1,0:T(8,128)S(1)}, u32[]{:S(2)}, u32[]{:S(2)}) collective-permute-start(f32[4,12,64,128]{3,2,1,0:T(8,128)S(1)} %copy-done.3), channel_id=1, source_target_pairs={{0,1},{1,0},{2,3},{3,2},{4,5},{5,4},{6,7},{7,6},{8,9},{9,8},{10,11... | collective-permute-start | bytes 4718600 | tf_op jit(solution)/shard_map/ppermute | solution.py:384
  72.2 9.3 %collective-permute-start.10 = (f32[4,64,128]{2,1,0:T(8,128)S(1)}, f32[4,64,128]{2,1,0:T(8,128)S(1)}, u32[]{:S(2)}, u32[]{:S(2)}) collective-permute-start(f32[4,64,128]{2,1,0:T(8,128)S(1)} %multiply_add_fusion.21), channel_id=1, source_target_pairs={{16,0},{18,2},{20,4},{22,6},{24,8},{26,10},{28,12},{30,14},{32,16}... | collective-permute-start | bytes 393224 | tf_op jit(solution)/shard_map/ppermute | solution.py:349
  81.8 9.1 %collective-permute-start.11 = (f32[4,64,128]{2,1,0:T(8,128)S(1)}, f32[4,64,128]{2,1,0:T(8,128)S(1)}, u32[]{:S(2)}, u32[]{:S(2)}) collective-permute-start(f32[4,64,128]{2,1,0:T(8,128)S(1)} %multiply_add_fusion.20), channel_id=1, source_target_pairs={{8,0},{10,2},{12,4},{14,6},{16,8},{18,10},{20,12},{22,14},{24,16},... | collective-permute-start | bytes 393224 | tf_op jit(solution)/shard_map/ppermute | solution.py:349
  84.8 9.5 %collective-permute-start.6 = (f32[4,64,128]{2,1,0:T(8,128)S(1)}, f32[4,64,128]{2,1,0:T(8,128)S(1)}, u32[]{:S(2)}, u32[]{:S(2)}) collective-permute-start(f32[4,64,128]{2,1,0:T(8,128)S(1)} %multiply_add_fusion.25), channel_id=1, source_target_pairs={{0,4},{2,6},{4,8},{6,10},{8,12},{10,14},{12,16},{14,18},{16,20},{1... | collective-permute-start | bytes 393224 | tf_op jit(solution)/shard_map/ppermute | solution.py:348
  91.0 15.0 %collective-permute-start.12 = (f32[4,64,128]{2,1,0:T(8,128)S(1)}, f32[4,64,128]{2,1,0:T(8,128)S(1)}, u32[]{:S(2)}, u32[]{:S(2)}) collective-permute-start(f32[4,64,128]{2,1,0:T(8,128)S(1)} %multiply_add_fusion.19), channel_id=1, source_target_pairs={{4,0},{6,2},{8,4},{10,6},{12,8},{14,10},{16,12},{18,14},{20,16},{2... | collective-permute-start | bytes 393224 | tf_op jit(solution)/shard_map/ppermute | solution.py:349
  94.4 14.7 %collective-permute-start.7 = (f32[4,64,128]{2,1,0:T(8,128)S(1)}, f32[4,64,128]{2,1,0:T(8,128)S(1)}, u32[]{:S(2)}, u32[]{:S(2)}) collective-permute-start(f32[4,64,128]{2,1,0:T(8,128)S(1)} %multiply_add_fusion.24), channel_id=1, source_target_pairs={{0,2},{2,4},{4,6},{6,8},{8,10},{10,12},{12,14},{14,16},{16,18},{18... | collective-permute-start | bytes 393224 | tf_op jit(solution)/shard_map/ppermute | solution.py:348
  106.1 11.1 %collective-permute-start.13 = (f32[4,64,128]{2,1,0:T(8,128)S(1)}, f32[4,64,128]{2,1,0:T(8,128)S(1)}, u32[]{:S(2)}, u32[]{:S(2)}) collective-permute-start(f32[4,64,128]{2,1,0:T(8,128)S(1)} %multiply_add_fusion.18), channel_id=1, source_target_pairs={{2,0},{4,2},{6,4},{8,6},{10,8},{12,10},{14,12},{16,14},{18,16},{20... | collective-permute-start | bytes 393224 | tf_op jit(solution)/shard_map/ppermute | solution.py:349
  126.5 16.5 %collective-permute-start.15 = (f32[5,64,128]{2,1,0:T(8,128)}, f32[5,64,128]{2,1,0:T(8,128)}, u32[]{:S(2)}, u32[]{:S(2)}) collective-permute-start(f32[5,64,128]{2,1,0:T(8,128)} %get-tuple-element.85), channel_id=1, source_target_pairs={{0,64},{2,66},{4,68},{6,70},{8,72},{10,74},{12,76},{14,78},{16,80}... | collective-permute-start | bytes 491528 | tf_op jit(solution)/shard_map/ppermute | solution.py:348
  131.0 12.0 %collective-permute-start.21 = (f32[5,64,128]{2,1,0:T(8,128)}, f32[5,64,128]{2,1,0:T(8,128)}, u32[]{:S(2)}, u32[]{:S(2)}) collective-permute-start(f32[5,64,128]{2,1,0:T(8,128)} %get-tuple-element.86), channel_id=1, source_target_pairs={{64,0},{66,2},{68,4},{70,6},{72,8},{74,10},{76,12},{78,14},{80,16}... | collective-permute-start | bytes 491528 | tf_op jit(solution)/shard_map/ppermute | solution.py:349
  136.9 72.5 %collective-permute-start.27 = (f32[5,8,64,128]{3,2,1,0:T(8,128)}, f32[5,8,64,128]{3,2,1,0:T(8,128)}, u32[]{:S(2)}, u32[]{:S(2)}) collective-permute-start(f32[5,8,64,128]{3,2,1,0:T(8,128)} %fusion.38), channel_id=1, source_target_pairs={{0,1},{1,0},{2,3},{3,2},{4,5},{5,4},{6,7},{7,6},{8,9},{9,8},{10,11... | collective-permute-start | bytes 3932168 | tf_op jit(solution)/shard_map/ppermute | solution.py:384
  140.4 78.2 %all-gather.11.cloned.1.call-start = ((), (), s32[]{:S(2)}) async-start(), calls=%async_computation.2 | async-start | bytes 1638400 | tf_op jit(solution)/shard_map/all_gather | solution.py:316
  149.1 12.0 %collective-permute-start.22 = (f32[5,64,128]{2,1,0:T(8,128)S(1)}, f32[5,64,128]{2,1,0:T(8,128)S(1)}, u32[]{:S(2)}, u32[]{:S(2)}) collective-permute-start(f32[5,64,128]{2,1,0:T(8,128)S(1)} %get-tuple-element.84), channel_id=1, source_target_pairs={{32,0},{34,2},{36,4},{38,6},{40,8},{42,10},{44,12},{46,14},{48,16}... | collective-permute-start | bytes 491528 | tf_op jit(solution)/shard_map/ppermute | solution.py:349
  150.9 13.8 %collective-permute-start.17 = (f32[5,64,128]{2,1,0:T(8,128)S(1)}, f32[5,64,128]{2,1,0:T(8,128)S(1)}, u32[]{:S(2)}, u32[]{:S(2)}) collective-permute-start(f32[5,64,128]{2,1,0:T(8,128)S(1)} %multiply_add_fusion.15), channel_id=1, source_target_pairs={{0,16},{2,18},{4,20},{6,22},{8,24},{10,26},{12,28},{14,30},{16,32}... | collective-permute-start | bytes 491528 | tf_op jit(solution)/shard_map/ppermute | solution.py:348
  161.2 13.7 %collective-permute-start.23 = (f32[5,64,128]{2,1,0:T(8,128)S(1)}, f32[5,64,128]{2,1,0:T(8,128)S(1)}, u32[]{:S(2)}, u32[]{:S(2)}) collective-permute-start(f32[5,64,128]{2,1,0:T(8,128)S(1)} %multiply_add_fusion.9), channel_id=1, source_target_pairs={{16,0},{18,2},{20,4},{22,6},{24,8},{26,10},{28,12},{30,14},{32,16}... | collective-permute-start | bytes 491528 | tf_op jit(solution)/shard_map/ppermute | solution.py:349
  164.8 12.1 %collective-permute-start.18 = (f32[5,64,128]{2,1,0:T(8,128)S(1)}, f32[5,64,128]{2,1,0:T(8,128)S(1)}, u32[]{:S(2)}, u32[]{:S(2)}) collective-permute-start(f32[5,64,128]{2,1,0:T(8,128)S(1)} %multiply_add_fusion.14), channel_id=1, source_target_pairs={{0,8},{2,10},{4,12},{6,14},{8,16},{10,18},{12,20},{14,22},{16,24},... | collective-permute-start | bytes 491528 | tf_op jit(solution)/shard_map/ppermute | solution.py:348
  175.0 9.8 %collective-permute-start.24 = (f32[5,64,128]{2,1,0:T(8,128)S(1)}, f32[5,64,128]{2,1,0:T(8,128)S(1)}, u32[]{:S(2)}, u32[]{:S(2)}) collective-permute-start(f32[5,64,128]{2,1,0:T(8,128)S(1)} %multiply_add_fusion.8), channel_id=1, source_target_pairs={{8,0},{10,2},{12,4},{14,6},{16,8},{18,10},{20,12},{22,14},{24,16},... | collective-permute-start | bytes 491528 | tf_op jit(solution)/shard_map/ppermute | solution.py:349
  177.0 12.4 %collective-permute-start.19 = (f32[5,64,128]{2,1,0:T(8,128)S(1)}, f32[5,64,128]{2,1,0:T(8,128)}, u32[]{:S(2)}, u32[]{:S(2)}) collective-permute-start(f32[5,64,128]{2,1,0:T(8,128)S(1)} %multiply_add_fusion.13), channel_id=1, source_target_pairs={{0,4},{2,6},{4,8},{6,10},{8,12},{10,14},{12,16},{14,18},{16,20},{1... | collective-permute-start | bytes 491528 | tf_op jit(solution)/shard_map/ppermute | solution.py:348
  184.9 11.8 %collective-permute-start.25 = (f32[5,64,128]{2,1,0:T(8,128)S(1)}, f32[5,64,128]{2,1,0:T(8,128)}, u32[]{:S(2)}, u32[]{:S(2)}) collective-permute-start(f32[5,64,128]{2,1,0:T(8,128)S(1)} %multiply_add_fusion.7), channel_id=1, source_target_pairs={{4,0},{6,2},{8,4},{10,6},{12,8},{14,10},{16,12},{18,14},{20,16},{2... | collective-permute-start | bytes 491528 | tf_op jit(solution)/shard_map/ppermute | solution.py:349
  190.4 9.2 %collective-permute-start.20 = (f32[5,64,128]{2,1,0:T(8,128)S(1)}, f32[5,64,128]{2,1,0:T(8,128)S(1)}, u32[]{:S(2)}, u32[]{:S(2)}) collective-permute-start(f32[5,64,128]{2,1,0:T(8,128)S(1)} %multiply_add_fusion.12), channel_id=1, source_target_pairs={{0,2},{2,4},{4,6},{6,8},{8,10},{10,12},{12,14},{14,16},{16,18},{18... | collective-permute-start | bytes 491528 | tf_op jit(solution)/shard_map/ppermute | solution.py:348
  197.7 11.5 %collective-permute-start.26 = (f32[5,64,128]{2,1,0:T(8,128)S(1)}, f32[5,64,128]{2,1,0:T(8,128)S(1)}, u32[]{:S(2)}, u32[]{:S(2)}) collective-permute-start(f32[5,64,128]{2,1,0:T(8,128)S(1)} %multiply_add_fusion.6), channel_id=1, source_target_pairs={{2,0},{4,2},{6,4},{8,6},{10,8},{12,10},{14,12},{16,14},{18,16},{20... | collective-permute-start | bytes 491528 | tf_op jit(solution)/shard_map/ppermute | solution.py:349
  (169 other events, 1997.2 us)
Sparse Core Ops, SparseCore 0:
  45.2 26.3 all-gather.6
  140.5 31.7 all-gather.8
  189.5 29.0 all-gather.10

commit v12 on v10

--- a/solution.py
+++ b/solution.py
@@ -178,7 +178,7 @@
         radix = min(2, -(-blocks // stride))
         rounds.append((stride, list(range(1, radix))))
         stride *= radix
-    return rounds
+    return rounds[::-1]
 
 
 def scan_coefs(rise_step, fall_step, shift):

time: 195 us -> 186 us (0.954)
  the two profiles are of different devices: /device:TPU:28 before, /device:TPU:30 now
where the time goes in v12:
time: 186 us; the launch traced here: 185 us
  starting transfers between devices  79 us (42%)
  waiting for transfers between devices  65.1 us (35%)
  other arithmetic  14.7 us (8%)
  local copies, waits for them, and re-layouts  13.8 us (7%)
  matrix products  9.96 us (5%)
  between operations  2.07 us (1%)
    ppermute x12, waiting for transfers between devices, wall_apply(): from_above = lax.ppermute(fall, 'gy', down_pairs)  51.1 us
    ppermute x12, starting transfers between devices, wall_apply(): from_below = lax.ppermute(rise, 'gy', up_pairs)  50.8 us
    ppermute x12, starting transfers between devices, wall_apply(): from_above = lax.ppermute(fall, 'gy', down_pairs)  22.2 us
    ppermute x12, waiting for transfers between devices, wall_apply(): from_below = lax.ppermute(rise, 'gy', up_pairs)  8.67 us
    ppermute x1, waiting for transfers between devices, halo(): above = lax.ppermute(block[:, :width], 'gy', down_pairs)  5.32 us
    add x2, other arithmetic, wall_apply(): local + rise_gain[None, :, None, None] * rise[first:first + size, None]  4.9 us
    dot_general x2, matrix products, span_slope(): jnp.einsum('fyzx,zw->fywx', other, other_block, precision=HIGHEST)  4.43 us
  transfers between devices with their start and end apart: 28, of which 16 were waited for; matrix products, arithmetic and copies ran while one was open for 13% of the time, Pallas kernels for 0%

profile of v12, /device:TPU:30, one launch (start us, length us, event | category | flops | bytes accessed | tf_op | source)
XLA Modules:
  0.0 184.7 jit_solution(6266174199645655277)
XLA Ops:
  3.0 3.4 %collective-permute-start = (f32[5,3,64,128]{3,2,1,0:T(8,128)}, f32[5,3,64,128]{3,2,1,0:T(8,128)S(1)}, u32[]{:S(2)}, u32[]{:S(2)}) collective-permute-start(f32[5,3,64,128]{3,2,1,0:T(8,128)} %get-tuple-element.51), channel_id=1, source_target_pairs={{0,2},{2,4},{4,6},{6,8},{8,10},{10,12},{12,14},{14,16},{16,18},{18... | collective-permute-start | bytes 1474568 | tf_op jit(solution)/shard_map/ppermute | solution.py:296
  6.4 2.4 %collective-permute-start.1 = (f32[5,3,64,128]{3,2,1,0:T(8,128)}, f32[5,3,64,128]{3,2,1,0:T(8,128)S(1)}, u32[]{:S(2)}, u32[]{:S(2)}) collective-permute-start(f32[5,3,64,128]{3,2,1,0:T(8,128)} %get-tuple-element.52), channel_id=1, source_target_pairs={{2,0},{4,2},{6,4},{8,6},{10,8},{12,10},{14,12},{16,14},{18,16},{20... | collective-permute-start | bytes 1474568 | tf_op jit(solution)/shard_map/ppermute | solution.py:297
  20.1 5.3 %collective-permute-done.1 = f32[5,3,64,128]{3,2,1,0:T(8,128)S(1)} collective-permute-done((f32[5,3,64,128]{3,2,1,0:T(8,128)}, f32[5,3,64,128]{3,2,1,0:T(8,128)S(1)}, u32[]{:S(2)}, u32[]{:S(2)}) %collective-permute-start.1) | collective-permute-done | bytes 491552 | tf_op jit(solution)/shard_map/ppermute | solution.py:297
  28.0 5.5 %collective-permute-start.2 = (f32[9,64,128]{2,1,0:T(8,128)S(1)}, f32[9,64,128]{2,1,0:T(8,128)S(1)}, u32[]{:S(2)}, u32[]{:S(2)}) collective-permute-start(f32[9,64,128]{2,1,0:T(8,128)S(1)} %pad_maximum_fusion.7), channel_id=1, source_target_pairs={{0,64},{2,66},{4,68},{6,70},{8,72},{10,74},{12,76},{14,78},{16,80}... | collective-permute-start | bytes 884744 | tf_op jit(solution)/shard_map/ppermute | solution.py:272
  36.4 2.2 %collective-permute-done.2 = f32[9,64,128]{2,1,0:T(8,128)S(1)} collective-permute-done((f32[9,64,128]{2,1,0:T(8,128)S(1)}, f32[9,64,128]{2,1,0:T(8,128)S(1)}, u32[]{:S(2)}, u32[]{:S(2)}) %collective-permute-start.2) | collective-permute-done | bytes 294944 | tf_op jit(solution)/shard_map/ppermute | solution.py:272
  40.0 4.5 %collective-permute-done.8 = f32[9,64,128]{2,1,0:T(8,128)S(1)} collective-permute-done((f32[9,64,128]{2,1,0:T(8,128)S(1)}, f32[9,64,128]{2,1,0:T(8,128)S(1)}, u32[]{:S(2)}, u32[]{:S(2)}) %collective-permute-start.8) | collective-permute-done | bytes 294944 | tf_op jit(solution)/shard_map/ppermute | solution.py:273
  46.1 4.2 %collective-permute-start.4 = (f32[9,64,128]{2,1,0:T(8,128)S(1)}, f32[9,64,128]{2,1,0:T(8,128)S(1)}, u32[]{:S(2)}, u32[]{:S(2)}) collective-permute-start(f32[9,64,128]{2,1,0:T(8,128)S(1)} %multiply_add_fusion.14), channel_id=1, source_target_pairs={{0,16},{2,18},{4,20},{6,22},{8,24},{10,26},{12,28},{14,30},{16,32}... | collective-permute-start | bytes 884744 | tf_op jit(solution)/shard_map/ppermute | solution.py:272
  50.3 2.9 %collective-permute-done.9 = f32[9,64,128]{2,1,0:T(8,128)S(1)} collective-permute-done((f32[9,64,128]{2,1,0:T(8,128)S(1)}, f32[9,64,128]{2,1,0:T(8,128)S(1)}, u32[]{:S(2)}, u32[]{:S(2)}) %collective-permute-start.9) | collective-permute-done | bytes 294944 | tf_op jit(solution)/shard_map/ppermute | solution.py:273
  57.5 6.1 %collective-permute-start.5 = (f32[9,64,128]{2,1,0:T(8,128)S(1)}, f32[9,64,128]{2,1,0:T(8,128)S(1)}, u32[]{:S(2)}, u32[]{:S(2)}) collective-permute-start(f32[9,64,128]{2,1,0:T(8,128)S(1)} %multiply_add_fusion.13), channel_id=1, source_target_pairs={{0,8},{2,10},{4,12},{6,14},{8,16},{10,18},{12,20},{14,22},{16,24},... | collective-permute-start | bytes 884744 | tf_op jit(solution)/shard_map/ppermute | solution.py:272
  65.5 3.4 %collective-permute-start.11 = (f32[9,64,128]{2,1,0:T(8,128)S(1)}, f32[9,64,128]{2,1,0:T(8,128)S(1)}, u32[]{:S(2)}, u32[]{:S(2)}) collective-permute-start(f32[9,64,128]{2,1,0:T(8,128)S(1)} %multiply_add_fusion.7), channel_id=1, source_target_pairs={{8,0},{10,2},{12,4},{14,6},{16,8},{18,10},{20,12},{22,14},{24,16},... | collective-permute-start | bytes 884744 | tf_op jit(solution)/shard_map/ppermute | solution.py:273
  69.1 4.1 %collective-permute-start.6 = (f32[9,64,128]{2,1,0:T(8,128)S(1)}, f32[9,64,128]{2,1,0:T(8,128)S(1)}, u32[]{:S(2)}, u32[]{:S(2)}) collective-permute-start(f32[9,64,128]{2,1,0:T(8,128)S(1)} %multiply_add_fusion.12), channel_id=1, source_target_pairs={{0,4},{2,6},{4,8},{6,10},{8,12},{10,14},{12,16},{14,18},{16,20},{1... | collective-permute-start | bytes 884744 | tf_op jit(solution)/shard_map/ppermute | solution.py:272
  73.2 3.0 %collective-permute-done.11 = f32[9,64,128]{2,1,0:T(8,128)S(1)} collective-permute-done((f32[9,64,128]{2,1,0:T(8,128)S(1)}, f32[9,64,128]{2,1,0:T(8,128)S(1)}, u32[]{:S(2)}, u32[]{:S(2)}) %collective-permute-start.11) | collective-permute-done | bytes 294944 | tf_op jit(solution)/shard_map/ppermute | solution.py:273
  78.3 4.1 %collective-permute-done.6 = f32[9,64,128]{2,1,0:T(8,128)S(1)} collective-permute-done((f32[9,64,128]{2,1,0:T(8,128)S(1)}, f32[9,64,128]{2,1,0:T(8,128)S(1)}, u32[]{:S(2)}, u32[]{:S(2)}) %collective-permute-start.6) | collective-permute-done | bytes 294944 | tf_op jit(solution)/shard_map/ppermute | solution.py:272
  82.5 9.2 %collective-permute-start.7 = (f32[9,64,128]{2,1,0:T(8,128)S(1)}, f32[9,64,128]{2,1,0:T(8,128)S(1)}, u32[]{:S(2)}, u32[]{:S(2)}) collective-permute-start(f32[9,64,128]{2,1,0:T(8,128)S(1)} %multiply_add_fusion.11), channel_id=1, source_target_pairs={{0,2},{2,4},{4,6},{6,8},{8,10},{10,12},{12,14},{14,16},{16,18},{18... | collective-permute-start | bytes 884744 | tf_op jit(solution)/shard_map/ppermute | solution.py:272
  97.4 7.2 %collective-permute-done.13 = f32[9,64,128]{2,1,0:T(8,128)S(1)} collective-permute-done((f32[9,64,128]{2,1,0:T(8,128)S(1)}, f32[9,64,128]{2,1,0:T(8,128)S(1)}, u32[]{:S(2)}, u32[]{:S(2)}) %collective-permute-start.13) | collective-permute-done | bytes 294944 | tf_op jit(solution)/shard_map/ppermute | solution.py:273
  108.9 6.7 %collective-permute-start.15 = (f32[5,64,128]{2,1,0:T(8,128)S(1)}, f32[5,64,128]{2,1,0:T(8,128)S(1)}, u32[]{:S(2)}, u32[]{:S(2)}) collective-permute-start(f32[5,64,128]{2,1,0:T(8,128)S(1)} %get-tuple-element.63), channel_id=1, source_target_pairs={{0,64},{2,66},{4,68},{6,70},{8,72},{10,74},{12,76},{14,78},{16,80}... | collective-permute-start | bytes 491528 | tf_op jit(solution)/shard_map/ppermute | solution.py:272
  119.0 2.9 %multiply_add_fusion.1 = f32[5,8,64,128]{3,2,1,0:T(8,128)} fusion(f32[5,64,128]{2,1,0:T(8,128)S(1)} %slice-done.1, f32[8]{0:T(128)S(1)} %copy-done.40, f32[5,64,128]{2,1,0:T(8,128)S(1)} %slice-done, f32[8]{0:T(128)S(1)} %copy-done.39, f32[5,64,128]{2,1,0:T(8,128)S(1)} %get-tuple-element.59, f32[8]{0:T(128)S(1)} %copy-done.26, ...), kind=kLoop, calls=%fused_computation.43 | loop fusion | flops 10158080 | bytes 3932672 | tf_op jit(solution)/shard_map/add | solution.py:284
  130.9 6.4 %collective-permute-done.22 = f32[5,64,128]{2,1,0:T(8,128)S(1)} collective-permute-done((f32[5,64,128]{2,1,0:T(8,128)S(1)}, f32[5,64,128]{2,1,0:T(8,128)S(1)}, u32[]{:S(2)}, u32[]{:S(2)}) %collective-permute-start.22) | collective-permute-done | bytes 163872 | tf_op jit(solution)/shard_map/ppermute | solution.py:273
  141.3 6.2 %collective-permute-done.23 = f32[5,64,128]{2,1,0:T(8,128)S(1)} collective-permute-done((f32[5,64,128]{2,1,0:T(8,128)S(1)}, f32[5,64,128]{2,1,0:T(8,128)S(1)}, u32[]{:S(2)}, u32[]{:S(2)}) %collective-permute-start.23) | collective-permute-done | bytes 163872 | tf_op jit(solution)/shard_map/ppermute | solution.py:273
  151.7 5.2 %collective-permute-done.24 = f32[5,64,128]{2,1,0:T(8,128)S(1)} collective-permute-done((f32[5,64,128]{2,1,0:T(8,128)S(1)}, f32[5,64,128]{2,1,0:T(8,128)S(1)}, u32[]{:S(2)}, u32[]{:S(2)}) %collective-permute-start.24) | collective-permute-done | bytes 163872 | tf_op jit(solution)/shard_map/ppermute | solution.py:273
  159.0 6.5 %collective-permute-start.20 = (f32[5,64,128]{2,1,0:T(8,128)S(1)}, f32[5,64,128]{2,1,0:T(8,128)S(1)}, u32[]{:S(2)}, u32[]{:S(2)}) collective-permute-start(f32[5,64,128]{2,1,0:T(8,128)S(1)} %multiply_add_fusion.24), channel_id=1, source_target_pairs={{0,2},{2,4},{4,6},{6,8},{8,10},{10,12},{12,14},{14,16},{16,18},{18... | collective-permute-start | bytes 491528 | tf_op jit(solution)/shard_map/ppermute | solution.py:272
  165.5 3.2 %collective-permute-done.25 = f32[5,64,128]{2,1,0:T(8,128)S(1)} collective-permute-done((f32[5,64,128]{2,1,0:T(8,128)S(1)}, f32[5,64,128]{2,1,0:T(8,128)S(1)}, u32[]{:S(2)}, u32[]{:S(2)}) %collective-permute-start.25) | collective-permute-done | bytes 163872 | tf_op jit(solution)/shard_map/ppermute | solution.py:273
  170.8 9.4 %collective-permute-done.26 = f32[5,64,128]{2,1,0:T(8,128)S(1)} collective-permute-done((f32[5,64,128]{2,1,0:T(8,128)S(1)}, f32[5,64,128]{2,1,0:T(8,128)S(1)}, u32[]{:S(2)}, u32[]{:S(2)}) %collective-permute-start.26) | collective-permute-done | bytes 163872 | tf_op jit(solution)/shard_map/ppermute | solution.py:273
  180.5 2.9 %fusion.4 = f32[5,8,64,128]{3,2,1,0:T(8,128)S(1)} fusion(f32[5,8,128,64]{2,3,1,0:T(8,128)S(1)} %fusion.89, f32[5,8,64,128]{3,2,1,0:T(8,128)S(1)} %collective-permute-done.27, f32[64,64,1,1]{0,1,3,2:T(8,128)S(1)} %copy-done.9, f32[5,8,64,128]{3,2,1,0:T(8,128)S(1)} %fusion.88, f32[5,64,128]{2,1,0:T(8,128)S(1)} %multiply_add_fusion.17, f32[8]{0:T(128)S(1)} %copy-done.54, ...), kind=kOutput, calls=%fused_computation.39 | convolution fusion | flops 261816320 | bytes 7553472 | tf_op jit(solution)/shard_map/fyzx,zw->fywx/dot_general | solution.py:310
  (237 shorter events, 65.6 us)
Async XLA Ops:
  3.0 17.1 %collective-permute-start = (f32[5,3,64,128]{3,2,1,0:T(8,128)}, f32[5,3,64,128]{3,2,1,0:T(8,128)S(1)}, u32[]{:S(2)}, u32[]{:S(2)}) collective-permute-start(f32[5,3,64,128]{3,2,1,0:T(8,128)} %get-tuple-element.51), channel_id=1, source_target_pairs={{0,2},{2,4},{4,6},{6,8},{8,10},{10,12},{12,14},{14,16},{16,18},{18... | collective-permute-start | bytes 1474568 | tf_op jit(solution)/shard_map/ppermute | solution.py:296
  6.4 19.0 %collective-permute-start.1 = (f32[5,3,64,128]{3,2,1,0:T(8,128)}, f32[5,3,64,128]{3,2,1,0:T(8,128)S(1)}, u32[]{:S(2)}, u32[]{:S(2)}) collective-permute-start(f32[5,3,64,128]{3,2,1,0:T(8,128)} %get-tuple-element.52), channel_id=1, source_target_pairs={{2,0},{4,2},{6,4},{8,6},{10,8},{12,10},{14,12},{16,14},{18,16},{20... | collective-permute-start | bytes 1474568 | tf_op jit(solution)/shard_map/ppermute | solution.py:297
  28.0 10.6 %collective-permute-start.2 = (f32[9,64,128]{2,1,0:T(8,128)S(1)}, f32[9,64,128]{2,1,0:T(8,128)S(1)}, u32[]{:S(2)}, u32[]{:S(2)}) collective-permute-start(f32[9,64,128]{2,1,0:T(8,128)S(1)} %pad_maximum_fusion.7), channel_id=1, source_target_pairs={{0,64},{2,66},{4,68},{6,70},{8,72},{10,74},{12,76},{14,78},{16,80}... | collective-permute-start | bytes 884744 | tf_op jit(solution)/shard_map/ppermute | solution.py:272
  33.6 11.0 %collective-permute-start.8 = (f32[9,64,128]{2,1,0:T(8,128)S(1)}, f32[9,64,128]{2,1,0:T(8,128)S(1)}, u32[]{:S(2)}, u32[]{:S(2)}) collective-permute-start(f32[9,64,128]{2,1,0:T(8,128)S(1)} %pad_maximum_fusion.8), channel_id=1, source_target_pairs={{64,0},{66,2},{68,4},{70,6},{72,8},{74,10},{76,12},{78,14},{80,16}... | collective-permute-start | bytes 884744 | tf_op jit(solution)/shard_map/ppermute | solution.py:273
  34.9 59.1 %collective-permute-start.14 = (f32[4,12,64,128]{3,2,1,0:T(8,128)S(1)}, f32[4,12,64,128]{3,2,1,0:T(8,128)S(1)}, u32[]{:S(2)}, u32[]{:S(2)}) collective-permute-start(f32[4,12,64,128]{3,2,1,0:T(8,128)S(1)} %fusion.1), channel_id=1, source_target_pairs={{0,1},{1,0},{2,3},{3,2},{4,5},{5,4},{6,7},{7,6},{8,9},{9,8},{10,11... | collective-permute-start | bytes 4718600 | tf_op jit(solution)/shard_map/ppermute | solution.py:309
  46.1 11.3 %collective-permute-start.4 = (f32[9,64,128]{2,1,0:T(8,128)S(1)}, f32[9,64,128]{2,1,0:T(8,128)S(1)}, u32[]{:S(2)}, u32[]{:S(2)}) collective-permute-start(f32[9,64,128]{2,1,0:T(8,128)S(1)} %multiply_add_fusion.14), channel_id=1, source_target_pairs={{0,16},{2,18},{4,20},{6,22},{8,24},{10,26},{12,28},{14,30},{16,32}... | collective-permute-start | bytes 884744 | tf_op jit(solution)/shard_map/ppermute | solution.py:272
  53.4 12.1 %collective-permute-start.10 = (f32[9,64,128]{2,1,0:T(8,128)S(1)}, f32[9,64,128]{2,1,0:T(8,128)S(1)}, u32[]{:S(2)}, u32[]{:S(2)}) collective-permute-start(f32[9,64,128]{2,1,0:T(8,128)S(1)} %multiply_add_fusion.8), channel_id=1, source_target_pairs={{16,0},{18,2},{20,4},{22,6},{24,8},{26,10},{28,12},{30,14},{32,16}... | collective-permute-start | bytes 884744 | tf_op jit(solution)/shard_map/ppermute | solution.py:273
  57.5 11.5 %collective-permute-start.5 = (f32[9,64,128]{2,1,0:T(8,128)S(1)}, f32[9,64,128]{2,1,0:T(8,128)S(1)}, u32[]{:S(2)}, u32[]{:S(2)}) collective-permute-start(f32[9,64,128]{2,1,0:T(8,128)S(1)} %multiply_add_fusion.13), channel_id=1, source_target_pairs={{0,8},{2,10},{4,12},{6,14},{8,16},{10,18},{12,20},{14,22},{16,24},... | collective-permute-start | bytes 884744 | tf_op jit(solution)/shard_map/ppermute | solution.py:272
  65.5 10.7 %collective-permute-start.11 = (f32[9,64,128]{2,1,0:T(8,128)S(1)}, f32[9,64,128]{2,1,0:T(8,128)S(1)}, u32[]{:S(2)}, u32[]{:S(2)}) collective-permute-start(f32[9,64,128]{2,1,0:T(8,128)S(1)} %multiply_add_fusion.7), channel_id=1, source_target_pairs={{8,0},{10,2},{12,4},{14,6},{16,8},{18,10},{20,12},{22,14},{24,16},... | collective-permute-start | bytes 884744 | tf_op jit(solution)/shard_map/ppermute | solution.py:273
  69.1 13.3 %collective-permute-start.6 = (f32[9,64,128]{2,1,0:T(8,128)S(1)}, f32[9,64,128]{2,1,0:T(8,128)S(1)}, u32[]{:S(2)}, u32[]{:S(2)}) collective-permute-start(f32[9,64,128]{2,1,0:T(8,128)S(1)} %multiply_add_fusion.12), channel_id=1, source_target_pairs={{0,4},{2,6},{4,8},{6,10},{8,12},{10,14},{12,16},{14,18},{16,20},{1... | collective-permute-start | bytes 884744 | tf_op jit(solution)/shard_map/ppermute | solution.py:272
  76.4 15.4 %collective-permute-start.12 = (f32[9,64,128]{2,1,0:T(8,128)S(1)}, f32[9,64,128]{2,1,0:T(8,128)S(1)}, u32[]{:S(2)}, u32[]{:S(2)}) collective-permute-start(f32[9,64,128]{2,1,0:T(8,128)S(1)} %multiply_add_fusion.6), channel_id=1, source_target_pairs={{4,0},{6,2},{8,4},{10,6},{12,8},{14,10},{16,12},{18,14},{20,16},{2... | collective-permute-start | bytes 884744 | tf_op jit(solution)/shard_map/ppermute | solution.py:273
  82.5 14.8 %collective-permute-start.7 = (f32[9,64,128]{2,1,0:T(8,128)S(1)}, f32[9,64,128]{2,1,0:T(8,128)S(1)}, u32[]{:S(2)}, u32[]{:S(2)}) collective-permute-start(f32[9,64,128]{2,1,0:T(8,128)S(1)} %multiply_add_fusion.11), channel_id=1, source_target_pairs={{0,2},{2,4},{4,6},{6,8},{8,10},{10,12},{12,14},{14,16},{16,18},{18... | collective-permute-start | bytes 884744 | tf_op jit(solution)/shard_map/ppermute | solution.py:272
  91.8 12.8 %collective-permute-start.13 = (f32[9,64,128]{2,1,0:T(8,128)S(1)}, f32[9,64,128]{2,1,0:T(8,128)S(1)}, u32[]{:S(2)}, u32[]{:S(2)}) collective-permute-start(f32[9,64,128]{2,1,0:T(8,128)S(1)} %multiply_add_fusion.5), channel_id=1, source_target_pairs={{2,0},{4,2},{6,4},{8,6},{10,8},{12,10},{14,12},{16,14},{18,16},{20... | collective-permute-start | bytes 884744 | tf_op jit(solution)/shard_map/ppermute | solution.py:273
  108.9 14.2 %collective-permute-start.15 = (f32[5,64,128]{2,1,0:T(8,128)S(1)}, f32[5,64,128]{2,1,0:T(8,128)S(1)}, u32[]{:S(2)}, u32[]{:S(2)}) collective-permute-start(f32[5,64,128]{2,1,0:T(8,128)S(1)} %get-tuple-element.63), channel_id=1, source_target_pairs={{0,64},{2,66},{4,68},{6,70},{8,72},{10,74},{12,76},{14,78},{16,80}... | collective-permute-start | bytes 491528 | tf_op jit(solution)/shard_map/ppermute | solution.py:272
  117.8 62.5 %collective-permute-start.27 = (f32[5,8,64,128]{3,2,1,0:T(8,128)S(1)}, f32[5,8,64,128]{3,2,1,0:T(8,128)S(1)}, u32[]{:S(2)}, u32[]{:S(2)}) collective-permute-start(f32[5,8,64,128]{3,2,1,0:T(8,128)S(1)} %fusion.34), channel_id=1, source_target_pairs={{0,1},{1,0},{2,3},{3,2},{4,5},{5,4},{6,7},{7,6},{8,9},{9,8},{10,11... | collective-permute-start | bytes 3932168 | tf_op jit(solution)/shard_map/ppermute | solution.py:309
  127.3 10.0 %collective-permute-start.22 = (f32[5,64,128]{2,1,0:T(8,128)S(1)}, f32[5,64,128]{2,1,0:T(8,128)S(1)}, u32[]{:S(2)}, u32[]{:S(2)}) collective-permute-start(f32[5,64,128]{2,1,0:T(8,128)S(1)} %get-tuple-element.62), channel_id=1, source_target_pairs={{32,0},{34,2},{36,4},{38,6},{40,8},{42,10},{44,12},{46,14},{48,16}... | collective-permute-start | bytes 491528 | tf_op jit(solution)/shard_map/ppermute | solution.py:273
  129.0 10.3 %collective-permute-start.17 = (f32[5,64,128]{2,1,0:T(8,128)S(1)}, f32[5,64,128]{2,1,0:T(8,128)S(1)}, u32[]{:S(2)}, u32[]{:S(2)}) collective-permute-start(f32[5,64,128]{2,1,0:T(8,128)S(1)} %multiply_add_fusion.27), channel_id=1, source_target_pairs={{0,16},{2,18},{4,20},{6,22},{8,24},{10,26},{12,28},{14,30},{16,32}... | collective-permute-start | bytes 491528 | tf_op jit(solution)/shard_map/ppermute | solution.py:272
  137.4 10.1 %collective-permute-start.23 = (f32[5,64,128]{2,1,0:T(8,128)S(1)}, f32[5,64,128]{2,1,0:T(8,128)S(1)}, u32[]{:S(2)}, u32[]{:S(2)}) collective-permute-start(f32[5,64,128]{2,1,0:T(8,128)S(1)} %multiply_add_fusion.21), channel_id=1, source_target_pairs={{16,0},{18,2},{20,4},{22,6},{24,8},{26,10},{28,12},{30,14},{32,16}... | collective-permute-start | bytes 491528 | tf_op jit(solution)/shard_map/ppermute | solution.py:273
  139.4 10.1 %collective-permute-start.18 = (f32[5,64,128]{2,1,0:T(8,128)S(1)}, f32[5,64,128]{2,1,0:T(8,128)S(1)}, u32[]{:S(2)}, u32[]{:S(2)}) collective-permute-start(f32[5,64,128]{2,1,0:T(8,128)S(1)} %multiply_add_fusion.26), channel_id=1, source_target_pairs={{0,8},{2,10},{4,12},{6,14},{8,16},{10,18},{12,20},{14,22},{16,24},... | collective-permute-start | bytes 491528 | tf_op jit(solution)/shard_map/ppermute | solution.py:272
  147.6 9.3 %collective-permute-start.24 = (f32[5,64,128]{2,1,0:T(8,128)S(1)}, f32[5,64,128]{2,1,0:T(8,128)S(1)}, u32[]{:S(2)}, u32[]{:S(2)}) collective-permute-start(f32[5,64,128]{2,1,0:T(8,128)S(1)} %multiply_add_fusion.20), channel_id=1, source_target_pairs={{8,0},{10,2},{12,4},{14,6},{16,8},{18,10},{20,12},{22,14},{24,16},... | collective-permute-start | bytes 491528 | tf_op jit(solution)/shard_map/ppermute | solution.py:273
  149.7 9.2 %collective-permute-start.19 = (f32[5,64,128]{2,1,0:T(8,128)S(1)}, f32[5,64,128]{2,1,0:T(8,128)S(1)}, u32[]{:S(2)}, u32[]{:S(2)}) collective-permute-start(f32[5,64,128]{2,1,0:T(8,128)S(1)} %multiply_add_fusion.25), channel_id=1, source_target_pairs={{0,4},{2,6},{4,8},{6,10},{8,12},{10,14},{12,16},{14,18},{16,20},{1... | collective-permute-start | bytes 491528 | tf_op jit(solution)/shard_map/ppermute | solution.py:272
  157.0 11.7 %collective-permute-start.25 = (f32[5,64,128]{2,1,0:T(8,128)S(1)}, f32[5,64,128]{2,1,0:T(8,128)S(1)}, u32[]{:S(2)}, u32[]{:S(2)}) collective-permute-start(f32[5,64,128]{2,1,0:T(8,128)S(1)} %multiply_add_fusion.19), channel_id=1, source_target_pairs={{4,0},{6,2},{8,4},{10,6},{12,8},{14,10},{16,12},{18,14},{20,16},{2... | collective-permute-start | bytes 491528 | tf_op jit(solution)/shard_map/ppermute | solution.py:273
  159.0 11.7 %collective-permute-start.20 = (f32[5,64,128]{2,1,0:T(8,128)S(1)}, f32[5,64,128]{2,1,0:T(8,128)S(1)}, u32[]{:S(2)}, u32[]{:S(2)}) collective-permute-start(f32[5,64,128]{2,1,0:T(8,128)S(1)} %multiply_add_fusion.24), channel_id=1, source_target_pairs={{0,2},{2,4},{4,6},{6,8},{8,10},{10,12},{12,14},{14,16},{16,18},{18... | collective-permute-start | bytes 491528 | tf_op jit(solution)/shard_map/ppermute | solution.py:272
  168.8 11.4 %collective-permute-start.26 = (f32[5,64,128]{2,1,0:T(8,128)S(1)}, f32[5,64,128]{2,1,0:T(8,128)S(1)}, u32[]{:S(2)}, u32[]{:S(2)}) collective-permute-start(f32[5,64,128]{2,1,0:T(8,128)S(1)} %multiply_add_fusion.18), channel_id=1, source_target_pairs={{2,0},{4,2},{6,4},{8,6},{10,8},{12,10},{14,12},{16,14},{18,16},{20... | collective-permute-start | bytes 491528 | tf_op jit(solution)/shard_map/ppermute | solution.py:273
  (62 other events, 561.2 us)

commit v13 on v9

--- a/solution.py
+++ b/solution.py
@@ -204,7 +204,7 @@
         radix = min(2, -(-blocks // stride))
         rounds.append((stride, list(range(1, radix))))
         stride *= radix
-    return rounds
+    return rounds[::-1]
 
 
 def scan_coefs(rise_step, fall_step, shift):

time: 199 us -> 192 us (0.965)
  the two profiles are of different devices: /device:TPU:28 before, /device:TPU:30 now
where the time goes in v13:
time: 192 us; the launch traced here: 191 us
  starting transfers between devices  92.8 us (48%)
  waiting for transfers between devices  53.8 us (28%)
  other arithmetic  19 us (10%)
  local copies, waits for them, and re-layouts  13.8 us (7%)
  matrix products  9.94 us (5%)
    ppermute x12, starting transfers between devices, wall_apply(): from_below = lax.ppermute(rise, 'gy', up_pairs)  64.8 us
    ppermute x12, waiting for transfers between devices, wall_apply(): from_above = lax.ppermute(fall, 'gy', down_pairs)  42.8 us
    ppermute x12, starting transfers between devices, wall_apply(): from_above = lax.ppermute(fall, 'gy', down_pairs)  21.9 us
    ppermute x12, waiting for transfers between devices, wall_apply(): from_below = lax.ppermute(rise, 'gy', up_pairs)  9.08 us
    add x2, other arithmetic, wall_apply(): local + rise_gain[None, :, None, None] * rise[first:first + size, None]  4.88 us
    unnamed x68, local copies, waits for them, and re-layouts  4.51 us
    dot_general x2, matrix products, span_slope(): jnp.einsum('fyzx,zw->fywx', other, other_block, precision=HIGHEST)  4.43 us
  transfers between devices with their start and end apart: 28, of which 14 were waited for; matrix products, arithmetic and copies ran while one was open for 12% of the time, Pallas kernels for 0%

profile of v13, /device:TPU:30, one launch (start us, length us, event | category | flops | bytes accessed | tf_op | source)
XLA Modules:
  0.0 191.1 jit_solution(4497437331632769697)
XLA Ops:
  2.5 2.0 %broadcast_divide_fusion = (f32[3,8,64,128]{3,2,1,0:T(8,128)S(1)}, f32[8,64,128]{2,1,0:T(8,128)}) fusion(f32[3,8,64,128]{3,2,1,0:T(8,128)} %param.8, f32[8,64,128]{2,1,0:T(8,128)} %param.7), kind=kLoop, calls=%fused_computation.103 | loop fusion | flops 524288 | bytes 2097152 | tf_op jit(solution)/shard_map/div | solution.py:388
  9.5 6.5 %collective-permute-start.2 = (f32[9,64,128]{2,1,0:T(8,128)}, f32[9,64,128]{2,1,0:T(8,128)}, u32[]{:S(2)}, u32[]{:S(2)}) collective-permute-start(f32[9,64,128]{2,1,0:T(8,128)} %pad_maximum_fusion.7), channel_id=1, source_target_pairs={{0,64},{2,66},{4,68},{6,70},{8,72},{10,74},{12,76},{14,78},{16,80}... | collective-permute-start | bytes 884744 | tf_op jit(solution)/shard_map/ppermute | solution.py:298
  19.1 2.6 %collective-permute-start = (f32[5,3,64,128]{3,2,1,0:T(8,128)}, f32[5,3,64,128]{3,2,1,0:T(8,128)S(1)}, u32[]{:S(2)}, u32[]{:S(2)}) collective-permute-start(f32[5,3,64,128]{3,2,1,0:T(8,128)} %get-tuple-element.51), channel_id=1, source_target_pairs={{0,2},{2,4},{4,6},{6,8},{8,10},{10,12},{12,14},{14,16},{16,18},{18... | collective-permute-start | bytes 1474568 | tf_op jit(solution)/shard_map/ppermute | solution.py:322
  21.7 3.3 %collective-permute-start.1 = (f32[5,3,64,128]{3,2,1,0:T(8,128)}, f32[5,3,64,128]{3,2,1,0:T(8,128)S(1)}, u32[]{:S(2)}, u32[]{:S(2)}) collective-permute-start(f32[5,3,64,128]{3,2,1,0:T(8,128)} %get-tuple-element.52), channel_id=1, source_target_pairs={{2,0},{4,2},{6,4},{8,6},{10,8},{12,10},{14,12},{16,14},{18,16},{20... | collective-permute-start | bytes 1474568 | tf_op jit(solution)/shard_map/ppermute | solution.py:323
  31.9 4.3 %collective-permute-start.3 = (f32[9,64,128]{2,1,0:T(8,128)S(1)}, f32[9,64,128]{2,1,0:T(8,128)S(1)}, u32[]{:S(2)}, u32[]{:S(2)}) collective-permute-start(f32[9,64,128]{2,1,0:T(8,128)S(1)} %multiply_add_fusion.15), channel_id=1, source_target_pairs={{0,32},{2,34},{4,36},{6,38},{8,40},{10,42},{12,44},{14,46},{16,48}... | collective-permute-start | bytes 884744 | tf_op jit(solution)/shard_map/ppermute | solution.py:298
  43.8 4.4 %collective-permute-start.4 = (f32[9,64,128]{2,1,0:T(8,128)S(1)}, f32[9,64,128]{2,1,0:T(8,128)S(1)}, u32[]{:S(2)}, u32[]{:S(2)}) collective-permute-start(f32[9,64,128]{2,1,0:T(8,128)S(1)} %multiply_add_fusion.14), channel_id=1, source_target_pairs={{0,16},{2,18},{4,20},{6,22},{8,24},{10,26},{12,28},{14,30},{16,32}... | collective-permute-start | bytes 884744 | tf_op jit(solution)/shard_map/ppermute | solution.py:298
  48.3 3.0 %collective-permute-start.10 = (f32[9,64,128]{2,1,0:T(8,128)S(1)}, f32[9,64,128]{2,1,0:T(8,128)S(1)}, u32[]{:S(2)}, u32[]{:S(2)}) collective-permute-start(f32[9,64,128]{2,1,0:T(8,128)S(1)} %multiply_add_fusion.8), channel_id=1, source_target_pairs={{16,0},{18,2},{20,4},{22,6},{24,8},{26,10},{28,12},{30,14},{32,16}... | collective-permute-start | bytes 884744 | tf_op jit(solution)/shard_map/ppermute | solution.py:299
  51.3 4.7 %collective-permute-done.4 = f32[9,64,128]{2,1,0:T(8,128)S(1)} collective-permute-done((f32[9,64,128]{2,1,0:T(8,128)S(1)}, f32[9,64,128]{2,1,0:T(8,128)S(1)}, u32[]{:S(2)}, u32[]{:S(2)}) %collective-permute-start.4) | collective-permute-done | bytes 294944 | tf_op jit(solution)/shard_map/ppermute | solution.py:298
  56.1 5.4 %collective-permute-start.5 = (f32[9,64,128]{2,1,0:T(8,128)S(1)}, f32[9,64,128]{2,1,0:T(8,128)S(1)}, u32[]{:S(2)}, u32[]{:S(2)}) collective-permute-start(f32[9,64,128]{2,1,0:T(8,128)S(1)} %multiply_add_fusion.13), channel_id=1, source_target_pairs={{0,8},{2,10},{4,12},{6,14},{8,16},{10,18},{12,20},{14,22},{16,24},... | collective-permute-start | bytes 884744 | tf_op jit(solution)/shard_map/ppermute | solution.py:298
  61.5 3.9 %collective-permute-done.10 = f32[9,64,128]{2,1,0:T(8,128)S(1)} collective-permute-done((f32[9,64,128]{2,1,0:T(8,128)S(1)}, f32[9,64,128]{2,1,0:T(8,128)S(1)}, u32[]{:S(2)}, u32[]{:S(2)}) %collective-permute-start.10) | collective-permute-done | bytes 294944 | tf_op jit(solution)/shard_map/ppermute | solution.py:299
  67.6 6.5 %collective-permute-start.6 = (f32[9,64,128]{2,1,0:T(8,128)S(1)}, f32[9,64,128]{2,1,0:T(8,128)S(1)}, u32[]{:S(2)}, u32[]{:S(2)}) collective-permute-start(f32[9,64,128]{2,1,0:T(8,128)S(1)} %multiply_add_fusion.12), channel_id=1, source_target_pairs={{0,4},{2,6},{4,8},{6,10},{8,12},{10,14},{12,16},{14,18},{16,20},{1... | collective-permute-start | bytes 884744 | tf_op jit(solution)/shard_map/ppermute | solution.py:298
  74.1 3.3 %collective-permute-done.11 = f32[9,64,128]{2,1,0:T(8,128)S(1)} collective-permute-done((f32[9,64,128]{2,1,0:T(8,128)S(1)}, f32[9,64,128]{2,1,0:T(8,128)S(1)}, u32[]{:S(2)}, u32[]{:S(2)}) %collective-permute-start.11) | collective-permute-done | bytes 294944 | tf_op jit(solution)/shard_map/ppermute | solution.py:299
  79.7 14.2 %collective-permute-start.7 = (f32[9,64,128]{2,1,0:T(8,128)S(1)}, f32[9,64,128]{2,1,0:T(8,128)S(1)}, u32[]{:S(2)}, u32[]{:S(2)}) collective-permute-start(f32[9,64,128]{2,1,0:T(8,128)S(1)} %multiply_add_fusion.11), channel_id=1, source_target_pairs={{0,2},{2,4},{4,6},{6,8},{8,10},{10,12},{12,14},{14,16},{16,18},{18... | collective-permute-start | bytes 884744 | tf_op jit(solution)/shard_map/ppermute | solution.py:298
  94.0 2.2 %collective-permute-start.13 = (f32[9,64,128]{2,1,0:T(8,128)S(1)}, f32[9,64,128]{2,1,0:T(8,128)S(1)}, u32[]{:S(2)}, u32[]{:S(2)}) collective-permute-start(f32[9,64,128]{2,1,0:T(8,128)S(1)} %multiply_add_fusion.5), channel_id=1, source_target_pairs={{2,0},{4,2},{6,4},{8,6},{10,8},{12,10},{14,12},{16,14},{18,16},{20... | collective-permute-start | bytes 884744 | tf_op jit(solution)/shard_map/ppermute | solution.py:299
  98.2 8.6 %collective-permute-done.13 = f32[9,64,128]{2,1,0:T(8,128)S(1)} collective-permute-done((f32[9,64,128]{2,1,0:T(8,128)S(1)}, f32[9,64,128]{2,1,0:T(8,128)S(1)}, u32[]{:S(2)}, u32[]{:S(2)}) %collective-permute-start.13) | collective-permute-done | bytes 294944 | tf_op jit(solution)/shard_map/ppermute | solution.py:299
  110.5 2.9 %multiply_add_fusion.1 = f32[5,8,64,128]{3,2,1,0:T(8,128)} fusion(f32[5,64,128]{2,1,0:T(8,128)S(1)} %slice-done.1, f32[8]{0:T(128)S(1)} %get-tuple-element.82, f32[5,64,128]{2,1,0:T(8,128)S(1)} %slice-done, f32[8]{0:T(128)S(1)} %get-tuple-element.79, f32[5,64,128]{2,1,0:T(8,128)S(1)} %get-tuple-element.69, f32[8]{0:T(128)S(1)} %get-tuple-element.110, ...), kind=kLoop, calls=%fused_computation.57 | loop fusion | flops 10158080 | bytes 3932672 | tf_op jit(solution)/shard_map/add | solution.py:310
  118.0 5.8 %collective-permute-start.15 = (f32[5,64,128]{2,1,0:T(8,128)S(1)}, f32[5,64,128]{2,1,0:T(8,128)S(1)}, u32[]{:S(2)}, u32[]{:S(2)}) collective-permute-start(f32[5,64,128]{2,1,0:T(8,128)S(1)} %get-tuple-element.73), channel_id=1, source_target_pairs={{0,64},{2,66},{4,68},{6,70},{8,72},{10,74},{12,76},{14,78},{16,80}... | collective-permute-start | bytes 491528 | tf_op jit(solution)/shard_map/ppermute | solution.py:298
  128.1 4.3 %collective-permute-done.21 = f32[5,64,128]{2,1,0:T(8,128)S(1)} collective-permute-done((f32[5,64,128]{2,1,0:T(8,128)S(1)}, f32[5,64,128]{2,1,0:T(8,128)S(1)}, u32[]{:S(2)}, u32[]{:S(2)}) %collective-permute-start.21) | collective-permute-done | bytes 163872 | tf_op jit(solution)/shard_map/ppermute | solution.py:299
  138.7 3.9 %collective-permute-done.22 = f32[5,64,128]{2,1,0:T(8,128)S(1)} collective-permute-done((f32[5,64,128]{2,1,0:T(8,128)S(1)}, f32[5,64,128]{2,1,0:T(8,128)S(1)}, u32[]{:S(2)}, u32[]{:S(2)}) %collective-permute-start.22) | collective-permute-done | bytes 163872 | tf_op jit(solution)/shard_map/ppermute | solution.py:299
  147.5 4.8 %collective-permute-done.23 = f32[5,64,128]{2,1,0:T(8,128)S(1)} collective-permute-done((f32[5,64,128]{2,1,0:T(8,128)S(1)}, f32[5,64,128]{2,1,0:T(8,128)S(1)}, u32[]{:S(2)}, u32[]{:S(2)}) %collective-permute-start.23) | collective-permute-done | bytes 163872 | tf_op jit(solution)/shard_map/ppermute | solution.py:299
  156.4 5.4 %collective-permute-done.24 = f32[5,64,128]{2,1,0:T(8,128)S(1)} collective-permute-done((f32[5,64,128]{2,1,0:T(8,128)S(1)}, f32[5,64,128]{2,1,0:T(8,128)S(1)}, u32[]{:S(2)}, u32[]{:S(2)}) %collective-permute-start.24) | collective-permute-done | bytes 163872 | tf_op jit(solution)/shard_map/ppermute | solution.py:299
  164.7 10.5 %collective-permute-start.20 = (f32[5,64,128]{2,1,0:T(8,128)S(1)}, f32[5,64,128]{2,1,0:T(8,128)S(1)}, u32[]{:S(2)}, u32[]{:S(2)}) collective-permute-start(f32[5,64,128]{2,1,0:T(8,128)S(1)} %multiply_add_fusion.24), channel_id=1, source_target_pairs={{0,2},{2,4},{4,6},{6,8},{8,10},{10,12},{12,14},{14,16},{16,18},{18... | collective-permute-start | bytes 491528 | tf_op jit(solution)/shard_map/ppermute | solution.py:298
  178.1 8.6 %collective-permute-done.26 = f32[5,64,128]{2,1,0:T(8,128)S(1)} collective-permute-done((f32[5,64,128]{2,1,0:T(8,128)S(1)}, f32[5,64,128]{2,1,0:T(8,128)S(1)}, u32[]{:S(2)}, u32[]{:S(2)}) %collective-permute-start.26) | collective-permute-done | bytes 163872 | tf_op jit(solution)/shard_map/ppermute | solution.py:299
  186.9 2.9 %fusion.4 = f32[5,8,64,128]{3,2,1,0:T(8,128)S(1)} fusion(f32[5,8,128,64]{2,3,1,0:T(8,128)S(1)} %fusion.104, f32[5,8,64,128]{3,2,1,0:T(8,128)S(1)} %collective-permute-done.27, f32[64,64,1,1]{0,1,3,2:T(8,128)S(1)} %copy-done.32, f32[5,8,64,128]{3,2,1,0:T(8,128)S(1)} %fusion.103, f32[5,64,128]{2,1,0:T(8,128)S(1)} %multiply_add_fusion.17, ...), kind=kOutput, calls=%fused_computation.53 | convolution fusion | flops 261816320 | bytes 7553472 | tf_op jit(solution)/shard_map/fyzx,zw->fywx/dot_general | solution.py:336
  (194 shorter events, 65.4 us)
Async XLA Ops:
  9.5 21.3 %collective-permute-start.2 = (f32[9,64,128]{2,1,0:T(8,128)}, f32[9,64,128]{2,1,0:T(8,128)}, u32[]{:S(2)}, u32[]{:S(2)}) collective-permute-start(f32[9,64,128]{2,1,0:T(8,128)} %pad_maximum_fusion.7), channel_id=1, source_target_pairs={{0,64},{2,66},{4,68},{6,70},{8,72},{10,74},{12,76},{14,78},{16,80}... | collective-permute-start | bytes 884744 | tf_op jit(solution)/shard_map/ppermute | solution.py:298
  16.8 19.4 %collective-permute-start.8 = (f32[9,64,128]{2,1,0:T(8,128)}, f32[9,64,128]{2,1,0:T(8,128)}, u32[]{:S(2)}, u32[]{:S(2)}) collective-permute-start(f32[9,64,128]{2,1,0:T(8,128)} %pad_maximum_fusion.8), channel_id=1, source_target_pairs={{64,0},{66,2},{68,4},{70,6},{72,8},{74,10},{76,12},{78,14},{80,16}... | collective-permute-start | bytes 884744 | tf_op jit(solution)/shard_map/ppermute | solution.py:299
  19.1 19.5 %collective-permute-start = (f32[5,3,64,128]{3,2,1,0:T(8,128)}, f32[5,3,64,128]{3,2,1,0:T(8,128)S(1)}, u32[]{:S(2)}, u32[]{:S(2)}) collective-permute-start(f32[5,3,64,128]{3,2,1,0:T(8,128)} %get-tuple-element.51), channel_id=1, source_target_pairs={{0,2},{2,4},{4,6},{6,8},{8,10},{10,12},{12,14},{14,16},{16,18},{18... | collective-permute-start | bytes 1474568 | tf_op jit(solution)/shard_map/ppermute | solution.py:322
  21.7 18.7 %collective-permute-start.1 = (f32[5,3,64,128]{3,2,1,0:T(8,128)}, f32[5,3,64,128]{3,2,1,0:T(8,128)S(1)}, u32[]{:S(2)}, u32[]{:S(2)}) collective-permute-start(f32[5,3,64,128]{3,2,1,0:T(8,128)} %get-tuple-element.52), channel_id=1, source_target_pairs={{2,0},{4,2},{6,4},{8,6},{10,8},{12,10},{14,12},{16,14},{18,16},{20... | collective-permute-start | bytes 1474568 | tf_op jit(solution)/shard_map/ppermute | solution.py:323
  31.9 11.8 %collective-permute-start.3 = (f32[9,64,128]{2,1,0:T(8,128)S(1)}, f32[9,64,128]{2,1,0:T(8,128)S(1)}, u32[]{:S(2)}, u32[]{:S(2)}) collective-permute-start(f32[9,64,128]{2,1,0:T(8,128)S(1)} %multiply_add_fusion.15), channel_id=1, source_target_pairs={{0,32},{2,34},{4,36},{6,38},{8,40},{10,42},{12,44},{14,46},{16,48}... | collective-permute-start | bytes 884744 | tf_op jit(solution)/shard_map/ppermute | solution.py:298
  37.3 10.9 %collective-permute-start.9 = (f32[9,64,128]{2,1,0:T(8,128)S(1)}, f32[9,64,128]{2,1,0:T(8,128)S(1)}, u32[]{:S(2)}, u32[]{:S(2)}) collective-permute-start(f32[9,64,128]{2,1,0:T(8,128)S(1)} %multiply_add_fusion.9), channel_id=1, source_target_pairs={{32,0},{34,2},{36,4},{38,6},{40,8},{42,10},{44,12},{46,14},{48,16}... | collective-permute-start | bytes 884744 | tf_op jit(solution)/shard_map/ppermute | solution.py:299
  41.4 72.0 %collective-permute-start.14 = (f32[4,12,64,128]{3,2,1,0:T(8,128)S(1)}, f32[4,12,64,128]{3,2,1,0:T(8,128)S(1)}, u32[]{:S(2)}, u32[]{:S(2)}) collective-permute-start(f32[4,12,64,128]{3,2,1,0:T(8,128)S(1)} %fusion.1), channel_id=1, source_target_pairs={{0,1},{1,0},{2,3},{3,2},{4,5},{5,4},{6,7},{7,6},{8,9},{9,8},{10,11... | collective-permute-start | bytes 4718600 | tf_op jit(solution)/shard_map/ppermute | solution.py:335
  43.8 12.2 %collective-permute-start.4 = (f32[9,64,128]{2,1,0:T(8,128)S(1)}, f32[9,64,128]{2,1,0:T(8,128)S(1)}, u32[]{:S(2)}, u32[]{:S(2)}) collective-permute-start(f32[9,64,128]{2,1,0:T(8,128)S(1)} %multiply_add_fusion.14), channel_id=1, source_target_pairs={{0,16},{2,18},{4,20},{6,22},{8,24},{10,26},{12,28},{14,30},{16,32}... | collective-permute-start | bytes 884744 | tf_op jit(solution)/shard_map/ppermute | solution.py:298
  48.3 17.1 %collective-permute-start.10 = (f32[9,64,128]{2,1,0:T(8,128)S(1)}, f32[9,64,128]{2,1,0:T(8,128)S(1)}, u32[]{:S(2)}, u32[]{:S(2)}) collective-permute-start(f32[9,64,128]{2,1,0:T(8,128)S(1)} %multiply_add_fusion.8), channel_id=1, source_target_pairs={{16,0},{18,2},{20,4},{22,6},{24,8},{26,10},{28,12},{30,14},{32,16}... | collective-permute-start | bytes 884744 | tf_op jit(solution)/shard_map/ppermute | solution.py:299
  56.1 11.4 %collective-permute-start.5 = (f32[9,64,128]{2,1,0:T(8,128)S(1)}, f32[9,64,128]{2,1,0:T(8,128)S(1)}, u32[]{:S(2)}, u32[]{:S(2)}) collective-permute-start(f32[9,64,128]{2,1,0:T(8,128)S(1)} %multiply_add_fusion.13), channel_id=1, source_target_pairs={{0,8},{2,10},{4,12},{6,14},{8,16},{10,18},{12,20},{14,22},{16,24},... | collective-permute-start | bytes 884744 | tf_op jit(solution)/shard_map/ppermute | solution.py:298
  65.5 11.9 %collective-permute-start.11 = (f32[9,64,128]{2,1,0:T(8,128)S(1)}, f32[9,64,128]{2,1,0:T(8,128)S(1)}, u32[]{:S(2)}, u32[]{:S(2)}) collective-permute-start(f32[9,64,128]{2,1,0:T(8,128)S(1)} %multiply_add_fusion.7), channel_id=1, source_target_pairs={{8,0},{10,2},{12,4},{14,6},{16,8},{18,10},{20,12},{22,14},{24,16},... | collective-permute-start | bytes 884744 | tf_op jit(solution)/shard_map/ppermute | solution.py:299
  67.6 12.0 %collective-permute-start.6 = (f32[9,64,128]{2,1,0:T(8,128)S(1)}, f32[9,64,128]{2,1,0:T(8,128)S(1)}, u32[]{:S(2)}, u32[]{:S(2)}) collective-permute-start(f32[9,64,128]{2,1,0:T(8,128)S(1)} %multiply_add_fusion.12), channel_id=1, source_target_pairs={{0,4},{2,6},{4,8},{6,10},{8,12},{10,14},{12,16},{14,18},{16,20},{1... | collective-permute-start | bytes 884744 | tf_op jit(solution)/shard_map/ppermute | solution.py:298
  77.5 16.3 %collective-permute-start.12 = (f32[9,64,128]{2,1,0:T(8,128)S(1)}, f32[9,64,128]{2,1,0:T(8,128)S(1)}, u32[]{:S(2)}, u32[]{:S(2)}) collective-permute-start(f32[9,64,128]{2,1,0:T(8,128)S(1)} %multiply_add_fusion.6), channel_id=1, source_target_pairs={{4,0},{6,2},{8,4},{10,6},{12,8},{14,10},{16,12},{18,14},{20,16},{2... | collective-permute-start | bytes 884744 | tf_op jit(solution)/shard_map/ppermute | solution.py:299
  79.7 18.4 %collective-permute-start.7 = (f32[9,64,128]{2,1,0:T(8,128)S(1)}, f32[9,64,128]{2,1,0:T(8,128)S(1)}, u32[]{:S(2)}, u32[]{:S(2)}) collective-permute-start(f32[9,64,128]{2,1,0:T(8,128)S(1)} %multiply_add_fusion.11), channel_id=1, source_target_pairs={{0,2},{2,4},{4,6},{6,8},{8,10},{10,12},{12,14},{14,16},{16,18},{18... | collective-permute-start | bytes 884744 | tf_op jit(solution)/shard_map/ppermute | solution.py:298
  94.0 12.8 %collective-permute-start.13 = (f32[9,64,128]{2,1,0:T(8,128)S(1)}, f32[9,64,128]{2,1,0:T(8,128)S(1)}, u32[]{:S(2)}, u32[]{:S(2)}) collective-permute-start(f32[9,64,128]{2,1,0:T(8,128)S(1)} %multiply_add_fusion.5), channel_id=1, source_target_pairs={{2,0},{4,2},{6,4},{8,6},{10,8},{12,10},{14,12},{16,14},{18,16},{20... | collective-permute-start | bytes 884744 | tf_op jit(solution)/shard_map/ppermute | solution.py:299
  118.0 10.1 %collective-permute-start.15 = (f32[5,64,128]{2,1,0:T(8,128)S(1)}, f32[5,64,128]{2,1,0:T(8,128)S(1)}, u32[]{:S(2)}, u32[]{:S(2)}) collective-permute-start(f32[5,64,128]{2,1,0:T(8,128)S(1)} %get-tuple-element.73), channel_id=1, source_target_pairs={{0,64},{2,66},{4,68},{6,70},{8,72},{10,74},{12,76},{14,78},{16,80}... | collective-permute-start | bytes 491528 | tf_op jit(solution)/shard_map/ppermute | solution.py:298
  126.0 60.9 %collective-permute-start.27 = (f32[5,8,64,128]{3,2,1,0:T(8,128)S(1)}, f32[5,8,64,128]{3,2,1,0:T(8,128)S(1)}, u32[]{:S(2)}, u32[]{:S(2)}) collective-permute-start(f32[5,8,64,128]{3,2,1,0:T(8,128)S(1)} %fusion.34), channel_id=1, source_target_pairs={{0,1},{1,0},{2,3},{3,2},{4,5},{5,4},{6,7},{7,6},{8,9},{9,8},{10,11... | collective-permute-start | bytes 3932168 | tf_op jit(solution)/shard_map/ppermute | solution.py:335
  142.7 9.6 %collective-permute-start.23 = (f32[5,64,128]{2,1,0:T(8,128)S(1)}, f32[5,64,128]{2,1,0:T(8,128)S(1)}, u32[]{:S(2)}, u32[]{:S(2)}) collective-permute-start(f32[5,64,128]{2,1,0:T(8,128)S(1)} %multiply_add_fusion.21), channel_id=1, source_target_pairs={{16,0},{18,2},{20,4},{22,6},{24,8},{26,10},{28,12},{30,14},{32,16}... | collective-permute-start | bytes 491528 | tf_op jit(solution)/shard_map/ppermute | solution.py:299
  145.6 8.7 %collective-permute-start.18 = (f32[5,64,128]{2,1,0:T(8,128)S(1)}, f32[5,64,128]{2,1,0:T(8,128)S(1)}, u32[]{:S(2)}, u32[]{:S(2)}) collective-permute-start(f32[5,64,128]{2,1,0:T(8,128)S(1)} %multiply_add_fusion.26), channel_id=1, source_target_pairs={{0,8},{2,10},{4,12},{6,14},{8,16},{10,18},{12,20},{14,22},{16,24},... | collective-permute-start | bytes 491528 | tf_op jit(solution)/shard_map/ppermute | solution.py:298
  152.4 9.3 %collective-permute-start.24 = (f32[5,64,128]{2,1,0:T(8,128)S(1)}, f32[5,64,128]{2,1,0:T(8,128)S(1)}, u32[]{:S(2)}, u32[]{:S(2)}) collective-permute-start(f32[5,64,128]{2,1,0:T(8,128)S(1)} %multiply_add_fusion.20), channel_id=1, source_target_pairs={{8,0},{10,2},{12,4},{14,6},{16,8},{18,10},{20,12},{22,14},{24,16},... | collective-permute-start | bytes 491528 | tf_op jit(solution)/shard_map/ppermute | solution.py:299
  154.4 10.2 %collective-permute-start.19 = (f32[5,64,128]{2,1,0:T(8,128)S(1)}, f32[5,64,128]{2,1,0:T(8,128)S(1)}, u32[]{:S(2)}, u32[]{:S(2)}) collective-permute-start(f32[5,64,128]{2,1,0:T(8,128)S(1)} %multiply_add_fusion.25), channel_id=1, source_target_pairs={{0,4},{2,6},{4,8},{6,10},{8,12},{10,14},{12,16},{14,18},{16,20},{1... | collective-permute-start | bytes 491528 | tf_op jit(solution)/shard_map/ppermute | solution.py:298
  161.8 13.4 %collective-permute-start.25 = (f32[5,64,128]{2,1,0:T(8,128)S(1)}, f32[5,64,128]{2,1,0:T(8,128)S(1)}, u32[]{:S(2)}, u32[]{:S(2)}) collective-permute-start(f32[5,64,128]{2,1,0:T(8,128)S(1)} %multiply_add_fusion.19), channel_id=1, source_target_pairs={{4,0},{6,2},{8,4},{10,6},{12,8},{14,10},{16,12},{18,14},{20,16},{2... | collective-permute-start | bytes 491528 | tf_op jit(solution)/shard_map/ppermute | solution.py:299
  164.7 13.3 %collective-permute-start.20 = (f32[5,64,128]{2,1,0:T(8,128)S(1)}, f32[5,64,128]{2,1,0:T(8,128)S(1)}, u32[]{:S(2)}, u32[]{:S(2)}) collective-permute-start(f32[5,64,128]{2,1,0:T(8,128)S(1)} %multiply_add_fusion.24), channel_id=1, source_target_pairs={{0,2},{2,4},{4,6},{6,8},{8,10},{10,12},{12,14},{14,16},{16,18},{18... | collective-permute-start | bytes 491528 | tf_op jit(solution)/shard_map/ppermute | solution.py:298
  175.3 11.4 %collective-permute-start.26 = (f32[5,64,128]{2,1,0:T(8,128)S(1)}, f32[5,64,128]{2,1,0:T(8,128)S(1)}, u32[]{:S(2)}, u32[]{:S(2)}) collective-permute-start(f32[5,64,128]{2,1,0:T(8,128)S(1)} %multiply_add_fusion.18), channel_id=1, source_target_pairs={{2,0},{4,2},{6,4},{8,6},{10,8},{12,10},{14,12},{16,14},{18,16},{20... | collective-permute-start | bytes 491528 | tf_op jit(solution)/shard_map/ppermute | solution.py:299
  (39 other events, 143.6 us)

commit v14 on v12

--- a/solution.py
+++ b/solution.py
@@ -178,7 +178,10 @@
         radix = min(2, -(-blocks // stride))
         rounds.append((stride, list(range(1, radix))))
         stride *= radix
-    return rounds[::-1]
+    reordered = []
+    for first in range(len(rounds) - 2 + len(rounds) % 2, -1, -2):
+        reordered += rounds[first : first + 2]
+    return reordered
 
 
 def scan_coefs(rise_step, fall_step, shift):

time: 186 us -> 201 us (1.081)
  waiting for transfers between devices: 65.1 us -> 95.2 us
  starting transfers between devices: 79 us -> 64.1 us
    ppermute x12, waiting for transfers between devices: 51.1 us -> 82.2 us  [wall_apply(): from_above = lax.ppermute(fall, 'gy', down_pairs)]
    ppermute x12, starting transfers between devices: 50.8 us -> 37.4 us  [wall_apply(): from_below = lax.ppermute(rise, 'gy', up_pairs)]
  transfers between devices with their start and end apart: 28 -> 28, of which waited for: 16 -> 15; matrix products, arithmetic and copies ran while one was open for 13% -> 12% of each run, Pallas kernels for 0% -> 0%
where the time goes in v14:
time: 201 us; the launch traced here: 200 us
  waiting for transfers between devices  95.2 us (47%)
  starting transfers between devices  64.1 us (32%)
  other arithmetic  14.7 us (7%)
  local copies, waits for them, and re-layouts  13.8 us (7%)
  matrix products  9.95 us (5%)
  between operations  2.08 us (1%)
    ppermute x12, waiting for transfers between devices, wall_apply(): from_above = lax.ppermute(fall, 'gy', down_pairs)  82.2 us
    ppermute x12, starting transfers between devices, wall_apply(): from_below = lax.ppermute(rise, 'gy', up_pairs)  37.4 us
    ppermute x12, starting transfers between devices, wall_apply(): from_above = lax.ppermute(fall, 'gy', down_pairs)  20.7 us
    ppermute x12, waiting for transfers between devices, wall_apply(): from_below = lax.ppermute(rise, 'gy', up_pairs)  7.66 us
    ppermute x1, waiting for transfers between devices, halo(): above = lax.ppermute(block[:, :width], 'gy', down_pairs)  5.32 us
    add x2, other arithmetic, wall_apply(): local + rise_gain[None, :, None, None] * rise[first:first + size, None]  4.9 us
    dot_general x2, matrix products, span_slope(): jnp.einsum('fyzx,zw->fywx', other, other_block, precision=HIGHEST)  4.43 us
  transfers between devices with their start and end apart: 28, of which 15 were waited for; matrix products, arithmetic and copies ran while one was open for 12% of the time, Pallas kernels for 0%

profile of v14, /device:TPU:30, one launch (start us, length us, event | category | flops | bytes accessed | tf_op | source)
XLA Modules:
  0.0 199.9 jit_solution(16510439786273928202)
XLA Ops:
  3.0 3.4 %collective-permute-start = (f32[5,3,64,128]{3,2,1,0:T(8,128)}, f32[5,3,64,128]{3,2,1,0:T(8,128)S(1)}, u32[]{:S(2)}, u32[]{:S(2)}) collective-permute-start(f32[5,3,64,128]{3,2,1,0:T(8,128)} %get-tuple-element.51), channel_id=1, source_target_pairs={{0,2},{2,4},{4,6},{6,8},{8,10},{10,12},{12,14},{14,16},{16,18},{18... | collective-permute-start | bytes 1474568 | tf_op jit(solution)/shard_map/ppermute | solution.py:299
  6.4 2.4 %collective-permute-start.1 = (f32[5,3,64,128]{3,2,1,0:T(8,128)}, f32[5,3,64,128]{3,2,1,0:T(8,128)S(1)}, u32[]{:S(2)}, u32[]{:S(2)}) collective-permute-start(f32[5,3,64,128]{3,2,1,0:T(8,128)} %get-tuple-element.52), channel_id=1, source_target_pairs={{2,0},{4,2},{6,4},{8,6},{10,8},{12,10},{14,12},{16,14},{18,16},{20... | collective-permute-start | bytes 1474568 | tf_op jit(solution)/shard_map/ppermute | solution.py:300
  20.1 5.3 %collective-permute-done.1 = f32[5,3,64,128]{3,2,1,0:T(8,128)S(1)} collective-permute-done((f32[5,3,64,128]{3,2,1,0:T(8,128)}, f32[5,3,64,128]{3,2,1,0:T(8,128)S(1)}, u32[]{:S(2)}, u32[]{:S(2)}) %collective-permute-start.1) | collective-permute-done | bytes 491552 | tf_op jit(solution)/shard_map/ppermute | solution.py:300
  28.0 3.8 %collective-permute-start.2 = (f32[9,64,128]{2,1,0:T(8,128)S(1)}, f32[9,64,128]{2,1,0:T(8,128)S(1)}, u32[]{:S(2)}, u32[]{:S(2)}) collective-permute-start(f32[9,64,128]{2,1,0:T(8,128)S(1)} %pad_maximum_fusion.7), channel_id=1, source_target_pairs={{0,32},{2,34},{4,36},{6,38},{8,40},{10,42},{12,44},{14,46},{16,48}... | collective-permute-start | bytes 884744 | tf_op jit(solution)/shard_map/ppermute | solution.py:275
  34.7 2.2 %collective-permute-done.2 = f32[9,64,128]{2,1,0:T(8,128)S(1)} collective-permute-done((f32[9,64,128]{2,1,0:T(8,128)S(1)}, f32[9,64,128]{2,1,0:T(8,128)S(1)}, u32[]{:S(2)}, u32[]{:S(2)}) %collective-permute-start.2) | collective-permute-done | bytes 294944 | tf_op jit(solution)/shard_map/ppermute | solution.py:275
  37.0 6.1 %collective-permute-start.3 = (f32[9,64,128]{2,1,0:T(8,128)S(1)}, f32[9,64,128]{2,1,0:T(8,128)S(1)}, u32[]{:S(2)}, u32[]{:S(2)}) collective-permute-start(f32[9,64,128]{2,1,0:T(8,128)S(1)} %multiply_add_fusion.15), channel_id=1, source_target_pairs={{0,64},{2,66},{4,68},{6,70},{8,72},{10,74},{12,76},{14,78},{16,80}... | collective-permute-start | bytes 884744 | tf_op jit(solution)/shard_map/ppermute | solution.py:275
  44.6 3.3 %collective-permute-done.3 = f32[9,64,128]{2,1,0:T(8,128)S(1)} collective-permute-done((f32[9,64,128]{2,1,0:T(8,128)S(1)}, f32[9,64,128]{2,1,0:T(8,128)S(1)}, u32[]{:S(2)}, u32[]{:S(2)}) %collective-permute-start.3) | collective-permute-done | bytes 294944 | tf_op jit(solution)/shard_map/ppermute | solution.py:275
  50.0 3.7 %collective-permute-done.9 = f32[9,64,128]{2,1,0:T(8,128)S(1)} collective-permute-done((f32[9,64,128]{2,1,0:T(8,128)S(1)}, f32[9,64,128]{2,1,0:T(8,128)S(1)}, u32[]{:S(2)}, u32[]{:S(2)}) %collective-permute-start.9) | collective-permute-done | bytes 294944 | tf_op jit(solution)/shard_map/ppermute | solution.py:276
  53.8 1.9 collective-permute-start.10
  58.7 11.6 %collective-permute-done.10 = f32[9,64,128]{2,1,0:T(8,128)S(1)} collective-permute-done((f32[9,64,128]{2,1,0:T(8,128)S(1)}, f32[9,64,128]{2,1,0:T(8,128)S(1)}, u32[]{:S(2)}, u32[]{:S(2)}) %collective-permute-start.10) | collective-permute-done | bytes 294944 | tf_op jit(solution)/shard_map/ppermute | solution.py:276
  74.4 7.1 %collective-permute-done.11 = f32[9,64,128]{2,1,0:T(8,128)S(1)} collective-permute-done((f32[9,64,128]{2,1,0:T(8,128)S(1)}, f32[9,64,128]{2,1,0:T(8,128)S(1)}, u32[]{:S(2)}, u32[]{:S(2)}) %collective-permute-start.11) | collective-permute-done | bytes 294944 | tf_op jit(solution)/shard_map/ppermute | solution.py:276
  85.6 12.8 %collective-permute-done.12 = f32[9,64,128]{2,1,0:T(8,128)S(1)} collective-permute-done((f32[9,64,128]{2,1,0:T(8,128)S(1)}, f32[9,64,128]{2,1,0:T(8,128)S(1)}, u32[]{:S(2)}, u32[]{:S(2)}) %collective-permute-start.12) | collective-permute-done | bytes 294944 | tf_op jit(solution)/shard_map/ppermute | solution.py:276
  98.6 2.1 %collective-permute-start.13 = (f32[9,64,128]{2,1,0:T(8,128)S(1)}, f32[9,64,128]{2,1,0:T(8,128)S(1)}, u32[]{:S(2)}, u32[]{:S(2)}) collective-permute-start(f32[9,64,128]{2,1,0:T(8,128)S(1)} %multiply_add_fusion.5), channel_id=1, source_target_pairs={{4,0},{6,2},{8,4},{10,6},{12,8},{14,10},{16,12},{18,14},{20,16},{2... | collective-permute-start | bytes 884744 | tf_op jit(solution)/shard_map/ppermute | solution.py:276
  104.2 8.7 %collective-permute-done.13 = f32[9,64,128]{2,1,0:T(8,128)S(1)} collective-permute-done((f32[9,64,128]{2,1,0:T(8,128)S(1)}, f32[9,64,128]{2,1,0:T(8,128)S(1)}, u32[]{:S(2)}, u32[]{:S(2)}) %collective-permute-start.13) | collective-permute-done | bytes 294944 | tf_op jit(solution)/shard_map/ppermute | solution.py:276
  112.9 2.0 %multiply_add_fusion = f32[4,12,64,128]{3,2,1,0:T(8,128)S(1)} fusion(f32[4,64,128]{2,1,0:T(8,128)S(1)} %slice.1165, f32[12]{0:T(128)S(1)} %get-tuple-element.86, f32[4,64,128]{2,1,0:T(8,128)S(1)} %slice.1162, f32[12]{0:T(128)S(1)} %get-tuple-element.85, f32[4,64,128]{2,1,0:T(8,128)S(1)} %get-tuple-element.34, f32[12]{0:T(128)S(1)} %get-tuple-element.191, ...), kind=kLoop, calls=%fused_computation.35 | loop fusion | flops 12189696 | bytes 3670784 | tf_op jit(solution)/shard_map/add | solution.py:287
  117.0 7.2 %collective-permute-start.15 = (f32[5,64,128]{2,1,0:T(8,128)S(1)}, f32[5,64,128]{2,1,0:T(8,128)S(1)}, u32[]{:S(2)}, u32[]{:S(2)}) collective-permute-start(f32[5,64,128]{2,1,0:T(8,128)S(1)} %get-tuple-element.63), channel_id=1, source_target_pairs={{0,32},{2,34},{4,36},{6,38},{8,40},{10,42},{12,44},{14,46},{16,48}... | collective-permute-start | bytes 491528 | tf_op jit(solution)/shard_map/ppermute | solution.py:275
  127.6 2.9 %multiply_add_fusion.1 = f32[5,8,64,128]{3,2,1,0:T(8,128)} fusion(f32[5,64,128]{2,1,0:T(8,128)S(1)} %slice-done.1, f32[8]{0:T(128)S(1)} %copy-done.40, f32[5,64,128]{2,1,0:T(8,128)S(1)} %slice-done, f32[8]{0:T(128)S(1)} %copy-done.39, f32[5,64,128]{2,1,0:T(8,128)S(1)} %get-tuple-element.59, f32[8]{0:T(128)S(1)} %copy-done.26, ...), kind=kLoop, calls=%fused_computation.43 | loop fusion | flops 10158080 | bytes 3932672 | tf_op jit(solution)/shard_map/add | solution.py:287
  131.8 5.0 %collective-permute-start.16 = (f32[5,64,128]{2,1,0:T(8,128)S(1)}, f32[5,64,128]{2,1,0:T(8,128)S(1)}, u32[]{:S(2)}, u32[]{:S(2)}) collective-permute-start(f32[5,64,128]{2,1,0:T(8,128)S(1)} %get-tuple-element.61), channel_id=1, source_target_pairs={{0,64},{2,66},{4,68},{6,70},{8,72},{10,74},{12,76},{14,78},{16,80}... | collective-permute-start | bytes 491528 | tf_op jit(solution)/shard_map/ppermute | solution.py:275
  142.7 5.2 %collective-permute-done.22 = f32[5,64,128]{2,1,0:T(8,128)S(1)} collective-permute-done((f32[5,64,128]{2,1,0:T(8,128)S(1)}, f32[5,64,128]{2,1,0:T(8,128)S(1)}, u32[]{:S(2)}, u32[]{:S(2)}) %collective-permute-start.22) | collective-permute-done | bytes 163872 | tf_op jit(solution)/shard_map/ppermute | solution.py:276
  151.9 9.0 %collective-permute-done.23 = f32[5,64,128]{2,1,0:T(8,128)S(1)} collective-permute-done((f32[5,64,128]{2,1,0:T(8,128)S(1)}, f32[5,64,128]{2,1,0:T(8,128)S(1)}, u32[]{:S(2)}, u32[]{:S(2)}) %collective-permute-start.23) | collective-permute-done | bytes 163872 | tf_op jit(solution)/shard_map/ppermute | solution.py:276
  165.1 5.8 %collective-permute-done.24 = f32[5,64,128]{2,1,0:T(8,128)S(1)} collective-permute-done((f32[5,64,128]{2,1,0:T(8,128)S(1)}, f32[5,64,128]{2,1,0:T(8,128)S(1)}, u32[]{:S(2)}, u32[]{:S(2)}) %collective-permute-start.24) | collective-permute-done | bytes 163872 | tf_op jit(solution)/shard_map/ppermute | solution.py:276
  175.0 8.6 %collective-permute-done.25 = f32[5,64,128]{2,1,0:T(8,128)S(1)} collective-permute-done((f32[5,64,128]{2,1,0:T(8,128)S(1)}, f32[5,64,128]{2,1,0:T(8,128)S(1)}, u32[]{:S(2)}, u32[]{:S(2)}) %collective-permute-start.25) | collective-permute-done | bytes 163872 | tf_op jit(solution)/shard_map/ppermute | solution.py:276
  185.7 9.7 %collective-permute-done.26 = f32[5,64,128]{2,1,0:T(8,128)S(1)} collective-permute-done((f32[5,64,128]{2,1,0:T(8,128)S(1)}, f32[5,64,128]{2,1,0:T(8,128)S(1)}, u32[]{:S(2)}, u32[]{:S(2)}) %collective-permute-start.26) | collective-permute-done | bytes 163872 | tf_op jit(solution)/shard_map/ppermute | solution.py:276
  195.6 2.9 %fusion.4 = f32[5,8,64,128]{3,2,1,0:T(8,128)S(1)} fusion(f32[5,8,128,64]{2,3,1,0:T(8,128)S(1)} %fusion.89, f32[5,8,64,128]{3,2,1,0:T(8,128)S(1)} %collective-permute-done.27, f32[64,64,1,1]{0,1,3,2:T(8,128)S(1)} %copy-done.9, f32[5,8,64,128]{3,2,1,0:T(8,128)S(1)} %fusion.88, f32[5,64,128]{2,1,0:T(8,128)S(1)} %multiply_add_fusion.17, f32[8]{0:T(128)S(1)} %copy-done.54, ...), kind=kOutput, calls=%fused_computation.39 | convolution fusion | flops 261816320 | bytes 7553472 | tf_op jit(solution)/shard_map/fyzx,zw->fywx/dot_general | solution.py:313
  (237 shorter events, 65.1 us)
Async XLA Ops:
  3.0 17.1 %collective-permute-start = (f32[5,3,64,128]{3,2,1,0:T(8,128)}, f32[5,3,64,128]{3,2,1,0:T(8,128)S(1)}, u32[]{:S(2)}, u32[]{:S(2)}) collective-permute-start(f32[5,3,64,128]{3,2,1,0:T(8,128)} %get-tuple-element.51), channel_id=1, source_target_pairs={{0,2},{2,4},{4,6},{6,8},{8,10},{10,12},{12,14},{14,16},{16,18},{18... | collective-permute-start | bytes 1474568 | tf_op jit(solution)/shard_map/ppermute | solution.py:299
  6.4 19.0 %collective-permute-start.1 = (f32[5,3,64,128]{3,2,1,0:T(8,128)}, f32[5,3,64,128]{3,2,1,0:T(8,128)S(1)}, u32[]{:S(2)}, u32[]{:S(2)}) collective-permute-start(f32[5,3,64,128]{3,2,1,0:T(8,128)} %get-tuple-element.52), channel_id=1, source_target_pairs={{2,0},{4,2},{6,4},{8,6},{10,8},{12,10},{14,12},{16,14},{18,16},{20... | collective-permute-start | bytes 1474568 | tf_op jit(solution)/shard_map/ppermute | solution.py:300
  31.9 11.2 %collective-permute-start.8 = (f32[9,64,128]{2,1,0:T(8,128)S(1)}, f32[9,64,128]{2,1,0:T(8,128)S(1)}, u32[]{:S(2)}, u32[]{:S(2)}) collective-permute-start(f32[9,64,128]{2,1,0:T(8,128)S(1)} %pad_maximum_fusion.8), channel_id=1, source_target_pairs={{32,0},{34,2},{36,4},{38,6},{40,8},{42,10},{44,12},{46,14},{48,16}... | collective-permute-start | bytes 884744 | tf_op jit(solution)/shard_map/ppermute | solution.py:276
  33.2 67.5 %collective-permute-start.14 = (f32[4,12,64,128]{3,2,1,0:T(8,128)S(1)}, f32[4,12,64,128]{3,2,1,0:T(8,128)S(1)}, u32[]{:S(2)}, u32[]{:S(2)}) collective-permute-start(f32[4,12,64,128]{3,2,1,0:T(8,128)S(1)} %fusion.1), channel_id=1, source_target_pairs={{0,1},{1,0},{2,3},{3,2},{4,5},{5,4},{6,7},{7,6},{8,9},{9,8},{10,11... | collective-permute-start | bytes 4718600 | tf_op jit(solution)/shard_map/ppermute | solution.py:312
  37.0 10.9 %collective-permute-start.3 = (f32[9,64,128]{2,1,0:T(8,128)S(1)}, f32[9,64,128]{2,1,0:T(8,128)S(1)}, u32[]{:S(2)}, u32[]{:S(2)}) collective-permute-start(f32[9,64,128]{2,1,0:T(8,128)S(1)} %multiply_add_fusion.15), channel_id=1, source_target_pairs={{0,64},{2,66},{4,68},{6,70},{8,72},{10,74},{12,76},{14,78},{16,80}... | collective-permute-start | bytes 884744 | tf_op jit(solution)/shard_map/ppermute | solution.py:275
  43.2 10.5 %collective-permute-start.9 = (f32[9,64,128]{2,1,0:T(8,128)S(1)}, f32[9,64,128]{2,1,0:T(8,128)S(1)}, u32[]{:S(2)}, u32[]{:S(2)}) collective-permute-start(f32[9,64,128]{2,1,0:T(8,128)S(1)} %multiply_add_fusion.9), channel_id=1, source_target_pairs={{64,0},{66,2},{68,4},{70,6},{72,8},{74,10},{76,12},{78,14},{80,16}... | collective-permute-start | bytes 884744 | tf_op jit(solution)/shard_map/ppermute | solution.py:276
  53.8 16.5 %collective-permute-start.10 = (f32[9,64,128]{2,1,0:T(8,128)S(1)}, f32[9,64,128]{2,1,0:T(8,128)S(1)}, u32[]{:S(2)}, u32[]{:S(2)}) collective-permute-start(f32[9,64,128]{2,1,0:T(8,128)S(1)} %multiply_add_fusion.8), channel_id=1, source_target_pairs={{8,0},{10,2},{12,4},{14,6},{16,8},{18,10},{20,12},{22,14},{24,16},... | collective-permute-start | bytes 884744 | tf_op jit(solution)/shard_map/ppermute | solution.py:276
  56.8 15.6 %collective-permute-start.5 = (f32[9,64,128]{2,1,0:T(8,128)S(1)}, f32[9,64,128]{2,1,0:T(8,128)S(1)}, u32[]{:S(2)}, u32[]{:S(2)}) collective-permute-start(f32[9,64,128]{2,1,0:T(8,128)S(1)} %multiply_add_fusion.13), channel_id=1, source_target_pairs={{0,16},{2,18},{4,20},{6,22},{8,24},{10,26},{12,28},{14,30},{16,32}... | collective-permute-start | bytes 884744 | tf_op jit(solution)/shard_map/ppermute | solution.py:275
  70.4 11.2 %collective-permute-start.11 = (f32[9,64,128]{2,1,0:T(8,128)S(1)}, f32[9,64,128]{2,1,0:T(8,128)S(1)}, u32[]{:S(2)}, u32[]{:S(2)}) collective-permute-start(f32[9,64,128]{2,1,0:T(8,128)S(1)} %multiply_add_fusion.7), channel_id=1, source_target_pairs={{16,0},{18,2},{20,4},{22,6},{24,8},{26,10},{28,12},{30,14},{32,16}... | collective-permute-start | bytes 884744 | tf_op jit(solution)/shard_map/ppermute | solution.py:276
  72.5 11.1 %collective-permute-start.6 = (f32[9,64,128]{2,1,0:T(8,128)S(1)}, f32[9,64,128]{2,1,0:T(8,128)S(1)}, u32[]{:S(2)}, u32[]{:S(2)}) collective-permute-start(f32[9,64,128]{2,1,0:T(8,128)S(1)} %multiply_add_fusion.12), channel_id=1, source_target_pairs={{0,2},{2,4},{4,6},{6,8},{8,10},{10,12},{12,14},{14,16},{16,18},{18... | collective-permute-start | bytes 884744 | tf_op jit(solution)/shard_map/ppermute | solution.py:275
  81.6 16.8 %collective-permute-start.12 = (f32[9,64,128]{2,1,0:T(8,128)S(1)}, f32[9,64,128]{2,1,0:T(8,128)S(1)}, u32[]{:S(2)}, u32[]{:S(2)}) collective-permute-start(f32[9,64,128]{2,1,0:T(8,128)S(1)} %multiply_add_fusion.6), channel_id=1, source_target_pairs={{2,0},{4,2},{6,4},{8,6},{10,8},{12,10},{14,12},{16,14},{18,16},{20... | collective-permute-start | bytes 884744 | tf_op jit(solution)/shard_map/ppermute | solution.py:276
  83.7 20.3 %collective-permute-start.7 = (f32[9,64,128]{2,1,0:T(8,128)S(1)}, f32[9,64,128]{2,1,0:T(8,128)S(1)}, u32[]{:S(2)}, u32[]{:S(2)}) collective-permute-start(f32[9,64,128]{2,1,0:T(8,128)S(1)} %multiply_add_fusion.11), channel_id=1, source_target_pairs={{0,4},{2,6},{4,8},{6,10},{8,12},{10,14},{12,16},{14,18},{16,20},{1... | collective-permute-start | bytes 884744 | tf_op jit(solution)/shard_map/ppermute | solution.py:275
  98.6 14.2 %collective-permute-start.13 = (f32[9,64,128]{2,1,0:T(8,128)S(1)}, f32[9,64,128]{2,1,0:T(8,128)S(1)}, u32[]{:S(2)}, u32[]{:S(2)}) collective-permute-start(f32[9,64,128]{2,1,0:T(8,128)S(1)} %multiply_add_fusion.5), channel_id=1, source_target_pairs={{4,0},{6,2},{8,4},{10,6},{12,8},{14,10},{16,12},{18,14},{20,16},{2... | collective-permute-start | bytes 884744 | tf_op jit(solution)/shard_map/ppermute | solution.py:276
  117.0 14.7 %collective-permute-start.15 = (f32[5,64,128]{2,1,0:T(8,128)S(1)}, f32[5,64,128]{2,1,0:T(8,128)S(1)}, u32[]{:S(2)}, u32[]{:S(2)}) collective-permute-start(f32[5,64,128]{2,1,0:T(8,128)S(1)} %get-tuple-element.63), channel_id=1, source_target_pairs={{0,32},{2,34},{4,36},{6,38},{8,40},{10,42},{12,44},{14,46},{16,48}... | collective-permute-start | bytes 491528 | tf_op jit(solution)/shard_map/ppermute | solution.py:275
  126.4 69.1 %collective-permute-start.27 = (f32[5,8,64,128]{3,2,1,0:T(8,128)S(1)}, f32[5,8,64,128]{3,2,1,0:T(8,128)S(1)}, u32[]{:S(2)}, u32[]{:S(2)}) collective-permute-start(f32[5,8,64,128]{3,2,1,0:T(8,128)S(1)} %fusion.34), channel_id=1, source_target_pairs={{0,1},{1,0},{2,3},{3,2},{4,5},{5,4},{6,7},{7,6},{8,9},{9,8},{10,11... | collective-permute-start | bytes 3932168 | tf_op jit(solution)/shard_map/ppermute | solution.py:312
  138.1 9.7 %collective-permute-start.22 = (f32[5,64,128]{2,1,0:T(8,128)S(1)}, f32[5,64,128]{2,1,0:T(8,128)S(1)}, u32[]{:S(2)}, u32[]{:S(2)}) collective-permute-start(f32[5,64,128]{2,1,0:T(8,128)S(1)} %get-tuple-element.62), channel_id=1, source_target_pairs={{64,0},{66,2},{68,4},{70,6},{72,8},{74,10},{76,12},{78,14},{80,16}... | collective-permute-start | bytes 491528 | tf_op jit(solution)/shard_map/ppermute | solution.py:276
  140.8 9.1 %collective-permute-start.17 = (f32[5,64,128]{2,1,0:T(8,128)S(1)}, f32[5,64,128]{2,1,0:T(8,128)S(1)}, u32[]{:S(2)}, u32[]{:S(2)}) collective-permute-start(f32[5,64,128]{2,1,0:T(8,128)S(1)} %multiply_add_fusion.27), channel_id=1, source_target_pairs={{0,8},{2,10},{4,12},{6,14},{8,16},{10,18},{12,20},{14,22},{16,24},... | collective-permute-start | bytes 491528 | tf_op jit(solution)/shard_map/ppermute | solution.py:275
  147.9 13.0 %collective-permute-start.23 = (f32[5,64,128]{2,1,0:T(8,128)S(1)}, f32[5,64,128]{2,1,0:T(8,128)S(1)}, u32[]{:S(2)}, u32[]{:S(2)}) collective-permute-start(f32[5,64,128]{2,1,0:T(8,128)S(1)} %multiply_add_fusion.21), channel_id=1, source_target_pairs={{8,0},{10,2},{12,4},{14,6},{16,8},{18,10},{20,12},{22,14},{24,16},... | collective-permute-start | bytes 491528 | tf_op jit(solution)/shard_map/ppermute | solution.py:276
  149.9 13.0 %collective-permute-start.18 = (f32[5,64,128]{2,1,0:T(8,128)S(1)}, f32[5,64,128]{2,1,0:T(8,128)S(1)}, u32[]{:S(2)}, u32[]{:S(2)}) collective-permute-start(f32[5,64,128]{2,1,0:T(8,128)S(1)} %multiply_add_fusion.26), channel_id=1, source_target_pairs={{0,16},{2,18},{4,20},{6,22},{8,24},{10,26},{12,28},{14,30},{16,32}... | collective-permute-start | bytes 491528 | tf_op jit(solution)/shard_map/ppermute | solution.py:275
  161.0 9.9 %collective-permute-start.24 = (f32[5,64,128]{2,1,0:T(8,128)S(1)}, f32[5,64,128]{2,1,0:T(8,128)S(1)}, u32[]{:S(2)}, u32[]{:S(2)}) collective-permute-start(f32[5,64,128]{2,1,0:T(8,128)S(1)} %multiply_add_fusion.20), channel_id=1, source_target_pairs={{16,0},{18,2},{20,4},{22,6},{24,8},{26,10},{28,12},{30,14},{32,16}... | collective-permute-start | bytes 491528 | tf_op jit(solution)/shard_map/ppermute | solution.py:276
  163.2 9.8 %collective-permute-start.19 = (f32[5,64,128]{2,1,0:T(8,128)S(1)}, f32[5,64,128]{2,1,0:T(8,128)S(1)}, u32[]{:S(2)}, u32[]{:S(2)}) collective-permute-start(f32[5,64,128]{2,1,0:T(8,128)S(1)} %multiply_add_fusion.25), channel_id=1, source_target_pairs={{0,2},{2,4},{4,6},{6,8},{8,10},{10,12},{12,14},{14,16},{16,18},{18... | collective-permute-start | bytes 491528 | tf_op jit(solution)/shard_map/ppermute | solution.py:275
  171.0 12.6 %collective-permute-start.25 = (f32[5,64,128]{2,1,0:T(8,128)S(1)}, f32[5,64,128]{2,1,0:T(8,128)S(1)}, u32[]{:S(2)}, u32[]{:S(2)}) collective-permute-start(f32[5,64,128]{2,1,0:T(8,128)S(1)} %multiply_add_fusion.19), channel_id=1, source_target_pairs={{2,0},{4,2},{6,4},{8,6},{10,8},{12,10},{14,12},{16,14},{18,16},{20... | collective-permute-start | bytes 491528 | tf_op jit(solution)/shard_map/ppermute | solution.py:276
  173.0 12.5 %collective-permute-start.20 = (f32[5,64,128]{2,1,0:T(8,128)S(1)}, f32[5,64,128]{2,1,0:T(8,128)S(1)}, u32[]{:S(2)}, u32[]{:S(2)}) collective-permute-start(f32[5,64,128]{2,1,0:T(8,128)S(1)} %multiply_add_fusion.24), channel_id=1, source_target_pairs={{0,4},{2,6},{4,8},{6,10},{8,12},{10,14},{12,16},{14,18},{16,20},{1... | collective-permute-start | bytes 491528 | tf_op jit(solution)/shard_map/ppermute | solution.py:275
  183.6 11.7 %collective-permute-start.26 = (f32[5,64,128]{2,1,0:T(8,128)S(1)}, f32[5,64,128]{2,1,0:T(8,128)S(1)}, u32[]{:S(2)}, u32[]{:S(2)}) collective-permute-start(f32[5,64,128]{2,1,0:T(8,128)S(1)} %multiply_add_fusion.18), channel_id=1, source_target_pairs={{4,0},{6,2},{8,4},{10,6},{12,8},{14,10},{16,12},{18,14},{20,16},{2... | collective-permute-start | bytes 491528 | tf_op jit(solution)/shard_map/ppermute | solution.py:276
  (62 other events, 590.9 us)

commit v15 on v12

--- a/solution.py
+++ b/solution.py
@@ -214,10 +214,10 @@
         return self.row[start : start + int(np.prod(shape))].reshape(shape)
 
 
-def plan_wall(bank, kinds_sizes, points, rows, pad, extras):
+def plan_wall(bank, kinds_sizes, points, rows, pads, extras):
     tables = [
         wall_tables(kind, points, rows, pad, extra)
-        for (kind, _), extra in zip(kinds_sizes, extras)
+        for (kind, _), pad, extra in zip(kinds_sizes, pads, extras)
     ]
     groups = [
         (
@@ -342,8 +342,10 @@
     other_block = jnp.asarray(span_full[span_own : 2 * span_own, :span_own], jnp.float32)
 
     bank = TableBank()
-    first_plan = plan_wall(bank, [("slope", 4), ("smooth", 5)], points, rows, 3, (2, 0))
-    second_plan = plan_wall(bank, [("slope", 5)], points, rows, 2, (0,))
+    first_plan = plan_wall(bank, [("slope", 4)], points, rows, (3,), (2,))
+    second_plan = plan_wall(
+        bank, [("slope", 5), ("smooth", 5)], points, rows, (2, 3), (0, 0)
+    )
     bank.lookup(position)
 
     state = jnp.concatenate(
@@ -359,7 +361,7 @@
     warmth_pad = push_pad / density
     basic_pad = jnp.concatenate([speed_pad, warmth_pad[None]], axis=0)
 
-    wall_grad, smoothed = wall_apply(bank, first_plan, [basic_pad, padded], rows, 3)
+    (wall_grad,) = wall_apply(bank, first_plan, [basic_pad], rows, 3)
 
     basic = basic_pad[:, 1 : rows + 5]
     speed = basic[:3]
@@ -370,7 +372,7 @@
     grad_span = span_slope(basic, own_block, other_block)
     gradients = [grad_stream, wall_grad, grad_span]
     flux_wall = flux_along(1, momentum, energy, speed, push, gradients)
-    (wall_term,) = wall_apply(bank, second_plan, [flux_wall], rows, 2)
+    wall_term, smoothed = wall_apply(bank, second_plan, [flux_wall, padded], rows, 2)
     own = slice(2, 2 + rows)
     gradients = [[part[own] for part in grad] for grad in gradients]
     speed, push = speed[:, own], push[own]

time: 186 us -> 189 us (1.016)
  waiting for transfers between devices: 65.1 us -> 67.6 us
  transfers between devices with their start and end apart: 28 -> 28, of which waited for: 16 -> 19; matrix products, arithmetic and copies ran while one was open for 13% -> 12% of each run, Pallas kernels for 0% -> 0%
where the time goes in v15:
time: 189 us; the launch traced here: 187 us
  starting transfers between devices  79.3 us (42%)
  waiting for transfers between devices  67.6 us (36%)
  other arithmetic  15.3 us (8%)
  local copies, waits for them, and re-layouts  13.4 us (7%)
  matrix products  9.84 us (5%)
  between operations  1.96 us (1%)
    ppermute x12, waiting for transfers between devices, wall_apply(): from_above = lax.ppermute(fall, 'gy', down_pairs)  51.7 us
    ppermute x12, starting transfers between devices, wall_apply(): from_below = lax.ppermute(rise, 'gy', up_pairs)  49.5 us
    ppermute x12, starting transfers between devices, wall_apply(): from_above = lax.ppermute(fall, 'gy', down_pairs)  23.7 us
    ppermute x12, waiting for transfers between devices, wall_apply(): from_below = lax.ppermute(rise, 'gy', up_pairs)  10.4 us
    ppermute x1, waiting for transfers between devices, halo(): above = lax.ppermute(block[:, :width], 'gy', down_pairs)  5.47 us
    add x2, other arithmetic, wall_apply(): local + rise_gain[None, :, None, None] * rise[first:first + size, None]  4.89 us
    dot_general x2, matrix products, stream_slope(): jnp.dot(flat_rows, stream_matrix, precision=HIGHEST, preferred_element_ty...  3.9 us
  transfers between devices with their start and end apart: 28, of which 19 were waited for; matrix products, arithmetic and copies ran while one was open for 12% of the time, Pallas kernels for 0%

profile of v15, /device:TPU:30, one launch (start us, length us, event | category | flops | bytes accessed | tf_op | source)
XLA Modules:
  0.0 187.3 jit_solution(15241259196357888633)
XLA Ops:
  3.0 3.4 %collective-permute-start = (f32[5,3,64,128]{3,2,1,0:T(8,128)}, f32[5,3,64,128]{3,2,1,0:T(8,128)S(1)}, u32[]{:S(2)}, u32[]{:S(2)}) collective-permute-start(f32[5,3,64,128]{3,2,1,0:T(8,128)} %get-tuple-element.50), channel_id=1, source_target_pairs={{0,2},{2,4},{4,6},{6,8},{8,10},{10,12},{12,14},{14,16},{16,18},{18... | collective-permute-start | bytes 1474568 | tf_op jit(solution)/shard_map/ppermute | solution.py:296
  20.0 5.5 %collective-permute-done.1 = f32[5,3,64,128]{3,2,1,0:T(8,128)S(1)} collective-permute-done((f32[5,3,64,128]{3,2,1,0:T(8,128)}, f32[5,3,64,128]{3,2,1,0:T(8,128)S(1)}, u32[]{:S(2)}, u32[]{:S(2)}) %collective-permute-start.1) | collective-permute-done | bytes 491552 | tf_op jit(solution)/shard_map/ppermute | solution.py:297
  29.3 5.5 %collective-permute-start.2 = (f32[4,64,128]{2,1,0:T(8,128)S(1)}, f32[4,64,128]{2,1,0:T(8,128)S(1)}, u32[]{:S(2)}, u32[]{:S(2)}) collective-permute-start(f32[4,64,128]{2,1,0:T(8,128)S(1)} %get-tuple-element.69), channel_id=1, source_target_pairs={{0,64},{2,66},{4,68},{6,70},{8,72},{10,74},{12,76},{14,78},{16,80}... | collective-permute-start | bytes 393224 | tf_op jit(solution)/shard_map/ppermute | solution.py:272
  37.6 5.6 %collective-permute-done.8 = f32[4,64,128]{2,1,0:T(8,128)S(1)} collective-permute-done((f32[4,64,128]{2,1,0:T(8,128)S(1)}, f32[4,64,128]{2,1,0:T(8,128)S(1)}, u32[]{:S(2)}, u32[]{:S(2)}) %collective-permute-start.8) | collective-permute-done | bytes 131104 | tf_op jit(solution)/shard_map/ppermute | solution.py:273
  47.2 4.8 %collective-permute-start.4 = (f32[4,64,128]{2,1,0:T(8,128)S(1)}, f32[4,64,128]{2,1,0:T(8,128)S(1)}, u32[]{:S(2)}, u32[]{:S(2)}) collective-permute-start(f32[4,64,128]{2,1,0:T(8,128)S(1)} %multiply_add_fusion.27), channel_id=1, source_target_pairs={{0,16},{2,18},{4,20},{6,22},{8,24},{10,26},{12,28},{14,30},{16,32}... | collective-permute-start | bytes 393224 | tf_op jit(solution)/shard_map/ppermute | solution.py:272
  52.2 2.5 %collective-permute-start.10 = (f32[4,64,128]{2,1,0:T(8,128)S(1)}, f32[4,64,128]{2,1,0:T(8,128)S(1)}, u32[]{:S(2)}, u32[]{:S(2)}) collective-permute-start(f32[4,64,128]{2,1,0:T(8,128)S(1)} %multiply_add_fusion.21), channel_id=1, source_target_pairs={{16,0},{18,2},{20,4},{22,6},{24,8},{26,10},{28,12},{30,14},{32,16}... | collective-permute-start | bytes 393224 | tf_op jit(solution)/shard_map/ppermute | solution.py:273
  55.7 5.5 %collective-permute-start.5 = (f32[4,64,128]{2,1,0:T(8,128)S(1)}, f32[4,64,128]{2,1,0:T(8,128)S(1)}, u32[]{:S(2)}, u32[]{:S(2)}) collective-permute-start(f32[4,64,128]{2,1,0:T(8,128)S(1)} %multiply_add_fusion.26), channel_id=1, source_target_pairs={{0,8},{2,10},{4,12},{6,14},{8,16},{10,18},{12,20},{14,22},{16,24},... | collective-permute-start | bytes 393224 | tf_op jit(solution)/shard_map/ppermute | solution.py:272
  61.5 2.8 %collective-permute-start.11 = (f32[4,64,128]{2,1,0:T(8,128)S(1)}, f32[4,64,128]{2,1,0:T(8,128)S(1)}, u32[]{:S(2)}, u32[]{:S(2)}) collective-permute-start(f32[4,64,128]{2,1,0:T(8,128)S(1)} %multiply_add_fusion.20), channel_id=1, source_target_pairs={{8,0},{10,2},{12,4},{14,6},{16,8},{18,10},{20,12},{22,14},{24,16},... | collective-permute-start | bytes 393224 | tf_op jit(solution)/shard_map/ppermute | solution.py:273
  64.4 4.8 %collective-permute-start.6 = (f32[4,64,128]{2,1,0:T(8,128)S(1)}, f32[4,64,128]{2,1,0:T(8,128)S(1)}, u32[]{:S(2)}, u32[]{:S(2)}) collective-permute-start(f32[4,64,128]{2,1,0:T(8,128)S(1)} %multiply_add_fusion.25), channel_id=1, source_target_pairs={{0,4},{2,6},{4,8},{6,10},{8,12},{10,14},{12,16},{14,18},{16,20},{1... | collective-permute-start | bytes 393224 | tf_op jit(solution)/shard_map/ppermute | solution.py:272
  73.2 10.5 %collective-permute-start.7 = (f32[4,64,128]{2,1,0:T(8,128)S(1)}, f32[4,64,128]{2,1,0:T(8,128)S(1)}, u32[]{:S(2)}, u32[]{:S(2)}) collective-permute-start(f32[4,64,128]{2,1,0:T(8,128)S(1)} %multiply_add_fusion.24), channel_id=1, source_target_pairs={{0,2},{2,4},{4,6},{6,8},{8,10},{10,12},{12,14},{14,16},{16,18},{18... | collective-permute-start | bytes 393224 | tf_op jit(solution)/shard_map/ppermute | solution.py:272
  86.2 8.6 %collective-permute-done.13 = f32[4,64,128]{2,1,0:T(8,128)S(1)} collective-permute-done((f32[4,64,128]{2,1,0:T(8,128)S(1)}, f32[4,64,128]{2,1,0:T(8,128)S(1)}, u32[]{:S(2)}, u32[]{:S(2)}) %collective-permute-start.13) | collective-permute-done | bytes 131104 | tf_op jit(solution)/shard_map/ppermute | solution.py:273
  103.0 2.5 %collective-permute-start.15 = (f32[10,64,128]{2,1,0:T(8,128)S(1)}, f32[10,64,128]{2,1,0:T(8,128)S(1)}, u32[]{:S(2)}, u32[]{:S(2)}) collective-permute-start(f32[10,64,128]{2,1,0:T(8,128)S(1)} %pad_maximum_fusion.7), channel_id=1, source_target_pairs={{0,64},{2,66},{4,68},{6,70},{8,72},{10,74},{12,76},{14,78},{16,80}... | collective-permute-start | bytes 983048 | tf_op jit(solution)/shard_map/ppermute | solution.py:272
  107.2 3.3 %collective-permute-done.15 = f32[10,64,128]{2,1,0:T(8,128)S(1)} collective-permute-done((f32[10,64,128]{2,1,0:T(8,128)S(1)}, f32[10,64,128]{2,1,0:T(8,128)S(1)}, u32[]{:S(2)}, u32[]{:S(2)}) %collective-permute-start.15) | collective-permute-done | bytes 327712 | tf_op jit(solution)/shard_map/ppermute | solution.py:272
  112.0 4.0 %collective-permute-done.21 = f32[10,64,128]{2,1,0:T(8,128)S(1)} collective-permute-done((f32[10,64,128]{2,1,0:T(8,128)S(1)}, f32[10,64,128]{2,1,0:T(8,128)S(1)}, u32[]{:S(2)}, u32[]{:S(2)}) %collective-permute-start.21) | collective-permute-done | bytes 327712 | tf_op jit(solution)/shard_map/ppermute | solution.py:273
  119.9 9.2 %collective-permute-done.22 = f32[10,64,128]{2,1,0:T(8,128)S(1)} collective-permute-done((f32[10,64,128]{2,1,0:T(8,128)S(1)}, f32[10,64,128]{2,1,0:T(8,128)S(1)}, u32[]{:S(2)}, u32[]{:S(2)}) %collective-permute-start.22) | collective-permute-done | bytes 327712 | tf_op jit(solution)/shard_map/ppermute | solution.py:273
  131.3 3.8 %collective-permute-start.18 = (f32[10,64,128]{2,1,0:T(8,128)S(1)}, f32[10,64,128]{2,1,0:T(8,128)S(1)}, u32[]{:S(2)}, u32[]{:S(2)}) collective-permute-start(f32[10,64,128]{2,1,0:T(8,128)S(1)} %multiply_add_fusion.11), channel_id=1, source_target_pairs={{0,8},{2,10},{4,12},{6,14},{8,16},{10,18},{12,20},{14,22},{16,24},... | collective-permute-start | bytes 983048 | tf_op jit(solution)/shard_map/ppermute | solution.py:272
  135.3 5.3 %collective-permute-done.23 = f32[10,64,128]{2,1,0:T(8,128)S(1)} collective-permute-done((f32[10,64,128]{2,1,0:T(8,128)S(1)}, f32[10,64,128]{2,1,0:T(8,128)S(1)}, u32[]{:S(2)}, u32[]{:S(2)}) %collective-permute-start.23) | collective-permute-done | bytes 327712 | tf_op jit(solution)/shard_map/ppermute | solution.py:273
  145.0 6.8 %collective-permute-done.24 = f32[10,64,128]{2,1,0:T(8,128)S(1)} collective-permute-done((f32[10,64,128]{2,1,0:T(8,128)S(1)}, f32[10,64,128]{2,1,0:T(8,128)S(1)}, u32[]{:S(2)}, u32[]{:S(2)}) %collective-permute-start.24) | collective-permute-done | bytes 327712 | tf_op jit(solution)/shard_map/ppermute | solution.py:273
  153.8 2.8 %collective-permute-done.19 = f32[10,64,128]{2,1,0:T(8,128)S(1)} collective-permute-done((f32[10,64,128]{2,1,0:T(8,128)S(1)}, f32[10,64,128]{2,1,0:T(8,128)S(1)}, u32[]{:S(2)}, u32[]{:S(2)}) %collective-permute-start.19) | collective-permute-done | bytes 327712 | tf_op jit(solution)/shard_map/ppermute | solution.py:272
  156.7 5.6 %collective-permute-start.20 = (f32[10,64,128]{2,1,0:T(8,128)S(1)}, f32[10,64,128]{2,1,0:T(8,128)S(1)}, u32[]{:S(2)}, u32[]{:S(2)}) collective-permute-start(f32[10,64,128]{2,1,0:T(8,128)S(1)} %multiply_add_fusion.9), channel_id=1, source_target_pairs={{0,2},{2,4},{4,6},{6,8},{8,10},{10,12},{12,14},{14,16},{16,18},{18... | collective-permute-start | bytes 983048 | tf_op jit(solution)/shard_map/ppermute | solution.py:272
  165.5 3.5 %collective-permute-start.26 = (f32[10,64,128]{2,1,0:T(8,128)S(1)}, f32[10,64,128]{2,1,0:T(8,128)S(1)}, u32[]{:S(2)}, u32[]{:S(2)}) collective-permute-start(f32[10,64,128]{2,1,0:T(8,128)S(1)} %multiply_add_fusion.3), channel_id=1, source_target_pairs={{2,0},{4,2},{6,4},{8,6},{10,8},{12,10},{14,12},{16,14},{18,16},{20... | collective-permute-start | bytes 983048 | tf_op jit(solution)/shard_map/ppermute | solution.py:273
  169.8 8.8 %collective-permute-done.26 = f32[10,64,128]{2,1,0:T(8,128)S(1)} collective-permute-done((f32[10,64,128]{2,1,0:T(8,128)S(1)}, f32[10,64,128]{2,1,0:T(8,128)S(1)}, u32[]{:S(2)}, u32[]{:S(2)}) %collective-permute-start.26) | collective-permute-done | bytes 327712 | tf_op jit(solution)/shard_map/ppermute | solution.py:273
  178.8 2.5 %convolution_add_fusion.1 = f32[5,8,64,128]{3,2,1,0:T(8,128)S(1)} fusion(f32[5,8,64,128]{3,2,1,0:T(8,128)S(1)} %bitcast_dynamic-update-slice_fusion.2, f32[128,128,1,1]{1,0,3,2:T(8,128)S(1)} %copy-done.53, f32[5,64,128]{2,1,0:T(8,128)S(1)} %get-tuple-element.62, f32[8]{0:T(128)S(1)} %get-tuple-element.72, f32[5,64,128]{2,1,0:T(8,128)S(1)} %get-tuple-element.60, ...), kind=kOutput, calls=%fused_computation.37 | convolution fusion | flops 512491520 | bytes 4981184 | tf_op jit(solution)/shard_map/dot_general | solution.py:303
  184.4 2.9 %multiply_add_fusion.1 = f32[5,8,64,128]{3,2,1,0:T(8,128)} fusion(f32[5,64,128]{2,1,0:T(8,128)S(1)} %get-tuple-element.61, f32[8]{0:T(128)S(1)} %get-tuple-element.74, f32[5,64,128]{2,1,0:T(8,128)S(1)} %get-tuple-element.59, f32[8]{0:T(128)S(1)} %get-tuple-element.71, f32[5,64,128]{2,1,0:T(8,128)S(1)} %get-tuple-element.57, f32[8]{0:T(128)S(1)} %copy-done.39, ...), kind=kLoop, calls=%fused_computation.44 | loop fusion | flops 10158080 | bytes 3932672 | tf_op jit(solution)/shard_map/add | solution.py:284
  (229 shorter events, 64.8 us)
Async XLA Ops:
  3.0 16.9 %collective-permute-start = (f32[5,3,64,128]{3,2,1,0:T(8,128)}, f32[5,3,64,128]{3,2,1,0:T(8,128)S(1)}, u32[]{:S(2)}, u32[]{:S(2)}) collective-permute-start(f32[5,3,64,128]{3,2,1,0:T(8,128)} %get-tuple-element.50), channel_id=1, source_target_pairs={{0,2},{2,4},{4,6},{6,8},{8,10},{10,12},{12,14},{14,16},{16,18},{18... | collective-permute-start | bytes 1474568 | tf_op jit(solution)/shard_map/ppermute | solution.py:296
  6.4 19.0 %collective-permute-start.1 = (f32[5,3,64,128]{3,2,1,0:T(8,128)}, f32[5,3,64,128]{3,2,1,0:T(8,128)S(1)}, u32[]{:S(2)}, u32[]{:S(2)}) collective-permute-start(f32[5,3,64,128]{3,2,1,0:T(8,128)} %get-tuple-element.51), channel_id=1, source_target_pairs={{2,0},{4,2},{6,4},{8,6},{10,8},{12,10},{14,12},{16,14},{18,16},{20... | collective-permute-start | bytes 1474568 | tf_op jit(solution)/shard_map/ppermute | solution.py:297
  26.5 70.5 %collective-permute-start.14 = (f32[4,12,64,128]{3,2,1,0:T(8,128)S(1)}, f32[4,12,64,128]{3,2,1,0:T(8,128)S(1)}, u32[]{:S(2)}, u32[]{:S(2)}) collective-permute-start(f32[4,12,64,128]{3,2,1,0:T(8,128)S(1)} %fusion.1), channel_id=1, source_target_pairs={{0,1},{1,0},{2,3},{3,2},{4,5},{5,4},{6,7},{7,6},{8,9},{9,8},{10,11... | collective-permute-start | bytes 4718600 | tf_op jit(solution)/shard_map/ppermute | solution.py:309
  29.3 8.3 %collective-permute-start.2 = (f32[4,64,128]{2,1,0:T(8,128)S(1)}, f32[4,64,128]{2,1,0:T(8,128)S(1)}, u32[]{:S(2)}, u32[]{:S(2)}) collective-permute-start(f32[4,64,128]{2,1,0:T(8,128)S(1)} %get-tuple-element.69), channel_id=1, source_target_pairs={{0,64},{2,66},{4,68},{6,70},{8,72},{10,74},{12,76},{14,78},{16,80}... | collective-permute-start | bytes 393224 | tf_op jit(solution)/shard_map/ppermute | solution.py:272
  34.8 8.4 %collective-permute-start.8 = (f32[4,64,128]{2,1,0:T(8,128)S(1)}, f32[4,64,128]{2,1,0:T(8,128)S(1)}, u32[]{:S(2)}, u32[]{:S(2)}) collective-permute-start(f32[4,64,128]{2,1,0:T(8,128)S(1)} %get-tuple-element.70), channel_id=1, source_target_pairs={{64,0},{66,2},{68,4},{70,6},{72,8},{74,10},{76,12},{78,14},{80,16}... | collective-permute-start | bytes 393224 | tf_op jit(solution)/shard_map/ppermute | solution.py:273
  47.2 8.4 %collective-permute-start.4 = (f32[4,64,128]{2,1,0:T(8,128)S(1)}, f32[4,64,128]{2,1,0:T(8,128)S(1)}, u32[]{:S(2)}, u32[]{:S(2)}) collective-permute-start(f32[4,64,128]{2,1,0:T(8,128)S(1)} %multiply_add_fusion.27), channel_id=1, source_target_pairs={{0,16},{2,18},{4,20},{6,22},{8,24},{10,26},{12,28},{14,30},{16,32}... | collective-permute-start | bytes 393224 | tf_op jit(solution)/shard_map/ppermute | solution.py:272
  52.2 9.3 %collective-permute-start.10 = (f32[4,64,128]{2,1,0:T(8,128)S(1)}, f32[4,64,128]{2,1,0:T(8,128)S(1)}, u32[]{:S(2)}, u32[]{:S(2)}) collective-permute-start(f32[4,64,128]{2,1,0:T(8,128)S(1)} %multiply_add_fusion.21), channel_id=1, source_target_pairs={{16,0},{18,2},{20,4},{22,6},{24,8},{26,10},{28,12},{30,14},{32,16}... | collective-permute-start | bytes 393224 | tf_op jit(solution)/shard_map/ppermute | solution.py:273
  55.7 8.6 %collective-permute-start.5 = (f32[4,64,128]{2,1,0:T(8,128)S(1)}, f32[4,64,128]{2,1,0:T(8,128)S(1)}, u32[]{:S(2)}, u32[]{:S(2)}) collective-permute-start(f32[4,64,128]{2,1,0:T(8,128)S(1)} %multiply_add_fusion.26), channel_id=1, source_target_pairs={{0,8},{2,10},{4,12},{6,14},{8,16},{10,18},{12,20},{14,22},{16,24},... | collective-permute-start | bytes 393224 | tf_op jit(solution)/shard_map/ppermute | solution.py:272
  61.5 9.0 %collective-permute-start.11 = (f32[4,64,128]{2,1,0:T(8,128)S(1)}, f32[4,64,128]{2,1,0:T(8,128)S(1)}, u32[]{:S(2)}, u32[]{:S(2)}) collective-permute-start(f32[4,64,128]{2,1,0:T(8,128)S(1)} %multiply_add_fusion.20), channel_id=1, source_target_pairs={{8,0},{10,2},{12,4},{14,6},{16,8},{18,10},{20,12},{22,14},{24,16},... | collective-permute-start | bytes 393224 | tf_op jit(solution)/shard_map/ppermute | solution.py:273
  64.4 8.7 %collective-permute-start.6 = (f32[4,64,128]{2,1,0:T(8,128)S(1)}, f32[4,64,128]{2,1,0:T(8,128)S(1)}, u32[]{:S(2)}, u32[]{:S(2)}) collective-permute-start(f32[4,64,128]{2,1,0:T(8,128)S(1)} %multiply_add_fusion.25), channel_id=1, source_target_pairs={{0,4},{2,6},{4,8},{6,10},{8,12},{10,14},{12,16},{14,18},{16,20},{1... | collective-permute-start | bytes 393224 | tf_op jit(solution)/shard_map/ppermute | solution.py:272
  70.6 13.1 %collective-permute-start.12 = (f32[4,64,128]{2,1,0:T(8,128)S(1)}, f32[4,64,128]{2,1,0:T(8,128)S(1)}, u32[]{:S(2)}, u32[]{:S(2)}) collective-permute-start(f32[4,64,128]{2,1,0:T(8,128)S(1)} %multiply_add_fusion.19), channel_id=1, source_target_pairs={{4,0},{6,2},{8,4},{10,6},{12,8},{14,10},{16,12},{18,14},{20,16},{2... | collective-permute-start | bytes 393224 | tf_op jit(solution)/shard_map/ppermute | solution.py:273
  73.2 13.0 %collective-permute-start.7 = (f32[4,64,128]{2,1,0:T(8,128)S(1)}, f32[4,64,128]{2,1,0:T(8,128)S(1)}, u32[]{:S(2)}, u32[]{:S(2)}) collective-permute-start(f32[4,64,128]{2,1,0:T(8,128)S(1)} %multiply_add_fusion.24), channel_id=1, source_target_pairs={{0,2},{2,4},{4,6},{6,8},{8,10},{10,12},{12,14},{14,16},{16,18},{18... | collective-permute-start | bytes 393224 | tf_op jit(solution)/shard_map/ppermute | solution.py:272
  83.8 11.1 %collective-permute-start.13 = (f32[4,64,128]{2,1,0:T(8,128)S(1)}, f32[4,64,128]{2,1,0:T(8,128)S(1)}, u32[]{:S(2)}, u32[]{:S(2)}) collective-permute-start(f32[4,64,128]{2,1,0:T(8,128)S(1)} %multiply_add_fusion.18), channel_id=1, source_target_pairs={{2,0},{4,2},{6,4},{8,6},{10,8},{12,10},{14,12},{16,14},{18,16},{20... | collective-permute-start | bytes 393224 | tf_op jit(solution)/shard_map/ppermute | solution.py:273
  105.5 10.5 %collective-permute-start.21 = (f32[10,64,128]{2,1,0:T(8,128)S(1)}, f32[10,64,128]{2,1,0:T(8,128)S(1)}, u32[]{:S(2)}, u32[]{:S(2)}) collective-permute-start(f32[10,64,128]{2,1,0:T(8,128)S(1)} %pad_maximum_fusion.8), channel_id=1, source_target_pairs={{64,0},{66,2},{68,4},{70,6},{72,8},{74,10},{76,12},{78,14},{80,16}... | collective-permute-start | bytes 983048 | tf_op jit(solution)/shard_map/ppermute | solution.py:273
  116.1 13.0 %collective-permute-start.22 = (f32[10,64,128]{2,1,0:T(8,128)S(1)}, f32[10,64,128]{2,1,0:T(8,128)S(1)}, u32[]{:S(2)}, u32[]{:S(2)}) collective-permute-start(f32[10,64,128]{2,1,0:T(8,128)S(1)} %multiply_add_fusion.7), channel_id=1, source_target_pairs={{32,0},{34,2},{36,4},{38,6},{40,8},{42,10},{44,12},{46,14},{48,16}... | collective-permute-start | bytes 983048 | tf_op jit(solution)/shard_map/ppermute | solution.py:273
  117.5 13.6 %collective-permute-start.17 = (f32[10,64,128]{2,1,0:T(8,128)S(1)}, f32[10,64,128]{2,1,0:T(8,128)S(1)}, u32[]{:S(2)}, u32[]{:S(2)}) collective-permute-start(f32[10,64,128]{2,1,0:T(8,128)S(1)} %multiply_add_fusion.12), channel_id=1, source_target_pairs={{0,16},{2,18},{4,20},{6,22},{8,24},{10,26},{12,28},{14,30},{16,32}... | collective-permute-start | bytes 983048 | tf_op jit(solution)/shard_map/ppermute | solution.py:272
  129.2 11.4 %collective-permute-start.23 = (f32[10,64,128]{2,1,0:T(8,128)S(1)}, f32[10,64,128]{2,1,0:T(8,128)S(1)}, u32[]{:S(2)}, u32[]{:S(2)}) collective-permute-start(f32[10,64,128]{2,1,0:T(8,128)S(1)} %multiply_add_fusion.6), channel_id=1, source_target_pairs={{16,0},{18,2},{20,4},{22,6},{24,8},{26,10},{28,12},{30,14},{32,16}... | collective-permute-start | bytes 983048 | tf_op jit(solution)/shard_map/ppermute | solution.py:273
  131.3 11.4 %collective-permute-start.18 = (f32[10,64,128]{2,1,0:T(8,128)S(1)}, f32[10,64,128]{2,1,0:T(8,128)S(1)}, u32[]{:S(2)}, u32[]{:S(2)}) collective-permute-start(f32[10,64,128]{2,1,0:T(8,128)S(1)} %multiply_add_fusion.11), channel_id=1, source_target_pairs={{0,8},{2,10},{4,12},{6,14},{8,16},{10,18},{12,20},{14,22},{16,24},... | collective-permute-start | bytes 983048 | tf_op jit(solution)/shard_map/ppermute | solution.py:272
  135.2 46.1 %collective-permute-start.27 = (f32[5,8,64,128]{3,2,1,0:T(8,128)S(1)}, f32[5,8,64,128]{3,2,1,0:T(8,128)S(1)}, u32[]{:S(2)}, u32[]{:S(2)}) collective-permute-start(f32[5,8,64,128]{3,2,1,0:T(8,128)S(1)} %get-tuple-element.6), channel_id=1, source_target_pairs={{0,1},{1,0},{2,3},{3,2},{4,5},{5,4},{6,7},{7,6},{8,9},{9,8},{10,11... | collective-permute-start | bytes 3932168 | tf_op jit(solution)/shard_map/ppermute | solution.py:309
  140.7 11.1 %collective-permute-start.24 = (f32[10,64,128]{2,1,0:T(8,128)S(1)}, f32[10,64,128]{2,1,0:T(8,128)S(1)}, u32[]{:S(2)}, u32[]{:S(2)}) collective-permute-start(f32[10,64,128]{2,1,0:T(8,128)S(1)} %multiply_add_fusion.5), channel_id=1, source_target_pairs={{8,0},{10,2},{12,4},{14,6},{16,8},{18,10},{20,12},{22,14},{24,16},... | collective-permute-start | bytes 983048 | tf_op jit(solution)/shard_map/ppermute | solution.py:273
  142.8 13.8 %collective-permute-start.19 = (f32[10,64,128]{2,1,0:T(8,128)S(1)}, f32[10,64,128]{2,1,0:T(8,128)S(1)}, u32[]{:S(2)}, u32[]{:S(2)}) collective-permute-start(f32[10,64,128]{2,1,0:T(8,128)S(1)} %multiply_add_fusion.10), channel_id=1, source_target_pairs={{0,4},{2,6},{4,8},{6,10},{8,12},{10,14},{12,16},{14,18},{16,20},{1... | collective-permute-start | bytes 983048 | tf_op jit(solution)/shard_map/ppermute | solution.py:272
  151.9 13.5 %collective-permute-start.25 = (f32[10,64,128]{2,1,0:T(8,128)S(1)}, f32[10,64,128]{2,1,0:T(8,128)S(1)}, u32[]{:S(2)}, u32[]{:S(2)}) collective-permute-start(f32[10,64,128]{2,1,0:T(8,128)S(1)} %multiply_add_fusion.4), channel_id=1, source_target_pairs={{4,0},{6,2},{8,4},{10,6},{12,8},{14,10},{16,12},{18,14},{20,16},{2... | collective-permute-start | bytes 983048 | tf_op jit(solution)/shard_map/ppermute | solution.py:273
  156.7 13.0 %collective-permute-start.20 = (f32[10,64,128]{2,1,0:T(8,128)S(1)}, f32[10,64,128]{2,1,0:T(8,128)S(1)}, u32[]{:S(2)}, u32[]{:S(2)}) collective-permute-start(f32[10,64,128]{2,1,0:T(8,128)S(1)} %multiply_add_fusion.9), channel_id=1, source_target_pairs={{0,2},{2,4},{4,6},{6,8},{8,10},{10,12},{12,14},{14,16},{16,18},{18... | collective-permute-start | bytes 983048 | tf_op jit(solution)/shard_map/ppermute | solution.py:272
  165.5 13.2 %collective-permute-start.26 = (f32[10,64,128]{2,1,0:T(8,128)S(1)}, f32[10,64,128]{2,1,0:T(8,128)S(1)}, u32[]{:S(2)}, u32[]{:S(2)}) collective-permute-start(f32[10,64,128]{2,1,0:T(8,128)S(1)} %multiply_add_fusion.3), channel_id=1, source_target_pairs={{2,0},{4,2},{6,4},{8,6},{10,8},{12,10},{14,12},{16,14},{18,16},{20... | collective-permute-start | bytes 983048 | tf_op jit(solution)/shard_map/ppermute | solution.py:273
  (58 other events, 240.1 us)

commit v16 on v12

--- a/solution.py
+++ b/solution.py
@@ -264,7 +264,13 @@
     sizes = [padded.shape[0] for padded in padded_groups]
     rise = jnp.concatenate([part[:, 0] for part in partials], axis=0)
     fall = jnp.concatenate([part[:, 1] for part in partials], axis=0)
-    for entries in rounds:
+    locals_ = [
+        taps(padded, bank.get(handles[0])[:, : handles[3]])
+        for padded, handles in zip(padded_groups, groups)
+    ]
+    for level, entries in enumerate(rounds):
+        if level == len(rounds) // 2:
+            rise, fall, locals_ = lax.optimization_barrier((rise, fall, locals_))
         rise_next, fall_next = rise, fall
         for shift, rise_handle, fall_handle in entries:
             up_pairs = [(i, i + shift) for i in range(count - shift)]
@@ -276,8 +282,7 @@
         rise, fall = rise_next, fall_next
     results = []
     first = 0
-    for padded, handles, size in zip(padded_groups, groups, sizes):
-        local = taps(padded, bank.get(handles[0])[:, : handles[3]])
+    for local, handles, size in zip(locals_, groups, sizes):
         rise_gain = bank.get(handles[1])
         fall_gain = bank.get(handles[2])
         results.append(

time: 186 us -> 189 us (1.016)
  starting transfers between devices: 79 us -> 95.8 us
  waiting for transfers between devices: 65.1 us -> 53.4 us
  local copies, waits for them, and re-layouts: 13.8 us -> 11.8 us
    ppermute x12, starting transfers between devices: 50.8 us -> 67.2 us  [wall_apply(): from_below = lax.ppermute(rise, 'gy', up_pairs)]
    ppermute x12, waiting for transfers between devices: 51.1 us -> 35.5 us  [wall_apply(): from_above = lax.ppermute(fall, 'gy', down_pairs)]
    add x3 -> x6, other arithmetic: 1.07 us -> 5.53 us  [taps(): summed = term if summed is None else summed + term]
    add x2, other arithmetic: 4.9 us -> 1.6 us  [wall_apply(): local + rise_gain[None, :, None, None] * rise[first:first + size, None]]
    ppermute x12, waiting for transfers between devices: 8.67 us -> 10.9 us  [wall_apply(): from_below = lax.ppermute(rise, 'gy', up_pairs)]
  transfers between devices with their start and end apart: 28 -> 28, of which waited for: 16 -> 18; matrix products, arithmetic and copies ran while one was open for 13% -> 14% of each run, Pallas kernels for 0% -> 0%
where the time goes in v16:
time: 189 us; the launch traced here: 187 us
  starting transfers between devices  95.8 us (51%)
  waiting for transfers between devices  53.4 us (28%)
  other arithmetic  15.9 us (8%)
  local copies, waits for them, and re-layouts  11.8 us (6%)
  matrix products  8.75 us (5%)
    ppermute x12, starting transfers between devices, wall_apply(): from_below = lax.ppermute(rise, 'gy', up_pairs)  67.2 us
    ppermute x12, waiting for transfers between devices, wall_apply(): from_above = lax.ppermute(fall, 'gy', down_pairs)  35.5 us
    ppermute x12, starting transfers between devices, wall_apply(): from_above = lax.ppermute(fall, 'gy', down_pairs)  22.6 us
    ppermute x12, waiting for transfers between devices, wall_apply(): from_below = lax.ppermute(rise, 'gy', up_pairs)  10.9 us
    ppermute x1, waiting for transfers between devices, halo(): above = lax.ppermute(block[:, :width], 'gy', down_pairs)  7.1 us
    add x6, other arithmetic, taps(): summed = term if summed is None else summed + term  5.53 us
  transfers between devices with their start and end apart: 28, of which 18 were waited for; matrix products, arithmetic and copies ran while one was open for 14% of the time, Pallas kernels for 0%

profile of v16, /device:TPU:30, one launch (start us, length us, event | category | flops | bytes accessed | tf_op | source)
XLA Modules:
  0.0 187.4 jit_solution(13931511131775984005)
XLA Ops:
  3.0 3.4 %collective-permute-start = (f32[5,3,64,128]{3,2,1,0:T(8,128)}, f32[5,3,64,128]{3,2,1,0:T(8,128)S(1)}, u32[]{:S(2)}, u32[]{:S(2)}) collective-permute-start(f32[5,3,64,128]{3,2,1,0:T(8,128)} %get-tuple-element.65), channel_id=1, source_target_pairs={{0,2},{2,4},{4,6},{6,8},{8,10},{10,12},{12,14},{14,16},{16,18},{18... | collective-permute-start | bytes 1474568 | tf_op jit(solution)/shard_map/ppermute | solution.py:301
  18.3 7.1 %collective-permute-done.1 = f32[5,3,64,128]{3,2,1,0:T(8,128)S(1)} collective-permute-done((f32[5,3,64,128]{3,2,1,0:T(8,128)}, f32[5,3,64,128]{3,2,1,0:T(8,128)S(1)}, u32[]{:S(2)}, u32[]{:S(2)}) %collective-permute-start.1) | collective-permute-done | bytes 491552 | tf_op jit(solution)/shard_map/ppermute | solution.py:302
  28.8 6.1 %collective-permute-start.2 = (f32[9,64,128]{2,1,0:T(8,128)S(1)}, f32[9,64,128]{2,1,0:T(8,128)S(1)}, u32[]{:S(2)}, u32[]{:S(2)}) collective-permute-start(f32[9,64,128]{2,1,0:T(8,128)S(1)} %pad_maximum_fusion.7), channel_id=1, source_target_pairs={{0,64},{2,66},{4,68},{6,70},{8,72},{10,74},{12,76},{14,78},{16,80}... | collective-permute-start | bytes 884744 | tf_op jit(solution)/shard_map/ppermute | solution.py:278
  39.9 4.6 %collective-permute-start.3 = (f32[9,64,128]{2,1,0:T(8,128)S(1)}, f32[9,64,128]{2,1,0:T(8,128)S(1)}, u32[]{:S(2)}, u32[]{:S(2)}) collective-permute-start(f32[9,64,128]{2,1,0:T(8,128)S(1)} %multiply_add_fusion.18), channel_id=1, source_target_pairs={{0,32},{2,34},{4,36},{6,38},{8,40},{10,42},{12,44},{14,46},{16,48}... | collective-permute-start | bytes 884744 | tf_op jit(solution)/shard_map/ppermute | solution.py:278
  45.9 4.0 %collective-permute-done.6 = f32[9,64,128]{2,1,0:T(8,128)S(1)} collective-permute-done((f32[9,64,128]{2,1,0:T(8,128)S(1)}, f32[9,64,128]{2,1,0:T(8,128)S(1)}, u32[]{:S(2)}, u32[]{:S(2)}) %collective-permute-start.6) | collective-permute-done | bytes 294944 | tf_op jit(solution)/shard_map/ppermute | solution.py:279
  52.1 6.3 %collective-permute-start.4 = (f32[9,64,128]{2,1,0:T(8,128)S(1)}, f32[9,64,128]{2,1,0:T(8,128)S(1)}, u32[]{:S(2)}, u32[]{:S(2)}) collective-permute-start(f32[9,64,128]{2,1,0:T(8,128)S(1)} %multiply_add_fusion.17), channel_id=1, source_target_pairs={{0,16},{2,18},{4,20},{6,22},{8,24},{10,26},{12,28},{14,30},{16,32}... | collective-permute-start | bytes 884744 | tf_op jit(solution)/shard_map/ppermute | solution.py:278
  58.5 5.7 %collective-permute-done.7 = f32[9,64,128]{2,1,0:T(8,128)S(1)} collective-permute-done((f32[9,64,128]{2,1,0:T(8,128)S(1)}, f32[9,64,128]{2,1,0:T(8,128)S(1)}, u32[]{:S(2)}, u32[]{:S(2)}) %collective-permute-start.7) | collective-permute-done | bytes 294944 | tf_op jit(solution)/shard_map/ppermute | solution.py:279
  64.9 4.6 %collective-permute-start.8 = (f32[9,64,128]{2,1,0:T(8,128)S(1)}, f32[9,64,128]{2,1,0:T(8,128)S(1)}, u32[]{:S(2)}, u32[]{:S(2)}) collective-permute-start(f32[9,64,128]{2,1,0:T(8,128)S(1)} %multiply_add_fusion.16), channel_id=1, source_target_pairs={{0,8},{2,10},{4,12},{6,14},{8,16},{10,18},{12,20},{14,22},{16,24},... | collective-permute-start | bytes 884744 | tf_op jit(solution)/shard_map/ppermute | solution.py:278
  71.6 3.7 %collective-permute-done.8 = f32[9,64,128]{2,1,0:T(8,128)S(1)} collective-permute-done((f32[9,64,128]{2,1,0:T(8,128)S(1)}, f32[9,64,128]{2,1,0:T(8,128)S(1)}, u32[]{:S(2)}, u32[]{:S(2)}) %collective-permute-start.8) | collective-permute-done | bytes 294944 | tf_op jit(solution)/shard_map/ppermute | solution.py:278
  75.4 4.9 %collective-permute-start.9 = (f32[9,64,128]{2,1,0:T(8,128)S(1)}, f32[9,64,128]{2,1,0:T(8,128)S(1)}, u32[]{:S(2)}, u32[]{:S(2)}) collective-permute-start(f32[9,64,128]{2,1,0:T(8,128)S(1)} %multiply_add_fusion.12), channel_id=1, source_target_pairs={{0,4},{2,6},{4,8},{6,10},{8,12},{10,14},{12,16},{14,18},{16,20},{1... | collective-permute-start | bytes 884744 | tf_op jit(solution)/shard_map/ppermute | solution.py:278
  83.7 4.8 %collective-permute-done.9 = f32[9,64,128]{2,1,0:T(8,128)S(1)} collective-permute-done((f32[9,64,128]{2,1,0:T(8,128)S(1)}, f32[9,64,128]{2,1,0:T(8,128)S(1)}, u32[]{:S(2)}, u32[]{:S(2)}) %collective-permute-start.9) | collective-permute-done | bytes 294944 | tf_op jit(solution)/shard_map/ppermute | solution.py:278
  88.6 9.5 %collective-permute-start.10 = (f32[9,64,128]{2,1,0:T(8,128)S(1)}, f32[9,64,128]{2,1,0:T(8,128)S(1)}, u32[]{:S(2)}, u32[]{:S(2)}) collective-permute-start(f32[9,64,128]{2,1,0:T(8,128)S(1)} %multiply_add_fusion.11), channel_id=1, source_target_pairs={{0,2},{2,4},{4,6},{6,8},{8,10},{10,12},{12,14},{14,16},{16,18},{18... | collective-permute-start | bytes 884744 | tf_op jit(solution)/shard_map/ppermute | solution.py:278
  103.8 7.3 %collective-permute-done.13 = f32[9,64,128]{2,1,0:T(8,128)S(1)} collective-permute-done((f32[9,64,128]{2,1,0:T(8,128)S(1)}, f32[9,64,128]{2,1,0:T(8,128)S(1)}, u32[]{:S(2)}, u32[]{:S(2)}) %collective-permute-start.13) | collective-permute-done | bytes 294944 | tf_op jit(solution)/shard_map/ppermute | solution.py:279
  114.0 4.1 %collective-permute-start.15 = (f32[5,64,128]{2,1,0:T(8,128)S(1)}, f32[5,64,128]{2,1,0:T(8,128)S(1)}, u32[]{:S(2)}, u32[]{:S(2)}) collective-permute-start(f32[5,64,128]{2,1,0:T(8,128)S(1)} %get-tuple-element.78), channel_id=1, source_target_pairs={{0,64},{2,66},{4,68},{6,70},{8,72},{10,74},{12,76},{14,78},{16,80}... | collective-permute-start | bytes 491528 | tf_op jit(solution)/shard_map/ppermute | solution.py:278
  123.8 3.0 %collective-permute-done.18 = f32[5,64,128]{2,1,0:T(8,128)S(1)} collective-permute-done((f32[5,64,128]{2,1,0:T(8,128)S(1)}, f32[5,64,128]{2,1,0:T(8,128)S(1)}, u32[]{:S(2)}, u32[]{:S(2)}) %collective-permute-start.18) | collective-permute-done | bytes 163872 | tf_op jit(solution)/shard_map/ppermute | solution.py:279
  129.4 4.6 %collective-permute-start.16 = (f32[5,64,128]{2,1,0:T(8,128)S(1)}, f32[5,64,128]{2,1,0:T(8,128)S(1)}, u32[]{:S(2)}, u32[]{:S(2)}) collective-permute-start(f32[5,64,128]{2,1,0:T(8,128)S(1)} %get-tuple-element.76), channel_id=1, source_target_pairs={{0,32},{2,34},{4,36},{6,38},{8,40},{10,42},{12,44},{14,46},{16,48}... | collective-permute-start | bytes 491528 | tf_op jit(solution)/shard_map/ppermute | solution.py:278
  136.9 5.7 %collective-permute-start.17 = (f32[5,64,128]{2,1,0:T(8,128)S(1)}, f32[5,64,128]{2,1,0:T(8,128)S(1)}, u32[]{:S(2)}, u32[]{:S(2)}) collective-permute-start(f32[5,64,128]{2,1,0:T(8,128)S(1)} %multiply_add_fusion.30), channel_id=1, source_target_pairs={{0,16},{2,18},{4,20},{6,22},{8,24},{10,26},{12,28},{14,30},{16,32}... | collective-permute-start | bytes 491528 | tf_op jit(solution)/shard_map/ppermute | solution.py:278
  145.7 2.6 %collective-permute-start.21 = (f32[5,64,128]{2,1,0:T(8,128)S(1)}, f32[5,64,128]{2,1,0:T(8,128)S(1)}, u32[]{:S(2)}, u32[]{:S(2)}) collective-permute-start(f32[5,64,128]{2,1,0:T(8,128)S(1)} %multiply_add_fusion.29), channel_id=1, source_target_pairs={{0,8},{2,10},{4,12},{6,14},{8,16},{10,18},{12,20},{14,22},{16,24},... | collective-permute-start | bytes 491528 | tf_op jit(solution)/shard_map/ppermute | solution.py:278
  149.6 3.3 %collective-permute-start.24 = (f32[5,64,128]{2,1,0:T(8,128)S(1)}, f32[5,64,128]{2,1,0:T(8,128)S(1)}, u32[]{:S(2)}, u32[]{:S(2)}) collective-permute-start(f32[5,64,128]{2,1,0:T(8,128)S(1)} %multiply_add_fusion.26), channel_id=1, source_target_pairs={{8,0},{10,2},{12,4},{14,6},{16,8},{18,10},{20,12},{22,14},{24,16},... | collective-permute-start | bytes 491528 | tf_op jit(solution)/shard_map/ppermute | solution.py:279
  153.0 3.8 %collective-permute-start.22 = (f32[5,64,128]{2,1,0:T(8,128)S(1)}, f32[5,64,128]{2,1,0:T(8,128)S(1)}, u32[]{:S(2)}, u32[]{:S(2)}) collective-permute-start(f32[5,64,128]{2,1,0:T(8,128)S(1)} %multiply_add_fusion.25), channel_id=1, source_target_pairs={{0,4},{2,6},{4,8},{6,10},{8,12},{10,14},{12,16},{14,18},{16,20},{1... | collective-permute-start | bytes 491528 | tf_op jit(solution)/shard_map/ppermute | solution.py:278
  156.8 2.5 %collective-permute-done.24 = f32[5,64,128]{2,1,0:T(8,128)S(1)} collective-permute-done((f32[5,64,128]{2,1,0:T(8,128)S(1)}, f32[5,64,128]{2,1,0:T(8,128)S(1)}, u32[]{:S(2)}, u32[]{:S(2)}) %collective-permute-start.24) | collective-permute-done | bytes 163872 | tf_op jit(solution)/shard_map/ppermute | solution.py:279
  161.8 10.5 %collective-permute-start.23 = (f32[5,64,128]{2,1,0:T(8,128)S(1)}, f32[5,64,128]{2,1,0:T(8,128)S(1)}, u32[]{:S(2)}, u32[]{:S(2)}) collective-permute-start(f32[5,64,128]{2,1,0:T(8,128)S(1)} %multiply_add_fusion.24), channel_id=1, source_target_pairs={{0,2},{2,4},{4,6},{6,8},{8,10},{10,12},{12,14},{14,16},{16,18},{18... | collective-permute-start | bytes 491528 | tf_op jit(solution)/shard_map/ppermute | solution.py:278
  172.8 2.4 %collective-permute-start.26 = (f32[5,64,128]{2,1,0:T(8,128)S(1)}, f32[5,64,128]{2,1,0:T(8,128)S(1)}, u32[]{:S(2)}, u32[]{:S(2)}) collective-permute-start(f32[5,64,128]{2,1,0:T(8,128)S(1)} %multiply_add_fusion.21), channel_id=1, source_target_pairs={{2,0},{4,2},{6,4},{8,6},{10,8},{12,10},{14,12},{16,14},{18,16},{20... | collective-permute-start | bytes 491528 | tf_op jit(solution)/shard_map/ppermute | solution.py:279
  175.4 8.9 %collective-permute-done.26 = f32[5,64,128]{2,1,0:T(8,128)S(1)} collective-permute-done((f32[5,64,128]{2,1,0:T(8,128)S(1)}, f32[5,64,128]{2,1,0:T(8,128)S(1)}, u32[]{:S(2)}, u32[]{:S(2)}) %collective-permute-start.26) | collective-permute-done | bytes 163872 | tf_op jit(solution)/shard_map/ppermute | solution.py:279
  (183 shorter events, 62.4 us)
Async XLA Ops:
  3.0 15.3 %collective-permute-start = (f32[5,3,64,128]{3,2,1,0:T(8,128)}, f32[5,3,64,128]{3,2,1,0:T(8,128)S(1)}, u32[]{:S(2)}, u32[]{:S(2)}) collective-permute-start(f32[5,3,64,128]{3,2,1,0:T(8,128)} %get-tuple-element.65), channel_id=1, source_target_pairs={{0,2},{2,4},{4,6},{6,8},{8,10},{10,12},{12,14},{14,16},{16,18},{18... | collective-permute-start | bytes 1474568 | tf_op jit(solution)/shard_map/ppermute | solution.py:301
  6.4 19.0 %collective-permute-start.1 = (f32[5,3,64,128]{3,2,1,0:T(8,128)}, f32[5,3,64,128]{3,2,1,0:T(8,128)S(1)}, u32[]{:S(2)}, u32[]{:S(2)}) collective-permute-start(f32[5,3,64,128]{3,2,1,0:T(8,128)} %get-tuple-element.66), channel_id=1, source_target_pairs={{2,0},{4,2},{6,4},{8,6},{10,8},{12,10},{14,12},{16,14},{18,16},{20... | collective-permute-start | bytes 1474568 | tf_op jit(solution)/shard_map/ppermute | solution.py:302
  27.4 11.0 %collective-permute-start.5 = (f32[9,64,128]{2,1,0:T(8,128)S(1)}, f32[9,64,128]{2,1,0:T(8,128)S(1)}, u32[]{:S(2)}, u32[]{:S(2)}) collective-permute-start(f32[9,64,128]{2,1,0:T(8,128)S(1)} %pad_maximum_fusion.8), channel_id=1, source_target_pairs={{64,0},{66,2},{68,4},{70,6},{72,8},{74,10},{76,12},{78,14},{80,16}... | collective-permute-start | bytes 884744 | tf_op jit(solution)/shard_map/ppermute | solution.py:279
  28.8 11.0 %collective-permute-start.2 = (f32[9,64,128]{2,1,0:T(8,128)S(1)}, f32[9,64,128]{2,1,0:T(8,128)S(1)}, u32[]{:S(2)}, u32[]{:S(2)}) collective-permute-start(f32[9,64,128]{2,1,0:T(8,128)S(1)} %pad_maximum_fusion.7), channel_id=1, source_target_pairs={{0,64},{2,66},{4,68},{6,70},{8,72},{10,74},{12,76},{14,78},{16,80}... | collective-permute-start | bytes 884744 | tf_op jit(solution)/shard_map/ppermute | solution.py:278
  34.9 65.5 %collective-permute-start.14 = (f32[4,12,64,128]{3,2,1,0:T(8,128)S(1)}, f32[4,12,64,128]{3,2,1,0:T(8,128)S(1)}, u32[]{:S(2)}, u32[]{:S(2)}) collective-permute-start(f32[4,12,64,128]{3,2,1,0:T(8,128)S(1)} %fusion.1), channel_id=1, source_target_pairs={{0,1},{1,0},{2,3},{3,2},{4,5},{5,4},{6,7},{7,6},{8,9},{9,8},{10,11... | collective-permute-start | bytes 4718600 | tf_op jit(solution)/shard_map/ppermute | solution.py:314
  38.5 11.4 %collective-permute-start.6 = (f32[9,64,128]{2,1,0:T(8,128)S(1)}, f32[9,64,128]{2,1,0:T(8,128)S(1)}, u32[]{:S(2)}, u32[]{:S(2)}) collective-permute-start(f32[9,64,128]{2,1,0:T(8,128)S(1)} %multiply_add_fusion.15), channel_id=1, source_target_pairs={{32,0},{34,2},{36,4},{38,6},{40,8},{42,10},{44,12},{46,14},{48,16}... | collective-permute-start | bytes 884744 | tf_op jit(solution)/shard_map/ppermute | solution.py:279
  39.9 12.0 %collective-permute-start.3 = (f32[9,64,128]{2,1,0:T(8,128)S(1)}, f32[9,64,128]{2,1,0:T(8,128)S(1)}, u32[]{:S(2)}, u32[]{:S(2)}) collective-permute-start(f32[9,64,128]{2,1,0:T(8,128)S(1)} %multiply_add_fusion.18), channel_id=1, source_target_pairs={{0,32},{2,34},{4,36},{6,38},{8,40},{10,42},{12,44},{14,46},{16,48}... | collective-permute-start | bytes 884744 | tf_op jit(solution)/shard_map/ppermute | solution.py:278
  50.0 14.2 %collective-permute-start.7 = (f32[9,64,128]{2,1,0:T(8,128)S(1)}, f32[9,64,128]{2,1,0:T(8,128)S(1)}, u32[]{:S(2)}, u32[]{:S(2)}) collective-permute-start(f32[9,64,128]{2,1,0:T(8,128)S(1)} %multiply_add_fusion.14), channel_id=1, source_target_pairs={{16,0},{18,2},{20,4},{22,6},{24,8},{26,10},{28,12},{30,14},{32,16}... | collective-permute-start | bytes 884744 | tf_op jit(solution)/shard_map/ppermute | solution.py:279
  52.1 12.7 %collective-permute-start.4 = (f32[9,64,128]{2,1,0:T(8,128)S(1)}, f32[9,64,128]{2,1,0:T(8,128)S(1)}, u32[]{:S(2)}, u32[]{:S(2)}) collective-permute-start(f32[9,64,128]{2,1,0:T(8,128)S(1)} %multiply_add_fusion.17), channel_id=1, source_target_pairs={{0,16},{2,18},{4,20},{6,22},{8,24},{10,26},{12,28},{14,30},{16,32}... | collective-permute-start | bytes 884744 | tf_op jit(solution)/shard_map/ppermute | solution.py:278
  64.9 10.4 %collective-permute-start.8 = (f32[9,64,128]{2,1,0:T(8,128)S(1)}, f32[9,64,128]{2,1,0:T(8,128)S(1)}, u32[]{:S(2)}, u32[]{:S(2)}) collective-permute-start(f32[9,64,128]{2,1,0:T(8,128)S(1)} %multiply_add_fusion.16), channel_id=1, source_target_pairs={{0,8},{2,10},{4,12},{6,14},{8,16},{10,18},{12,20},{14,22},{16,24},... | collective-permute-start | bytes 884744 | tf_op jit(solution)/shard_map/ppermute | solution.py:278
  69.6 12.0 %collective-permute-start.11 = (f32[9,64,128]{2,1,0:T(8,128)S(1)}, f32[9,64,128]{2,1,0:T(8,128)S(1)}, u32[]{:S(2)}, u32[]{:S(2)}) collective-permute-start(f32[9,64,128]{2,1,0:T(8,128)S(1)} %multiply_add_fusion.13), channel_id=1, source_target_pairs={{8,0},{10,2},{12,4},{14,6},{16,8},{18,10},{20,12},{22,14},{24,16},... | collective-permute-start | bytes 884744 | tf_op jit(solution)/shard_map/ppermute | solution.py:279
  75.4 13.1 %collective-permute-start.9 = (f32[9,64,128]{2,1,0:T(8,128)S(1)}, f32[9,64,128]{2,1,0:T(8,128)S(1)}, u32[]{:S(2)}, u32[]{:S(2)}) collective-permute-start(f32[9,64,128]{2,1,0:T(8,128)S(1)} %multiply_add_fusion.12), channel_id=1, source_target_pairs={{0,4},{2,6},{4,8},{6,10},{8,12},{10,14},{12,16},{14,18},{16,20},{1... | collective-permute-start | bytes 884744 | tf_op jit(solution)/shard_map/ppermute | solution.py:278
  81.7 16.4 %collective-permute-start.12 = (f32[9,64,128]{2,1,0:T(8,128)S(1)}, f32[9,64,128]{2,1,0:T(8,128)S(1)}, u32[]{:S(2)}, u32[]{:S(2)}) collective-permute-start(f32[9,64,128]{2,1,0:T(8,128)S(1)} %multiply_add_fusion.9), channel_id=1, source_target_pairs={{4,0},{6,2},{8,4},{10,6},{12,8},{14,10},{16,12},{18,14},{20,16},{2... | collective-permute-start | bytes 884744 | tf_op jit(solution)/shard_map/ppermute | solution.py:279
  88.6 15.1 %collective-permute-start.10 = (f32[9,64,128]{2,1,0:T(8,128)S(1)}, f32[9,64,128]{2,1,0:T(8,128)S(1)}, u32[]{:S(2)}, u32[]{:S(2)}) collective-permute-start(f32[9,64,128]{2,1,0:T(8,128)S(1)} %multiply_add_fusion.11), channel_id=1, source_target_pairs={{0,2},{2,4},{4,6},{6,8},{8,10},{10,12},{12,14},{14,16},{16,18},{18... | collective-permute-start | bytes 884744 | tf_op jit(solution)/shard_map/ppermute | solution.py:278
  98.2 12.8 %collective-permute-start.13 = (f32[9,64,128]{2,1,0:T(8,128)S(1)}, f32[9,64,128]{2,1,0:T(8,128)S(1)}, u32[]{:S(2)}, u32[]{:S(2)}) collective-permute-start(f32[9,64,128]{2,1,0:T(8,128)S(1)} %multiply_add_fusion.8), channel_id=1, source_target_pairs={{2,0},{4,2},{6,4},{8,6},{10,8},{12,10},{14,12},{16,14},{18,16},{20... | collective-permute-start | bytes 884744 | tf_op jit(solution)/shard_map/ppermute | solution.py:279
  114.0 9.8 %collective-permute-start.15 = (f32[5,64,128]{2,1,0:T(8,128)S(1)}, f32[5,64,128]{2,1,0:T(8,128)S(1)}, u32[]{:S(2)}, u32[]{:S(2)}) collective-permute-start(f32[5,64,128]{2,1,0:T(8,128)S(1)} %get-tuple-element.78), channel_id=1, source_target_pairs={{0,64},{2,66},{4,68},{6,70},{8,72},{10,74},{12,76},{14,78},{16,80}... | collective-permute-start | bytes 491528 | tf_op jit(solution)/shard_map/ppermute | solution.py:278
  118.1 8.7 %collective-permute-start.18 = (f32[5,64,128]{2,1,0:T(8,128)S(1)}, f32[5,64,128]{2,1,0:T(8,128)S(1)}, u32[]{:S(2)}, u32[]{:S(2)}) collective-permute-start(f32[5,64,128]{2,1,0:T(8,128)S(1)} %get-tuple-element.77), channel_id=1, source_target_pairs={{64,0},{66,2},{68,4},{70,6},{72,8},{74,10},{76,12},{78,14},{80,16}... | collective-permute-start | bytes 491528 | tf_op jit(solution)/shard_map/ppermute | solution.py:279
  120.3 64.1 %collective-permute-start.27 = (f32[5,8,64,128]{3,2,1,0:T(8,128)S(1)}, f32[5,8,64,128]{3,2,1,0:T(8,128)S(1)}, u32[]{:S(2)}, u32[]{:S(2)}) collective-permute-start(f32[5,8,64,128]{3,2,1,0:T(8,128)S(1)} %fusion.34), channel_id=1, source_target_pairs={{0,1},{1,0},{2,3},{3,2},{4,5},{5,4},{6,7},{7,6},{8,9},{9,8},{10,11... | collective-permute-start | bytes 3932168 | tf_op jit(solution)/shard_map/ppermute | solution.py:314
  134.2 10.6 %collective-permute-start.20 = (f32[5,64,128]{2,1,0:T(8,128)S(1)}, f32[5,64,128]{2,1,0:T(8,128)S(1)}, u32[]{:S(2)}, u32[]{:S(2)}) collective-permute-start(f32[5,64,128]{2,1,0:T(8,128)S(1)} %multiply_add_fusion.27), channel_id=1, source_target_pairs={{16,0},{18,2},{20,4},{22,6},{24,8},{26,10},{28,12},{30,14},{32,16}... | collective-permute-start | bytes 491528 | tf_op jit(solution)/shard_map/ppermute | solution.py:279
  136.9 8.7 %collective-permute-start.17 = (f32[5,64,128]{2,1,0:T(8,128)S(1)}, f32[5,64,128]{2,1,0:T(8,128)S(1)}, u32[]{:S(2)}, u32[]{:S(2)}) collective-permute-start(f32[5,64,128]{2,1,0:T(8,128)S(1)} %multiply_add_fusion.30), channel_id=1, source_target_pairs={{0,16},{2,18},{4,20},{6,22},{8,24},{10,26},{12,28},{14,30},{16,32}... | collective-permute-start | bytes 491528 | tf_op jit(solution)/shard_map/ppermute | solution.py:278
  149.6 9.8 %collective-permute-start.24 = (f32[5,64,128]{2,1,0:T(8,128)S(1)}, f32[5,64,128]{2,1,0:T(8,128)S(1)}, u32[]{:S(2)}, u32[]{:S(2)}) collective-permute-start(f32[5,64,128]{2,1,0:T(8,128)S(1)} %multiply_add_fusion.26), channel_id=1, source_target_pairs={{8,0},{10,2},{12,4},{14,6},{16,8},{18,10},{20,12},{22,14},{24,16},... | collective-permute-start | bytes 491528 | tf_op jit(solution)/shard_map/ppermute | solution.py:279
  159.4 13.3 %collective-permute-start.25 = (f32[5,64,128]{2,1,0:T(8,128)S(1)}, f32[5,64,128]{2,1,0:T(8,128)S(1)}, u32[]{:S(2)}, u32[]{:S(2)}) collective-permute-start(f32[5,64,128]{2,1,0:T(8,128)S(1)} %multiply_add_fusion.22), channel_id=1, source_target_pairs={{4,0},{6,2},{8,4},{10,6},{12,8},{14,10},{16,12},{18,14},{20,16},{2... | collective-permute-start | bytes 491528 | tf_op jit(solution)/shard_map/ppermute | solution.py:279
  161.8 13.5 %collective-permute-start.23 = (f32[5,64,128]{2,1,0:T(8,128)S(1)}, f32[5,64,128]{2,1,0:T(8,128)S(1)}, u32[]{:S(2)}, u32[]{:S(2)}) collective-permute-start(f32[5,64,128]{2,1,0:T(8,128)S(1)} %multiply_add_fusion.24), channel_id=1, source_target_pairs={{0,2},{2,4},{4,6},{6,8},{8,10},{10,12},{12,14},{14,16},{16,18},{18... | collective-permute-start | bytes 491528 | tf_op jit(solution)/shard_map/ppermute | solution.py:278
  172.8 11.4 %collective-permute-start.26 = (f32[5,64,128]{2,1,0:T(8,128)S(1)}, f32[5,64,128]{2,1,0:T(8,128)S(1)}, u32[]{:S(2)}, u32[]{:S(2)}) collective-permute-start(f32[5,64,128]{2,1,0:T(8,128)S(1)} %multiply_add_fusion.21), channel_id=1, source_target_pairs={{2,0},{4,2},{6,4},{8,6},{10,8},{12,10},{14,12},{16,14},{18,16},{20... | collective-permute-start | bytes 491528 | tf_op jit(solution)/shard_map/ppermute | solution.py:279
  (33 other events, 219.3 us)

commit v17 on v16

--- a/solution.py
+++ b/solution.py
@@ -269,7 +269,7 @@
         for padded, handles in zip(padded_groups, groups)
     ]
     for level, entries in enumerate(rounds):
-        if level == len(rounds) // 2:
+        if level == len(rounds) - 1:
             rise, fall, locals_ = lax.optimization_barrier((rise, fall, locals_))
         rise_next, fall_next = rise, fall
         for shift, rise_handle, fall_handle in entries:

time: 189 us -> 188 us (level)
    ppermute x12, waiting for transfers between devices: 10.9 us -> 2.02 us  [wall_apply(): from_below = lax.ppermute(rise, 'gy', up_pairs)]
    ppermute x12, waiting for transfers between devices: 35.5 us -> 43.8 us  [wall_apply(): from_above = lax.ppermute(fall, 'gy', down_pairs)]
  transfers between devices with their start and end apart: 28 -> 28, of which waited for: 18 -> 15; matrix products, arithmetic and copies ran while one was open for 14% -> 14% of each run, Pallas kernels for 0% -> 0%
where the time goes in v17:
time: 188 us; the launch traced here: 187 us
  starting transfers between devices  95.7 us (51%)
  waiting for transfers between devices  52.9 us (28%)
  other arithmetic  15.9 us (8%)
  local copies, waits for them, and re-layouts  11.8 us (6%)
  matrix products  8.75 us (5%)
    ppermute x12, starting transfers between devices, wall_apply(): from_below = lax.ppermute(rise, 'gy', up_pairs)  67.5 us
    ppermute x12, waiting for transfers between devices, wall_apply(): from_above = lax.ppermute(fall, 'gy', down_pairs)  43.8 us
    ppermute x12, starting transfers between devices, wall_apply(): from_above = lax.ppermute(fall, 'gy', down_pairs)  22.2 us
    ppermute x1, waiting for transfers between devices, halo(): above = lax.ppermute(block[:, :width], 'gy', down_pairs)  7.11 us
    add x6, other arithmetic, taps(): summed = term if summed is None else summed + term  5.54 us
  transfers between devices with their start and end apart: 28, of which 15 were waited for; matrix products, arithmetic and copies ran while one was open for 14% of the time, Pallas kernels for 0%

profile of v17, /device:TPU:30, one launch (start us, length us, event | category | flops | bytes accessed | tf_op | source)
XLA Modules:
  0.0 186.9 jit_solution(5635632766650675951)
XLA Ops:
  3.0 3.4 %collective-permute-start = (f32[5,3,64,128]{3,2,1,0:T(8,128)}, f32[5,3,64,128]{3,2,1,0:T(8,128)S(1)}, u32[]{:S(2)}, u32[]{:S(2)}) collective-permute-start(f32[5,3,64,128]{3,2,1,0:T(8,128)} %get-tuple-element.65), channel_id=1, source_target_pairs={{0,2},{2,4},{4,6},{6,8},{8,10},{10,12},{12,14},{14,16},{16,18},{18... | collective-permute-start | bytes 1474568 | tf_op jit(solution)/shard_map/ppermute | solution.py:301
  6.4 2.4 %collective-permute-start.1 = (f32[5,3,64,128]{3,2,1,0:T(8,128)}, f32[5,3,64,128]{3,2,1,0:T(8,128)S(1)}, u32[]{:S(2)}, u32[]{:S(2)}) collective-permute-start(f32[5,3,64,128]{3,2,1,0:T(8,128)} %get-tuple-element.66), channel_id=1, source_target_pairs={{2,0},{4,2},{6,4},{8,6},{10,8},{12,10},{14,12},{16,14},{18,16},{20... | collective-permute-start | bytes 1474568 | tf_op jit(solution)/shard_map/ppermute | solution.py:302
  18.3 7.1 %collective-permute-done.1 = f32[5,3,64,128]{3,2,1,0:T(8,128)S(1)} collective-permute-done((f32[5,3,64,128]{3,2,1,0:T(8,128)}, f32[5,3,64,128]{3,2,1,0:T(8,128)S(1)}, u32[]{:S(2)}, u32[]{:S(2)}) %collective-permute-start.1) | collective-permute-done | bytes 491552 | tf_op jit(solution)/shard_map/ppermute | solution.py:302
  28.7 6.1 %collective-permute-start.2 = (f32[9,64,128]{2,1,0:T(8,128)S(1)}, f32[9,64,128]{2,1,0:T(8,128)S(1)}, u32[]{:S(2)}, u32[]{:S(2)}) collective-permute-start(f32[9,64,128]{2,1,0:T(8,128)S(1)} %pad_maximum_fusion.7), channel_id=1, source_target_pairs={{0,64},{2,66},{4,68},{6,70},{8,72},{10,74},{12,76},{14,78},{16,80}... | collective-permute-start | bytes 884744 | tf_op jit(solution)/shard_map/ppermute | solution.py:278
  41.3 4.6 %collective-permute-start.3 = (f32[9,64,128]{2,1,0:T(8,128)S(1)}, f32[9,64,128]{2,1,0:T(8,128)S(1)}, u32[]{:S(2)}, u32[]{:S(2)}) collective-permute-start(f32[9,64,128]{2,1,0:T(8,128)S(1)} %multiply_add_fusion.18), channel_id=1, source_target_pairs={{0,32},{2,34},{4,36},{6,38},{8,40},{10,42},{12,44},{14,46},{16,48}... | collective-permute-start | bytes 884744 | tf_op jit(solution)/shard_map/ppermute | solution.py:278
  46.0 5.4 %collective-permute-done.8 = f32[9,64,128]{2,1,0:T(8,128)S(1)} collective-permute-done((f32[9,64,128]{2,1,0:T(8,128)S(1)}, f32[9,64,128]{2,1,0:T(8,128)S(1)}, u32[]{:S(2)}, u32[]{:S(2)}) %collective-permute-start.8) | collective-permute-done | bytes 294944 | tf_op jit(solution)/shard_map/ppermute | solution.py:279
  53.5 6.3 %collective-permute-start.4 = (f32[9,64,128]{2,1,0:T(8,128)S(1)}, f32[9,64,128]{2,1,0:T(8,128)S(1)}, u32[]{:S(2)}, u32[]{:S(2)}) collective-permute-start(f32[9,64,128]{2,1,0:T(8,128)S(1)} %multiply_add_fusion.17), channel_id=1, source_target_pairs={{0,16},{2,18},{4,20},{6,22},{8,24},{10,26},{12,28},{14,30},{16,32}... | collective-permute-start | bytes 884744 | tf_op jit(solution)/shard_map/ppermute | solution.py:278
  59.9 5.7 %collective-permute-done.9 = f32[9,64,128]{2,1,0:T(8,128)S(1)} collective-permute-done((f32[9,64,128]{2,1,0:T(8,128)S(1)}, f32[9,64,128]{2,1,0:T(8,128)S(1)}, u32[]{:S(2)}, u32[]{:S(2)}) %collective-permute-start.9) | collective-permute-done | bytes 294944 | tf_op jit(solution)/shard_map/ppermute | solution.py:279
  67.8 6.0 %collective-permute-start.5 = (f32[9,64,128]{2,1,0:T(8,128)S(1)}, f32[9,64,128]{2,1,0:T(8,128)S(1)}, u32[]{:S(2)}, u32[]{:S(2)}) collective-permute-start(f32[9,64,128]{2,1,0:T(8,128)S(1)} %multiply_add_fusion.16), channel_id=1, source_target_pairs={{0,8},{2,10},{4,12},{6,14},{8,16},{10,18},{12,20},{14,22},{16,24},... | collective-permute-start | bytes 884744 | tf_op jit(solution)/shard_map/ppermute | solution.py:278
  73.9 3.4 %collective-permute-done.10 = f32[9,64,128]{2,1,0:T(8,128)S(1)} collective-permute-done((f32[9,64,128]{2,1,0:T(8,128)S(1)}, f32[9,64,128]{2,1,0:T(8,128)S(1)}, u32[]{:S(2)}, u32[]{:S(2)}) %collective-permute-start.10) | collective-permute-done | bytes 294944 | tf_op jit(solution)/shard_map/ppermute | solution.py:279
  79.5 8.4 %collective-permute-start.6 = (f32[9,64,128]{2,1,0:T(8,128)S(1)}, f32[9,64,128]{2,1,0:T(8,128)S(1)}, u32[]{:S(2)}, u32[]{:S(2)}) collective-permute-start(f32[9,64,128]{2,1,0:T(8,128)S(1)} %multiply_add_fusion.15), channel_id=1, source_target_pairs={{0,4},{2,6},{4,8},{6,10},{8,12},{10,14},{12,16},{14,18},{16,20},{1... | collective-permute-start | bytes 884744 | tf_op jit(solution)/shard_map/ppermute | solution.py:278
  88.0 5.7 %collective-permute-done.11 = f32[9,64,128]{2,1,0:T(8,128)S(1)} collective-permute-done((f32[9,64,128]{2,1,0:T(8,128)S(1)}, f32[9,64,128]{2,1,0:T(8,128)S(1)}, u32[]{:S(2)}, u32[]{:S(2)}) %collective-permute-start.11) | collective-permute-done | bytes 294944 | tf_op jit(solution)/shard_map/ppermute | solution.py:279
  93.9 2.9 %collective-permute-start.12 = (f32[9,64,128]{2,1,0:T(8,128)S(1)}, f32[9,64,128]{2,1,0:T(8,128)S(1)}, u32[]{:S(2)}, u32[]{:S(2)}) collective-permute-start(f32[9,64,128]{2,1,0:T(8,128)S(1)} %multiply_add_fusion.14), channel_id=1, source_target_pairs={{0,2},{2,4},{4,6},{6,8},{8,10},{10,12},{12,14},{14,16},{16,18},{18... | collective-permute-start | bytes 884744 | tf_op jit(solution)/shard_map/ppermute | solution.py:278
  96.8 3.1 %collective-permute-start.13 = (f32[9,64,128]{2,1,0:T(8,128)S(1)}, f32[9,64,128]{2,1,0:T(8,128)S(1)}, u32[]{:S(2)}, u32[]{:S(2)}) collective-permute-start(f32[9,64,128]{2,1,0:T(8,128)S(1)} %multiply_add_fusion.9), channel_id=1, source_target_pairs={{2,0},{4,2},{6,4},{8,6},{10,8},{12,10},{14,12},{16,14},{18,16},{20... | collective-permute-start | bytes 884744 | tf_op jit(solution)/shard_map/ppermute | solution.py:279
  103.4 6.2 %collective-permute-done.13 = f32[9,64,128]{2,1,0:T(8,128)S(1)} collective-permute-done((f32[9,64,128]{2,1,0:T(8,128)S(1)}, f32[9,64,128]{2,1,0:T(8,128)S(1)}, u32[]{:S(2)}, u32[]{:S(2)}) %collective-permute-start.13) | collective-permute-done | bytes 294944 | tf_op jit(solution)/shard_map/ppermute | solution.py:279
  112.5 3.0 %collective-permute-start.15 = (f32[5,64,128]{2,1,0:T(8,128)S(1)}, f32[5,64,128]{2,1,0:T(8,128)S(1)}, u32[]{:S(2)}, u32[]{:S(2)}) collective-permute-start(f32[5,64,128]{2,1,0:T(8,128)S(1)} %get-tuple-element.78), channel_id=1, source_target_pairs={{0,64},{2,66},{4,68},{6,70},{8,72},{10,74},{12,76},{14,78},{16,80}... | collective-permute-start | bytes 491528 | tf_op jit(solution)/shard_map/ppermute | solution.py:278
  121.3 3.0 %collective-permute-done.20 = f32[5,64,128]{2,1,0:T(8,128)S(1)} collective-permute-done((f32[5,64,128]{2,1,0:T(8,128)S(1)}, f32[5,64,128]{2,1,0:T(8,128)S(1)}, u32[]{:S(2)}, u32[]{:S(2)}) %collective-permute-start.20) | collective-permute-done | bytes 163872 | tf_op jit(solution)/shard_map/ppermute | solution.py:279
  126.9 4.6 %collective-permute-start.16 = (f32[5,64,128]{2,1,0:T(8,128)S(1)}, f32[5,64,128]{2,1,0:T(8,128)S(1)}, u32[]{:S(2)}, u32[]{:S(2)}) collective-permute-start(f32[5,64,128]{2,1,0:T(8,128)S(1)} %get-tuple-element.76), channel_id=1, source_target_pairs={{0,32},{2,34},{4,36},{6,38},{8,40},{10,42},{12,44},{14,46},{16,48}... | collective-permute-start | bytes 491528 | tf_op jit(solution)/shard_map/ppermute | solution.py:278
  134.3 5.7 %collective-permute-start.17 = (f32[5,64,128]{2,1,0:T(8,128)S(1)}, f32[5,64,128]{2,1,0:T(8,128)S(1)}, u32[]{:S(2)}, u32[]{:S(2)}) collective-permute-start(f32[5,64,128]{2,1,0:T(8,128)S(1)} %multiply_add_fusion.30), channel_id=1, source_target_pairs={{0,16},{2,18},{4,20},{6,22},{8,24},{10,26},{12,28},{14,30},{16,32}... | collective-permute-start | bytes 491528 | tf_op jit(solution)/shard_map/ppermute | solution.py:278
  140.0 2.3 %collective-permute-done.22 = f32[5,64,128]{2,1,0:T(8,128)S(1)} collective-permute-done((f32[5,64,128]{2,1,0:T(8,128)S(1)}, f32[5,64,128]{2,1,0:T(8,128)S(1)}, u32[]{:S(2)}, u32[]{:S(2)}) %collective-permute-start.22) | collective-permute-done | bytes 163872 | tf_op jit(solution)/shard_map/ppermute | solution.py:279
  144.7 5.8 %collective-permute-start.18 = (f32[5,64,128]{2,1,0:T(8,128)S(1)}, f32[5,64,128]{2,1,0:T(8,128)S(1)}, u32[]{:S(2)}, u32[]{:S(2)}) collective-permute-start(f32[5,64,128]{2,1,0:T(8,128)S(1)} %multiply_add_fusion.29), channel_id=1, source_target_pairs={{0,8},{2,10},{4,12},{6,14},{8,16},{10,18},{12,20},{14,22},{16,24},... | collective-permute-start | bytes 491528 | tf_op jit(solution)/shard_map/ppermute | solution.py:278
  153.9 8.4 %collective-permute-start.19 = (f32[5,64,128]{2,1,0:T(8,128)S(1)}, f32[5,64,128]{2,1,0:T(8,128)S(1)}, u32[]{:S(2)}, u32[]{:S(2)}) collective-permute-start(f32[5,64,128]{2,1,0:T(8,128)S(1)} %multiply_add_fusion.28), channel_id=1, source_target_pairs={{0,4},{2,6},{4,8},{6,10},{8,12},{10,14},{12,16},{14,18},{16,20},{1... | collective-permute-start | bytes 491528 | tf_op jit(solution)/shard_map/ppermute | solution.py:278
  165.2 5.8 %collective-permute-start.25 = (f32[5,64,128]{2,1,0:T(8,128)S(1)}, f32[5,64,128]{2,1,0:T(8,128)S(1)}, u32[]{:S(2)}, u32[]{:S(2)}) collective-permute-start(f32[5,64,128]{2,1,0:T(8,128)S(1)} %multiply_add_fusion.27), channel_id=1, source_target_pairs={{0,2},{2,4},{4,6},{6,8},{8,10},{10,12},{12,14},{14,16},{16,18},{18... | collective-permute-start | bytes 491528 | tf_op jit(solution)/shard_map/ppermute | solution.py:278
  174.3 9.4 %collective-permute-done.26 = f32[5,64,128]{2,1,0:T(8,128)S(1)} collective-permute-done((f32[5,64,128]{2,1,0:T(8,128)S(1)}, f32[5,64,128]{2,1,0:T(8,128)S(1)}, u32[]{:S(2)}, u32[]{:S(2)}) %collective-permute-start.26) | collective-permute-done | bytes 163872 | tf_op jit(solution)/shard_map/ppermute | solution.py:279
  (183 shorter events, 60.4 us)
Async XLA Ops:
  3.0 15.3 %collective-permute-start = (f32[5,3,64,128]{3,2,1,0:T(8,128)}, f32[5,3,64,128]{3,2,1,0:T(8,128)S(1)}, u32[]{:S(2)}, u32[]{:S(2)}) collective-permute-start(f32[5,3,64,128]{3,2,1,0:T(8,128)} %get-tuple-element.65), channel_id=1, source_target_pairs={{0,2},{2,4},{4,6},{6,8},{8,10},{10,12},{12,14},{14,16},{16,18},{18... | collective-permute-start | bytes 1474568 | tf_op jit(solution)/shard_map/ppermute | solution.py:301
  6.4 19.0 %collective-permute-start.1 = (f32[5,3,64,128]{3,2,1,0:T(8,128)}, f32[5,3,64,128]{3,2,1,0:T(8,128)S(1)}, u32[]{:S(2)}, u32[]{:S(2)}) collective-permute-start(f32[5,3,64,128]{3,2,1,0:T(8,128)} %get-tuple-element.66), channel_id=1, source_target_pairs={{2,0},{4,2},{6,4},{8,6},{10,8},{12,10},{14,12},{16,14},{18,16},{20... | collective-permute-start | bytes 1474568 | tf_op jit(solution)/shard_map/ppermute | solution.py:302
  27.3 12.5 %collective-permute-start.7 = (f32[9,64,128]{2,1,0:T(8,128)S(1)}, f32[9,64,128]{2,1,0:T(8,128)S(1)}, u32[]{:S(2)}, u32[]{:S(2)}) collective-permute-start(f32[9,64,128]{2,1,0:T(8,128)S(1)} %pad_maximum_fusion.8), channel_id=1, source_target_pairs={{64,0},{66,2},{68,4},{70,6},{72,8},{74,10},{76,12},{78,14},{80,16}... | collective-permute-start | bytes 884744 | tf_op jit(solution)/shard_map/ppermute | solution.py:279
  28.7 12.5 %collective-permute-start.2 = (f32[9,64,128]{2,1,0:T(8,128)S(1)}, f32[9,64,128]{2,1,0:T(8,128)S(1)}, u32[]{:S(2)}, u32[]{:S(2)}) collective-permute-start(f32[9,64,128]{2,1,0:T(8,128)S(1)} %pad_maximum_fusion.7), channel_id=1, source_target_pairs={{0,64},{2,66},{4,68},{6,70},{8,72},{10,74},{12,76},{14,78},{16,80}... | collective-permute-start | bytes 884744 | tf_op jit(solution)/shard_map/ppermute | solution.py:278
  34.7 65.2 %collective-permute-start.14 = (f32[4,12,64,128]{3,2,1,0:T(8,128)S(1)}, f32[4,12,64,128]{3,2,1,0:T(8,128)S(1)}, u32[]{:S(2)}, u32[]{:S(2)}) collective-permute-start(f32[4,12,64,128]{3,2,1,0:T(8,128)S(1)} %fusion.1), channel_id=1, source_target_pairs={{0,1},{1,0},{2,3},{3,2},{4,5},{5,4},{6,7},{7,6},{8,9},{9,8},{10,11... | collective-permute-start | bytes 4718600 | tf_op jit(solution)/shard_map/ppermute | solution.py:314
  39.9 11.5 %collective-permute-start.8 = (f32[9,64,128]{2,1,0:T(8,128)S(1)}, f32[9,64,128]{2,1,0:T(8,128)S(1)}, u32[]{:S(2)}, u32[]{:S(2)}) collective-permute-start(f32[9,64,128]{2,1,0:T(8,128)S(1)} %multiply_add_fusion.13), channel_id=1, source_target_pairs={{32,0},{34,2},{36,4},{38,6},{40,8},{42,10},{44,12},{46,14},{48,16}... | collective-permute-start | bytes 884744 | tf_op jit(solution)/shard_map/ppermute | solution.py:279
  41.3 12.1 %collective-permute-start.3 = (f32[9,64,128]{2,1,0:T(8,128)S(1)}, f32[9,64,128]{2,1,0:T(8,128)S(1)}, u32[]{:S(2)}, u32[]{:S(2)}) collective-permute-start(f32[9,64,128]{2,1,0:T(8,128)S(1)} %multiply_add_fusion.18), channel_id=1, source_target_pairs={{0,32},{2,34},{4,36},{6,38},{8,40},{10,42},{12,44},{14,46},{16,48}... | collective-permute-start | bytes 884744 | tf_op jit(solution)/shard_map/ppermute | solution.py:278
  51.5 14.2 %collective-permute-start.9 = (f32[9,64,128]{2,1,0:T(8,128)S(1)}, f32[9,64,128]{2,1,0:T(8,128)S(1)}, u32[]{:S(2)}, u32[]{:S(2)}) collective-permute-start(f32[9,64,128]{2,1,0:T(8,128)S(1)} %multiply_add_fusion.12), channel_id=1, source_target_pairs={{16,0},{18,2},{20,4},{22,6},{24,8},{26,10},{28,12},{30,14},{32,16}... | collective-permute-start | bytes 884744 | tf_op jit(solution)/shard_map/ppermute | solution.py:279
  53.5 14.2 %collective-permute-start.4 = (f32[9,64,128]{2,1,0:T(8,128)S(1)}, f32[9,64,128]{2,1,0:T(8,128)S(1)}, u32[]{:S(2)}, u32[]{:S(2)}) collective-permute-start(f32[9,64,128]{2,1,0:T(8,128)S(1)} %multiply_add_fusion.17), channel_id=1, source_target_pairs={{0,16},{2,18},{4,20},{6,22},{8,24},{10,26},{12,28},{14,30},{16,32}... | collective-permute-start | bytes 884744 | tf_op jit(solution)/shard_map/ppermute | solution.py:278
  65.8 11.6 %collective-permute-start.10 = (f32[9,64,128]{2,1,0:T(8,128)S(1)}, f32[9,64,128]{2,1,0:T(8,128)S(1)}, u32[]{:S(2)}, u32[]{:S(2)}) collective-permute-start(f32[9,64,128]{2,1,0:T(8,128)S(1)} %multiply_add_fusion.11), channel_id=1, source_target_pairs={{8,0},{10,2},{12,4},{14,6},{16,8},{18,10},{20,12},{22,14},{24,16},... | collective-permute-start | bytes 884744 | tf_op jit(solution)/shard_map/ppermute | solution.py:279
  67.8 11.6 %collective-permute-start.5 = (f32[9,64,128]{2,1,0:T(8,128)S(1)}, f32[9,64,128]{2,1,0:T(8,128)S(1)}, u32[]{:S(2)}, u32[]{:S(2)}) collective-permute-start(f32[9,64,128]{2,1,0:T(8,128)S(1)} %multiply_add_fusion.16), channel_id=1, source_target_pairs={{0,8},{2,10},{4,12},{6,14},{8,16},{10,18},{12,20},{14,22},{16,24},... | collective-permute-start | bytes 884744 | tf_op jit(solution)/shard_map/ppermute | solution.py:278
  77.4 16.2 %collective-permute-start.11 = (f32[9,64,128]{2,1,0:T(8,128)S(1)}, f32[9,64,128]{2,1,0:T(8,128)S(1)}, u32[]{:S(2)}, u32[]{:S(2)}) collective-permute-start(f32[9,64,128]{2,1,0:T(8,128)S(1)} %multiply_add_fusion.10), channel_id=1, source_target_pairs={{4,0},{6,2},{8,4},{10,6},{12,8},{14,10},{16,12},{18,14},{20,16},{2... | collective-permute-start | bytes 884744 | tf_op jit(solution)/shard_map/ppermute | solution.py:279
  79.5 14.3 %collective-permute-start.6 = (f32[9,64,128]{2,1,0:T(8,128)S(1)}, f32[9,64,128]{2,1,0:T(8,128)S(1)}, u32[]{:S(2)}, u32[]{:S(2)}) collective-permute-start(f32[9,64,128]{2,1,0:T(8,128)S(1)} %multiply_add_fusion.15), channel_id=1, source_target_pairs={{0,4},{2,6},{4,8},{6,10},{8,12},{10,14},{12,16},{14,18},{16,20},{1... | collective-permute-start | bytes 884744 | tf_op jit(solution)/shard_map/ppermute | solution.py:278
  93.9 9.4 %collective-permute-start.12 = (f32[9,64,128]{2,1,0:T(8,128)S(1)}, f32[9,64,128]{2,1,0:T(8,128)S(1)}, u32[]{:S(2)}, u32[]{:S(2)}) collective-permute-start(f32[9,64,128]{2,1,0:T(8,128)S(1)} %multiply_add_fusion.14), channel_id=1, source_target_pairs={{0,2},{2,4},{4,6},{6,8},{8,10},{10,12},{12,14},{14,16},{16,18},{18... | collective-permute-start | bytes 884744 | tf_op jit(solution)/shard_map/ppermute | solution.py:278
  96.8 12.8 %collective-permute-start.13 = (f32[9,64,128]{2,1,0:T(8,128)S(1)}, f32[9,64,128]{2,1,0:T(8,128)S(1)}, u32[]{:S(2)}, u32[]{:S(2)}) collective-permute-start(f32[9,64,128]{2,1,0:T(8,128)S(1)} %multiply_add_fusion.9), channel_id=1, source_target_pairs={{2,0},{4,2},{6,4},{8,6},{10,8},{12,10},{14,12},{16,14},{18,16},{20... | collective-permute-start | bytes 884744 | tf_op jit(solution)/shard_map/ppermute | solution.py:279
  117.7 66.1 %collective-permute-start.27 = (f32[5,8,64,128]{3,2,1,0:T(8,128)S(1)}, f32[5,8,64,128]{3,2,1,0:T(8,128)S(1)}, u32[]{:S(2)}, u32[]{:S(2)}) collective-permute-start(f32[5,8,64,128]{3,2,1,0:T(8,128)S(1)} %fusion.34), channel_id=1, source_target_pairs={{0,1},{1,0},{2,3},{3,2},{4,5},{5,4},{6,7},{7,6},{8,9},{9,8},{10,11... | collective-permute-start | bytes 3932168 | tf_op jit(solution)/shard_map/ppermute | solution.py:314
  131.7 10.7 %collective-permute-start.22 = (f32[5,64,128]{2,1,0:T(8,128)S(1)}, f32[5,64,128]{2,1,0:T(8,128)S(1)}, u32[]{:S(2)}, u32[]{:S(2)}) collective-permute-start(f32[5,64,128]{2,1,0:T(8,128)S(1)} %multiply_add_fusion.25), channel_id=1, source_target_pairs={{16,0},{18,2},{20,4},{22,6},{24,8},{26,10},{28,12},{30,14},{32,16}... | collective-permute-start | bytes 491528 | tf_op jit(solution)/shard_map/ppermute | solution.py:279
  134.3 10.3 %collective-permute-start.17 = (f32[5,64,128]{2,1,0:T(8,128)S(1)}, f32[5,64,128]{2,1,0:T(8,128)S(1)}, u32[]{:S(2)}, u32[]{:S(2)}) collective-permute-start(f32[5,64,128]{2,1,0:T(8,128)S(1)} %multiply_add_fusion.30), channel_id=1, source_target_pairs={{0,16},{2,18},{4,20},{6,22},{8,24},{10,26},{12,28},{14,30},{16,32}... | collective-permute-start | bytes 491528 | tf_op jit(solution)/shard_map/ppermute | solution.py:278
  142.4 9.3 %collective-permute-start.23 = (f32[5,64,128]{2,1,0:T(8,128)S(1)}, f32[5,64,128]{2,1,0:T(8,128)S(1)}, u32[]{:S(2)}, u32[]{:S(2)}) collective-permute-start(f32[5,64,128]{2,1,0:T(8,128)S(1)} %multiply_add_fusion.24), channel_id=1, source_target_pairs={{8,0},{10,2},{12,4},{14,6},{16,8},{18,10},{20,12},{22,14},{24,16},... | collective-permute-start | bytes 491528 | tf_op jit(solution)/shard_map/ppermute | solution.py:279
  144.7 9.0 %collective-permute-start.18 = (f32[5,64,128]{2,1,0:T(8,128)S(1)}, f32[5,64,128]{2,1,0:T(8,128)S(1)}, u32[]{:S(2)}, u32[]{:S(2)}) collective-permute-start(f32[5,64,128]{2,1,0:T(8,128)S(1)} %multiply_add_fusion.29), channel_id=1, source_target_pairs={{0,8},{2,10},{4,12},{6,14},{8,16},{10,18},{12,20},{14,22},{16,24},... | collective-permute-start | bytes 491528 | tf_op jit(solution)/shard_map/ppermute | solution.py:278
  151.9 11.7 %collective-permute-start.24 = (f32[5,64,128]{2,1,0:T(8,128)S(1)}, f32[5,64,128]{2,1,0:T(8,128)S(1)}, u32[]{:S(2)}, u32[]{:S(2)}) collective-permute-start(f32[5,64,128]{2,1,0:T(8,128)S(1)} %multiply_add_fusion.23), channel_id=1, source_target_pairs={{4,0},{6,2},{8,4},{10,6},{12,8},{14,10},{16,12},{18,14},{20,16},{2... | collective-permute-start | bytes 491528 | tf_op jit(solution)/shard_map/ppermute | solution.py:279
  153.9 11.3 %collective-permute-start.19 = (f32[5,64,128]{2,1,0:T(8,128)S(1)}, f32[5,64,128]{2,1,0:T(8,128)S(1)}, u32[]{:S(2)}, u32[]{:S(2)}) collective-permute-start(f32[5,64,128]{2,1,0:T(8,128)S(1)} %multiply_add_fusion.28), channel_id=1, source_target_pairs={{0,4},{2,6},{4,8},{6,10},{8,12},{10,14},{12,16},{14,18},{16,20},{1... | collective-permute-start | bytes 491528 | tf_op jit(solution)/shard_map/ppermute | solution.py:278
  165.2 9.0 %collective-permute-start.25 = (f32[5,64,128]{2,1,0:T(8,128)S(1)}, f32[5,64,128]{2,1,0:T(8,128)S(1)}, u32[]{:S(2)}, u32[]{:S(2)}) collective-permute-start(f32[5,64,128]{2,1,0:T(8,128)S(1)} %multiply_add_fusion.27), channel_id=1, source_target_pairs={{0,2},{2,4},{4,6},{6,8},{8,10},{10,12},{12,14},{14,16},{16,18},{18... | collective-permute-start | bytes 491528 | tf_op jit(solution)/shard_map/ppermute | solution.py:278
  172.3 11.4 %collective-permute-start.26 = (f32[5,64,128]{2,1,0:T(8,128)S(1)}, f32[5,64,128]{2,1,0:T(8,128)S(1)}, u32[]{:S(2)}, u32[]{:S(2)}) collective-permute-start(f32[5,64,128]{2,1,0:T(8,128)S(1)} %multiply_add_fusion.22), channel_id=1, source_target_pairs={{2,0},{4,2},{6,4},{8,6},{10,8},{12,10},{14,12},{16,14},{18,16},{20... | collective-permute-start | bytes 491528 | tf_op jit(solution)/shard_map/ppermute | solution.py:279
  (33 other events, 135.8 us)

commit v18 on v12

--- a/solution.py
+++ b/solution.py
@@ -178,7 +178,8 @@
         radix = min(2, -(-blocks // stride))
         rounds.append((stride, list(range(1, radix))))
         stride *= radix
-    return rounds[::-1]
+    longest_first = rounds[::-1]
+    return longest_first[0::2] + longest_first[1::2]
 
 
 def scan_coefs(rise_step, fall_step, shift):

time: 186 us -> 183 us (0.984)
  waiting for transfers between devices: 65.1 us -> 61.6 us
    ppermute x12, waiting for transfers between devices: 51.1 us -> 43.8 us  [wall_apply(): from_above = lax.ppermute(fall, 'gy', down_pairs)]
    ppermute x12, starting transfers between devices: 22.2 us -> 26.8 us  [wall_apply(): from_above = lax.ppermute(fall, 'gy', down_pairs)]
    ppermute x12, starting transfers between devices: 50.8 us -> 46.7 us  [wall_apply(): from_below = lax.ppermute(rise, 'gy', up_pairs)]
    ppermute x12, waiting for transfers between devices: 8.67 us -> 12.4 us  [wall_apply(): from_below = lax.ppermute(rise, 'gy', up_pairs)]
  transfers between devices with their start and end apart: 28 -> 28, of which waited for: 16 -> 16; matrix products, arithmetic and copies ran while one was open for 13% -> 14% of each run, Pallas kernels for 0% -> 0%
where the time goes in v18:
time: 183 us; the launch traced here: 182 us
  starting transfers between devices  79.5 us (43%)
  waiting for transfers between devices  61.6 us (34%)
  other arithmetic  14.7 us (8%)
  local copies, waits for them, and re-layouts  13.8 us (8%)
  matrix products  9.91 us (5%)
  between operations  2.07 us (1%)
    ppermute x12, starting transfers between devices, wall_apply(): from_below = lax.ppermute(rise, 'gy', up_pairs)  46.7 us
    ppermute x12, waiting for transfers between devices, wall_apply(): from_above = lax.ppermute(fall, 'gy', down_pairs)  43.8 us
    ppermute x12, starting transfers between devices, wall_apply(): from_above = lax.ppermute(fall, 'gy', down_pairs)  26.8 us
    ppermute x12, waiting for transfers between devices, wall_apply(): from_below = lax.ppermute(rise, 'gy', up_pairs)  12.4 us
    ppermute x1, waiting for transfers between devices, halo(): above = lax.ppermute(block[:, :width], 'gy', down_pairs)  5.32 us
    add x2, other arithmetic, wall_apply(): local + rise_gain[None, :, None, None] * rise[first:first + size, None]  4.9 us
    dot_general x2, matrix products, span_slope(): jnp.einsum('fyzx,zw->fywx', other, other_block, precision=HIGHEST)  4.4 us
  transfers between devices with their start and end apart: 28, of which 16 were waited for; matrix products, arithmetic and copies ran while one was open for 14% of the time, Pallas kernels for 0%

profile of v18, /device:TPU:30, one launch (start us, length us, event | category | flops | bytes accessed | tf_op | source)
XLA Modules:
  0.0 181.6 jit_solution(1716989937842888159)
XLA Ops:
  3.0 3.4 %collective-permute-start = (f32[5,3,64,128]{3,2,1,0:T(8,128)}, f32[5,3,64,128]{3,2,1,0:T(8,128)S(1)}, u32[]{:S(2)}, u32[]{:S(2)}) collective-permute-start(f32[5,3,64,128]{3,2,1,0:T(8,128)} %get-tuple-element.51), channel_id=1, source_target_pairs={{0,2},{2,4},{4,6},{6,8},{8,10},{10,12},{12,14},{14,16},{16,18},{18... | collective-permute-start | bytes 1474568 | tf_op jit(solution)/shard_map/ppermute | solution.py:297
  20.1 5.3 %collective-permute-done.1 = f32[5,3,64,128]{3,2,1,0:T(8,128)S(1)} collective-permute-done((f32[5,3,64,128]{3,2,1,0:T(8,128)}, f32[5,3,64,128]{3,2,1,0:T(8,128)S(1)}, u32[]{:S(2)}, u32[]{:S(2)}) %collective-permute-start.1) | collective-permute-done | bytes 491552 | tf_op jit(solution)/shard_map/ppermute | solution.py:298
  28.0 5.5 %collective-permute-start.2 = (f32[9,64,128]{2,1,0:T(8,128)S(1)}, f32[9,64,128]{2,1,0:T(8,128)S(1)}, u32[]{:S(2)}, u32[]{:S(2)}) collective-permute-start(f32[9,64,128]{2,1,0:T(8,128)S(1)} %pad_maximum_fusion.7), channel_id=1, source_target_pairs={{0,64},{2,66},{4,68},{6,70},{8,72},{10,74},{12,76},{14,78},{16,80}... | collective-permute-start | bytes 884744 | tf_op jit(solution)/shard_map/ppermute | solution.py:273
  40.6 3.6 %collective-permute-done.8 = f32[9,64,128]{2,1,0:T(8,128)S(1)} collective-permute-done((f32[9,64,128]{2,1,0:T(8,128)S(1)}, f32[9,64,128]{2,1,0:T(8,128)S(1)}, u32[]{:S(2)}, u32[]{:S(2)}) %collective-permute-start.8) | collective-permute-done | bytes 294944 | tf_op jit(solution)/shard_map/ppermute | solution.py:274
  46.4 2.9 %collective-permute-done.3 = f32[9,64,128]{2,1,0:T(8,128)S(1)} collective-permute-done((f32[9,64,128]{2,1,0:T(8,128)S(1)}, f32[9,64,128]{2,1,0:T(8,128)S(1)}, u32[]{:S(2)}, u32[]{:S(2)}) %collective-permute-start.3) | collective-permute-done | bytes 294944 | tf_op jit(solution)/shard_map/ppermute | solution.py:273
  51.6 3.8 %collective-permute-done.9 = f32[9,64,128]{2,1,0:T(8,128)S(1)} collective-permute-done((f32[9,64,128]{2,1,0:T(8,128)S(1)}, f32[9,64,128]{2,1,0:T(8,128)S(1)}, u32[]{:S(2)}, u32[]{:S(2)}) %collective-permute-start.9) | collective-permute-done | bytes 294944 | tf_op jit(solution)/shard_map/ppermute | solution.py:274
  57.5 3.7 %collective-permute-done.4 = f32[9,64,128]{2,1,0:T(8,128)S(1)} collective-permute-done((f32[9,64,128]{2,1,0:T(8,128)S(1)}, f32[9,64,128]{2,1,0:T(8,128)S(1)}, u32[]{:S(2)}, u32[]{:S(2)}) %collective-permute-start.4) | collective-permute-done | bytes 294944 | tf_op jit(solution)/shard_map/ppermute | solution.py:273
  63.3 5.3 %collective-permute-done.10 = f32[9,64,128]{2,1,0:T(8,128)S(1)} collective-permute-done((f32[9,64,128]{2,1,0:T(8,128)S(1)}, f32[9,64,128]{2,1,0:T(8,128)S(1)}, u32[]{:S(2)}, u32[]{:S(2)}) %collective-permute-start.10) | collective-permute-done | bytes 294944 | tf_op jit(solution)/shard_map/ppermute | solution.py:274
  70.2 4.3 %collective-permute-start.6 = (f32[9,64,128]{2,1,0:T(8,128)S(1)}, f32[9,64,128]{2,1,0:T(8,128)S(1)}, u32[]{:S(2)}, u32[]{:S(2)}) collective-permute-start(f32[9,64,128]{2,1,0:T(8,128)S(1)} %multiply_add_fusion.12), channel_id=1, source_target_pairs={{0,8},{2,10},{4,12},{6,14},{8,16},{10,18},{12,20},{14,22},{16,24},... | collective-permute-start | bytes 884744 | tf_op jit(solution)/shard_map/ppermute | solution.py:273
  74.5 4.6 %collective-permute-done.11 = f32[9,64,128]{2,1,0:T(8,128)S(1)} collective-permute-done((f32[9,64,128]{2,1,0:T(8,128)S(1)}, f32[9,64,128]{2,1,0:T(8,128)S(1)}, u32[]{:S(2)}, u32[]{:S(2)}) %collective-permute-start.11) | collective-permute-done | bytes 294944 | tf_op jit(solution)/shard_map/ppermute | solution.py:274
  81.3 10.6 %collective-permute-start.7 = (f32[9,64,128]{2,1,0:T(8,128)S(1)}, f32[9,64,128]{2,1,0:T(8,128)S(1)}, u32[]{:S(2)}, u32[]{:S(2)}) collective-permute-start(f32[9,64,128]{2,1,0:T(8,128)S(1)} %multiply_add_fusion.11), channel_id=1, source_target_pairs={{0,2},{2,4},{4,6},{6,8},{8,10},{10,12},{12,14},{14,16},{16,18},{18... | collective-permute-start | bytes 884744 | tf_op jit(solution)/shard_map/ppermute | solution.py:273
  92.0 3.4 %collective-permute-start.13 = (f32[9,64,128]{2,1,0:T(8,128)S(1)}, f32[9,64,128]{2,1,0:T(8,128)S(1)}, u32[]{:S(2)}, u32[]{:S(2)}) collective-permute-start(f32[9,64,128]{2,1,0:T(8,128)S(1)} %multiply_add_fusion.5), channel_id=1, source_target_pairs={{2,0},{4,2},{6,4},{8,6},{10,8},{12,10},{14,12},{16,14},{18,16},{20... | collective-permute-start | bytes 884744 | tf_op jit(solution)/shard_map/ppermute | solution.py:274
  98.9 5.9 %collective-permute-done.13 = f32[9,64,128]{2,1,0:T(8,128)S(1)} collective-permute-done((f32[9,64,128]{2,1,0:T(8,128)S(1)}, f32[9,64,128]{2,1,0:T(8,128)S(1)}, u32[]{:S(2)}, u32[]{:S(2)}) %collective-permute-start.13) | collective-permute-done | bytes 294944 | tf_op jit(solution)/shard_map/ppermute | solution.py:274
  109.1 4.4 %collective-permute-start.15 = (f32[5,64,128]{2,1,0:T(8,128)S(1)}, f32[5,64,128]{2,1,0:T(8,128)S(1)}, u32[]{:S(2)}, u32[]{:S(2)}) collective-permute-start(f32[5,64,128]{2,1,0:T(8,128)S(1)} %get-tuple-element.63), channel_id=1, source_target_pairs={{0,64},{2,66},{4,68},{6,70},{8,72},{10,74},{12,76},{14,78},{16,80}... | collective-permute-start | bytes 491528 | tf_op jit(solution)/shard_map/ppermute | solution.py:273
  116.9 2.9 %multiply_add_fusion.1 = f32[5,8,64,128]{3,2,1,0:T(8,128)} fusion(f32[5,64,128]{2,1,0:T(8,128)S(1)} %slice-done.1, f32[8]{0:T(128)S(1)} %copy-done.40, f32[5,64,128]{2,1,0:T(8,128)S(1)} %slice-done, f32[8]{0:T(128)S(1)} %copy-done.39, f32[5,64,128]{2,1,0:T(8,128)S(1)} %get-tuple-element.59, f32[8]{0:T(128)S(1)} %copy-done.26, ...), kind=kLoop, calls=%fused_computation.43 | loop fusion | flops 10158080 | bytes 3932672 | tf_op jit(solution)/shard_map/add | solution.py:285
  125.8 5.4 %collective-permute-start.22 = (f32[5,64,128]{2,1,0:T(8,128)S(1)}, f32[5,64,128]{2,1,0:T(8,128)S(1)}, u32[]{:S(2)}, u32[]{:S(2)}) collective-permute-start(f32[5,64,128]{2,1,0:T(8,128)S(1)} %get-tuple-element.62), channel_id=1, source_target_pairs={{16,0},{18,2},{20,4},{22,6},{24,8},{26,10},{28,12},{30,14},{32,16}... | collective-permute-start | bytes 491528 | tf_op jit(solution)/shard_map/ppermute | solution.py:274
  135.6 3.2 %collective-permute-start.23 = (f32[5,64,128]{2,1,0:T(8,128)S(1)}, f32[5,64,128]{2,1,0:T(8,128)S(1)}, u32[]{:S(2)}, u32[]{:S(2)}) collective-permute-start(f32[5,64,128]{2,1,0:T(8,128)S(1)} %multiply_add_fusion.21), channel_id=1, source_target_pairs={{4,0},{6,2},{8,4},{10,6},{12,8},{14,10},{16,12},{18,14},{20,16},{2... | collective-permute-start | bytes 491528 | tf_op jit(solution)/shard_map/ppermute | solution.py:274
  138.8 2.8 %collective-permute-done.17 = f32[5,64,128]{2,1,0:T(8,128)S(1)} collective-permute-done((f32[5,64,128]{2,1,0:T(8,128)S(1)}, f32[5,64,128]{2,1,0:T(8,128)S(1)}, u32[]{:S(2)}, u32[]{:S(2)}) %collective-permute-start.17) | collective-permute-done | bytes 163872 | tf_op jit(solution)/shard_map/ppermute | solution.py:273
  143.0 4.3 %collective-permute-done.23 = f32[5,64,128]{2,1,0:T(8,128)S(1)} collective-permute-done((f32[5,64,128]{2,1,0:T(8,128)S(1)}, f32[5,64,128]{2,1,0:T(8,128)S(1)}, u32[]{:S(2)}, u32[]{:S(2)}) %collective-permute-start.23) | collective-permute-done | bytes 163872 | tf_op jit(solution)/shard_map/ppermute | solution.py:274
  148.9 2.7 %collective-permute-start.19 = (f32[5,64,128]{2,1,0:T(8,128)S(1)}, f32[5,64,128]{2,1,0:T(8,128)S(1)}, u32[]{:S(2)}, u32[]{:S(2)}) collective-permute-start(f32[5,64,128]{2,1,0:T(8,128)S(1)} %multiply_add_fusion.25), channel_id=1, source_target_pairs={{0,8},{2,10},{4,12},{6,14},{8,16},{10,18},{12,20},{14,22},{16,24},... | collective-permute-start | bytes 491528 | tf_op jit(solution)/shard_map/ppermute | solution.py:273
  151.6 4.2 %collective-permute-done.24 = f32[5,64,128]{2,1,0:T(8,128)S(1)} collective-permute-done((f32[5,64,128]{2,1,0:T(8,128)S(1)}, f32[5,64,128]{2,1,0:T(8,128)S(1)}, u32[]{:S(2)}, u32[]{:S(2)}) %collective-permute-start.24) | collective-permute-done | bytes 163872 | tf_op jit(solution)/shard_map/ppermute | solution.py:274
  157.9 7.6 %collective-permute-start.20 = (f32[5,64,128]{2,1,0:T(8,128)S(1)}, f32[5,64,128]{2,1,0:T(8,128)S(1)}, u32[]{:S(2)}, u32[]{:S(2)}) collective-permute-start(f32[5,64,128]{2,1,0:T(8,128)S(1)} %multiply_add_fusion.24), channel_id=1, source_target_pairs={{0,2},{2,4},{4,6},{6,8},{8,10},{10,12},{12,14},{14,16},{16,18},{18... | collective-permute-start | bytes 491528 | tf_op jit(solution)/shard_map/ppermute | solution.py:273
  168.5 8.6 %collective-permute-done.26 = f32[5,64,128]{2,1,0:T(8,128)S(1)} collective-permute-done((f32[5,64,128]{2,1,0:T(8,128)S(1)}, f32[5,64,128]{2,1,0:T(8,128)S(1)}, u32[]{:S(2)}, u32[]{:S(2)}) %collective-permute-start.26) | collective-permute-done | bytes 163872 | tf_op jit(solution)/shard_map/ppermute | solution.py:274
  177.4 2.8 %fusion.4 = f32[5,8,64,128]{3,2,1,0:T(8,128)S(1)} fusion(f32[5,8,128,64]{2,3,1,0:T(8,128)S(1)} %fusion.89, f32[5,8,64,128]{3,2,1,0:T(8,128)S(1)} %collective-permute-done.27, f32[64,64,1,1]{0,1,3,2:T(8,128)S(1)} %copy-done.9, f32[5,8,64,128]{3,2,1,0:T(8,128)S(1)} %fusion.88, f32[5,64,128]{2,1,0:T(8,128)S(1)} %multiply_add_fusion.17, f32[8]{0:T(128)S(1)} %copy-done.54, ...), kind=kOutput, calls=%fused_computation.39 | convolution fusion | flops 261816320 | bytes 7553472 | tf_op jit(solution)/shard_map/fyzx,zw->fywx/dot_general | solution.py:311
  (237 shorter events, 68.0 us)
Async XLA Ops:
  3.0 17.1 %collective-permute-start = (f32[5,3,64,128]{3,2,1,0:T(8,128)}, f32[5,3,64,128]{3,2,1,0:T(8,128)S(1)}, u32[]{:S(2)}, u32[]{:S(2)}) collective-permute-start(f32[5,3,64,128]{3,2,1,0:T(8,128)} %get-tuple-element.51), channel_id=1, source_target_pairs={{0,2},{2,4},{4,6},{6,8},{8,10},{10,12},{12,14},{14,16},{16,18},{18... | collective-permute-start | bytes 1474568 | tf_op jit(solution)/shard_map/ppermute | solution.py:297
  6.4 19.0 %collective-permute-start.1 = (f32[5,3,64,128]{3,2,1,0:T(8,128)}, f32[5,3,64,128]{3,2,1,0:T(8,128)S(1)}, u32[]{:S(2)}, u32[]{:S(2)}) collective-permute-start(f32[5,3,64,128]{3,2,1,0:T(8,128)} %get-tuple-element.52), channel_id=1, source_target_pairs={{2,0},{4,2},{6,4},{8,6},{10,8},{12,10},{14,12},{16,14},{18,16},{20... | collective-permute-start | bytes 1474568 | tf_op jit(solution)/shard_map/ppermute | solution.py:298
  28.0 10.6 %collective-permute-start.2 = (f32[9,64,128]{2,1,0:T(8,128)S(1)}, f32[9,64,128]{2,1,0:T(8,128)S(1)}, u32[]{:S(2)}, u32[]{:S(2)}) collective-permute-start(f32[9,64,128]{2,1,0:T(8,128)S(1)} %pad_maximum_fusion.7), channel_id=1, source_target_pairs={{0,64},{2,66},{4,68},{6,70},{8,72},{10,74},{12,76},{14,78},{16,80}... | collective-permute-start | bytes 884744 | tf_op jit(solution)/shard_map/ppermute | solution.py:273
  33.6 10.7 %collective-permute-start.8 = (f32[9,64,128]{2,1,0:T(8,128)S(1)}, f32[9,64,128]{2,1,0:T(8,128)S(1)}, u32[]{:S(2)}, u32[]{:S(2)}) collective-permute-start(f32[9,64,128]{2,1,0:T(8,128)S(1)} %pad_maximum_fusion.8), channel_id=1, source_target_pairs={{64,0},{66,2},{68,4},{70,6},{72,8},{74,10},{76,12},{78,14},{80,16}... | collective-permute-start | bytes 884744 | tf_op jit(solution)/shard_map/ppermute | solution.py:274
  34.9 60.6 %collective-permute-start.14 = (f32[4,12,64,128]{3,2,1,0:T(8,128)S(1)}, f32[4,12,64,128]{3,2,1,0:T(8,128)S(1)}, u32[]{:S(2)}, u32[]{:S(2)}) collective-permute-start(f32[4,12,64,128]{3,2,1,0:T(8,128)S(1)} %fusion.1), channel_id=1, source_target_pairs={{0,1},{1,0},{2,3},{3,2},{4,5},{5,4},{6,7},{7,6},{8,9},{9,8},{10,11... | collective-permute-start | bytes 4718600 | tf_op jit(solution)/shard_map/ppermute | solution.py:310
  38.7 10.6 %collective-permute-start.3 = (f32[9,64,128]{2,1,0:T(8,128)S(1)}, f32[9,64,128]{2,1,0:T(8,128)S(1)}, u32[]{:S(2)}, u32[]{:S(2)}) collective-permute-start(f32[9,64,128]{2,1,0:T(8,128)S(1)} %multiply_add_fusion.15), channel_id=1, source_target_pairs={{0,16},{2,18},{4,20},{6,22},{8,24},{10,26},{12,28},{14,30},{16,32}... | collective-permute-start | bytes 884744 | tf_op jit(solution)/shard_map/ppermute | solution.py:273
  44.4 11.0 %collective-permute-start.9 = (f32[9,64,128]{2,1,0:T(8,128)S(1)}, f32[9,64,128]{2,1,0:T(8,128)S(1)}, u32[]{:S(2)}, u32[]{:S(2)}) collective-permute-start(f32[9,64,128]{2,1,0:T(8,128)S(1)} %multiply_add_fusion.9), channel_id=1, source_target_pairs={{16,0},{18,2},{20,4},{22,6},{24,8},{26,10},{28,12},{30,14},{32,16}... | collective-permute-start | bytes 884744 | tf_op jit(solution)/shard_map/ppermute | solution.py:274
  49.4 11.8 %collective-permute-start.4 = (f32[9,64,128]{2,1,0:T(8,128)S(1)}, f32[9,64,128]{2,1,0:T(8,128)S(1)}, u32[]{:S(2)}, u32[]{:S(2)}) collective-permute-start(f32[9,64,128]{2,1,0:T(8,128)S(1)} %multiply_add_fusion.14), channel_id=1, source_target_pairs={{0,4},{2,6},{4,8},{6,10},{8,12},{10,14},{12,16},{14,18},{16,20},{1... | collective-permute-start | bytes 884744 | tf_op jit(solution)/shard_map/ppermute | solution.py:273
  55.5 13.1 %collective-permute-start.10 = (f32[9,64,128]{2,1,0:T(8,128)S(1)}, f32[9,64,128]{2,1,0:T(8,128)S(1)}, u32[]{:S(2)}, u32[]{:S(2)}) collective-permute-start(f32[9,64,128]{2,1,0:T(8,128)S(1)} %multiply_add_fusion.8), channel_id=1, source_target_pairs={{4,0},{6,2},{8,4},{10,6},{12,8},{14,10},{16,12},{18,14},{20,16},{2... | collective-permute-start | bytes 884744 | tf_op jit(solution)/shard_map/ppermute | solution.py:274
  68.7 10.4 %collective-permute-start.11 = (f32[9,64,128]{2,1,0:T(8,128)S(1)}, f32[9,64,128]{2,1,0:T(8,128)S(1)}, u32[]{:S(2)}, u32[]{:S(2)}) collective-permute-start(f32[9,64,128]{2,1,0:T(8,128)S(1)} %multiply_add_fusion.7), channel_id=1, source_target_pairs={{32,0},{34,2},{36,4},{38,6},{40,8},{42,10},{44,12},{46,14},{48,16}... | collective-permute-start | bytes 884744 | tf_op jit(solution)/shard_map/ppermute | solution.py:274
  70.2 11.0 %collective-permute-start.6 = (f32[9,64,128]{2,1,0:T(8,128)S(1)}, f32[9,64,128]{2,1,0:T(8,128)S(1)}, u32[]{:S(2)}, u32[]{:S(2)}) collective-permute-start(f32[9,64,128]{2,1,0:T(8,128)S(1)} %multiply_add_fusion.12), channel_id=1, source_target_pairs={{0,8},{2,10},{4,12},{6,14},{8,16},{10,18},{12,20},{14,22},{16,24},... | collective-permute-start | bytes 884744 | tf_op jit(solution)/shard_map/ppermute | solution.py:273
  79.2 12.7 %collective-permute-start.12 = (f32[9,64,128]{2,1,0:T(8,128)S(1)}, f32[9,64,128]{2,1,0:T(8,128)S(1)}, u32[]{:S(2)}, u32[]{:S(2)}) collective-permute-start(f32[9,64,128]{2,1,0:T(8,128)S(1)} %multiply_add_fusion.6), channel_id=1, source_target_pairs={{8,0},{10,2},{12,4},{14,6},{16,8},{18,10},{20,12},{22,14},{24,16},... | collective-permute-start | bytes 884744 | tf_op jit(solution)/shard_map/ppermute | solution.py:274
  81.3 17.5 %collective-permute-start.7 = (f32[9,64,128]{2,1,0:T(8,128)S(1)}, f32[9,64,128]{2,1,0:T(8,128)S(1)}, u32[]{:S(2)}, u32[]{:S(2)}) collective-permute-start(f32[9,64,128]{2,1,0:T(8,128)S(1)} %multiply_add_fusion.11), channel_id=1, source_target_pairs={{0,2},{2,4},{4,6},{6,8},{8,10},{10,12},{12,14},{14,16},{16,18},{18... | collective-permute-start | bytes 884744 | tf_op jit(solution)/shard_map/ppermute | solution.py:273
  92.0 12.8 %collective-permute-start.13 = (f32[9,64,128]{2,1,0:T(8,128)S(1)}, f32[9,64,128]{2,1,0:T(8,128)S(1)}, u32[]{:S(2)}, u32[]{:S(2)}) collective-permute-start(f32[9,64,128]{2,1,0:T(8,128)S(1)} %multiply_add_fusion.5), channel_id=1, source_target_pairs={{2,0},{4,2},{6,4},{8,6},{10,8},{12,10},{14,12},{16,14},{18,16},{20... | collective-permute-start | bytes 884744 | tf_op jit(solution)/shard_map/ppermute | solution.py:274
  109.1 11.9 %collective-permute-start.15 = (f32[5,64,128]{2,1,0:T(8,128)S(1)}, f32[5,64,128]{2,1,0:T(8,128)S(1)}, u32[]{:S(2)}, u32[]{:S(2)}) collective-permute-start(f32[5,64,128]{2,1,0:T(8,128)S(1)} %get-tuple-element.63), channel_id=1, source_target_pairs={{0,64},{2,66},{4,68},{6,70},{8,72},{10,74},{12,76},{14,78},{16,80}... | collective-permute-start | bytes 491528 | tf_op jit(solution)/shard_map/ppermute | solution.py:273
  115.7 61.5 %collective-permute-start.27 = (f32[5,8,64,128]{3,2,1,0:T(8,128)S(1)}, f32[5,8,64,128]{3,2,1,0:T(8,128)S(1)}, u32[]{:S(2)}, u32[]{:S(2)}) collective-permute-start(f32[5,8,64,128]{3,2,1,0:T(8,128)S(1)} %fusion.34), channel_id=1, source_target_pairs={{0,1},{1,0},{2,3},{3,2},{4,5},{5,4},{6,7},{7,6},{8,9},{9,8},{10,11... | collective-permute-start | bytes 3932168 | tf_op jit(solution)/shard_map/ppermute | solution.py:310
  122.3 8.9 %collective-permute-start.16 = (f32[5,64,128]{2,1,0:T(8,128)S(1)}, f32[5,64,128]{2,1,0:T(8,128)S(1)}, u32[]{:S(2)}, u32[]{:S(2)}) collective-permute-start(f32[5,64,128]{2,1,0:T(8,128)S(1)} %get-tuple-element.61), channel_id=1, source_target_pairs={{0,16},{2,18},{4,20},{6,22},{8,24},{10,26},{12,28},{14,30},{16,32}... | collective-permute-start | bytes 491528 | tf_op jit(solution)/shard_map/ppermute | solution.py:273
  125.8 9.7 %collective-permute-start.22 = (f32[5,64,128]{2,1,0:T(8,128)S(1)}, f32[5,64,128]{2,1,0:T(8,128)S(1)}, u32[]{:S(2)}, u32[]{:S(2)}) collective-permute-start(f32[5,64,128]{2,1,0:T(8,128)S(1)} %get-tuple-element.62), channel_id=1, source_target_pairs={{16,0},{18,2},{20,4},{22,6},{24,8},{26,10},{28,12},{30,14},{32,16}... | collective-permute-start | bytes 491528 | tf_op jit(solution)/shard_map/ppermute | solution.py:274
  131.4 10.3 %collective-permute-start.17 = (f32[5,64,128]{2,1,0:T(8,128)S(1)}, f32[5,64,128]{2,1,0:T(8,128)S(1)}, u32[]{:S(2)}, u32[]{:S(2)}) collective-permute-start(f32[5,64,128]{2,1,0:T(8,128)S(1)} %multiply_add_fusion.27), channel_id=1, source_target_pairs={{0,4},{2,6},{4,8},{6,10},{8,12},{10,14},{12,16},{14,18},{16,20},{1... | collective-permute-start | bytes 491528 | tf_op jit(solution)/shard_map/ppermute | solution.py:273
  135.6 11.7 %collective-permute-start.23 = (f32[5,64,128]{2,1,0:T(8,128)S(1)}, f32[5,64,128]{2,1,0:T(8,128)S(1)}, u32[]{:S(2)}, u32[]{:S(2)}) collective-permute-start(f32[5,64,128]{2,1,0:T(8,128)S(1)} %multiply_add_fusion.21), channel_id=1, source_target_pairs={{4,0},{6,2},{8,4},{10,6},{12,8},{14,10},{16,12},{18,14},{20,16},{2... | collective-permute-start | bytes 491528 | tf_op jit(solution)/shard_map/ppermute | solution.py:274
  148.9 8.9 %collective-permute-start.19 = (f32[5,64,128]{2,1,0:T(8,128)S(1)}, f32[5,64,128]{2,1,0:T(8,128)S(1)}, u32[]{:S(2)}, u32[]{:S(2)}) collective-permute-start(f32[5,64,128]{2,1,0:T(8,128)S(1)} %multiply_add_fusion.25), channel_id=1, source_target_pairs={{0,8},{2,10},{4,12},{6,14},{8,16},{10,18},{12,20},{14,22},{16,24},... | collective-permute-start | bytes 491528 | tf_op jit(solution)/shard_map/ppermute | solution.py:273
  155.9 9.7 %collective-permute-start.25 = (f32[5,64,128]{2,1,0:T(8,128)S(1)}, f32[5,64,128]{2,1,0:T(8,128)S(1)}, u32[]{:S(2)}, u32[]{:S(2)}) collective-permute-start(f32[5,64,128]{2,1,0:T(8,128)S(1)} %multiply_add_fusion.19), channel_id=1, source_target_pairs={{8,0},{10,2},{12,4},{14,6},{16,8},{18,10},{20,12},{22,14},{24,16},... | collective-permute-start | bytes 491528 | tf_op jit(solution)/shard_map/ppermute | solution.py:274
  157.9 10.5 %collective-permute-start.20 = (f32[5,64,128]{2,1,0:T(8,128)S(1)}, f32[5,64,128]{2,1,0:T(8,128)S(1)}, u32[]{:S(2)}, u32[]{:S(2)}) collective-permute-start(f32[5,64,128]{2,1,0:T(8,128)S(1)} %multiply_add_fusion.24), channel_id=1, source_target_pairs={{0,2},{2,4},{4,6},{6,8},{8,10},{10,12},{12,14},{14,16},{16,18},{18... | collective-permute-start | bytes 491528 | tf_op jit(solution)/shard_map/ppermute | solution.py:273
  165.7 11.4 %collective-permute-start.26 = (f32[5,64,128]{2,1,0:T(8,128)S(1)}, f32[5,64,128]{2,1,0:T(8,128)S(1)}, u32[]{:S(2)}, u32[]{:S(2)}) collective-permute-start(f32[5,64,128]{2,1,0:T(8,128)S(1)} %multiply_add_fusion.18), channel_id=1, source_target_pairs={{2,0},{4,2},{6,4},{8,6},{10,8},{12,10},{14,12},{16,14},{18,16},{20... | collective-permute-start | bytes 491528 | tf_op jit(solution)/shard_map/ppermute | solution.py:274
  (62 other events, 531.6 us)

commit v19 on v18

--- a/solution.py
+++ b/solution.py
@@ -179,7 +179,11 @@
         rounds.append((stride, list(range(1, radix))))
         stride *= radix
     longest_first = rounds[::-1]
-    return longest_first[0::2] + longest_first[1::2]
+    half = (len(longest_first) + 1) // 2
+    order = []
+    for index in range(half):
+        order += longest_first[index : index + 1] + longest_first[half + index : half + index + 1]
+    return order
 
 
 def scan_coefs(rise_step, fall_step, shift):

time: 183 us -> 186 us (1.016)
  the two profiles are of different devices: /device:TPU:30 before, /device:TPU:94 now
where the time goes in v19:
time: 186 us; the launch traced here: 185 us
  starting transfers between devices  81.3 us (44%)
  waiting for transfers between devices  63.2 us (34%)
  other arithmetic  14.7 us (8%)
  local copies, waits for them, and re-layouts  13.8 us (7%)
  matrix products  9.96 us (5%)
  between operations  2.03 us (1%)
    ppermute x12, waiting for transfers between devices, wall_apply(): from_above = lax.ppermute(fall, 'gy', down_pairs)  39.9 us
    ppermute x12, starting transfers between devices, wall_apply(): from_below = lax.ppermute(rise, 'gy', up_pairs)  38.3 us
    ppermute x12, starting transfers between devices, wall_apply(): from_above = lax.ppermute(fall, 'gy', down_pairs)  36.9 us
    ppermute x12, waiting for transfers between devices, wall_apply(): from_below = lax.ppermute(rise, 'gy', up_pairs)  18.3 us
    ppermute x1, waiting for transfers between devices, halo(): above = lax.ppermute(block[:, :width], 'gy', down_pairs)  5.03 us
    add x2, other arithmetic, wall_apply(): local + rise_gain[None, :, None, None] * rise[first:first + size, None]  4.9 us
    dot_general x2, matrix products, span_slope(): jnp.einsum('fyzx,zw->fywx', other, other_block, precision=HIGHEST)  4.43 us
  transfers between devices with their start and end apart: 28, of which 18 were waited for; matrix products, arithmetic and copies ran while one was open for 13% of the time, Pallas kernels for 0%

profile of v19, /device:TPU:94, one launch (start us, length us, event | category | flops | bytes accessed | tf_op | source)
XLA Modules:
  0.0 185.0 jit_solution(16646947368622938094)
XLA Ops:
  3.0 3.1 %collective-permute-start = (f32[5,3,64,128]{3,2,1,0:T(8,128)}, f32[5,3,64,128]{3,2,1,0:T(8,128)S(1)}, u32[]{:S(2)}, u32[]{:S(2)}) collective-permute-start(f32[5,3,64,128]{3,2,1,0:T(8,128)} %get-tuple-element.51), channel_id=1, source_target_pairs={{0,2},{2,4},{4,6},{6,8},{8,10},{10,12},{12,14},{14,16},{16,18},{18... | collective-permute-start | bytes 1474568 | tf_op jit(solution)/shard_map/ppermute | solution.py:301
  6.1 2.7 %collective-permute-start.1 = (f32[5,3,64,128]{3,2,1,0:T(8,128)}, f32[5,3,64,128]{3,2,1,0:T(8,128)S(1)}, u32[]{:S(2)}, u32[]{:S(2)}) collective-permute-start(f32[5,3,64,128]{3,2,1,0:T(8,128)} %get-tuple-element.52), channel_id=1, source_target_pairs={{2,0},{4,2},{6,4},{8,6},{10,8},{12,10},{14,12},{16,14},{18,16},{20... | collective-permute-start | bytes 1474568 | tf_op jit(solution)/shard_map/ppermute | solution.py:302
  20.1 5.0 %collective-permute-done.1 = f32[5,3,64,128]{3,2,1,0:T(8,128)S(1)} collective-permute-done((f32[5,3,64,128]{3,2,1,0:T(8,128)}, f32[5,3,64,128]{3,2,1,0:T(8,128)S(1)}, u32[]{:S(2)}, u32[]{:S(2)}) %collective-permute-start.1) | collective-permute-done | bytes 491552 | tf_op jit(solution)/shard_map/ppermute | solution.py:302
  29.1 6.1 %collective-permute-start.8 = (f32[9,64,128]{2,1,0:T(8,128)S(1)}, f32[9,64,128]{2,1,0:T(8,128)S(1)}, u32[]{:S(2)}, u32[]{:S(2)}) collective-permute-start(f32[9,64,128]{2,1,0:T(8,128)S(1)} %pad_maximum_fusion.8), channel_id=1, source_target_pairs={{64,0},{66,2},{68,4},{70,6},{72,8},{74,10},{76,12},{78,14},{80,16}... | collective-permute-start | bytes 884744 | tf_op jit(solution)/shard_map/ppermute | solution.py:278
  40.8 3.9 %collective-permute-start.9 = (f32[9,64,128]{2,1,0:T(8,128)S(1)}, f32[9,64,128]{2,1,0:T(8,128)S(1)}, u32[]{:S(2)}, u32[]{:S(2)}) collective-permute-start(f32[9,64,128]{2,1,0:T(8,128)S(1)} %multiply_add_fusion.9), channel_id=1, source_target_pairs={{8,0},{10,2},{12,4},{14,6},{16,8},{18,10},{20,12},{22,14},{24,16},... | collective-permute-start | bytes 884744 | tf_op jit(solution)/shard_map/ppermute | solution.py:278
  44.9 3.2 %collective-permute-done.3 = f32[9,64,128]{2,1,0:T(8,128)S(1)} collective-permute-done((f32[9,64,128]{2,1,0:T(8,128)S(1)}, f32[9,64,128]{2,1,0:T(8,128)S(1)}, u32[]{:S(2)}, u32[]{:S(2)}) %collective-permute-start.3) | collective-permute-done | bytes 294944 | tf_op jit(solution)/shard_map/ppermute | solution.py:277
  61.0 3.3 %collective-permute-start.11 = (f32[9,64,128]{2,1,0:T(8,128)S(1)}, f32[9,64,128]{2,1,0:T(8,128)S(1)}, u32[]{:S(2)}, u32[]{:S(2)}) collective-permute-start(f32[9,64,128]{2,1,0:T(8,128)S(1)} %multiply_add_fusion.7), channel_id=1, source_target_pairs={{4,0},{6,2},{8,4},{10,6},{12,8},{14,10},{16,12},{18,14},{20,16},{2... | collective-permute-start | bytes 884744 | tf_op jit(solution)/shard_map/ppermute | solution.py:278
  64.4 4.3 %collective-permute-done.5 = f32[9,64,128]{2,1,0:T(8,128)S(1)} collective-permute-done((f32[9,64,128]{2,1,0:T(8,128)S(1)}, f32[9,64,128]{2,1,0:T(8,128)S(1)}, u32[]{:S(2)}, u32[]{:S(2)}) %collective-permute-start.5) | collective-permute-done | bytes 294944 | tf_op jit(solution)/shard_map/ppermute | solution.py:277
  68.9 3.3 %collective-permute-start.6 = (f32[9,64,128]{2,1,0:T(8,128)S(1)}, f32[9,64,128]{2,1,0:T(8,128)S(1)}, u32[]{:S(2)}, u32[]{:S(2)}) collective-permute-start(f32[9,64,128]{2,1,0:T(8,128)S(1)} %multiply_add_fusion.12), channel_id=1, source_target_pairs={{0,16},{2,18},{4,20},{6,22},{8,24},{10,26},{12,28},{14,30},{16,32}... | collective-permute-start | bytes 884744 | tf_op jit(solution)/shard_map/ppermute | solution.py:277
  72.2 4.5 %collective-permute-done.11 = f32[9,64,128]{2,1,0:T(8,128)S(1)} collective-permute-done((f32[9,64,128]{2,1,0:T(8,128)S(1)}, f32[9,64,128]{2,1,0:T(8,128)S(1)}, u32[]{:S(2)}, u32[]{:S(2)}) %collective-permute-start.11) | collective-permute-done | bytes 294944 | tf_op jit(solution)/shard_map/ppermute | solution.py:278
  78.7 3.3 %collective-permute-done.6 = f32[9,64,128]{2,1,0:T(8,128)S(1)} collective-permute-done((f32[9,64,128]{2,1,0:T(8,128)S(1)}, f32[9,64,128]{2,1,0:T(8,128)S(1)}, u32[]{:S(2)}, u32[]{:S(2)}) %collective-permute-start.6) | collective-permute-done | bytes 294944 | tf_op jit(solution)/shard_map/ppermute | solution.py:277
  82.1 9.5 %collective-permute-start.7 = (f32[9,64,128]{2,1,0:T(8,128)S(1)}, f32[9,64,128]{2,1,0:T(8,128)S(1)}, u32[]{:S(2)}, u32[]{:S(2)}) collective-permute-start(f32[9,64,128]{2,1,0:T(8,128)S(1)} %multiply_add_fusion.11), channel_id=1, source_target_pairs={{0,2},{2,4},{4,6},{6,8},{8,10},{10,12},{12,14},{14,16},{16,18},{18... | collective-permute-start | bytes 884744 | tf_op jit(solution)/shard_map/ppermute | solution.py:277
  97.3 7.2 %collective-permute-done.13 = f32[9,64,128]{2,1,0:T(8,128)S(1)} collective-permute-done((f32[9,64,128]{2,1,0:T(8,128)S(1)}, f32[9,64,128]{2,1,0:T(8,128)S(1)}, u32[]{:S(2)}, u32[]{:S(2)}) %collective-permute-start.13) | collective-permute-done | bytes 294944 | tf_op jit(solution)/shard_map/ppermute | solution.py:278
  110.1 6.1 %collective-permute-start.21 = (f32[5,64,128]{2,1,0:T(8,128)S(1)}, f32[5,64,128]{2,1,0:T(8,128)S(1)}, u32[]{:S(2)}, u32[]{:S(2)}) collective-permute-start(f32[5,64,128]{2,1,0:T(8,128)S(1)} %get-tuple-element.64), channel_id=1, source_target_pairs={{64,0},{66,2},{68,4},{70,6},{72,8},{74,10},{76,12},{78,14},{80,16}... | collective-permute-start | bytes 491528 | tf_op jit(solution)/shard_map/ppermute | solution.py:278
  118.2 2.9 %multiply_add_fusion.1 = f32[5,8,64,128]{3,2,1,0:T(8,128)} fusion(f32[5,64,128]{2,1,0:T(8,128)S(1)} %slice-done.1, f32[8]{0:T(128)S(1)} %copy-done.40, f32[5,64,128]{2,1,0:T(8,128)S(1)} %slice-done, f32[8]{0:T(128)S(1)} %copy-done.39, f32[5,64,128]{2,1,0:T(8,128)S(1)} %get-tuple-element.59, f32[8]{0:T(128)S(1)} %copy-done.26, ...), kind=kLoop, calls=%fused_computation.43 | loop fusion | flops 10158080 | bytes 3932672 | tf_op jit(solution)/shard_map/add | solution.py:289
  125.9 3.9 %collective-permute-start.22 = (f32[5,64,128]{2,1,0:T(8,128)S(1)}, f32[5,64,128]{2,1,0:T(8,128)S(1)}, u32[]{:S(2)}, u32[]{:S(2)}) collective-permute-start(f32[5,64,128]{2,1,0:T(8,128)S(1)} %get-tuple-element.62), channel_id=1, source_target_pairs={{8,0},{10,2},{12,4},{14,6},{16,8},{18,10},{20,12},{22,14},{24,16},... | collective-permute-start | bytes 491528 | tf_op jit(solution)/shard_map/ppermute | solution.py:278
  133.0 3.6 %collective-permute-done.22 = f32[5,64,128]{2,1,0:T(8,128)S(1)} collective-permute-done((f32[5,64,128]{2,1,0:T(8,128)S(1)}, f32[5,64,128]{2,1,0:T(8,128)S(1)}, u32[]{:S(2)}, u32[]{:S(2)}) %collective-permute-start.22) | collective-permute-done | bytes 163872 | tf_op jit(solution)/shard_map/ppermute | solution.py:278
  138.8 3.3 %collective-permute-start.18 = (f32[5,64,128]{2,1,0:T(8,128)S(1)}, f32[5,64,128]{2,1,0:T(8,128)S(1)}, u32[]{:S(2)}, u32[]{:S(2)}) collective-permute-start(f32[5,64,128]{2,1,0:T(8,128)S(1)} %multiply_add_fusion.26), channel_id=1, source_target_pairs={{0,4},{2,6},{4,8},{6,10},{8,12},{10,14},{12,16},{14,18},{16,20},{1... | collective-permute-start | bytes 491528 | tf_op jit(solution)/shard_map/ppermute | solution.py:277
  148.2 2.9 %collective-permute-start.19 = (f32[5,64,128]{2,1,0:T(8,128)S(1)}, f32[5,64,128]{2,1,0:T(8,128)S(1)}, u32[]{:S(2)}, u32[]{:S(2)}) collective-permute-start(f32[5,64,128]{2,1,0:T(8,128)S(1)} %multiply_add_fusion.25), channel_id=1, source_target_pairs={{0,16},{2,18},{4,20},{6,22},{8,24},{10,26},{12,28},{14,30},{16,32}... | collective-permute-start | bytes 491528 | tf_op jit(solution)/shard_map/ppermute | solution.py:277
  151.1 6.4 %collective-permute-done.24 = f32[5,64,128]{2,1,0:T(8,128)S(1)} collective-permute-done((f32[5,64,128]{2,1,0:T(8,128)S(1)}, f32[5,64,128]{2,1,0:T(8,128)S(1)}, u32[]{:S(2)}, u32[]{:S(2)}) %collective-permute-start.24) | collective-permute-done | bytes 163872 | tf_op jit(solution)/shard_map/ppermute | solution.py:278
  159.6 6.7 %collective-permute-start.20 = (f32[5,64,128]{2,1,0:T(8,128)S(1)}, f32[5,64,128]{2,1,0:T(8,128)S(1)}, u32[]{:S(2)}, u32[]{:S(2)}) collective-permute-start(f32[5,64,128]{2,1,0:T(8,128)S(1)} %multiply_add_fusion.24), channel_id=1, source_target_pairs={{0,2},{2,4},{4,6},{6,8},{8,10},{10,12},{12,14},{14,16},{16,18},{18... | collective-permute-start | bytes 491528 | tf_op jit(solution)/shard_map/ppermute | solution.py:277
  166.3 2.6 %collective-permute-done.25 = f32[5,64,128]{2,1,0:T(8,128)S(1)} collective-permute-done((f32[5,64,128]{2,1,0:T(8,128)S(1)}, f32[5,64,128]{2,1,0:T(8,128)S(1)}, u32[]{:S(2)}, u32[]{:S(2)}) %collective-permute-start.25) | collective-permute-done | bytes 163872 | tf_op jit(solution)/shard_map/ppermute | solution.py:278
  171.1 9.4 %collective-permute-done.26 = f32[5,64,128]{2,1,0:T(8,128)S(1)} collective-permute-done((f32[5,64,128]{2,1,0:T(8,128)S(1)}, f32[5,64,128]{2,1,0:T(8,128)S(1)}, u32[]{:S(2)}, u32[]{:S(2)}) %collective-permute-start.26) | collective-permute-done | bytes 163872 | tf_op jit(solution)/shard_map/ppermute | solution.py:278
  180.7 2.9 %fusion.4 = f32[5,8,64,128]{3,2,1,0:T(8,128)S(1)} fusion(f32[5,8,128,64]{2,3,1,0:T(8,128)S(1)} %fusion.89, f32[5,8,64,128]{3,2,1,0:T(8,128)S(1)} %collective-permute-done.27, f32[64,64,1,1]{0,1,3,2:T(8,128)S(1)} %copy-done.9, f32[5,8,64,128]{3,2,1,0:T(8,128)S(1)} %fusion.88, f32[5,64,128]{2,1,0:T(8,128)S(1)} %multiply_add_fusion.17, f32[8]{0:T(128)S(1)} %copy-done.54, ...), kind=kOutput, calls=%fused_computation.39 | convolution fusion | flops 261816320 | bytes 7553472 | tf_op jit(solution)/shard_map/fyzx,zw->fywx/dot_general | solution.py:315
  (237 shorter events, 72.8 us)
Async XLA Ops:
  3.0 17.1 %collective-permute-start = (f32[5,3,64,128]{3,2,1,0:T(8,128)}, f32[5,3,64,128]{3,2,1,0:T(8,128)S(1)}, u32[]{:S(2)}, u32[]{:S(2)}) collective-permute-start(f32[5,3,64,128]{3,2,1,0:T(8,128)} %get-tuple-element.51), channel_id=1, source_target_pairs={{0,2},{2,4},{4,6},{6,8},{8,10},{10,12},{12,14},{14,16},{16,18},{18... | collective-permute-start | bytes 1474568 | tf_op jit(solution)/shard_map/ppermute | solution.py:301
  6.1 19.0 %collective-permute-start.1 = (f32[5,3,64,128]{3,2,1,0:T(8,128)}, f32[5,3,64,128]{3,2,1,0:T(8,128)S(1)}, u32[]{:S(2)}, u32[]{:S(2)}) collective-permute-start(f32[5,3,64,128]{3,2,1,0:T(8,128)} %get-tuple-element.52), channel_id=1, source_target_pairs={{2,0},{4,2},{6,4},{8,6},{10,8},{12,10},{14,12},{16,14},{18,16},{20... | collective-permute-start | bytes 1474568 | tf_op jit(solution)/shard_map/ppermute | solution.py:302
  27.7 11.0 %collective-permute-start.2 = (f32[9,64,128]{2,1,0:T(8,128)S(1)}, f32[9,64,128]{2,1,0:T(8,128)S(1)}, u32[]{:S(2)}, u32[]{:S(2)}) collective-permute-start(f32[9,64,128]{2,1,0:T(8,128)S(1)} %pad_maximum_fusion.7), channel_id=1, source_target_pairs={{0,64},{2,66},{4,68},{6,70},{8,72},{10,74},{12,76},{14,78},{16,80}... | collective-permute-start | bytes 884744 | tf_op jit(solution)/shard_map/ppermute | solution.py:277
  29.1 11.7 %collective-permute-start.8 = (f32[9,64,128]{2,1,0:T(8,128)S(1)}, f32[9,64,128]{2,1,0:T(8,128)S(1)}, u32[]{:S(2)}, u32[]{:S(2)}) collective-permute-start(f32[9,64,128]{2,1,0:T(8,128)S(1)} %pad_maximum_fusion.8), channel_id=1, source_target_pairs={{64,0},{66,2},{68,4},{70,6},{72,8},{74,10},{76,12},{78,14},{80,16}... | collective-permute-start | bytes 884744 | tf_op jit(solution)/shard_map/ppermute | solution.py:278
  35.2 58.7 %collective-permute-start.14 = (f32[4,12,64,128]{3,2,1,0:T(8,128)S(1)}, f32[4,12,64,128]{3,2,1,0:T(8,128)S(1)}, u32[]{:S(2)}, u32[]{:S(2)}) collective-permute-start(f32[4,12,64,128]{3,2,1,0:T(8,128)S(1)} %fusion.1), channel_id=1, source_target_pairs={{0,1},{1,0},{2,3},{3,2},{4,5},{5,4},{6,7},{7,6},{8,9},{9,8},{10,11... | collective-permute-start | bytes 4718600 | tf_op jit(solution)/shard_map/ppermute | solution.py:314
  38.8 9.3 %collective-permute-start.3 = (f32[9,64,128]{2,1,0:T(8,128)S(1)}, f32[9,64,128]{2,1,0:T(8,128)S(1)}, u32[]{:S(2)}, u32[]{:S(2)}) collective-permute-start(f32[9,64,128]{2,1,0:T(8,128)S(1)} %multiply_add_fusion.15), channel_id=1, source_target_pairs={{0,8},{2,10},{4,12},{6,14},{8,16},{10,18},{12,20},{14,22},{16,24},... | collective-permute-start | bytes 884744 | tf_op jit(solution)/shard_map/ppermute | solution.py:277
  40.8 11.4 %collective-permute-start.9 = (f32[9,64,128]{2,1,0:T(8,128)S(1)}, f32[9,64,128]{2,1,0:T(8,128)S(1)}, u32[]{:S(2)}, u32[]{:S(2)}) collective-permute-start(f32[9,64,128]{2,1,0:T(8,128)S(1)} %multiply_add_fusion.9), channel_id=1, source_target_pairs={{8,0},{10,2},{12,4},{14,6},{16,8},{18,10},{20,12},{22,14},{24,16},... | collective-permute-start | bytes 884744 | tf_op jit(solution)/shard_map/ppermute | solution.py:278
  48.2 8.6 %collective-permute-start.4 = (f32[9,64,128]{2,1,0:T(8,128)S(1)}, f32[9,64,128]{2,1,0:T(8,128)S(1)}, u32[]{:S(2)}, u32[]{:S(2)}) collective-permute-start(f32[9,64,128]{2,1,0:T(8,128)S(1)} %multiply_add_fusion.14), channel_id=1, source_target_pairs={{0,32},{2,34},{4,36},{6,38},{8,40},{10,42},{12,44},{14,46},{16,48}... | collective-permute-start | bytes 884744 | tf_op jit(solution)/shard_map/ppermute | solution.py:277
  56.9 11.9 %collective-permute-start.5 = (f32[9,64,128]{2,1,0:T(8,128)S(1)}, f32[9,64,128]{2,1,0:T(8,128)S(1)}, u32[]{:S(2)}, u32[]{:S(2)}) collective-permute-start(f32[9,64,128]{2,1,0:T(8,128)S(1)} %multiply_add_fusion.13), channel_id=1, source_target_pairs={{0,4},{2,6},{4,8},{6,10},{8,12},{10,14},{12,16},{14,18},{16,20},{1... | collective-permute-start | bytes 884744 | tf_op jit(solution)/shard_map/ppermute | solution.py:277
  61.0 15.6 %collective-permute-start.11 = (f32[9,64,128]{2,1,0:T(8,128)S(1)}, f32[9,64,128]{2,1,0:T(8,128)S(1)}, u32[]{:S(2)}, u32[]{:S(2)}) collective-permute-start(f32[9,64,128]{2,1,0:T(8,128)S(1)} %multiply_add_fusion.7), channel_id=1, source_target_pairs={{4,0},{6,2},{8,4},{10,6},{12,8},{14,10},{16,12},{18,14},{20,16},{2... | collective-permute-start | bytes 884744 | tf_op jit(solution)/shard_map/ppermute | solution.py:278
  68.9 13.1 %collective-permute-start.6 = (f32[9,64,128]{2,1,0:T(8,128)S(1)}, f32[9,64,128]{2,1,0:T(8,128)S(1)}, u32[]{:S(2)}, u32[]{:S(2)}) collective-permute-start(f32[9,64,128]{2,1,0:T(8,128)S(1)} %multiply_add_fusion.12), channel_id=1, source_target_pairs={{0,16},{2,18},{4,20},{6,22},{8,24},{10,26},{12,28},{14,30},{16,32}... | collective-permute-start | bytes 884744 | tf_op jit(solution)/shard_map/ppermute | solution.py:277
  76.7 14.8 %collective-permute-start.12 = (f32[9,64,128]{2,1,0:T(8,128)S(1)}, f32[9,64,128]{2,1,0:T(8,128)S(1)}, u32[]{:S(2)}, u32[]{:S(2)}) collective-permute-start(f32[9,64,128]{2,1,0:T(8,128)S(1)} %multiply_add_fusion.6), channel_id=1, source_target_pairs={{16,0},{18,2},{20,4},{22,6},{24,8},{26,10},{28,12},{30,14},{32,16}... | collective-permute-start | bytes 884744 | tf_op jit(solution)/shard_map/ppermute | solution.py:278
  82.1 15.1 %collective-permute-start.7 = (f32[9,64,128]{2,1,0:T(8,128)S(1)}, f32[9,64,128]{2,1,0:T(8,128)S(1)}, u32[]{:S(2)}, u32[]{:S(2)}) collective-permute-start(f32[9,64,128]{2,1,0:T(8,128)S(1)} %multiply_add_fusion.11), channel_id=1, source_target_pairs={{0,2},{2,4},{4,6},{6,8},{8,10},{10,12},{12,14},{14,16},{16,18},{18... | collective-permute-start | bytes 884744 | tf_op jit(solution)/shard_map/ppermute | solution.py:277
  91.7 12.8 %collective-permute-start.13 = (f32[9,64,128]{2,1,0:T(8,128)S(1)}, f32[9,64,128]{2,1,0:T(8,128)S(1)}, u32[]{:S(2)}, u32[]{:S(2)}) collective-permute-start(f32[9,64,128]{2,1,0:T(8,128)S(1)} %multiply_add_fusion.5), channel_id=1, source_target_pairs={{2,0},{4,2},{6,4},{8,6},{10,8},{12,10},{14,12},{16,14},{18,16},{20... | collective-permute-start | bytes 884744 | tf_op jit(solution)/shard_map/ppermute | solution.py:278
  108.8 13.6 %collective-permute-start.15 = (f32[5,64,128]{2,1,0:T(8,128)S(1)}, f32[5,64,128]{2,1,0:T(8,128)S(1)}, u32[]{:S(2)}, u32[]{:S(2)}) collective-permute-start(f32[5,64,128]{2,1,0:T(8,128)S(1)} %get-tuple-element.63), channel_id=1, source_target_pairs={{0,64},{2,66},{4,68},{6,70},{8,72},{10,74},{12,76},{14,78},{16,80}... | collective-permute-start | bytes 491528 | tf_op jit(solution)/shard_map/ppermute | solution.py:277
  110.1 12.3 %collective-permute-start.21 = (f32[5,64,128]{2,1,0:T(8,128)S(1)}, f32[5,64,128]{2,1,0:T(8,128)S(1)}, u32[]{:S(2)}, u32[]{:S(2)}) collective-permute-start(f32[5,64,128]{2,1,0:T(8,128)S(1)} %get-tuple-element.64), channel_id=1, source_target_pairs={{64,0},{66,2},{68,4},{70,6},{72,8},{74,10},{76,12},{78,14},{80,16}... | collective-permute-start | bytes 491528 | tf_op jit(solution)/shard_map/ppermute | solution.py:278
  117.0 63.6 %collective-permute-start.27 = (f32[5,8,64,128]{3,2,1,0:T(8,128)S(1)}, f32[5,8,64,128]{3,2,1,0:T(8,128)S(1)}, u32[]{:S(2)}, u32[]{:S(2)}) collective-permute-start(f32[5,8,64,128]{3,2,1,0:T(8,128)S(1)} %fusion.34), channel_id=1, source_target_pairs={{0,1},{1,0},{2,3},{3,2},{4,5},{5,4},{6,7},{7,6},{8,9},{9,8},{10,11... | collective-permute-start | bytes 3932168 | tf_op jit(solution)/shard_map/ppermute | solution.py:314
  125.9 10.6 %collective-permute-start.22 = (f32[5,64,128]{2,1,0:T(8,128)S(1)}, f32[5,64,128]{2,1,0:T(8,128)S(1)}, u32[]{:S(2)}, u32[]{:S(2)}) collective-permute-start(f32[5,64,128]{2,1,0:T(8,128)S(1)} %get-tuple-element.62), channel_id=1, source_target_pairs={{8,0},{10,2},{12,4},{14,6},{16,8},{18,10},{20,12},{22,14},{24,16},... | collective-permute-start | bytes 491528 | tf_op jit(solution)/shard_map/ppermute | solution.py:278
  138.8 9.2 %collective-permute-start.18 = (f32[5,64,128]{2,1,0:T(8,128)S(1)}, f32[5,64,128]{2,1,0:T(8,128)S(1)}, u32[]{:S(2)}, u32[]{:S(2)}) collective-permute-start(f32[5,64,128]{2,1,0:T(8,128)S(1)} %multiply_add_fusion.26), channel_id=1, source_target_pairs={{0,4},{2,6},{4,8},{6,10},{8,12},{10,14},{12,16},{14,18},{16,20},{1... | collective-permute-start | bytes 491528 | tf_op jit(solution)/shard_map/ppermute | solution.py:277
  144.4 13.1 %collective-permute-start.24 = (f32[5,64,128]{2,1,0:T(8,128)S(1)}, f32[5,64,128]{2,1,0:T(8,128)S(1)}, u32[]{:S(2)}, u32[]{:S(2)}) collective-permute-start(f32[5,64,128]{2,1,0:T(8,128)S(1)} %multiply_add_fusion.20), channel_id=1, source_target_pairs={{4,0},{6,2},{8,4},{10,6},{12,8},{14,10},{16,12},{18,14},{20,16},{2... | collective-permute-start | bytes 491528 | tf_op jit(solution)/shard_map/ppermute | solution.py:278
  148.2 11.3 %collective-permute-start.19 = (f32[5,64,128]{2,1,0:T(8,128)S(1)}, f32[5,64,128]{2,1,0:T(8,128)S(1)}, u32[]{:S(2)}, u32[]{:S(2)}) collective-permute-start(f32[5,64,128]{2,1,0:T(8,128)S(1)} %multiply_add_fusion.25), channel_id=1, source_target_pairs={{0,16},{2,18},{4,20},{6,22},{8,24},{10,26},{12,28},{14,30},{16,32}... | collective-permute-start | bytes 491528 | tf_op jit(solution)/shard_map/ppermute | solution.py:277
  157.6 11.4 %collective-permute-start.25 = (f32[5,64,128]{2,1,0:T(8,128)S(1)}, f32[5,64,128]{2,1,0:T(8,128)S(1)}, u32[]{:S(2)}, u32[]{:S(2)}) collective-permute-start(f32[5,64,128]{2,1,0:T(8,128)S(1)} %multiply_add_fusion.19), channel_id=1, source_target_pairs={{16,0},{18,2},{20,4},{22,6},{24,8},{26,10},{28,12},{30,14},{32,16}... | collective-permute-start | bytes 491528 | tf_op jit(solution)/shard_map/ppermute | solution.py:278
  159.6 11.4 %collective-permute-start.20 = (f32[5,64,128]{2,1,0:T(8,128)S(1)}, f32[5,64,128]{2,1,0:T(8,128)S(1)}, u32[]{:S(2)}, u32[]{:S(2)}) collective-permute-start(f32[5,64,128]{2,1,0:T(8,128)S(1)} %multiply_add_fusion.24), channel_id=1, source_target_pairs={{0,2},{2,4},{4,6},{6,8},{8,10},{10,12},{12,14},{14,16},{16,18},{18... | collective-permute-start | bytes 491528 | tf_op jit(solution)/shard_map/ppermute | solution.py:277
  169.0 11.4 %collective-permute-start.26 = (f32[5,64,128]{2,1,0:T(8,128)S(1)}, f32[5,64,128]{2,1,0:T(8,128)S(1)}, u32[]{:S(2)}, u32[]{:S(2)}) collective-permute-start(f32[5,64,128]{2,1,0:T(8,128)S(1)} %multiply_add_fusion.18), channel_id=1, source_target_pairs={{2,0},{4,2},{6,4},{8,6},{10,8},{12,10},{14,12},{16,14},{18,16},{20... | collective-permute-start | bytes 491528 | tf_op jit(solution)/shard_map/ppermute | solution.py:278
  (62 other events, 589.2 us)
